TPU v7x, 32 devices: a whole 2x2x4 slice. The times are simulated.
32 devices in a mesh: ctx: 8 (over z, core), head: 4 (over y, x).
Axes of the slice: x: 2, y: 2, z: 4, core: 2. Of those that a mesh axis runs over, the one named last changes fastest.
Arguments:
- queries: bfloat16 [4096, 4096], P('ctx', 'head'), may hold values from -6 to 6
- keys: bfloat16 [4096, 4096], P('ctx', 'head'), may hold values from -6 to 6
- values: bfloat16 [4096, 4096], P('ctx', 'head'), may hold values from -6 to 6
- output_grad: bfloat16 [4096, 4096], P('ctx', 'head'), may hold values from -0.09375 to 0.09375
- out_weight: bfloat16 [4096, 4096], P('head'), may hold values from -0.09375 to 0.09375
Outputs:
- grad_queries: bfloat16 [4096, 4096], P('ctx', 'head')
- grad_keys: bfloat16 [4096, 4096], P('ctx', 'head')
- grad_values: bfloat16 [4096, 4096], P('ctx', 'head')
All inputs are finite; a program needn't handle non-finite values.
Results may differ from a plain program's by a relative error of at most 0.01.
Values may be sent and summed in bfloat16 or wider, within the bound.
No kernel may reach another device: no remote copies, remote signals or barrier semaphores. Data moves between devices by JAX's collectives and lax.ppermute only.
A program may use at most 64 MiB of HBM per device.

v0:
```python
import jax
import jax.numpy as jnp
from jax import lax
from jax.sharding import PartitionSpec as P

DH = 128


def entering(shard, axis, combine, identity, reverse):
    size, position = (lax.axis_size(axis), lax.axis_index(axis))
    everything = lax.all_gather(shard.astype(jnp.bfloat16), axis)
    start = jnp.broadcast_to(jnp.asarray(identity, shard.dtype), shard.shape)

    def hop(k, before):
        at = size - 1 - k if reverse else k
        reached = at > position if reverse else at < position
        new = combine(before, everything[at].astype(shard.dtype))
        return jnp.where(reached, new, before)

    return lax.fori_loop(0, size, hop, start)


def combine_add(earlier, later):
    return earlier + later


def shards(queries, keys, values, output_grad, out_weight):
    row_count = queries.shape[0]
    width = queries.shape[1]
    heads = width // DH
    block_len = min(row_count, 512)
    blocks = row_count // block_len
    scale_factor = DH ** (-0.5)
    highest = lax.Precision.HIGHEST
    grad_heads = lax.dot_general(
        lax.all_gather(output_grad, "head", axis=1, tiled=True),
        out_weight,
        (((1,), (1,)), ((), ())),
        preferred_element_type=jnp.float32,
    ).astype(jnp.bfloat16)
    shape = (blocks, block_len, heads, DH)
    q_blocks = queries.reshape(shape)
    k_blocks = keys.reshape(shape)
    v_blocks = values.reshape(shape)
    g_blocks = grad_heads.reshape(shape)
    kv_blocks = jnp.einsum(
        "nshd,nshe->nhde", k_blocks, v_blocks, preferred_element_type=jnp.float32
    )
    qg_blocks = jnp.einsum(
        "nthd,nthe->nhde", q_blocks, g_blocks, preferred_element_type=jnp.float32
    )
    kv_running = jnp.cumsum(kv_blocks, axis=0)
    qg_running = jnp.flip(jnp.cumsum(jnp.flip(qg_blocks, 0), axis=0), 0)
    kv_total = kv_running[-1]
    qg_total = qg_running[0]
    zeros = jnp.zeros_like(kv_total)
    kv_before = entering(kv_total, "ctx", combine_add, zeros, False)
    qg_after = entering(qg_total, "ctx", combine_add, zeros, True)
    kv_entry = kv_before[None] + kv_running - kv_blocks
    qg_entry = qg_after[None] + qg_running - qg_blocks
    rows = jnp.arange(block_len)
    causal = (rows[:, None] >= rows[None, :])[None, None]
    score_grad = (
        jnp.einsum("nthe,nshe->nhts", g_blocks, v_blocks, preferred_element_type=jnp.float32)
        * scale_factor
    )
    score_grad = jnp.where(causal, score_grad, 0.0).astype(jnp.bfloat16)
    score_fwd = (
        jnp.einsum("nthd,nshd->nhts", q_blocks, k_blocks, preferred_element_type=jnp.float32)
        * scale_factor
    )
    score_fwd = jnp.where(causal, score_fwd, 0.0).astype(jnp.bfloat16)
    grad_q = jnp.einsum("nhts,nshd->nthd", score_grad, k_blocks, preferred_element_type=jnp.float32)
    grad_q = grad_q + scale_factor * jnp.einsum(
        "nthe,nhde->nthd", g_blocks.astype(jnp.float32), kv_entry, precision=highest
    )
    grad_k = jnp.einsum("nhts,nthd->nshd", score_grad, q_blocks, preferred_element_type=jnp.float32)
    grad_k = grad_k + scale_factor * jnp.einsum(
        "nshe,nhde->nshd", v_blocks.astype(jnp.float32), qg_entry, precision=highest
    )
    grad_v = jnp.einsum("nhts,nthe->nshe", score_fwd, g_blocks, preferred_element_type=jnp.float32)
    grad_v = grad_v + scale_factor * jnp.einsum(
        "nshd,nhde->nshe", k_blocks.astype(jnp.float32), qg_entry, precision=highest
    )
    flat = (row_count, width)
    return (
        grad_q.reshape(flat).astype(jnp.bfloat16),
        grad_k.reshape(flat).astype(jnp.bfloat16),
        grad_v.reshape(flat).astype(jnp.bfloat16),
    )


def solution(mesh):
    return jax.shard_map(
        shards,
        mesh=mesh,
        in_specs=(
            P("ctx", "head"),
            P("ctx", "head"),
            P("ctx", "head"),
            P("ctx", "head"),
            P("head", None),
        ),
        out_specs=(P("ctx", "head"), P("ctx", "head"), P("ctx", "head")),
        check_vma=False,
    )
```

profile of v0, /device:TPU:0, one launch (start us, length us, event | category | flops | bytes accessed | tf_op | source)
XLA Modules:
  0.0 156.4 jit_solution(4270446481108130848)
XLA Ops:
  8.4 2.6 %fusion.37 = (bf16[8,128,128]{2,1,0:T(8,128)(2,1)}, f32[8,128,128]{2,1,0:T(8,128)}) fusion(bf16[512,1024]{1,0:T(8,128)(2,1)S(1)} %copy-done, bf16[512,1024]{1,0:T(8,128)(2,1)} %param.10), kind=kOutput, calls=%fused_computation.44 | convolution fusion | flops 134348800 | bytes 2883584 | tf_op jit(solution)/shard_map/nshd,nshe->nhde/dot_general | solution.py:46
  11.9 53.4 %all-gather.6.cloned.1.call-done = bf16[512,4096]{1,0:T(8,128)(2,1)} async-done(((bf16[512,1024]{1,0:T(8,128)(2,1)}), bf16[512,4096]{1,0:T(8,128)(2,1)}) %all-gather.6.cloned.1.call-update) | async-done | bytes 4194320 | tf_op jit(solution)/shard_map/all_gather | solution.py:36
  65.3 10.1 %convolution_convert_fusion = bf16[512,1024]{1,0:T(8,128)(2,1)} fusion(bf16[512,4096]{1,0:T(8,128)(2,1)} %all-gather.6.cloned.1.call-done, bf16[1024,4096]{1,0:T(8,128)(2,1)} %param.13), kind=kOutput, calls=%fused_computation.14 | convolution fusion | flops 4295491584 | bytes 13631488 | tf_op jit(solution)/shard_map/dot_general | solution.py:35
  75.4 1.5 copy.45
  77.0 2.9 %fusion.38 = (bf16[8,128,128]{1,2,0:T(8,128)(2,1)S(1)}, f32[8,128,128]{1,2,0:T(8,128)}) fusion(bf16[512,8,128]{0,2,1:T(8,128)(2,1)S(1)} %bitcast.112, bf16[512,1024]{1,0:T(8,128)(2,1)} %param.9), kind=kOutput, calls=%fused_computation.45 | convolution fusion | flops 134348800 | bytes 2883584 | tf_op jit(solution)/shard_map/nthd,nthe->nhde/dot_general | solution.py:49
  80.7 15.3 %all-gather.8.cloned.1.call-done = bf16[64,128,128]{2,1,0:T(8,128)(2,1)} async-done(((bf16[8,128,128]{2,1,0:T(8,128)(2,1)}), bf16[64,128,128]{2,1,0:T(8,128)(2,1)}) %all-gather.8.cloned.1.call-update) | async-done | bytes 2097168 | tf_op jit(solution)/shard_map/all_gather | solution.py:11
  96.0 10.1 %while.30 = (s32[]{:T(128)}, f32[8,128,128]{2,1,0:T(8,128)S(1)}, s32[]{:T(128)}, bf16[8,8,128,128]{3,2,1,0:T(8,128)(2,1)}, s32[]{:T(128)}, /*index=5*/s32[]{:T(128)}) while((s32[]{:T(128)}, f32[8,128,128]{2,1,0:T(8,128)S(1)}, s32[]{:T(128)}, bf16[8,8,128,128]{3,2,1,0:T(8,128)(2,1)}, s32[]{:T(128)}, /*index=5*/s32[]{:T(128)}) %tuple.89), condition=%wide.region_1.2_spmd.clone, body=%wide.region_0.0_spmd.clone.sunk | while | flops 524292 | bytes 1310821 | solution.py:20
  98.5 1.2 add_select_fusion.4
  99.8 1.2 add_select_fusion.4
  101.1 1.2 add_select_fusion.4
  103.6 1.2 add_select_fusion.4
  104.8 1.3 add_select_fusion.4
  106.1 2.8 %select_convert_fusion.1 = bf16[8,512,512]{2,1,0:T(8,128)(2,1)S(1)} fusion(pred[512,512]{1,0:T(8,128)(4,1)S(1)} %copy-done.8, bf16[512,8,128]{0,2,1:T(8,128)(2,1)} %bitcast.113, bf16[512,1024]{1,0:T(8,128)(2,1)S(1)} %copy-done), kind=kOutput, calls=%fused_computation.3 | convolution fusion | flops 543162368 | bytes 6553600 | tf_op jit(solution)/shard_map/nthe,nshe->nhts/dot_general | solution.py:64
  109.0 1.5 fusion.16
  111.6 2.2 %fusion.7 = bf16[8,128,512]{2,1,0:T(8,128)(2,1)} fusion(f32[8,512,128]{1,2,0:T(8,128)S(1)} %fusion.16, bf16[512,8,128]{0,2,1:T(8,128)(2,1)S(1)} %bitcast.115, f32[8,128,128]{2,1,0:T(8,128)S(1)} %copy-done.7, f32[8,128,128]{2,1,0:T(8,128)S(1)} %get-tuple-element.192), kind=kOutput, calls=%fused_computation.12 | convolution fusion | flops 807141376 | bytes 5242880 | tf_op jit(solution)/shard_map/nthe,nhde->nthd/dot_general | solution.py:74
  113.7 2.3 %copy.41 = bf16[512,1024]{1,0:T(8,128)(2,1)} copy(bf16[512,1024]{0,1:T(8,128)(2,1)} %bitcast.116) | data formatting | bytes 2097152
  116.0 4.9 %fusion = f32[8,128,512]{2,1,0:T(8,128)} fusion(bf16[512,8,128]{0,2,1:T(8,128)(2,1)} %bitcast.114, pred[512,512]{1,0:T(8,128)(4,1)S(1)} %copy-done.8, bf16[512,1024]{1,0:T(8,128)(2,1)} %param.9, bf16[512,1024]{1,0:T(8,128)(2,1)S(1)} %copy-done.2), kind=kOutput, calls=%fused_computation.4 | convolution fusion | flops 1080033280 | bytes 5505024 | tf_op jit(solution)/shard_map/nhts,nthe->nshe/dot_general | solution.py:81
  120.9 5.4 %all-gather.10.cloned.1.call-done = bf16[64,128,128]{2,1,0:T(8,128)(2,1)} async-done(((bf16[8,128,128]{2,1,0:T(8,128)(2,1)}), bf16[64,128,128]{2,1,0:T(8,128)(2,1)}) %all-gather.10.cloned.1.call-update) | async-done | bytes 2097168 | tf_op jit(solution)/shard_map/all_gather | solution.py:11
  126.3 10.1 %while.31 = (s32[]{:T(128)}, f32[8,128,128]{2,1,0:T(8,128)S(1)}, s32[]{:T(128)}, bf16[8,8,128,128]{3,2,1,0:T(8,128)(2,1)}, s32[]{:T(128)}, /*index=5*/s32[]{:T(128)}, s32[]{:T(128)}, s32[]{:T(128)}) while((s32[]{:T(128)}, f32[8,128,128]{2,1,0:T(8,128)S(1)}, s32[]{:T(128)}, bf16[8,8,128,128]{3,2,1,0:T(8,128)(2,1)}, s32[]{:T(128)}, ...), condition=%wide.region_3.4_spmd.clone, body=%wide.region_2.3_spmd.clone.sunk | while | flops 524296 | bytes 1310883 | solution.py:20
  136.6 3.6 %fusion.19 = f32[8,128,512]{2,1,0:T(8,128)} fusion(f32[8,128,128]{1,2,0:T(8,128)} %get-tuple-element.253, f32[8,128,128]{1,2,0:T(8,128)S(1)} %copy.36, bf16[512,1024]{1,0:T(8,128)(2,1)S(1)} %copy-done), kind=kOutput, calls=%fused_computation.25 | convolution fusion | flops 805568512 | bytes 4194304 | tf_op jit(solution)/shard_map/nshe,nhde->nshd/dot_general | solution.py:78
  140.1 2.1 %add_convert_fusion = bf16[8,128,512]{2,1,0:T(8,128)(2,1)} fusion(f32[8,128,512]{2,1,0:T(8,128)S(1)} %copy-done.6, f32[8,128,128]{1,2,0:T(8,128)S(1)} %copy-done.5, f32[8,128,128]{1,2,0:T(8,128)S(1)} %copy.36, bf16[512,1024]{1,0:T(8,128)(2,1)S(1)} %copy-done.2), kind=kOutput, calls=%fused_computation.13 | convolution fusion | flops 807141376 | bytes 5242880 | tf_op jit(solution)/shard_map/nshd,nhde->nshe/dot_general | solution.py:82
  142.3 2.3 %copy.43 = bf16[512,1024]{1,0:T(8,128)(2,1)} copy(bf16[512,1024]{0,1:T(8,128)(2,1)} %bitcast.117) | data formatting | bytes 2097152
  144.6 4.0 %fusion.6 = bf16[8,128,512]{2,1,0:T(8,128)(2,1)S(1)} fusion(f32[8,128,512]{2,1,0:T(8,128)} %fusion.19, bf16[8,512,512]{2,1,0:T(8,128)(2,1)} %copy-done.1, bf16[512,1024]{1,0:T(8,128)(2,1)} %param.9), kind=kOutput, calls=%fused_computation.10 | convolution fusion | flops 538443776 | bytes 8388608 | tf_op jit(solution)/shard_map/nhts,nthd->nshd/dot_general | solution.py:77
  148.6 1.3 copy.42
  (40 shorter events, 17.7 us)
Async XLA Ops:
  7.2 1.2 copy-start
  7.2 58.1 %all-gather.6.cloned.1.call-start = ((), (), s32[]{:S(2)}) async-start(), calls=%async_computation | async-start | bytes 5242880 | tf_op jit(solution)/shard_map/all_gather | solution.py:36
  7.9 88.1 %all-gather.8.cloned.1.call-start = ((), (), s32[]{:S(2)}) async-start(), calls=%async_computation.1 | async-start | bytes 2359296 | tf_op jit(solution)/shard_map/all_gather | solution.py:11
  11.1 115.2 %all-gather.10.cloned.1.call-start = ((), (), s32[]{:S(2)}) async-start(), calls=%async_computation.2 | async-start | bytes 2359296 | tf_op jit(solution)/shard_map/all_gather | solution.py:11
  76.9 19.1 %copy-start.3 = (bf16[512,1024]{0,1:T(8,128)(2,1)}, bf16[512,1024]{0,1:T(8,128)(2,1)S(1)}, u32[]{:S(2)}) copy-start(bf16[512,1024]{0,1:T(8,128)(2,1)S(1)} %copy.45) | copy-start | bytes 3145732
  80.7 25.4 %copy-start.8 = (pred[512,512]{1,0:T(8,128)(4,1)S(1)}, pred[512,512]{1,0:T(8,128)(4,1)}, u32[]{:S(2)}) copy-start(pred[512,512]{1,0:T(8,128)(4,1)} %iota_compare_fusion) | copy-start | bytes 786436
  106.1 2.9 %copy-start.2 = (bf16[512,1024]{1,0:T(8,128)(2,1)S(1)}, bf16[512,1024]{1,0:T(8,128)(2,1)}, u32[]{:S(2)}) copy-start(bf16[512,1024]{1,0:T(8,128)(2,1)} %param.10) | copy-start | bytes 3145732
  109.0 4.7 %copy-start.1 = (bf16[8,512,512]{2,1,0:T(8,128)(2,1)}, bf16[8,512,512]{2,1,0:T(8,128)(2,1)S(1)}, u32[]{:S(2)}) copy-start(bf16[8,512,512]{2,1,0:T(8,128)(2,1)S(1)} %select_convert_fusion.1) | copy-start | bytes 12582916
  109.0 2.0 %copy-start.4 = (bf16[512,1024]{0,1:T(8,128)(2,1)S(1)}, bf16[512,1024]{0,1:T(8,128)(2,1)}, u32[]{:S(2)}) copy-start(bf16[512,1024]{0,1:T(8,128)(2,1)} %copy-done.3) | copy-start | bytes 3145732
  109.0 2.5 %copy-start.7 = (f32[8,128,128]{2,1,0:T(8,128)S(1)}, f32[8,128,128]{2,1,0:T(8,128)}, u32[]{:S(2)}) copy-start(f32[8,128,128]{2,1,0:T(8,128)} %get-tuple-element.251) | copy-start | bytes 1572868
  136.5 3.6 %copy-start.5 = (f32[8,128,128]{1,2,0:T(8,128)S(1)}, f32[8,128,128]{1,2,0:T(8,128)}, u32[]{:S(2)}) copy-start(f32[8,128,128]{1,2,0:T(8,128)} %get-tuple-element.253) | copy-start | bytes 1572868
  136.6 3.6 %copy-start.6 = (f32[8,128,512]{2,1,0:T(8,128)S(1)}, f32[8,128,512]{2,1,0:T(8,128)}, u32[]{:S(2)}) copy-start(f32[8,128,512]{2,1,0:T(8,128)} %fusion) | copy-start | bytes 6291460
Sparse Core Ops, SparseCore 0:
  9.9 55.3 all-gather.5
  66.9 29.0 all-gather.7
  97.6 28.5 all-gather.9
where the time goes:
time: 157 us; the launch traced here: 156 us
  waiting for transfers between devices  74.8 us (48%)
  matrix products  36.8 us (23%)
  other arithmetic  20.6 us (13%)
  between operations  13.9 us (9%)
  local copies, waits for them, and re-layouts  9.84 us (6%)
    all_gather x1, waiting for transfers between devices, shards(): lax.all_gather(output_grad, 'head', axis=1, tiled=True)  53.4 us
    all_gather x2, waiting for transfers between devices, entering(): everything = lax.all_gather(shard.astype(jnp.bfloat16), axis)  20.7 us
    select_n x16, other arithmetic, hop(): return jnp.where(reached, new, before)  19.8 us
    dot_general x1, matrix products, shards(): lax.dot_general(lax.all_gather(output_grad, 'head', axis=1, tiled=True),...  10.1 us
    unnamed x21, local copies, waits for them, and re-layouts  7.3 us
    dot_general x1, matrix products, shards(): jnp.einsum('nhts,nthe->nshe', score_fwd, g_blocks, preferred_element_type...  4.9 us
    dot_general x1, matrix products, shards(): jnp.einsum('nhts,nthd->nshd', score_grad, q_blocks, preferred_element_typ...  4.01 us
    dot_general x1, matrix products, shards(): jnp.einsum('nshe,nhde->nshd', v_blocks.astype(jnp.float32), qg_entry, pre...  3.57 us
  transfers between devices with their start and end apart: 3, of which 3 were waited for; matrix products, arithmetic and copies ran while one was open for 27% of the time, Pallas kernels for 0%

commit v1 on v0

v1 whole, which is shorter than its diff:
```python
import jax
import jax.numpy as jnp
from jax import lax
from jax.sharding import PartitionSpec as P

DH = 128


def flip_pairs(n, bit):
    return [(a, a ^ bit) for a in range(n)]


def project(og, out_weight, head_size):
    cols = og.shape[1]

    def weight_cols(source, lo, width):
        return lax.dynamic_slice_in_dim(out_weight, source * cols + lo, width, axis=1)

    def mm(a, b):
        return lax.dot_general(
            a, b, (((1,), (1,)), ((), ())), preferred_element_type=jnp.float32
        )

    if head_size != 4:
        full = lax.all_gather(og, "head", axis=1, tiled=True)
        return mm(full, out_weight)
    me = lax.axis_index("head")
    half = cols // 2
    from_x = lax.ppermute(og, "head", flip_pairs(4, 1))
    from_y = lax.ppermute(og, "head", flip_pairs(4, 2))
    diag_a = lax.ppermute(from_x[:, :half], "head", flip_pairs(4, 2))
    diag_b = lax.ppermute(from_y[:, half:], "head", flip_pairs(4, 1))
    acc = mm(og, weight_cols(me, 0, cols))
    acc = acc + mm(from_x, weight_cols(me ^ 1, 0, cols))
    acc = acc + mm(from_y, weight_cols(me ^ 2, 0, cols))
    acc = acc + mm(diag_a, weight_cols(me ^ 3, 0, half))
    acc = acc + mm(diag_b, weight_cols(me ^ 3, half, half))
    return acc


def ctx_exclusive(state, ctx_size, reverse):
    p = lax.axis_index("ctx")
    core = p % 2
    chips = ctx_size // 2
    rounded = state.astype(jnp.bfloat16)
    partner = lax.ppermute(rounded, "ctx", flip_pairs(ctx_size, 1))
    chip_sum = rounded.astype(jnp.float32) + partner.astype(jnp.float32)
    half = state.shape[1] // 2
    mine = lax.dynamic_slice_in_dim(chip_sum, core * half, half, axis=1)
    run = mine
    others = jnp.zeros_like(mine)
    step = 1
    while step < chips:
        if reverse:
            pairs = [(2 * (z + step) + c, 2 * z + c) for z in range(chips - step) for c in range(2)]
        else:
            pairs = [(2 * z + c, 2 * (z + step) + c) for z in range(chips - step) for c in range(2)]
        got = lax.ppermute(run.astype(jnp.bfloat16), "ctx", pairs).astype(jnp.float32)
        run = run + got
        others = others + got
        step *= 2
    theirs = lax.ppermute(others, "ctx", flip_pairs(ctx_size, 1))
    lower = jnp.where(core == 0, others, theirs)
    upper = jnp.where(core == 0, theirs, others)
    chips_side = jnp.concatenate([lower, upper], axis=1)
    same_chip = (core == 0) if reverse else (core == 1)
    return chips_side + jnp.where(same_chip, partner.astype(jnp.float32), 0.0)


def make_shards(ctx_size, head_size):
    def shards(queries, keys, values, output_grad, out_weight):
        row_count = queries.shape[0]
        width = queries.shape[1]
        heads = width // DH
        block_len = min(row_count, 512)
        blocks = row_count // block_len
        scale_factor = DH ** (-0.5)
        highest = lax.Precision.HIGHEST
        shape = (blocks, block_len, heads, DH)
        q_blocks = queries.reshape(shape)
        k_blocks = keys.reshape(shape)
        v_blocks = values.reshape(shape)
        kv_blocks = jnp.einsum(
            "nshd,nshe->nhde", k_blocks, v_blocks, preferred_element_type=jnp.float32
        )
        kv_running = jnp.cumsum(kv_blocks, axis=0)
        kv_before = ctx_exclusive(kv_running[-1], ctx_size, False)
        kv_entry = kv_before[None] + kv_running - kv_blocks
        rows = jnp.arange(block_len)
        causal = (rows[:, None] >= rows[None, :])[None, None]
        score_fwd = (
            jnp.einsum("nthd,nshd->nhts", q_blocks, k_blocks, preferred_element_type=jnp.float32)
            * scale_factor
        )
        score_fwd = jnp.where(causal, score_fwd, 0.0).astype(jnp.bfloat16)

        grad_heads = project(output_grad, out_weight, head_size).astype(jnp.bfloat16)
        g_blocks = grad_heads.reshape(shape)
        qg_blocks = jnp.einsum(
            "nthd,nthe->nhde", q_blocks, g_blocks, preferred_element_type=jnp.float32
        )
        qg_running = jnp.flip(jnp.cumsum(jnp.flip(qg_blocks, 0), axis=0), 0)
        qg_after = ctx_exclusive(qg_running[0], ctx_size, True)
        qg_entry = qg_after[None] + qg_running - qg_blocks

        score_grad = (
            jnp.einsum("nthe,nshe->nhts", g_blocks, v_blocks, preferred_element_type=jnp.float32)
            * scale_factor
        )
        score_grad = jnp.where(causal, score_grad, 0.0).astype(jnp.bfloat16)
        grad_q = jnp.einsum("nhts,nshd->nthd", score_grad, k_blocks, preferred_element_type=jnp.float32)
        grad_q = grad_q + scale_factor * jnp.einsum(
            "nthe,nhde->nthd", g_blocks.astype(jnp.float32), kv_entry, precision=highest
        )
        grad_k = jnp.einsum("nhts,nthd->nshd", score_grad, q_blocks, preferred_element_type=jnp.float32)
        grad_k = grad_k + scale_factor * jnp.einsum(
            "nshe,nhde->nshd", v_blocks.astype(jnp.float32), qg_entry, precision=highest
        )
        grad_v = jnp.einsum("nhts,nthe->nshe", score_fwd, g_blocks, preferred_element_type=jnp.float32)
        grad_v = grad_v + scale_factor * jnp.einsum(
            "nshd,nhde->nshe", k_blocks.astype(jnp.float32), qg_entry, precision=highest
        )
        flat = (row_count, width)
        return (
            grad_q.reshape(flat).astype(jnp.bfloat16),
            grad_k.reshape(flat).astype(jnp.bfloat16),
            grad_v.reshape(flat).astype(jnp.bfloat16),
        )

    return shards


def solution(mesh):
    return jax.shard_map(
        make_shards(mesh.shape["ctx"], mesh.shape["head"]),
        mesh=mesh,
        in_specs=(
            P("ctx", "head"),
            P("ctx", "head"),
            P("ctx", "head"),
            P("ctx", "head"),
            P("head", None),
        ),
        out_specs=(P("ctx", "head"), P("ctx", "head"), P("ctx", "head")),
        check_vma=False,
    )
```

time: 157 us -> 94 us (0.60)
  waiting for transfers between devices: 74.8 us -> 29.3 us
  starting transfers between devices: 0.12 us -> 20 us
  other arithmetic: 20.6 us -> 3.75 us
  between operations: 13.9 us -> 1.05 us
  matrix products: 36.8 us -> 30.2 us
    all_gather x3 -> x0, waiting for transfers between devices: 74.1 us -> none  [the longest x1 53.4 us: shards(): lax.all_gather(output_grad, 'head', axis=1, tiled=True)]
    ppermute x0 -> x12, waiting for transfers between devices: none -> 29.3 us  [the longest x4 12.5 us: ctx_exclusive(): lax.ppermute(run.astype(jnp.bfloat16), 'ctx', pairs).astype(jnp.float32)]
    ppermute x0 -> x12, starting transfers between devices: none -> 20 us  [the longest x4 13.2 us: ctx_exclusive(): lax.ppermute(run.astype(jnp.bfloat16), 'ctx', pairs).astype(jnp.float32)]
    select_n x16 -> x2, other arithmetic: 19.8 us -> 1.11 us  [ctx_exclusive(): lower = jnp.where(core == 0, others, theirs)]
    dot_general x1, matrix products: 3.57 us -> 1.02 us  [shards(): jnp.einsum('nshe,nhde->nshd', v_blocks.astype(jnp.float32), qg_entry, pre...]
    dot_general x1, matrix products: 4.01 us -> 2.11 us  [shards(): jnp.einsum('nhts,nthd->nshd', score_grad, q_blocks, preferred_element_typ...]
    add x0 -> x2, other arithmetic: none -> 1.66 us  [ctx_exclusive(): others = others + got]
    unnamed x21 -> x35, local copies, waits for them, and re-layouts: 7.3 us -> 8 us
  transfers between devices with their start and end apart: 3 -> 12, of which waited for: 3 -> 7; matrix products, arithmetic and copies ran while one was open for 27% -> 24% of each run, Pallas kernels for 0% -> 0%
where the time goes in v1:
time: 94 us; the launch traced here: 93.3 us
  matrix products  30.2 us (32%)
  waiting for transfers between devices  29.3 us (31%)
  starting transfers between devices  20 us (21%)
  local copies, waits for them, and re-layouts  9.12 us (10%)
  other arithmetic  3.75 us (4%)
  between operations  1.05 us (1%)
    ppermute x4, starting transfers between devices, ctx_exclusive(): lax.ppermute(run.astype(jnp.bfloat16), 'ctx', pairs).astype(jnp.float32)  13.2 us
    ppermute x4, waiting for transfers between devices, ctx_exclusive(): lax.ppermute(run.astype(jnp.bfloat16), 'ctx', pairs).astype(jnp.float32)  12.5 us
    ppermute x1, waiting for transfers between devices, project(): from_x = lax.ppermute(og, 'head', flip_pairs(4, 1))  10.7 us
    dot_general x5, matrix products, mm(): lax.dot_general(a, b, (((1,), (1,)), ((), ())), preferred_element_type=jn...  10.3 us
    unnamed x35, local copies, waits for them, and re-layouts  8 us
    dot_general x1, matrix products, shards(): jnp.einsum('nhts,nthe->nshe', score_fwd, g_blocks, preferred_element_type...  4.58 us
    ppermute x1, waiting for transfers between devices, project(): diag_a = lax.ppermute(from_x[:, :half], 'head', flip_pairs(4, 2))  3.34 us
    dot_general x1, matrix products, shards(): jnp.einsum('nshd,nhde->nshe', k_blocks.astype(jnp.float32), qg_entry, pre...  3.03 us
  transfers between devices with their start and end apart: 12, of which 7 were waited for; matrix products, arithmetic and copies ran while one was open for 24% of the time, Pallas kernels for 0%

profile of v1, /device:TPU:0, one launch (start us, length us, event | category | flops | bytes accessed | tf_op | source)
XLA Modules:
  0.0 93.3 jit_solution(9260503181487992842)
XLA Ops:
  1.9 2.6 %fusion.66 = (bf16[8,128,128]{2,1,0:T(8,128)(2,1)S(1)}, f32[8,128,128]{2,1,0:T(8,128)}) fusion(bf16[512,1024]{1,0:T(8,128)(2,1)S(1)} %copy-done, bf16[512,1024]{1,0:T(8,128)(2,1)} %param.6), kind=kOutput, calls=%fused_computation.81 | convolution fusion | flops 134348800 | bytes 2883584 | tf_op jit(solution)/shard_map/nshd,nshe->nhde/dot_general | solution.py:83
  6.8 4.9 %collective-permute-start.5 = (bf16[8,64,128]{2,1,0:T(8,128)(2,1)S(1)}, bf16[8,64,128]{2,1,0:T(8,128)(2,1)S(1)}, u32[]{:S(2)}, u32[]{:S(2)}) collective-permute-start(bf16[8,64,128]{2,1,0:T(8,128)(2,1)S(1)} %fusion.54), channel_id=1, source_target_pairs={{0,8},{4,12},{8,16},{12,20},{16,24},{20,28},{1,9},{5,13},{9,17},{1... | collective-permute-start | bytes 393224 | tf_op jit(solution)/shard_map/ppermute | solution.py:58
  11.6 1.6 %collective-permute-start = (bf16[512,1024]{1,0:T(8,128)(2,1)}, bf16[512,1024]{1,0:T(8,128)(2,1)S(1)}, u32[]{:S(2)}, u32[]{:S(2)}) collective-permute-start(bf16[512,1024]{1,0:T(8,128)(2,1)} %param.8), channel_id=1, source_target_pairs={{0,1},{1,0},{2,3},{3,2},{4,5},{5,4},{6,7},{7,6},{8,9},{9,8},{10,11... | collective-permute-start | bytes 3145736 | tf_op jit(solution)/shard_map/ppermute | solution.py:29
  14.8 5.4 %collective-permute-start.6 = (bf16[8,64,128]{2,1,0:T(8,128)(2,1)S(1)}, bf16[8,64,128]{2,1,0:T(8,128)(2,1)S(1)}, u32[]{:S(2)}, u32[]{:S(2)}) collective-permute-start(bf16[8,64,128]{2,1,0:T(8,128)(2,1)S(1)} %fusion.50), channel_id=1, source_target_pairs={{0,16},{4,20},{8,24},{12,28},{1,17},{5,21},{9,25},{13,29},{2,18},{... | collective-permute-start | bytes 393224 | tf_op jit(solution)/shard_map/ppermute | solution.py:58
  20.3 2.4 %collective-permute-done.6 = bf16[8,64,128]{2,1,0:T(8,128)(2,1)S(1)} collective-permute-done((bf16[8,64,128]{2,1,0:T(8,128)(2,1)S(1)}, bf16[8,64,128]{2,1,0:T(8,128)(2,1)S(1)}, u32[]{:S(2)}, u32[]{:S(2)}) %collective-permute-start.6) | collective-permute-done | bytes 131104 | tf_op jit(solution)/shard_map/ppermute | solution.py:58
  22.8 3.3 %fusion.12 = f32[1024,512]{1,0:T(8,128)S(1)} fusion(bf16[512,1024]{1,0:T(8,128)(2,1)} %param.8, bf16[1024,4096]{1,0:T(8,128)(2,1)} %param.9, s32[]{:T(128)S(6)} %select_n.71), kind=kOutput, calls=%fused_computation.17 | convolution fusion | flops 1073741824 | bytes 5242884 | tf_op jit(solution)/shard_map/dot_general | solution.py:20
  26.2 10.7 %collective-permute-done = bf16[512,1024]{1,0:T(8,128)(2,1)S(1)} collective-permute-done((bf16[512,1024]{1,0:T(8,128)(2,1)}, bf16[512,1024]{1,0:T(8,128)(2,1)S(1)}, u32[]{:S(2)}, u32[]{:S(2)}) %collective-permute-start) | collective-permute-done | bytes 1048608 | tf_op jit(solution)/shard_map/ppermute | solution.py:29
  36.9 1.6 %collective-permute-start.2 = (bf16[512,512]{1,0:T(8,128)(2,1)S(1)}, bf16[512,512]{1,0:T(8,128)(2,1)S(1)}, u32[]{:S(2)}, u32[]{:S(2)}) collective-permute-start(bf16[512,512]{1,0:T(8,128)(2,1)S(1)} %slice.8), channel_id=1, source_target_pairs={{0,2},{1,3},{2,0},{3,1},{4,6},{5,7},{6,4},{7,5},{8,10},{9,11},{10,... | collective-permute-start | bytes 1572872 | tf_op jit(solution)/shard_map/ppermute | solution.py:31
  39.5 1.6 %collective-permute-start.3 = (bf16[512,512]{1,0:T(8,128)(2,1)S(1)}, bf16[512,512]{1,0:T(8,128)(2,1)S(1)}, u32[]{:S(2)}, u32[]{:S(2)}) collective-permute-start(bf16[512,512]{1,0:T(8,128)(2,1)S(1)} %slice.9), channel_id=1, source_target_pairs={{0,1},{1,0},{2,3},{3,2},{4,5},{5,4},{6,7},{7,6},{8,9},{9,8},{10,11... | collective-permute-start | bytes 1572872 | tf_op jit(solution)/shard_map/ppermute | solution.py:32
  41.1 2.9 %fusion.10 = f32[1024,512]{1,0:T(8,128)S(1)} fusion(bf16[512,1024]{1,0:T(8,128)(2,1)S(1)} %collective-permute-done, bf16[1024,4096]{1,0:T(8,128)(2,1)} %param.9, s32[]{:T(128)S(6)} %select_n.72), kind=kOutput, calls=%fused_computation.15 | convolution fusion | flops 1073741824 | bytes 5242884 | tf_op jit(solution)/shard_map/dot_general | solution.py:20
  44.0 2.5 %fusion.8 = f32[1024,512]{1,0:T(8,128)S(1)} fusion(bf16[512,1024]{1,0:T(8,128)(2,1)} %collective-permute-done.1, bf16[1024,4096]{1,0:T(8,128)(2,1)S(1)} %bitcast.113, s32[]{:T(128)S(6)} %select_n.73), kind=kOutput, calls=%fused_computation.13 | convolution fusion | flops 1073741824 | bytes 5242884 | tf_op jit(solution)/shard_map/dot_general | solution.py:20
  46.5 3.3 %collective-permute-done.2 = bf16[512,512]{1,0:T(8,128)(2,1)S(1)} collective-permute-done((bf16[512,512]{1,0:T(8,128)(2,1)S(1)}, bf16[512,512]{1,0:T(8,128)(2,1)S(1)}, u32[]{:S(2)}, u32[]{:S(2)}) %collective-permute-start.2) | collective-permute-done | bytes 524320 | tf_op jit(solution)/shard_map/ppermute | solution.py:31
  50.6 1.6 %collective-permute-done.3 = bf16[512,512]{1,0:T(8,128)(2,1)S(1)} collective-permute-done((bf16[512,512]{1,0:T(8,128)(2,1)S(1)}, bf16[512,512]{1,0:T(8,128)(2,1)S(1)}, u32[]{:S(2)}, u32[]{:S(2)}) %collective-permute-start.3) | collective-permute-done | bytes 524320 | tf_op jit(solution)/shard_map/ppermute | solution.py:32
  54.5 1.5 %select_convert_fusion.1 = bf16[8,512,512]{2,1,0:T(8,128)(2,1)S(1)} fusion(pred[512,512]{1,0:T(8,128)(4,1)S(1)} %iota_compare_fusion, bf16[512,8,128]{0,2,1:T(8,128)(2,1)S(1)} %bitcast.106, bf16[512,1024]{1,0:T(8,128)(2,1)S(1)} %copy-done), kind=kOutput, calls=%fused_computation.1 | convolution fusion | flops 543162368 | bytes 6553600 | tf_op jit(solution)/shard_map/nthe,nshe->nhts/dot_general | solution.py:107
  56.2 1.6 %collective-permute-start.9 = (bf16[8,64,128]{2,1,0:T(8,128)(2,1)S(1)}, bf16[8,64,128]{2,1,0:T(8,128)(2,1)S(1)}, u32[]{:S(2)}, u32[]{:S(2)}) collective-permute-start(bf16[8,64,128]{2,1,0:T(8,128)(2,1)S(1)} %fusion.55), channel_id=1, source_target_pairs={{8,0},{12,4},{16,8},{20,12},{24,16},{28,20},{9,1},{13,5},{17,9},{2... | collective-permute-start | bytes 393224 | tf_op jit(solution)/shard_map/ppermute | solution.py:58
  57.8 1.5 %fusion.22 = f32[8,512,128]{1,2,0:T(8,128)S(1)} fusion(bf16[8,512,512]{2,1,0:T(8,128)(2,1)S(1)} %select_convert_fusion.1, bf16[512,1024]{1,0:T(8,128)(2,1)S(1)} %copy-done.3), kind=kOutput, calls=%fused_computation.26 | convolution fusion | flops 536870912 | bytes 7340032 | tf_op jit(solution)/shard_map/nhts,nshd->nthd/dot_general | solution.py:111
  59.3 4.9 %collective-permute-done.9 = bf16[8,64,128]{2,1,0:T(8,128)(2,1)S(1)} collective-permute-done((bf16[8,64,128]{2,1,0:T(8,128)(2,1)S(1)}, bf16[8,64,128]{2,1,0:T(8,128)(2,1)S(1)}, u32[]{:S(2)}, u32[]{:S(2)}) %collective-permute-start.9) | collective-permute-done | bytes 131104 | tf_op jit(solution)/shard_map/ppermute | solution.py:58
  66.4 2.1 %fusion.7 = bf16[8,128,512]{2,1,0:T(8,128)(2,1)} fusion(f32[8,512,128]{1,2,0:T(8,128)S(1)} %fusion.22, bf16[512,8,128]{0,2,1:T(8,128)(2,1)S(1)} %bitcast.107, f32[8,128,128]{2,1,0:T(8,128)S(1)} %copy-done.10, f32[8,64,128]{2,1,0:T(8,128)S(1)} %get-tuple-element.9, f32[8,64,128]{2,1,0:T(8,128)S(1)} %get-tuple-element.8, pred[]{:T(512)S(6)} %eq.14, ...), kind=kOutput, calls=%fused_computation.10 | convolution fusion | flops 807665664 | bytes 5505025 | tf_op jit(solution)/shard_map/nthe,nhde->nthd/dot_general | solution.py:112
  68.6 2.3 %copy.20 = bf16[512,1024]{1,0:T(8,128)(2,1)} copy(bf16[512,1024]{0,1:T(8,128)(2,1)} %bitcast.109) | data formatting | bytes 2097152
  70.8 5.2 %collective-permute-done.10 = bf16[8,64,128]{2,1,0:T(8,128)(2,1)} collective-permute-done((bf16[8,64,128]{2,1,0:T(8,128)(2,1)}, bf16[8,64,128]{2,1,0:T(8,128)(2,1)}, u32[]{:S(2)}, u32[]{:S(2)}) %collective-permute-start.10) | collective-permute-done | bytes 131104 | tf_op jit(solution)/shard_map/ppermute | solution.py:58
  76.0 1.6 %convert_add_fusion = f32[8,64,128]{2,1,0:T(8,128)} fusion(bf16[8,64,128]{2,1,0:T(8,128)(2,1)S(1)} %collective-permute-done.9, bf16[8,64,128]{2,1,0:T(8,128)(2,1)} %collective-permute-done.10), kind=kLoop, calls=%fused_computation.55 | loop fusion | flops 196608 | bytes 524288 | tf_op jit(solution)/shard_map/add | solution.py:60
  77.6 4.6 %fusion = f32[8,128,512]{2,1,0:T(8,128)} fusion(bf16[512,8,128]{0,2,1:T(8,128)(2,1)S(1)} %bitcast.108, pred[512,512]{1,0:T(8,128)(4,1)} %copy-done.13, bf16[512,1024]{1,0:T(8,128)(2,1)} %param.5, bf16[512,1024]{1,0:T(8,128)(2,1)S(1)} %copy-done.3), kind=kOutput, calls=%fused_computation.2 | convolution fusion | flops 1080033280 | bytes 5505024 | tf_op jit(solution)/shard_map/nhts,nthe->nshe/dot_general | solution.py:119
  83.3 3.0 %add_convert_fusion = bf16[8,128,512]{2,1,0:T(8,128)(2,1)S(1)} fusion(f32[8,128,512]{2,1,0:T(8,128)} %fusion, f32[8,128,128]{2,1,0:T(8,128)} %get-tuple-element.13, f32[8,64,128]{2,1,0:T(8,128)S(1)} %get-tuple-element.7, f32[8,64,128]{2,1,0:T(8,128)S(1)} %get-tuple-element.6, pred[]{:T(512)S(6)} %eq.7, bf16[8,128,128]{2,1,0:T(8,128)(2,1)S(1)} %collective-permute-done.8, ...), kind=kOutput, calls=%fused_computation.11 | convolution fusion | flops 807665664 | bytes 5505025 | tf_op jit(solution)/shard_map/nshd,nhde->nshe/dot_general | solution.py:120
  89.9 2.1 %fusion.6 = bf16[8,128,512]{2,1,0:T(8,128)(2,1)S(1)} fusion(f32[8,128,512]{2,1,0:T(8,128)S(1)} %fusion.25, bf16[8,512,512]{2,1,0:T(8,128)(2,1)S(1)} %copy-done.2, bf16[512,1024]{1,0:T(8,128)(2,1)} %param.5), kind=kOutput, calls=%fused_computation.8 | convolution fusion | flops 538443776 | bytes 8388608 | tf_op jit(solution)/shard_map/nhts,nthd->nshd/dot_general | solution.py:115
  (63 shorter events, 17.6 us)
Async XLA Ops:
  4.4 1.6 %collective-permute-start.4 = (bf16[8,128,128]{2,1,0:T(8,128)(2,1)S(1)}, bf16[8,128,128]{2,1,0:T(8,128)(2,1)S(1)}, u32[]{:S(2)}, u32[]{:S(2)}) collective-permute-start(bf16[8,128,128]{2,1,0:T(8,128)(2,1)S(1)} %get-tuple-element.10), channel_id=1, source_target_pairs={{0,4},{4,0},{8,12},{12,8},{16,20},{20,16},{24,28},{28,24},{1,5},{5... | collective-permute-start | bytes 786440 | tf_op jit(solution)/shard_map/ppermute | solution.py:46
  6.8 7.9 %collective-permute-start.5 = (bf16[8,64,128]{2,1,0:T(8,128)(2,1)S(1)}, bf16[8,64,128]{2,1,0:T(8,128)(2,1)S(1)}, u32[]{:S(2)}, u32[]{:S(2)}) collective-permute-start(bf16[8,64,128]{2,1,0:T(8,128)(2,1)S(1)} %fusion.54), channel_id=1, source_target_pairs={{0,8},{4,12},{8,16},{12,20},{16,24},{20,28},{1,9},{5,13},{9,17},{1... | collective-permute-start | bytes 393224 | tf_op jit(solution)/shard_map/ppermute | solution.py:58
  11.6 25.2 %collective-permute-start = (bf16[512,1024]{1,0:T(8,128)(2,1)}, bf16[512,1024]{1,0:T(8,128)(2,1)S(1)}, u32[]{:S(2)}, u32[]{:S(2)}) collective-permute-start(bf16[512,1024]{1,0:T(8,128)(2,1)} %param.8), channel_id=1, source_target_pairs={{0,1},{1,0},{2,3},{3,2},{4,5},{5,4},{6,7},{7,6},{8,9},{9,8},{10,11... | collective-permute-start | bytes 3145736 | tf_op jit(solution)/shard_map/ppermute | solution.py:29
  13.2 25.3 %collective-permute-start.1 = (bf16[512,1024]{1,0:T(8,128)(2,1)}, bf16[512,1024]{1,0:T(8,128)(2,1)}, u32[]{:S(2)}, u32[]{:S(2)}) collective-permute-start(bf16[512,1024]{1,0:T(8,128)(2,1)} %param.8), channel_id=1, source_target_pairs={{0,2},{1,3},{2,0},{3,1},{4,6},{5,7},{6,4},{7,5},{8,10},{9,11},{10,... | collective-permute-start | bytes 3145736 | tf_op jit(solution)/shard_map/ppermute | solution.py:30
  14.8 7.9 %collective-permute-start.6 = (bf16[8,64,128]{2,1,0:T(8,128)(2,1)S(1)}, bf16[8,64,128]{2,1,0:T(8,128)(2,1)S(1)}, u32[]{:S(2)}, u32[]{:S(2)}) collective-permute-start(bf16[8,64,128]{2,1,0:T(8,128)(2,1)S(1)} %fusion.50), channel_id=1, source_target_pairs={{0,16},{4,20},{8,24},{12,28},{1,17},{5,21},{9,25},{13,29},{2,18},{... | collective-permute-start | bytes 393224 | tf_op jit(solution)/shard_map/ppermute | solution.py:58
  20.3 34.2 %copy-start.13 = (pred[512,512]{1,0:T(8,128)(4,1)}, pred[512,512]{1,0:T(8,128)(4,1)S(1)}, u32[]{:S(2)}) copy-start(pred[512,512]{1,0:T(8,128)(4,1)S(1)} %iota_compare_fusion) | copy-start | bytes 786436
  22.7 3.4 %collective-permute-start.7 = (f32[8,64,128]{2,1,0:T(8,128)S(1)}, f32[8,64,128]{2,1,0:T(8,128)S(1)}, u32[]{:S(2)}, u32[]{:S(2)}) collective-permute-start(f32[8,64,128]{2,1,0:T(8,128)S(1)} %convert_add_fusion.2), channel_id=1, source_target_pairs={{0,4},{4,0},{8,12},{12,8},{16,20},{20,16},{24,28},{28,24},{1,5},{5... | collective-permute-start | bytes 786440 | tf_op jit(solution)/shard_map/ppermute | solution.py:62
  22.8 21.2 %slice-start = ((s8[8388608]{0:T(1024)(128)(4,1)}), s8[4194304]{0:T(1024)(128)(4,1)S(1)}, s32[]{:S(2)}) async-start(s8[8388608]{0:T(1024)(128)(4,1)} %bitcast.112), calls=%async_computation | async-start | bytes 8388608
  26.2 17.8 %slice-start.1 = ((s8[8388608]{0:T(1024)(128)(4,1)}), s8[4194304]{0:T(1024)(128)(4,1)S(1)}, s32[]{:S(2)}) async-start(s8[8388608]{0:T(1024)(128)(4,1)} %bitcast.112), calls=%async_computation.1 | async-start | bytes 8388608
  36.9 13.0 %collective-permute-start.2 = (bf16[512,512]{1,0:T(8,128)(2,1)S(1)}, bf16[512,512]{1,0:T(8,128)(2,1)S(1)}, u32[]{:S(2)}, u32[]{:S(2)}) collective-permute-start(bf16[512,512]{1,0:T(8,128)(2,1)S(1)} %slice.8), channel_id=1, source_target_pairs={{0,2},{1,3},{2,0},{3,1},{4,6},{5,7},{6,4},{7,5},{8,10},{9,11},{10,... | collective-permute-start | bytes 1572872 | tf_op jit(solution)/shard_map/ppermute | solution.py:31
  39.5 12.7 %collective-permute-start.3 = (bf16[512,512]{1,0:T(8,128)(2,1)S(1)}, bf16[512,512]{1,0:T(8,128)(2,1)S(1)}, u32[]{:S(2)}, u32[]{:S(2)}) collective-permute-start(bf16[512,512]{1,0:T(8,128)(2,1)S(1)} %slice.9), channel_id=1, source_target_pairs={{0,1},{1,0},{2,3},{3,2},{4,5},{5,4},{6,7},{7,6},{8,9},{9,8},{10,11... | collective-permute-start | bytes 1572872 | tf_op jit(solution)/shard_map/ppermute | solution.py:32
  50.6 2.6 %copy-start.5 = (bf16[512,1024]{1,0:T(8,128)(2,1)S(1)}, bf16[512,1024]{1,0:T(8,128)(2,1)}, u32[]{:S(2)}) copy-start(bf16[512,1024]{1,0:T(8,128)(2,1)} %param.5) | copy-start | bytes 3145732
  54.5 3.3 %copy-start.3 = (bf16[512,1024]{1,0:T(8,128)(2,1)S(1)}, bf16[512,1024]{1,0:T(8,128)(2,1)}, u32[]{:S(2)}) copy-start(bf16[512,1024]{1,0:T(8,128)(2,1)} %param.6) | copy-start | bytes 3145732
  54.5 1.6 %collective-permute-start.8 = (bf16[8,128,128]{2,1,0:T(8,128)(2,1)S(1)}, bf16[8,128,128]{2,1,0:T(8,128)(2,1)S(1)}, u32[]{:S(2)}, u32[]{:S(2)}) collective-permute-start(bf16[8,128,128]{2,1,0:T(8,128)(2,1)S(1)} %get-tuple-element.12), channel_id=1, source_target_pairs={{0,4},{4,0},{8,12},{12,8},{16,20},{20,16},{24,28},{28,24},{1,5},{5... | collective-permute-start | bytes 786440 | tf_op jit(solution)/shard_map/ppermute | solution.py:46
  56.0 3.3 %copy-start.1 = (bf16[8,512,512]{2,1,0:T(8,128)(2,1)}, bf16[8,512,512]{2,1,0:T(8,128)(2,1)S(1)}, u32[]{:S(2)}) copy-start(bf16[8,512,512]{2,1,0:T(8,128)(2,1)S(1)} %select_convert_fusion.1) | copy-start | bytes 12582916
  56.2 10.3 %copy-start.10 = (f32[8,128,128]{2,1,0:T(8,128)S(1)}, f32[8,128,128]{2,1,0:T(8,128)}, u32[]{:S(2)}) copy-start(f32[8,128,128]{2,1,0:T(8,128)} %get-tuple-element.11) | copy-start | bytes 1572868
  56.2 10.3 %copy-start.12 = (bf16[8,128,128]{2,1,0:T(8,128)(2,1)S(1)}, bf16[8,128,128]{2,1,0:T(8,128)(2,1)}, u32[]{:S(2)}) copy-start(bf16[8,128,128]{2,1,0:T(8,128)(2,1)} %copy-done.11) | copy-start | bytes 786436
  56.2 8.1 %collective-permute-start.9 = (bf16[8,64,128]{2,1,0:T(8,128)(2,1)S(1)}, bf16[8,64,128]{2,1,0:T(8,128)(2,1)S(1)}, u32[]{:S(2)}, u32[]{:S(2)}) collective-permute-start(bf16[8,64,128]{2,1,0:T(8,128)(2,1)S(1)} %fusion.55), channel_id=1, source_target_pairs={{8,0},{12,4},{16,8},{20,12},{24,16},{28,20},{9,1},{13,5},{17,9},{2... | collective-permute-start | bytes 393224 | tf_op jit(solution)/shard_map/ppermute | solution.py:58
  65.0 11.0 %collective-permute-start.10 = (bf16[8,64,128]{2,1,0:T(8,128)(2,1)}, bf16[8,64,128]{2,1,0:T(8,128)(2,1)}, u32[]{:S(2)}, u32[]{:S(2)}) collective-permute-start(bf16[8,64,128]{2,1,0:T(8,128)(2,1)} %fusion.51), channel_id=1, source_target_pairs={{16,0},{20,4},{24,8},{28,12},{17,1},{21,5},{25,9},{29,13},{18,2},{... | collective-permute-start | bytes 393224 | tf_op jit(solution)/shard_map/ppermute | solution.py:58
  77.6 4.6 %collective-permute-start.11 = (f32[8,64,128]{2,1,0:T(8,128)}, f32[8,64,128]{2,1,0:T(8,128)}, u32[]{:S(2)}, u32[]{:S(2)}) collective-permute-start(f32[8,64,128]{2,1,0:T(8,128)} %convert_add_fusion), channel_id=1, source_target_pairs={{0,4},{4,0},{8,12},{12,8},{16,20},{20,16},{24,28},{28,24},{1,5},{5... | collective-permute-start | bytes 786440 | tf_op jit(solution)/shard_map/ppermute | solution.py:62
  83.3 3.1 %copy-start.6 = (f32[8,64,128]{2,1,0:T(8,128)}, f32[8,64,128]{2,1,0:T(8,128)S(1)}, u32[]{:S(2)}) copy-start(f32[8,64,128]{2,1,0:T(8,128)S(1)} %get-tuple-element.6) | copy-start | bytes 786436
  83.3 3.1 %copy-start.8 = (f32[8,64,128]{2,1,0:T(8,128)}, f32[8,64,128]{2,1,0:T(8,128)S(1)}, u32[]{:S(2)}) copy-start(f32[8,64,128]{2,1,0:T(8,128)S(1)} %get-tuple-element.7) | copy-start | bytes 786436
  86.3 1.4 %copy-start.4 = (f32[8,128,128]{2,1,0:T(8,128)S(1)}, f32[8,128,128]{2,1,0:T(8,128)}, u32[]{:S(2)}) copy-start(f32[8,128,128]{2,1,0:T(8,128)} %get-tuple-element.13) | copy-start | bytes 1572868
  87.7 2.2 %copy-start.2 = (bf16[8,512,512]{2,1,0:T(8,128)(2,1)S(1)}, bf16[8,512,512]{2,1,0:T(8,128)(2,1)}, u32[]{:S(2)}) copy-start(bf16[8,512,512]{2,1,0:T(8,128)(2,1)} %copy-done.1) | copy-start | bytes 12582916
  (4 other events, 4.6 us)

commit v2 on v1

--- a/solution.py
+++ b/solution.py
@@ -10,7 +10,7 @@
     return [(a, a ^ bit) for a in range(n)]
 
 
-def project(og, out_weight, head_size):
+def project(og, out_weight, head_size, tied):
     cols = og.shape[1]
 
     def weight_cols(source, lo, width):
@@ -23,11 +23,13 @@
 
     if head_size != 4:
         full = lax.all_gather(og, "head", axis=1, tiled=True)
-        return mm(full, out_weight)
+        full, tied = lax.optimization_barrier((full, tied))
+        return mm(full, out_weight), tied
     me = lax.axis_index("head")
     half = cols // 2
     from_x = lax.ppermute(og, "head", flip_pairs(4, 1))
     from_y = lax.ppermute(og, "head", flip_pairs(4, 2))
+    from_x, from_y, tied = lax.optimization_barrier((from_x, from_y, tied))
     diag_a = lax.ppermute(from_x[:, :half], "head", flip_pairs(4, 2))
     diag_b = lax.ppermute(from_y[:, half:], "head", flip_pairs(4, 1))
     acc = mm(og, weight_cols(me, 0, cols))
@@ -35,7 +37,7 @@
     acc = acc + mm(from_y, weight_cols(me ^ 2, 0, cols))
     acc = acc + mm(diag_a, weight_cols(me ^ 3, 0, half))
     acc = acc + mm(diag_b, weight_cols(me ^ 3, half, half))
-    return acc
+    return acc, tied
 
 
 def ctx_exclusive(state, ctx_size, reverse):
@@ -47,24 +49,41 @@
     chip_sum = rounded.astype(jnp.float32) + partner.astype(jnp.float32)
     half = state.shape[1] // 2
     mine = lax.dynamic_slice_in_dim(chip_sum, core * half, half, axis=1)
-    run = mine
     others = jnp.zeros_like(mine)
-    step = 1
-    while step < chips:
-        if reverse:
-            pairs = [(2 * (z + step) + c, 2 * z + c) for z in range(chips - step) for c in range(2)]
-        else:
-            pairs = [(2 * z + c, 2 * (z + step) + c) for z in range(chips - step) for c in range(2)]
-        got = lax.ppermute(run.astype(jnp.bfloat16), "ctx", pairs).astype(jnp.float32)
-        run = run + got
-        others = others + got
-        step *= 2
+    if chips <= 4:
+        sent = mine.astype(jnp.bfloat16)
+        for step in range(1, chips):
+            if reverse:
+                pairs = [(2 * (z + step) + c, 2 * z + c) for z in range(chips - step) for c in range(2)]
+            else:
+                pairs = [(2 * z + c, 2 * (z + step) + c) for z in range(chips - step) for c in range(2)]
+            others = others + lax.ppermute(sent, "ctx", pairs).astype(jnp.float32)
+    else:
+        run = mine
+        step = 1
+        while step < chips:
+            if reverse:
+                pairs = [(2 * (z + step) + c, 2 * z + c) for z in range(chips - step) for c in range(2)]
+            else:
+                pairs = [(2 * z + c, 2 * (z + step) + c) for z in range(chips - step) for c in range(2)]
+            got = lax.ppermute(run.astype(jnp.bfloat16), "ctx", pairs).astype(jnp.float32)
+            run = run + got
+            others = others + got
+            step *= 2
     theirs = lax.ppermute(others, "ctx", flip_pairs(ctx_size, 1))
     lower = jnp.where(core == 0, others, theirs)
     upper = jnp.where(core == 0, theirs, others)
     chips_side = jnp.concatenate([lower, upper], axis=1)
     same_chip = (core == 0) if reverse else (core == 1)
     return chips_side + jnp.where(same_chip, partner.astype(jnp.float32), 0.0)
+
+
+def state_mm(spec, x, state):
+    high = state.astype(jnp.bfloat16)
+    low = (state - high.astype(jnp.float32)).astype(jnp.bfloat16)
+    return jnp.einsum(spec, x, high, preferred_element_type=jnp.float32) + jnp.einsum(
+        spec, x, low, preferred_element_type=jnp.float32
+    )
 
 
 def make_shards(ctx_size, head_size):
@@ -75,13 +94,15 @@
         block_len = min(row_count, 512)
         blocks = row_count // block_len
         scale_factor = DH ** (-0.5)
-        highest = lax.Precision.HIGHEST
         shape = (blocks, block_len, heads, DH)
         q_blocks = queries.reshape(shape)
         k_blocks = keys.reshape(shape)
         v_blocks = values.reshape(shape)
+        grad_heads, (k_tied, v_tied) = project(output_grad, out_weight, head_size, (keys, values))
+        grad_heads = grad_heads.astype(jnp.bfloat16)
         kv_blocks = jnp.einsum(
-            "nshd,nshe->nhde", k_blocks, v_blocks, preferred_element_type=jnp.float32
+            "nshd,nshe->nhde", k_tied.reshape(shape), v_tied.reshape(shape),
+            preferred_element_type=jnp.float32,
         )
         kv_running = jnp.cumsum(kv_blocks, axis=0)
         kv_before = ctx_exclusive(kv_running[-1], ctx_size, False)
@@ -94,7 +115,6 @@
         )
         score_fwd = jnp.where(causal, score_fwd, 0.0).astype(jnp.bfloat16)
 
-        grad_heads = project(output_grad, out_weight, head_size).astype(jnp.bfloat16)
         g_blocks = grad_heads.reshape(shape)
         qg_blocks = jnp.einsum(
             "nthd,nthe->nhde", q_blocks, g_blocks, preferred_element_type=jnp.float32
@@ -109,17 +129,11 @@
         )
         score_grad = jnp.where(causal, score_grad, 0.0).astype(jnp.bfloat16)
         grad_q = jnp.einsum("nhts,nshd->nthd", score_grad, k_blocks, preferred_element_type=jnp.float32)
-        grad_q = grad_q + scale_factor * jnp.einsum(
-            "nthe,nhde->nthd", g_blocks.astype(jnp.float32), kv_entry, precision=highest
-        )
+        grad_q = grad_q + state_mm("nthe,nhde->nthd", g_blocks, scale_factor * kv_entry)
         grad_k = jnp.einsum("nhts,nthd->nshd", score_grad, q_blocks, preferred_element_type=jnp.float32)
-        grad_k = grad_k + scale_factor * jnp.einsum(
-            "nshe,nhde->nshd", v_blocks.astype(jnp.float32), qg_entry, precision=highest
-        )
+        grad_k = grad_k + state_mm("nshe,nhde->nshd", v_blocks, scale_factor * qg_entry)
         grad_v = jnp.einsum("nhts,nthe->nshe", score_fwd, g_blocks, preferred_element_type=jnp.float32)
-        grad_v = grad_v + scale_factor * jnp.einsum(
-            "nshd,nhde->nshe", k_blocks.astype(jnp.float32), qg_entry, precision=highest
-        )
+        grad_v = grad_v + state_mm("nshd,nhde->nshe", k_blocks, scale_factor * qg_entry)
         flat = (row_count, width)
         return (
             grad_q.reshape(flat).astype(jnp.bfloat16),

time: 94 us -> 114 us (1.21)
  waiting for transfers between devices: 29.3 us -> 38.9 us
  matrix products: 30.2 us -> 35.7 us
  other arithmetic: 3.75 us -> 7.26 us
    ppermute x1, waiting for transfers between devices: 1.63 us -> 8.44 us  [project(): diag_b = lax.ppermute(from_y[:, half:], 'head', flip_pairs(4, 1))]
    ppermute x1, waiting for transfers between devices: 10.7 us -> 16.6 us  [project(): from_x = lax.ppermute(og, 'head', flip_pairs(4, 1))]
    dot_general x5, matrix products: 10.3 us -> 15.1 us  [mm(): lax.dot_general(a, b, (((1,), (1,)), ((), ())), preferred_element_type=jn...]
    ppermute x1, waiting for transfers between devices: 3.34 us -> 0.01 us  [project(): diag_a = lax.ppermute(from_x[:, :half], 'head', flip_pairs(4, 2))]
    slice x1, local copies, waits for them, and re-layouts: 0.04 us -> 2.22 us  [project(): diag_a = lax.ppermute(from_x[:, :half], 'head', flip_pairs(4, 2))]
    ppermute x1, starting transfers between devices: 1.56 us -> 3 us  [project(): from_x = lax.ppermute(og, 'head', flip_pairs(4, 1))]
    select_n x2, other arithmetic: 1.11 us -> 2.46 us  [ctx_exclusive(): lower = jnp.where(core == 0, others, theirs)]
    ppermute x1, waiting for transfers between devices: 0.01 us -> 1.35 us  [project(): from_y = lax.ppermute(og, 'head', flip_pairs(4, 2))]
  transfers between devices with their start and end apart: 12 -> 14, of which waited for: 7 -> 6; matrix products, arithmetic and copies ran while one was open for 24% -> 29% of each run, Pallas kernels for 0% -> 0%
where the time goes in v2:
time: 114 us; the launch traced here: 113 us
  waiting for transfers between devices  38.9 us (34%)
  matrix products  35.7 us (31%)
  starting transfers between devices  20.1 us (18%)
  local copies, waits for them, and re-layouts  9.68 us (8%)
  other arithmetic  7.26 us (6%)
    ppermute x1, waiting for transfers between devices, project(): from_x = lax.ppermute(og, 'head', flip_pairs(4, 1))  16.6 us
    dot_general x5, matrix products, mm(): lax.dot_general(a, b, (((1,), (1,)), ((), ())), preferred_element_type=jn...  15.1 us
    ppermute x6, starting transfers between devices, ctx_exclusive(): others = others + lax.ppermute(sent, 'ctx', pairs).astype(jnp.float32)  13.3 us
    ppermute x6, waiting for transfers between devices, ctx_exclusive(): others = others + lax.ppermute(sent, 'ctx', pairs).astype(jnp.float32)  12.4 us
    ppermute x1, waiting for transfers between devices, project(): diag_b = lax.ppermute(from_y[:, half:], 'head', flip_pairs(4, 1))  8.44 us
    unnamed x23, local copies, waits for them, and re-layouts  6.88 us
    dot_general x3, matrix products, state_mm(): jnp.einsum(spec, x, low, preferred_element_type=jnp.float32)  4.67 us
    dot_general x1, matrix products, shards(): jnp.einsum('nhts,nthe->nshe', score_fwd, g_blocks, preferred_element_type...  4.55 us
  transfers between devices with their start and end apart: 14, of which 6 were waited for; matrix products, arithmetic and copies ran while one was open for 29% of the time, Pallas kernels for 0%

profile of v2, /device:TPU:0, one launch (start us, length us, event | category | flops | bytes accessed | tf_op | source)
XLA Modules:
  0.0 112.5 jit_solution(17939749378931117314)
XLA Ops:
  0.6 3.0 %collective-permute-start = (bf16[512,1024]{1,0:T(8,128)(2,1)}, bf16[512,1024]{1,0:T(8,128)(2,1)}, u32[]{:S(2)}, u32[]{:S(2)}) collective-permute-start(bf16[512,1024]{1,0:T(8,128)(2,1)} %param.8), channel_id=1, source_target_pairs={{0,1},{1,0},{2,3},{3,2},{4,5},{5,4},{6,7},{7,6},{8,9},{9,8},{10,11... | collective-permute-start | bytes 3145736 | tf_op jit(solution)/shard_map/ppermute | solution.py:30
  3.6 1.5 %collective-permute-start.1 = (bf16[512,1024]{1,0:T(8,128)(2,1)}, bf16[512,1024]{1,0:T(8,128)(2,1)S(1)}, u32[]{:S(2)}, u32[]{:S(2)}) collective-permute-start(bf16[512,1024]{1,0:T(8,128)(2,1)} %param.8), channel_id=1, source_target_pairs={{0,2},{1,3},{2,0},{3,1},{4,6},{5,7},{6,4},{7,5},{8,10},{9,11},{10,... | collective-permute-start | bytes 3145736 | tf_op jit(solution)/shard_map/ppermute | solution.py:31
  5.9 4.6 %fusion.16 = f32[1024,512]{1,0:T(8,128)} fusion(bf16[512,1024]{1,0:T(8,128)(2,1)} %param.8, bf16[1024,4096]{1,0:T(8,128)(2,1)} %param.9, s32[]{:T(128)S(6)} %select_n.71), kind=kOutput, calls=%fused_computation.21 | convolution fusion | flops 1073741824 | bytes 5242884 | tf_op jit(solution)/shard_map/dot_general | solution.py:20
  10.5 16.6 %collective-permute-done = bf16[512,1024]{1,0:T(8,128)(2,1)} collective-permute-done((bf16[512,1024]{1,0:T(8,128)(2,1)}, bf16[512,1024]{1,0:T(8,128)(2,1)}, u32[]{:S(2)}, u32[]{:S(2)}) %collective-permute-start) | collective-permute-done | bytes 1048608 | tf_op jit(solution)/shard_map/ppermute | solution.py:30
  28.5 2.2 %slice.6 = bf16[512,512]{1,0:T(8,128)(2,1)} slice(bf16[512,1024]{1,0:T(8,128)(2,1)} %collective-permute-done), slice={[0:512], [0:512]} | slice | bytes 1048576 | tf_op jit(solution)/shard_map/slice | solution.py:33
  30.7 1.5 %collective-permute-start.2 = (bf16[512,512]{1,0:T(8,128)(2,1)}, bf16[512,512]{1,0:T(8,128)(2,1)}, u32[]{:S(2)}, u32[]{:S(2)}) collective-permute-start(bf16[512,512]{1,0:T(8,128)(2,1)} %slice.6), channel_id=1, source_target_pairs={{0,2},{1,3},{2,0},{3,1},{4,6},{5,7},{6,4},{7,5},{8,10},{9,11},{10,... | collective-permute-start | bytes 1572872 | tf_op jit(solution)/shard_map/ppermute | solution.py:33
  34.0 3.3 %fusion.14 = f32[512,1024]{0,1:T(8,128)S(1)} fusion(bf16[512,1024]{1,0:T(8,128)(2,1)} %collective-permute-done, bf16[1024,4096]{1,0:T(8,128)(2,1)} %param.9, s32[]{:T(128)S(6)} %select_n.72), kind=kOutput, calls=%fused_computation.19 | convolution fusion | flops 1073741824 | bytes 5242884 | tf_op jit(solution)/shard_map/dot_general | solution.py:20
  37.4 5.5 %collective-permute-start.7 = (bf16[8,64,128]{2,1,0:T(8,128)(2,1)S(1)}, bf16[8,64,128]{2,1,0:T(8,128)(2,1)S(1)}, u32[]{:S(2)}, u32[]{:S(2)}) collective-permute-start(bf16[8,64,128]{2,1,0:T(8,128)(2,1)S(1)} %fusion.58), channel_id=1, source_target_pairs={{0,24},{4,28},{1,25},{5,29},{2,26},{6,30},{3,27},{7,31}} | collective-permute-start | bytes 393224 | tf_op jit(solution)/shard_map/ppermute | solution.py:60
  44.3 2.5 %collective-permute-start.5 = (bf16[8,64,128]{2,1,0:T(8,128)(2,1)S(1)}, bf16[8,64,128]{2,1,0:T(8,128)(2,1)S(1)}, u32[]{:S(2)}, u32[]{:S(2)}) collective-permute-start(bf16[8,64,128]{2,1,0:T(8,128)(2,1)S(1)} %fusion.58), channel_id=1, source_target_pairs={{0,8},{4,12},{8,16},{12,20},{16,24},{20,28},{1,9},{5,13},{9,17},{1... | collective-permute-start | bytes 393224 | tf_op jit(solution)/shard_map/ppermute | solution.py:60
  46.7 2.9 %fusion.12 = f32[512,1024]{0,1:T(8,128)S(1)} fusion(bf16[512,1024]{1,0:T(8,128)(2,1)S(1)} %copy-done.9, bf16[1024,4096]{1,0:T(8,128)(2,1)} %param.9, s32[]{:T(128)S(6)} %select_n.73), kind=kOutput, calls=%fused_computation.17 | convolution fusion | flops 1073741824 | bytes 5242884 | tf_op jit(solution)/shard_map/dot_general | solution.py:20
  50.3 1.7 %collective-permute-done.5 = bf16[8,64,128]{2,1,0:T(8,128)(2,1)S(1)} collective-permute-done((bf16[8,64,128]{2,1,0:T(8,128)(2,1)S(1)}, bf16[8,64,128]{2,1,0:T(8,128)(2,1)S(1)}, u32[]{:S(2)}, u32[]{:S(2)}) %collective-permute-start.5) | collective-permute-done | bytes 131104 | tf_op jit(solution)/shard_map/ppermute | solution.py:60
  52.7 2.3 %fusion.40 = f32[512,1024]{0,1:T(8,128)S(1)} fusion(bf16[512,512]{1,0:T(8,128)(2,1)} %collective-permute-done.2, bf16[1024,4096]{1,0:T(8,128)(2,1)} %param.9, s32[]{:T(128)S(6)} %select_n.74), kind=kOutput, calls=%fused_computation.42 | convolution fusion | flops 536870912 | bytes 3670020 | tf_op jit(solution)/shard_map/dot_general | solution.py:20
  55.0 8.4 %collective-permute-done.3 = bf16[512,512]{1,0:T(8,128)(2,1)S(1)} collective-permute-done((bf16[512,512]{1,0:T(8,128)(2,1)S(1)}, bf16[512,512]{1,0:T(8,128)(2,1)S(1)}, u32[]{:S(2)}, u32[]{:S(2)}) %collective-permute-start.3) | collective-permute-done | bytes 524320 | tf_op jit(solution)/shard_map/ppermute | solution.py:34
  63.5 2.1 %fusion.11 = bf16[512,1024]{0,1:T(8,128)(2,1)S(1)} fusion(f32[512,1024]{0,1:T(8,128)S(1)} %fusion.40, f32[512,1024]{0,1:T(8,128)S(1)} %fusion.12, f32[512,1024]{0,1:T(8,128)S(1)} %fusion.14, f32[1024,512]{1,0:T(8,128)S(1)} %copy-done.7, bf16[512,512]{1,0:T(8,128)(2,1)S(1)} %collective-permute-done.3, bf16[1024,4096]{1,0:T(8,128)(2,1)} %param.9, ...), kind=kOutput, calls=%fused_computation.15 | convolution fusion | flops 539492352 | bytes 11010052 | tf_op jit(solution)/shard_map/dot_general | solution.py:20
  67.0 4.5 %fusion = f32[8,128,512]{2,1,0:T(8,128)} fusion(bf16[512,8,128]{0,2,1:T(8,128)(2,1)S(1)} %bitcast.122, pred[512,512]{1,0:T(8,128)(4,1)} %iota_compare_fusion, bf16[512,1024]{1,0:T(8,128)(2,1)} %param.5, bf16[512,1024]{1,0:T(8,128)(2,1)S(1)} %copy-done.1), kind=kOutput, calls=%fused_computation.2 | convolution fusion | flops 1080033280 | bytes 5505024 | tf_op jit(solution)/shard_map/nhts,nthe->nshe/dot_general | solution.py:135
  71.5 2.5 %select_convert_fusion.1 = bf16[8,512,512]{2,1,0:T(8,128)(2,1)S(1)} fusion(pred[512,512]{1,0:T(8,128)(4,1)} %iota_compare_fusion, bf16[512,8,128]{0,2,1:T(8,128)(2,1)S(1)} %bitcast.123, bf16[512,1024]{1,0:T(8,128)(2,1)S(1)} %copy-done), kind=kOutput, calls=%fused_computation.1 | convolution fusion | flops 543162368 | bytes 6553600 | tf_op jit(solution)/shard_map/nthe,nshe->nhts/dot_general | solution.py:127
  82.5 5.6 %collective-permute-done.12 = bf16[8,64,128]{2,1,0:T(8,128)(2,1)S(1)} collective-permute-done((bf16[8,64,128]{2,1,0:T(8,128)(2,1)S(1)}, bf16[8,64,128]{2,1,0:T(8,128)(2,1)S(1)}, u32[]{:S(2)}, u32[]{:S(2)}) %collective-permute-start.12) | collective-permute-done | bytes 131104 | tf_op jit(solution)/shard_map/ppermute | solution.py:60
  88.1 5.2 %collective-permute-done.11 = bf16[8,64,128]{2,1,0:T(8,128)(2,1)S(1)} collective-permute-done((bf16[8,64,128]{2,1,0:T(8,128)(2,1)S(1)}, bf16[8,64,128]{2,1,0:T(8,128)(2,1)S(1)}, u32[]{:S(2)}, u32[]{:S(2)}) %collective-permute-start.11) | collective-permute-done | bytes 131104 | tf_op jit(solution)/shard_map/ppermute | solution.py:60
  93.4 1.6 %fusion.7 = bf16[8,128,512]{2,1,0:T(8,128)(2,1)S(1)} fusion(f32[8,128,512]{2,1,0:T(8,128)S(1)} %fusion.60, f32[8,128,512]{2,1,0:T(8,128)S(1)} %fusion.56, bf16[8,512,512]{2,1,0:T(8,128)(2,1)S(1)} %select_convert_fusion.1, bf16[512,1024]{1,0:T(8,128)(2,1)S(1)} %copy-done.1), kind=kOutput, calls=%fused_computation.10 | convolution fusion | flops 538443776 | bytes 10485760 | tf_op jit(solution)/shard_map/nhts,nshd->nthd/dot_general | solution.py:131
  99.5 1.9 %fusion.29 = f32[8,128,512]{2,1,0:T(8,128)} fusion(f32[8,128,128]{2,1,0:T(8,128)S(1)} %fusion.55, bf16[512,1024]{1,0:T(8,128)(2,1)S(1)} %copy-done.1), kind=kOutput, calls=%fused_computation.33 | convolution fusion | flops 134348800 | bytes 3670016 | tf_op jit(solution)/shard_map/nshd,nhde->nshe/dot_general | solution.py:84
  102.3 1.9 %fusion.6 = bf16[8,128,512]{2,1,0:T(8,128)(2,1)} fusion(f32[8,128,512]{2,1,0:T(8,128)S(1)} %fusion.33, f32[8,128,512]{2,1,0:T(8,128)S(1)} %fusion.31, bf16[8,512,512]{2,1,0:T(8,128)(2,1)S(1)} %copy-done.3, bf16[512,1024]{1,0:T(8,128)(2,1)S(1)} %copy-done.6), kind=kOutput, calls=%fused_computation.8 | convolution fusion | flops 538443776 | bytes 10485760 | tf_op jit(solution)/shard_map/nhts,nthd->nshd/dot_general | solution.py:133
  104.2 2.3 %copy.29 = bf16[512,1024]{1,0:T(8,128)(2,1)} copy(bf16[512,1024]{0,1:T(8,128)(2,1)} %bitcast.126) | data formatting | bytes 2097152
  106.5 3.8 %add_convert_fusion = bf16[8,128,512]{2,1,0:T(8,128)(2,1)} fusion(f32[8,128,512]{2,1,0:T(8,128)} %fusion, f32[8,128,512]{2,1,0:T(8,128)} %fusion.29, f32[8,128,128]{2,1,0:T(8,128)S(1)} %fusion.55, bf16[512,1024]{1,0:T(8,128)(2,1)S(1)} %copy-done.1), kind=kOutput, calls=%fused_computation.16 | convolution fusion | flops 136314880 | bytes 6815744 | tf_op jit(solution)/shard_map/nshd,nhde->nshe/dot_general | solution.py:84
  110.2 2.3 %copy.30 = bf16[512,1024]{1,0:T(8,128)(2,1)} copy(bf16[512,1024]{0,1:T(8,128)(2,1)} %bitcast.128) | data formatting | bytes 2097152
  (57 shorter events, 22.1 us)
Async XLA Ops:
  0.6 32.1 %copy-start = (bf16[512,1024]{1,0:T(8,128)(2,1)S(1)}, bf16[512,1024]{1,0:T(8,128)(2,1)}, u32[]{:S(2)}) copy-start(bf16[512,1024]{1,0:T(8,128)(2,1)} %param.7) | copy-start | bytes 3145732
  0.6 26.5 %collective-permute-start = (bf16[512,1024]{1,0:T(8,128)(2,1)}, bf16[512,1024]{1,0:T(8,128)(2,1)}, u32[]{:S(2)}, u32[]{:S(2)}) collective-permute-start(bf16[512,1024]{1,0:T(8,128)(2,1)} %param.8), channel_id=1, source_target_pairs={{0,1},{1,0},{2,3},{3,2},{4,5},{5,4},{6,7},{7,6},{8,9},{9,8},{10,11... | collective-permute-start | bytes 3145736 | tf_op jit(solution)/shard_map/ppermute | solution.py:30
  3.6 24.8 %collective-permute-start.1 = (bf16[512,1024]{1,0:T(8,128)(2,1)}, bf16[512,1024]{1,0:T(8,128)(2,1)S(1)}, u32[]{:S(2)}, u32[]{:S(2)}) collective-permute-start(bf16[512,1024]{1,0:T(8,128)(2,1)} %param.8), channel_id=1, source_target_pairs={{0,2},{1,3},{2,0},{3,1},{4,6},{5,7},{6,4},{7,5},{8,10},{9,11},{10,... | collective-permute-start | bytes 3145736 | tf_op jit(solution)/shard_map/ppermute | solution.py:31
  5.9 26.3 %copy-start.1 = (bf16[512,1024]{1,0:T(8,128)(2,1)S(1)}, bf16[512,1024]{1,0:T(8,128)(2,1)}, u32[]{:S(2)}) copy-start(bf16[512,1024]{1,0:T(8,128)(2,1)} %param.6) | copy-start | bytes 3145732
  28.5 2.2 %copy-start.8 = (bf16[512,1024]{1,0:T(8,128)(2,1)}, bf16[512,1024]{1,0:T(8,128)(2,1)S(1)}, u32[]{:S(2)}) copy-start(bf16[512,1024]{1,0:T(8,128)(2,1)S(1)} %collective-permute-done.1) | copy-start | bytes 3145732
  30.7 22.0 %collective-permute-start.2 = (bf16[512,512]{1,0:T(8,128)(2,1)}, bf16[512,512]{1,0:T(8,128)(2,1)}, u32[]{:S(2)}, u32[]{:S(2)}) collective-permute-start(bf16[512,512]{1,0:T(8,128)(2,1)} %slice.6), channel_id=1, source_target_pairs={{0,2},{1,3},{2,0},{3,1},{4,6},{5,7},{6,4},{7,5},{8,10},{9,11},{10,... | collective-permute-start | bytes 1572872 | tf_op jit(solution)/shard_map/ppermute | solution.py:33
  34.0 12.7 %copy-start.9 = (bf16[512,1024]{1,0:T(8,128)(2,1)S(1)}, bf16[512,1024]{1,0:T(8,128)(2,1)}, u32[]{:S(2)}) copy-start(bf16[512,1024]{1,0:T(8,128)(2,1)} %copy-done.8) | copy-start | bytes 3145732
  34.0 3.3 %collective-permute-start.4 = (bf16[8,128,128]{2,1,0:T(8,128)(2,1)S(1)}, bf16[8,128,128]{2,1,0:T(8,128)(2,1)S(1)}, u32[]{:S(2)}, u32[]{:S(2)}) collective-permute-start(bf16[8,128,128]{2,1,0:T(8,128)(2,1)S(1)} %get-tuple-element.18), channel_id=1, source_target_pairs={{0,4},{4,0},{8,12},{12,8},{16,20},{20,16},{24,28},{28,24},{1,5},{5... | collective-permute-start | bytes 786440 | tf_op jit(solution)/shard_map/ppermute | solution.py:48
  37.4 12.9 %collective-permute-start.7 = (bf16[8,64,128]{2,1,0:T(8,128)(2,1)S(1)}, bf16[8,64,128]{2,1,0:T(8,128)(2,1)S(1)}, u32[]{:S(2)}, u32[]{:S(2)}) collective-permute-start(bf16[8,64,128]{2,1,0:T(8,128)(2,1)S(1)} %fusion.58), channel_id=1, source_target_pairs={{0,24},{4,28},{1,25},{5,29},{2,26},{6,30},{3,27},{7,31}} | collective-permute-start | bytes 393224 | tf_op jit(solution)/shard_map/ppermute | solution.py:60
  43.0 7.3 %collective-permute-start.6 = (bf16[8,64,128]{2,1,0:T(8,128)(2,1)S(1)}, bf16[8,64,128]{2,1,0:T(8,128)(2,1)S(1)}, u32[]{:S(2)}, u32[]{:S(2)}) collective-permute-start(bf16[8,64,128]{2,1,0:T(8,128)(2,1)S(1)} %fusion.58), channel_id=1, source_target_pairs={{0,16},{4,20},{8,24},{12,28},{1,17},{5,21},{9,25},{13,29},{2,18},{... | collective-permute-start | bytes 393224 | tf_op jit(solution)/shard_map/ppermute | solution.py:60
  44.3 7.7 %collective-permute-start.5 = (bf16[8,64,128]{2,1,0:T(8,128)(2,1)S(1)}, bf16[8,64,128]{2,1,0:T(8,128)(2,1)S(1)}, u32[]{:S(2)}, u32[]{:S(2)}) collective-permute-start(bf16[8,64,128]{2,1,0:T(8,128)(2,1)S(1)} %fusion.58), channel_id=1, source_target_pairs={{0,8},{4,12},{8,16},{12,20},{16,24},{20,28},{1,9},{5,13},{9,17},{1... | collective-permute-start | bytes 393224 | tf_op jit(solution)/shard_map/ppermute | solution.py:60
  49.7 13.8 %collective-permute-start.3 = (bf16[512,512]{1,0:T(8,128)(2,1)S(1)}, bf16[512,512]{1,0:T(8,128)(2,1)S(1)}, u32[]{:S(2)}, u32[]{:S(2)}) collective-permute-start(bf16[512,512]{1,0:T(8,128)(2,1)S(1)} %slice.7), channel_id=1, source_target_pairs={{0,1},{1,0},{2,3},{3,2},{4,5},{5,4},{6,7},{7,6},{8,9},{9,8},{10,11... | collective-permute-start | bytes 1572872 | tf_op jit(solution)/shard_map/ppermute | solution.py:34
  52.7 10.7 %copy-start.7 = (f32[1024,512]{1,0:T(8,128)S(1)}, f32[1024,512]{1,0:T(8,128)}, u32[]{:S(2)}) copy-start(f32[1024,512]{1,0:T(8,128)} %fusion.16) | copy-start | bytes 6291460
  52.7 21.4 %collective-permute-start.8 = (f32[8,64,128]{2,1,0:T(8,128)}, f32[8,64,128]{2,1,0:T(8,128)}, u32[]{:S(2)}, u32[]{:S(2)}) collective-permute-start(f32[8,64,128]{2,1,0:T(8,128)} %convert_add_fusion.1), channel_id=1, source_target_pairs={{0,4},{4,0},{8,12},{12,8},{16,20},{20,16},{24,28},{28,24},{1,5},{5... | collective-permute-start | bytes 786440 | tf_op jit(solution)/shard_map/ppermute | solution.py:73
  55.0 10.6 %copy-start.5 = (bf16[512,1024]{1,0:T(8,128)(2,1)S(1)}, bf16[512,1024]{1,0:T(8,128)(2,1)}, u32[]{:S(2)}) copy-start(bf16[512,1024]{1,0:T(8,128)(2,1)} %param.5) | copy-start | bytes 3145732
  67.0 9.1 %collective-permute-start.9 = (bf16[8,128,128]{2,1,0:T(8,128)(2,1)}, bf16[8,128,128]{2,1,0:T(8,128)(2,1)}, u32[]{:S(2)}, u32[]{:S(2)}) collective-permute-start(bf16[8,128,128]{2,1,0:T(8,128)(2,1)} %get-tuple-element.20), channel_id=1, source_target_pairs={{0,4},{4,0},{8,12},{12,8},{16,20},{20,16},{24,28},{28,24},{1,5},{5... | collective-permute-start | bytes 786440 | tf_op jit(solution)/shard_map/ppermute | solution.py:48
  71.5 4.0 %copy-start.4 = (f32[8,128,128]{2,1,0:T(8,128)S(1)}, f32[8,128,128]{2,1,0:T(8,128)}, u32[]{:S(2)}) copy-start(f32[8,128,128]{2,1,0:T(8,128)} %get-tuple-element.19) | copy-start | bytes 1572868
  74.1 19.4 %copy-start.2 = (bf16[8,512,512]{2,1,0:T(8,128)(2,1)}, bf16[8,512,512]{2,1,0:T(8,128)(2,1)S(1)}, u32[]{:S(2)}) copy-start(bf16[8,512,512]{2,1,0:T(8,128)(2,1)S(1)} %select_convert_fusion.1) | copy-start | bytes 12582916
  78.0 10.1 %collective-permute-start.12 = (bf16[8,64,128]{2,1,0:T(8,128)(2,1)S(1)}, bf16[8,64,128]{2,1,0:T(8,128)(2,1)S(1)}, u32[]{:S(2)}, u32[]{:S(2)}) collective-permute-start(bf16[8,64,128]{2,1,0:T(8,128)(2,1)S(1)} %fusion.57), channel_id=1, source_target_pairs={{24,0},{28,4},{25,1},{29,5},{26,2},{30,6},{27,3},{31,7}} | collective-permute-start | bytes 393224 | tf_op jit(solution)/shard_map/ppermute | solution.py:60
  79.3 14.0 %collective-permute-start.11 = (bf16[8,64,128]{2,1,0:T(8,128)(2,1)S(1)}, bf16[8,64,128]{2,1,0:T(8,128)(2,1)S(1)}, u32[]{:S(2)}, u32[]{:S(2)}) collective-permute-start(bf16[8,64,128]{2,1,0:T(8,128)(2,1)S(1)} %fusion.57), channel_id=1, source_target_pairs={{16,0},{20,4},{24,8},{28,12},{17,1},{21,5},{25,9},{29,13},{18,2},{... | collective-permute-start | bytes 393224 | tf_op jit(solution)/shard_map/ppermute | solution.py:60
  80.6 12.7 %collective-permute-start.10 = (bf16[8,64,128]{2,1,0:T(8,128)(2,1)S(1)}, bf16[8,64,128]{2,1,0:T(8,128)(2,1)S(1)}, u32[]{:S(2)}, u32[]{:S(2)}) collective-permute-start(bf16[8,64,128]{2,1,0:T(8,128)(2,1)S(1)} %fusion.57), channel_id=1, source_target_pairs={{8,0},{12,4},{16,8},{20,12},{24,16},{28,20},{9,1},{13,5},{17,9},{2... | collective-permute-start | bytes 393224 | tf_op jit(solution)/shard_map/ppermute | solution.py:60
  93.3 3.0 %collective-permute-start.13 = (f32[8,64,128]{2,1,0:T(8,128)S(1)}, f32[8,64,128]{2,1,0:T(8,128)}, u32[]{:S(2)}, u32[]{:S(2)}) collective-permute-start(f32[8,64,128]{2,1,0:T(8,128)S(1)} %convert_add_fusion), channel_id=1, source_target_pairs={{0,4},{4,0},{8,12},{12,8},{16,20},{20,16},{24,28},{28,24},{1,5},{5... | collective-permute-start | bytes 786440 | tf_op jit(solution)/shard_map/ppermute | solution.py:73
  99.0 2.9 %copy-start.3 = (bf16[8,512,512]{2,1,0:T(8,128)(2,1)S(1)}, bf16[8,512,512]{2,1,0:T(8,128)(2,1)}, u32[]{:S(2)}) copy-start(bf16[8,512,512]{2,1,0:T(8,128)(2,1)} %copy-done.2) | copy-start | bytes 12582916
  99.5 2.9 %copy-start.6 = (bf16[512,1024]{1,0:T(8,128)(2,1)S(1)}, bf16[512,1024]{1,0:T(8,128)(2,1)}, u32[]{:S(2)}) copy-start(bf16[512,1024]{1,0:T(8,128)(2,1)} %param.5) | copy-start | bytes 3145732

commit v3 on v2

--- a/solution.py
+++ b/solution.py
@@ -10,7 +10,7 @@
     return [(a, a ^ bit) for a in range(n)]
 
 
-def project(og, out_weight, head_size, tied):
+def project(og, out_weight, ctx_size, head_size, tied):
     cols = og.shape[1]
 
     def weight_cols(source, lo, width):
@@ -26,17 +26,18 @@
         full, tied = lax.optimization_barrier((full, tied))
         return mm(full, out_weight), tied
     me = lax.axis_index("head")
-    half = cols // 2
+    core = lax.axis_index("ctx") % 2
     from_x = lax.ppermute(og, "head", flip_pairs(4, 1))
     from_y = lax.ppermute(og, "head", flip_pairs(4, 2))
-    from_x, from_y, tied = lax.optimization_barrier((from_x, from_y, tied))
-    diag_a = lax.ppermute(from_x[:, :half], "head", flip_pairs(4, 2))
-    diag_b = lax.ppermute(from_y[:, half:], "head", flip_pairs(4, 1))
+    relayed = jnp.where(core == 0, from_x, from_y)
+    devices = [(p, j) for p in range(ctx_size) for j in range(4)]
+    route = [(p * 4 + j, p * 4 + (j ^ (2 if p % 2 == 0 else 1))) for p, j in devices]
+    diag = lax.ppermute(relayed, ("ctx", "head"), route)
+    diag, tied = lax.optimization_barrier((diag, tied))
     acc = mm(og, weight_cols(me, 0, cols))
     acc = acc + mm(from_x, weight_cols(me ^ 1, 0, cols))
     acc = acc + mm(from_y, weight_cols(me ^ 2, 0, cols))
-    acc = acc + mm(diag_a, weight_cols(me ^ 3, 0, half))
-    acc = acc + mm(diag_b, weight_cols(me ^ 3, half, half))
+    acc = acc + mm(diag, weight_cols(me ^ 3, 0, cols))
     return acc, tied
 
 
@@ -98,7 +99,7 @@
         q_blocks = queries.reshape(shape)
         k_blocks = keys.reshape(shape)
         v_blocks = values.reshape(shape)
-        grad_heads, (k_tied, v_tied) = project(output_grad, out_weight, head_size, (keys, values))
+        grad_heads, (k_tied, v_tied) = project(output_grad, out_weight, ctx_size, head_size, (keys, values))
         grad_heads = grad_heads.astype(jnp.bfloat16)
         kv_blocks = jnp.einsum(
             "nshd,nshe->nhde", k_tied.reshape(shape), v_tied.reshape(shape),

time: 114 us -> 107 us (0.939)
  the two profiles are of different devices: /device:TPU:0 before, /device:TPU:17 now
where the time goes in v3:
time: 107 us
  matrix products  41.8 us (39%)
  waiting for transfers between devices  31.8 us (30%)
  starting transfers between devices  21.1 us (20%)
  local copies, waits for them, and re-layouts  7.89 us (7%)
  other arithmetic  3.29 us (3%)
    ppermute x1, waiting for transfers between devices, project(): from_y = lax.ppermute(og, 'head', flip_pairs(4, 2))  21.8 us
    dot_general x4, matrix products, mm(): lax.dot_general(a, b, (((1,), (1,)), ((), ())), preferred_element_type=jn...  14.8 us
    ppermute x6, starting transfers between devices, ctx_exclusive(): others = others + lax.ppermute(sent, 'ctx', pairs).astype(jnp.float32)  12.6 us
    ppermute x6, waiting for transfers between devices, ctx_exclusive(): others = others + lax.ppermute(sent, 'ctx', pairs).astype(jnp.float32)  6.61 us
    unnamed x29, local copies, waits for them, and re-layouts  6.57 us
    dot_general x3, matrix products, state_mm(): jnp.einsum(spec, x, low, preferred_element_type=jnp.float32)  6 us
    dot_general x1, matrix products, shards(): jnp.einsum('nhts,nthd->nshd', score_grad, q_blocks, preferred_element_typ...  5.63 us
    dot_general x1, matrix products, shards(): jnp.einsum('nhts,nthe->nshe', score_fwd, g_blocks, preferred_element_type...  4.56 us
  transfers between devices with their start and end apart: 13, of which 4 were waited for; matrix products, arithmetic and copies ran while one was open for 25% of the time, Pallas kernels for 0%

profile of v3, /device:TPU:17, one launch (start us, length us, event | category | flops | bytes accessed | tf_op | source)
XLA Modules:
  0.0 106.7 jit_solution(3178154553833343958)
XLA Ops:
  3.2 21.8 %collective-permute-done.1 = bf16[512,1024]{1,0:T(8,128)(2,1)S(1)} collective-permute-done((bf16[512,1024]{1,0:T(8,128)(2,1)}, bf16[512,1024]{1,0:T(8,128)(2,1)S(1)}, u32[]{:S(2)}, u32[]{:S(2)}) %collective-permute-start.1) | collective-permute-done | bytes 1048608 | tf_op jit(solution)/shard_map/ppermute | solution.py:31
  28.0 4.3 %fusion.15 = f32[1024,512]{1,0:T(8,128)} fusion(bf16[512,1024]{1,0:T(8,128)(2,1)S(1)} %copy-done.12, bf16[1024,4096]{1,0:T(8,128)(2,1)} %param.9, s32[]{:T(128)S(6)} %select_n.78), kind=kOutput, calls=%fused_computation.20 | convolution fusion | flops 1073741824 | bytes 5242884 | tf_op jit(solution)/shard_map/dot_general | solution.py:20
  32.4 2.6 %fusion.11 = f32[1024,512]{1,0:T(8,128)} fusion(bf16[512,1024]{1,0:T(8,128)(2,1)S(1)} %collective-permute-done.1, bf16[1024,4096]{1,0:T(8,128)(2,1)S(1)} %copy-done.11, s32[]{:T(128)S(6)} %select_n.80), kind=kOutput, calls=%fused_computation.16 | convolution fusion | flops 1073741824 | bytes 5242884 | tf_op jit(solution)/shard_map/dot_general | solution.py:20
  35.0 2.6 %fusion.13 = f32[1024,512]{1,0:T(8,128)} fusion(bf16[512,1024]{1,0:T(8,128)(2,1)S(1)} %collective-permute-done, bf16[1024,4096]{1,0:T(8,128)(2,1)S(1)} %copy-done.11, s32[]{:T(128)S(6)} %select_n.79), kind=kOutput, calls=%fused_computation.18 | convolution fusion | flops 1073741824 | bytes 5242884 | tf_op jit(solution)/shard_map/dot_general | solution.py:20
  37.7 2.4 %collective-permute-done.2 = bf16[512,1024]{1,0:T(8,128)(2,1)} collective-permute-done((bf16[512,1024]{1,0:T(8,128)(2,1)S(1)}, bf16[512,1024]{1,0:T(8,128)(2,1)}, u32[]{:S(2)}, u32[]{:S(2)}) %collective-permute-start.2) | collective-permute-done | bytes 1048608 | tf_op jit(solution)/shard_map/ppermute | solution.py:35
  40.1 1.3 %copy.36 = bf16[512,1024]{0,1:T(8,128)(2,1)} copy(bf16[512,1024]{1,0:T(8,128)(2,1)S(1)} %copy-done.1) | data formatting | bytes 2097152 | tf_op jit(solution)/shard_map/reshape.7
  41.4 5.2 %fusion.8 = bf16[512,1024]{0,1:T(8,128)(2,1)S(1)} fusion(f32[1024,512]{1,0:T(8,128)} %fusion.11, f32[1024,512]{1,0:T(8,128)} %fusion.15, f32[1024,512]{1,0:T(8,128)} %fusion.13, bf16[512,1024]{1,0:T(8,128)(2,1)} %collective-permute-done.2, bf16[1024,4096]{1,0:T(8,128)(2,1)} %param.9, s32[]{:T(128)S(6)} %select_n.84), kind=kOutput, calls=%fused_computation.12 | convolution fusion | flops 1075838976 | bytes 10485764 | tf_op jit(solution)/shard_map/dot_general | solution.py:20
  47.9 2.7 %collective-permute-start.8 = (bf16[8,128,128]{2,1,0:T(8,128)(2,1)S(1)}, bf16[8,128,128]{2,1,0:T(8,128)(2,1)S(1)}, u32[]{:S(2)}, u32[]{:S(2)}) collective-permute-start(bf16[8,128,128]{2,1,0:T(8,128)(2,1)S(1)} %get-tuple-element.18), channel_id=1, source_target_pairs={{0,4},{4,0},{8,12},{12,8},{16,20},{20,16},{24,28},{28,24},{1,5},{5... | collective-permute-start | bytes 786440 | tf_op jit(solution)/shard_map/ppermute | solution.py:49
  50.6 1.4 %fusion.67 = (bf16[8,128,128]{2,1,0:T(8,128)(2,1)}, f32[8,128,128]{2,1,0:T(8,128)}) fusion(bf16[512,8,128]{0,2,1:T(8,128)(2,1)S(1)} %bitcast.121, bf16[512,1024]{1,0:T(8,128)(2,1)S(1)} %copy-done), kind=kOutput, calls=%fused_computation.81 | convolution fusion | flops 134348800 | bytes 2883584 | tf_op jit(solution)/shard_map/nshd,nshe->nhde/dot_general | solution.py:104
  54.0 2.6 %collective-permute-start.10 = (bf16[8,64,128]{2,1,0:T(8,128)(2,1)S(1)}, bf16[8,64,128]{2,1,0:T(8,128)(2,1)}, u32[]{:S(2)}, u32[]{:S(2)}) collective-permute-start(bf16[8,64,128]{2,1,0:T(8,128)(2,1)S(1)} %fusion.52), channel_id=1, source_target_pairs={{16,0},{20,4},{24,8},{28,12},{17,1},{21,5},{25,9},{29,13},{18,2},{... | collective-permute-start | bytes 393224 | tf_op jit(solution)/shard_map/ppermute | solution.py:61
  56.6 1.9 %collective-permute-start.9 = (bf16[8,64,128]{2,1,0:T(8,128)(2,1)S(1)}, bf16[8,64,128]{2,1,0:T(8,128)(2,1)}, u32[]{:S(2)}, u32[]{:S(2)}) collective-permute-start(bf16[8,64,128]{2,1,0:T(8,128)(2,1)S(1)} %fusion.52), channel_id=1, source_target_pairs={{8,0},{12,4},{16,8},{20,12},{24,16},{28,20},{9,1},{13,5},{17,9},{2... | collective-permute-start | bytes 393224 | tf_op jit(solution)/shard_map/ppermute | solution.py:61
  58.5 4.6 %fusion = f32[8,128,512]{2,1,0:T(8,128)} fusion(bf16[512,8,128]{0,2,1:T(8,128)(2,1)S(1)} %bitcast.115, pred[512,512]{1,0:T(8,128)(4,1)} %iota_compare_fusion, bf16[512,1024]{1,0:T(8,128)(2,1)} %param.5, bf16[512,1024]{1,0:T(8,128)(2,1)S(1)} %copy-done.1), kind=kOutput, calls=%fused_computation.2 | convolution fusion | flops 1080033280 | bytes 5505024 | tf_op jit(solution)/shard_map/nhts,nthe->nshe/dot_general | solution.py:136
  66.1 4.8 %collective-permute-start.4 = (bf16[8,64,128]{2,1,0:T(8,128)(2,1)S(1)}, bf16[8,64,128]{2,1,0:T(8,128)(2,1)S(1)}, u32[]{:S(2)}, u32[]{:S(2)}) collective-permute-start(bf16[8,64,128]{2,1,0:T(8,128)(2,1)S(1)} %fusion.53), channel_id=1, source_target_pairs={{0,8},{4,12},{8,16},{12,20},{16,24},{20,28},{1,9},{5,13},{9,17},{1... | collective-permute-start | bytes 393224 | tf_op jit(solution)/shard_map/ppermute | solution.py:61
  72.0 1.4 %collective-permute-start.12 = (f32[8,64,128]{2,1,0:T(8,128)S(1)}, f32[8,64,128]{2,1,0:T(8,128)S(1)}, u32[]{:S(2)}, u32[]{:S(2)}) collective-permute-start(f32[8,64,128]{2,1,0:T(8,128)S(1)} %convert_add_fusion), channel_id=1, source_target_pairs={{0,4},{4,0},{8,12},{12,8},{16,20},{20,16},{24,28},{28,24},{1,5},{5... | collective-permute-start | bytes 786440 | tf_op jit(solution)/shard_map/ppermute | solution.py:74
  73.4 2.5 %select_convert_fusion.1 = bf16[8,512,512]{2,1,0:T(8,128)(2,1)S(1)} fusion(pred[512,512]{1,0:T(8,128)(4,1)} %iota_compare_fusion, bf16[512,8,128]{0,2,1:T(8,128)(2,1)S(1)} %bitcast.116, bf16[512,1024]{1,0:T(8,128)(2,1)S(1)} %copy-done), kind=kOutput, calls=%fused_computation.1 | convolution fusion | flops 543162368 | bytes 6553600 | tf_op jit(solution)/shard_map/nthe,nshe->nhts/dot_general | solution.py:128
  76.0 6.6 %collective-permute-done.4 = bf16[8,64,128]{2,1,0:T(8,128)(2,1)S(1)} collective-permute-done((bf16[8,64,128]{2,1,0:T(8,128)(2,1)S(1)}, bf16[8,64,128]{2,1,0:T(8,128)(2,1)S(1)}, u32[]{:S(2)}, u32[]{:S(2)}) %collective-permute-start.4) | collective-permute-done | bytes 131104 | tf_op jit(solution)/shard_map/ppermute | solution.py:61
  83.4 1.8 %fusion.34 = f32[8,128,512]{2,1,0:T(8,128)} fusion(f32[8,128,128]{2,1,0:T(8,128)S(1)} %fusion.50, bf16[512,1024]{1,0:T(8,128)(2,1)S(1)} %copy-done), kind=kOutput, calls=%fused_computation.36 | convolution fusion | flops 134348800 | bytes 3670016 | tf_op jit(solution)/shard_map/nshe,nhde->nshd/dot_general | solution.py:85
  85.2 1.8 %fusion.32 = f32[8,128,512]{2,1,0:T(8,128)} fusion(f32[8,128,128]{2,1,0:T(8,128)S(1)} %fusion.50, bf16[512,1024]{1,0:T(8,128)(2,1)S(1)} %copy-done), kind=kOutput, calls=%fused_computation.34 | convolution fusion | flops 134742016 | bytes 3670016 | tf_op jit(solution)/shard_map/nshe,nhde->nshd/dot_general | solution.py:85
  87.0 1.9 %fusion.30 = f32[8,128,512]{2,1,0:T(8,128)} fusion(f32[8,128,128]{2,1,0:T(8,128)S(1)} %fusion.50, bf16[512,1024]{1,0:T(8,128)(2,1)S(1)} %copy-done.1), kind=kOutput, calls=%fused_computation.32 | convolution fusion | flops 134348800 | bytes 3670016 | tf_op jit(solution)/shard_map/nshd,nhde->nshe/dot_general | solution.py:85
  89.9 1.6 %fusion.7 = bf16[8,128,512]{2,1,0:T(8,128)(2,1)S(1)} fusion(f32[8,128,512]{2,1,0:T(8,128)S(1)} %fusion.55, f32[8,128,512]{2,1,0:T(8,128)S(1)} %fusion.51, bf16[8,512,512]{2,1,0:T(8,128)(2,1)S(1)} %select_convert_fusion.1, bf16[512,1024]{1,0:T(8,128)(2,1)S(1)} %copy-done.1), kind=kOutput, calls=%fused_computation.10 | convolution fusion | flops 538443776 | bytes 10485760 | tf_op jit(solution)/shard_map/nhts,nshd->nthd/dot_general | solution.py:132
  92.8 5.6 %fusion.6 = bf16[8,128,512]{2,1,0:T(8,128)(2,1)} fusion(f32[8,128,512]{2,1,0:T(8,128)} %fusion.34, f32[8,128,512]{2,1,0:T(8,128)} %fusion.32, bf16[8,512,512]{2,1,0:T(8,128)(2,1)} %copy-done.2, bf16[512,1024]{1,0:T(8,128)(2,1)} %param.5), kind=kOutput, calls=%fused_computation.8 | convolution fusion | flops 538443776 | bytes 10485760 | tf_op jit(solution)/shard_map/nhts,nthd->nshd/dot_general | solution.py:134
  98.4 2.3 %copy.26 = bf16[512,1024]{1,0:T(8,128)(2,1)} copy(bf16[512,1024]{0,1:T(8,128)(2,1)} %bitcast.119) | data formatting | bytes 2097152
  100.7 3.7 %add_convert_fusion = bf16[8,128,512]{2,1,0:T(8,128)(2,1)} fusion(f32[8,128,512]{2,1,0:T(8,128)} %fusion, f32[8,128,512]{2,1,0:T(8,128)} %fusion.30, f32[8,128,128]{2,1,0:T(8,128)S(1)} %copy-done.4, bf16[512,1024]{1,0:T(8,128)(2,1)S(1)} %copy-done.1), kind=kOutput, calls=%fused_computation.13 | convolution fusion | flops 136314880 | bytes 6815744 | tf_op jit(solution)/shard_map/nshd,nhde->nshe/dot_general | solution.py:85
  104.5 2.3 %copy.27 = bf16[512,1024]{1,0:T(8,128)(2,1)} copy(bf16[512,1024]{0,1:T(8,128)(2,1)} %bitcast.122) | data formatting | bytes 2097152
  (59 shorter events, 16.0 us)
Async XLA Ops:
  0.6 50.0 %copy-start = (bf16[512,1024]{1,0:T(8,128)(2,1)S(1)}, bf16[512,1024]{1,0:T(8,128)(2,1)}, u32[]{:S(2)}) copy-start(bf16[512,1024]{1,0:T(8,128)(2,1)} %param.7) | copy-start | bytes 3145732
  0.6 24.3 %collective-permute-start.1 = (bf16[512,1024]{1,0:T(8,128)(2,1)}, bf16[512,1024]{1,0:T(8,128)(2,1)S(1)}, u32[]{:S(2)}, u32[]{:S(2)}) collective-permute-start(bf16[512,1024]{1,0:T(8,128)(2,1)} %param.8), channel_id=1, source_target_pairs={{0,2},{1,3},{2,0},{3,1},{4,6},{5,7},{6,4},{7,5},{8,10},{9,11},{10,... | collective-permute-start | bytes 3145736 | tf_op jit(solution)/shard_map/ppermute | solution.py:31
  2.0 23.9 %collective-permute-start = (bf16[512,1024]{1,0:T(8,128)(2,1)}, bf16[512,1024]{1,0:T(8,128)(2,1)S(1)}, u32[]{:S(2)}, u32[]{:S(2)}) collective-permute-start(bf16[512,1024]{1,0:T(8,128)(2,1)} %param.8), channel_id=1, source_target_pairs={{0,1},{1,0},{2,3},{3,2},{4,5},{5,4},{6,7},{7,6},{8,9},{9,8},{10,11... | collective-permute-start | bytes 3145736 | tf_op jit(solution)/shard_map/ppermute | solution.py:30
  3.2 24.9 %copy-start.12 = (bf16[512,1024]{1,0:T(8,128)(2,1)S(1)}, bf16[512,1024]{1,0:T(8,128)(2,1)}, u32[]{:S(2)}) copy-start(bf16[512,1024]{1,0:T(8,128)(2,1)} %param.8) | copy-start | bytes 3145732
  26.0 14.1 %collective-permute-start.2 = (bf16[512,1024]{1,0:T(8,128)(2,1)S(1)}, bf16[512,1024]{1,0:T(8,128)(2,1)}, u32[]{:S(2)}, u32[]{:S(2)}) collective-permute-start(bf16[512,1024]{1,0:T(8,128)(2,1)S(1)} %broadcast_select_fusion), channel_id=1, source_target_pairs={{0,2},{1,3},{2,0},{3,1},{4,5},{5,4},{6,7},{7,6},{8,10},{9,11},{10,... | collective-permute-start | bytes 3145736 | tf_op jit(solution)/shard_map/ppermute | solution.py:35
  28.0 4.3 %copy-start.11 = (bf16[1024,4096]{1,0:T(8,128)(2,1)S(1)}, bf16[1024,4096]{1,0:T(8,128)(2,1)}, u32[]{:S(2)}) copy-start(bf16[1024,4096]{1,0:T(8,128)(2,1)} %param.9) | copy-start | bytes 25165828
  35.0 5.1 %copy-start.1 = (bf16[512,1024]{1,0:T(8,128)(2,1)S(1)}, bf16[512,1024]{1,0:T(8,128)(2,1)}, u32[]{:S(2)}) copy-start(bf16[512,1024]{1,0:T(8,128)(2,1)} %param.6) | copy-start | bytes 3145732
  41.4 5.2 %copy-start.6 = (bf16[512,1024]{1,0:T(8,128)(2,1)S(1)}, bf16[512,1024]{1,0:T(8,128)(2,1)}, u32[]{:S(2)}) copy-start(bf16[512,1024]{1,0:T(8,128)(2,1)} %param.5) | copy-start | bytes 3145732
  46.6 4.1 %copy-start.7 = (bf16[512,1024]{0,1:T(8,128)(2,1)S(1)}, bf16[512,1024]{0,1:T(8,128)(2,1)}, u32[]{:S(2)}) copy-start(bf16[512,1024]{0,1:T(8,128)(2,1)} %copy.36) | copy-start | bytes 3145732
  47.9 4.1 %collective-permute-start.8 = (bf16[8,128,128]{2,1,0:T(8,128)(2,1)S(1)}, bf16[8,128,128]{2,1,0:T(8,128)(2,1)S(1)}, u32[]{:S(2)}, u32[]{:S(2)}) collective-permute-start(bf16[8,128,128]{2,1,0:T(8,128)(2,1)S(1)} %get-tuple-element.18), channel_id=1, source_target_pairs={{0,4},{4,0},{8,12},{12,8},{16,20},{20,16},{24,28},{28,24},{1,5},{5... | collective-permute-start | bytes 786440 | tf_op jit(solution)/shard_map/ppermute | solution.py:49
  52.0 11.1 %collective-permute-start.3 = (bf16[8,128,128]{2,1,0:T(8,128)(2,1)}, bf16[8,128,128]{2,1,0:T(8,128)(2,1)S(1)}, u32[]{:S(2)}, u32[]{:S(2)}) collective-permute-start(bf16[8,128,128]{2,1,0:T(8,128)(2,1)} %get-tuple-element.16), channel_id=1, source_target_pairs={{0,4},{4,0},{8,12},{12,8},{16,20},{20,16},{24,28},{28,24},{1,5},{5... | collective-permute-start | bytes 786440 | tf_op jit(solution)/shard_map/ppermute | solution.py:49
  52.7 13.4 %collective-permute-start.11 = (bf16[8,64,128]{2,1,0:T(8,128)(2,1)S(1)}, bf16[8,64,128]{2,1,0:T(8,128)(2,1)}, u32[]{:S(2)}, u32[]{:S(2)}) collective-permute-start(bf16[8,64,128]{2,1,0:T(8,128)(2,1)S(1)} %fusion.52), channel_id=1, source_target_pairs={{24,0},{28,4},{25,1},{29,5},{26,2},{30,6},{27,3},{31,7}} | collective-permute-start | bytes 393224 | tf_op jit(solution)/shard_map/ppermute | solution.py:61
  54.0 16.9 %collective-permute-start.10 = (bf16[8,64,128]{2,1,0:T(8,128)(2,1)S(1)}, bf16[8,64,128]{2,1,0:T(8,128)(2,1)}, u32[]{:S(2)}, u32[]{:S(2)}) collective-permute-start(bf16[8,64,128]{2,1,0:T(8,128)(2,1)S(1)} %fusion.52), channel_id=1, source_target_pairs={{16,0},{20,4},{24,8},{28,12},{17,1},{21,5},{25,9},{29,13},{18,2},{... | collective-permute-start | bytes 393224 | tf_op jit(solution)/shard_map/ppermute | solution.py:61
  56.6 14.3 %collective-permute-start.9 = (bf16[8,64,128]{2,1,0:T(8,128)(2,1)S(1)}, bf16[8,64,128]{2,1,0:T(8,128)(2,1)}, u32[]{:S(2)}, u32[]{:S(2)}) collective-permute-start(bf16[8,64,128]{2,1,0:T(8,128)(2,1)S(1)} %fusion.52), channel_id=1, source_target_pairs={{8,0},{12,4},{16,8},{20,12},{24,16},{28,20},{9,1},{13,5},{17,9},{2... | collective-permute-start | bytes 393224 | tf_op jit(solution)/shard_map/ppermute | solution.py:61
  64.1 11.8 %collective-permute-start.6 = (bf16[8,64,128]{2,1,0:T(8,128)(2,1)S(1)}, bf16[8,64,128]{2,1,0:T(8,128)(2,1)S(1)}, u32[]{:S(2)}, u32[]{:S(2)}) collective-permute-start(bf16[8,64,128]{2,1,0:T(8,128)(2,1)S(1)} %fusion.53), channel_id=1, source_target_pairs={{0,24},{4,28},{1,25},{5,29},{2,26},{6,30},{3,27},{7,31}} | collective-permute-start | bytes 393224 | tf_op jit(solution)/shard_map/ppermute | solution.py:61
  64.8 11.2 %collective-permute-start.5 = (bf16[8,64,128]{2,1,0:T(8,128)(2,1)S(1)}, bf16[8,64,128]{2,1,0:T(8,128)(2,1)S(1)}, u32[]{:S(2)}, u32[]{:S(2)}) collective-permute-start(bf16[8,64,128]{2,1,0:T(8,128)(2,1)S(1)} %fusion.53), channel_id=1, source_target_pairs={{0,16},{4,20},{8,24},{12,28},{1,17},{5,21},{9,25},{13,29},{2,18},{... | collective-permute-start | bytes 393224 | tf_op jit(solution)/shard_map/ppermute | solution.py:61
  66.1 16.5 %collective-permute-start.4 = (bf16[8,64,128]{2,1,0:T(8,128)(2,1)S(1)}, bf16[8,64,128]{2,1,0:T(8,128)(2,1)S(1)}, u32[]{:S(2)}, u32[]{:S(2)}) collective-permute-start(bf16[8,64,128]{2,1,0:T(8,128)(2,1)S(1)} %fusion.53), channel_id=1, source_target_pairs={{0,8},{4,12},{8,16},{12,20},{16,24},{20,28},{1,9},{5,13},{9,17},{1... | collective-permute-start | bytes 393224 | tf_op jit(solution)/shard_map/ppermute | solution.py:61
  72.0 11.2 %copy-start.8 = (f32[8,128,128]{2,1,0:T(8,128)S(1)}, f32[8,128,128]{2,1,0:T(8,128)}, u32[]{:S(2)}) copy-start(f32[8,128,128]{2,1,0:T(8,128)} %get-tuple-element.19) | copy-start | bytes 1572868
  72.0 11.2 %copy-start.10 = (bf16[8,128,128]{2,1,0:T(8,128)(2,1)S(1)}, bf16[8,128,128]{2,1,0:T(8,128)(2,1)}, u32[]{:S(2)}) copy-start(bf16[8,128,128]{2,1,0:T(8,128)(2,1)} %copy-done.9) | copy-start | bytes 786436
  72.0 11.1 %collective-permute-start.12 = (f32[8,64,128]{2,1,0:T(8,128)S(1)}, f32[8,64,128]{2,1,0:T(8,128)S(1)}, u32[]{:S(2)}, u32[]{:S(2)}) collective-permute-start(f32[8,64,128]{2,1,0:T(8,128)S(1)} %convert_add_fusion), channel_id=1, source_target_pairs={{0,4},{4,0},{8,12},{12,8},{16,20},{20,16},{24,28},{28,24},{1,5},{5... | collective-permute-start | bytes 786440 | tf_op jit(solution)/shard_map/ppermute | solution.py:74
  75.9 13.9 %copy-start.2 = (bf16[8,512,512]{2,1,0:T(8,128)(2,1)}, bf16[8,512,512]{2,1,0:T(8,128)(2,1)S(1)}, u32[]{:S(2)}) copy-start(bf16[8,512,512]{2,1,0:T(8,128)(2,1)S(1)} %select_convert_fusion.1) | copy-start | bytes 12582916
  82.6 6.3 %collective-permute-start.7 = (f32[8,64,128]{2,1,0:T(8,128)S(1)}, f32[8,64,128]{2,1,0:T(8,128)S(1)}, u32[]{:S(2)}, u32[]{:S(2)}) collective-permute-start(f32[8,64,128]{2,1,0:T(8,128)S(1)} %convert_add_fusion.1), channel_id=1, source_target_pairs={{0,4},{4,0},{8,12},{12,8},{16,20},{20,16},{24,28},{28,24},{1,5},{5... | collective-permute-start | bytes 786440 | tf_op jit(solution)/shard_map/ppermute | solution.py:74
  83.4 3.6 %copy-start.3 = (f32[8,128,128]{2,1,0:T(8,128)}, f32[8,128,128]{2,1,0:T(8,128)S(1)}, u32[]{:S(2)}) copy-start(f32[8,128,128]{2,1,0:T(8,128)S(1)} %fusion.50) | copy-start | bytes 1572868
  98.4 2.3 %copy-start.4 = (f32[8,128,128]{2,1,0:T(8,128)S(1)}, f32[8,128,128]{2,1,0:T(8,128)}, u32[]{:S(2)}) copy-start(f32[8,128,128]{2,1,0:T(8,128)} %copy-done.3) | copy-start | bytes 1572868
  (2 other events, 2.7 us)

commit v4 on v3

--- a/solution.py
+++ b/solution.py
@@ -1,6 +1,7 @@
 import jax
 import jax.numpy as jnp
 from jax import lax
+from jax.experimental import pallas as pl
 from jax.sharding import PartitionSpec as P
 
 DH = 128
@@ -79,12 +80,96 @@
     return chips_side + jnp.where(same_chip, partner.astype(jnp.float32), 0.0)
 
 
-def state_mm(spec, x, state):
+NT = (((1,), (1,)), ((), ()))
+
+
+def split_state(state):
     high = state.astype(jnp.bfloat16)
     low = (state - high.astype(jnp.float32)).astype(jnp.bfloat16)
-    return jnp.einsum(spec, x, high, preferred_element_type=jnp.float32) + jnp.einsum(
-        spec, x, low, preferred_element_type=jnp.float32
-    )
+    return high, low
+
+
+def scores_kernel(scale, q_ref, k_ref, v_ref, g_ref, kv_ref, gq_ref, gk_ref, gv_ref):
+    q, k, v, g = q_ref[...], k_ref[...], v_ref[...], g_ref[...]
+    length = q.shape[0]
+    row = lax.broadcasted_iota(jnp.int32, (length, length), 0)
+    col = lax.broadcasted_iota(jnp.int32, (length, length), 1)
+
+    def score(a, b, keep):
+        s = lax.dot_general(a, b, NT, preferred_element_type=jnp.float32) * scale
+        return jnp.where(keep, s, 0.0).astype(jnp.bfloat16)
+
+    score_grad = score(g, v, row >= col)
+    score_grad_t = score(v, g, row <= col)
+    score_fwd_t = score(k, q, row <= col)
+    high, low = split_state(kv_ref[0, 0])
+    gq = jnp.dot(score_grad, k, preferred_element_type=jnp.float32)
+    gq = gq + lax.dot_general(g, high, NT, preferred_element_type=jnp.float32)
+    gq = gq + lax.dot_general(g, low, NT, preferred_element_type=jnp.float32)
+    gq_ref[...] = gq.astype(jnp.bfloat16)
+    gk_ref[...] = jnp.dot(score_grad_t, q, preferred_element_type=jnp.float32)
+    gv_ref[...] = jnp.dot(score_fwd_t, g, preferred_element_type=jnp.float32)
+
+
+def state_kernel(k_ref, v_ref, qg_ref, gkp_ref, gvp_ref, gk_ref, gv_ref):
+    k, v = k_ref[...], v_ref[...]
+    high, low = split_state(qg_ref[0, 0])
+    gk = gkp_ref[...] + lax.dot_general(v, high, NT, preferred_element_type=jnp.float32)
+    gk = gk + lax.dot_general(v, low, NT, preferred_element_type=jnp.float32)
+    gv = gvp_ref[...] + jnp.dot(k, high, preferred_element_type=jnp.float32)
+    gv = gv + jnp.dot(k, low, preferred_element_type=jnp.float32)
+    gk_ref[...] = gk.astype(jnp.bfloat16)
+    gv_ref[...] = gv.astype(jnp.bfloat16)
+
+
+def specs(blocks, block_len, heads):
+    tok = pl.BlockSpec((block_len, DH), lambda n, h: (n, h))
+    st = pl.BlockSpec((1, 1, DH, DH), lambda n, h: (n, h, 0, 0))
+    return tok, st
+
+
+def attention_part(q, k, v, g, kv_scaled, blocks, block_len, heads, scale):
+    tok, st = specs(blocks, block_len, heads)
+    rows, width = q.shape
+    steps = blocks * heads
+    flops = steps * (6 * 2 * block_len * block_len * DH + 2 * 2 * block_len * DH * DH)
+    return pl.pallas_call(
+        lambda *refs: scores_kernel(scale, *refs),
+        grid=(blocks, heads),
+        in_specs=[tok, tok, tok, tok, st],
+        out_specs=[tok, tok, tok],
+        out_shape=[
+            jax.ShapeDtypeStruct((rows, width), jnp.bfloat16),
+            jax.ShapeDtypeStruct((rows, width), jnp.float32),
+            jax.ShapeDtypeStruct((rows, width), jnp.float32),
+        ],
+        cost_estimate=pl.CostEstimate(
+            flops=flops, transcendentals=0, bytes_accessed=rows * width * 18
+        ),
+        name="attention_part",
+    )(q, k, v, g, kv_scaled)
+
+
+def state_part(k, v, qg_scaled, gk_part, gv_part, blocks, block_len, heads):
+    tok, st = specs(blocks, block_len, heads)
+    rows, width = k.shape
+    steps = blocks * heads
+    return pl.pallas_call(
+        state_kernel,
+        grid=(blocks, heads),
+        in_specs=[tok, tok, st, tok, tok],
+        out_specs=[tok, tok],
+        out_shape=[
+            jax.ShapeDtypeStruct((rows, width), jnp.bfloat16),
+            jax.ShapeDtypeStruct((rows, width), jnp.bfloat16),
+        ],
+        cost_estimate=pl.CostEstimate(
+            flops=steps * 4 * 2 * block_len * DH * DH,
+            transcendentals=0,
+            bytes_accessed=rows * width * 16,
+        ),
+        name="state_part",
+    )(k, v, qg_scaled, gk_part, gv_part)
 
 
 def make_shards(ctx_size, head_size):
@@ -108,14 +193,10 @@
         kv_running = jnp.cumsum(kv_blocks, axis=0)
         kv_before = ctx_exclusive(kv_running[-1], ctx_size, False)
         kv_entry = kv_before[None] + kv_running - kv_blocks
-        rows = jnp.arange(block_len)
-        causal = (rows[:, None] >= rows[None, :])[None, None]
-        score_fwd = (
-            jnp.einsum("nthd,nshd->nhts", q_blocks, k_blocks, preferred_element_type=jnp.float32)
-            * scale_factor
-        )
-        score_fwd = jnp.where(causal, score_fwd, 0.0).astype(jnp.bfloat16)
-
+        gq, gk_part, gv_part = attention_part(
+            queries, keys, values, grad_heads, scale_factor * kv_entry,
+            blocks, block_len, heads, scale_factor,
+        )
         g_blocks = grad_heads.reshape(shape)
         qg_blocks = jnp.einsum(
             "nthd,nthe->nhde", q_blocks, g_blocks, preferred_element_type=jnp.float32
@@ -123,24 +204,10 @@
         qg_running = jnp.flip(jnp.cumsum(jnp.flip(qg_blocks, 0), axis=0), 0)
         qg_after = ctx_exclusive(qg_running[0], ctx_size, True)
         qg_entry = qg_after[None] + qg_running - qg_blocks
-
-        score_grad = (
-            jnp.einsum("nthe,nshe->nhts", g_blocks, v_blocks, preferred_element_type=jnp.float32)
-            * scale_factor
-        )
-        score_grad = jnp.where(causal, score_grad, 0.0).astype(jnp.bfloat16)
-        grad_q = jnp.einsum("nhts,nshd->nthd", score_grad, k_blocks, preferred_element_type=jnp.float32)
-        grad_q = grad_q + state_mm("nthe,nhde->nthd", g_blocks, scale_factor * kv_entry)
-        grad_k = jnp.einsum("nhts,nthd->nshd", score_grad, q_blocks, preferred_element_type=jnp.float32)
-        grad_k = grad_k + state_mm("nshe,nhde->nshd", v_blocks, scale_factor * qg_entry)
-        grad_v = jnp.einsum("nhts,nthe->nshe", score_fwd, g_blocks, preferred_element_type=jnp.float32)
-        grad_v = grad_v + state_mm("nshd,nhde->nshe", k_blocks, scale_factor * qg_entry)
-        flat = (row_count, width)
-        return (
-            grad_q.reshape(flat).astype(jnp.bfloat16),
-            grad_k.reshape(flat).astype(jnp.bfloat16),
-            grad_v.reshape(flat).astype(jnp.bfloat16),
-        )
+        gk, gv = state_part(
+            keys, values, scale_factor * qg_entry, gk_part, gv_part, blocks, block_len, heads
+        )
+        return gq, gk, gv
 
     return shards
 

time: 107 us -> 100 us (0.935)
  the two profiles are of different devices: /device:TPU:17 before, /device:TPU:0 now
where the time goes in v4:
time: 100 us; the launch traced here: 99.5 us
  waiting for transfers between devices  36.9 us (37%)
  starting transfers between devices  19.9 us (20%)
  Pallas kernels  18.7 us (19%)
  matrix products  17.6 us (18%)
  other arithmetic  4.29 us (4%)
  local copies, waits for them, and re-layouts  1.11 us (1%)
    ppermute x1, waiting for transfers between devices, project(): from_x = lax.ppermute(og, 'head', flip_pairs(4, 1))  21.9 us
    dot_general x4, matrix products, mm(): lax.dot_general(a, b, (((1,), (1,)), ((), ())), preferred_element_type=jn...  14.4 us
    ppermute x6, starting transfers between devices, ctx_exclusive(): others = others + lax.ppermute(sent, 'ctx', pairs).astype(jnp.float32)  13.2 us
    pallas_call x1, Pallas kernels, attention_part(): pl.pallas_call(lambda *refs: scores_kernel(scale, *refs), grid=(blocks, h...  11.1 us
    ppermute x6, waiting for transfers between devices, ctx_exclusive(): others = others + lax.ppermute(sent, 'ctx', pairs).astype(jnp.float32)  10.5 us
    pallas_call x1, Pallas kernels, state_part(): pl.pallas_call(state_kernel, grid=(blocks, heads), in_specs=[tok, tok, st...  7.6 us
    ppermute x1, waiting for transfers between devices, project(): diag = lax.ppermute(relayed, ('ctx', 'head'), route)  3.07 us
    ppermute x1, starting transfers between devices, project(): from_x = lax.ppermute(og, 'head', flip_pairs(4, 1))  3 us
  transfers between devices with their start and end apart: 13, of which 6 were waited for; matrix products, arithmetic and copies ran while one was open for 18% of the time, Pallas kernels for 11%

profile of v4, /device:TPU:0, one launch (start us, length us, event | category | flops | bytes accessed | tf_op | source)
XLA Modules:
  0.0 99.5 jit_solution(1825395075226116436)
XLA Ops:
  0.6 3.0 %collective-permute-start = (bf16[512,1024]{1,0:T(8,128)(2,1)}, bf16[512,1024]{1,0:T(8,128)(2,1)S(1)}, u32[]{:S(2)}, u32[]{:S(2)}) collective-permute-start(bf16[512,1024]{1,0:T(8,128)(2,1)} %param.8), channel_id=1, source_target_pairs={{0,1},{1,0},{2,3},{3,2},{4,5},{5,4},{6,7},{7,6},{8,9},{9,8},{10,11... | collective-permute-start | bytes 3145736 | tf_op jit(solution)/shard_map/ppermute | solution.py:31
  3.6 1.5 %collective-permute-start.1 = (bf16[512,1024]{1,0:T(8,128)(2,1)}, bf16[512,1024]{1,0:T(8,128)(2,1)S(1)}, u32[]{:S(2)}, u32[]{:S(2)}) collective-permute-start(bf16[512,1024]{1,0:T(8,128)(2,1)} %param.8), channel_id=1, source_target_pairs={{0,2},{1,3},{2,0},{3,1},{4,6},{5,7},{6,4},{7,5},{8,10},{9,11},{10,... | collective-permute-start | bytes 3145736 | tf_op jit(solution)/shard_map/ppermute | solution.py:32
  5.2 21.9 %collective-permute-done = bf16[512,1024]{1,0:T(8,128)(2,1)S(1)} collective-permute-done((bf16[512,1024]{1,0:T(8,128)(2,1)}, bf16[512,1024]{1,0:T(8,128)(2,1)S(1)}, u32[]{:S(2)}, u32[]{:S(2)}) %collective-permute-start) | collective-permute-done | bytes 1048608 | tf_op jit(solution)/shard_map/ppermute | solution.py:31
  27.0 1.5 %collective-permute-done.1 = bf16[512,1024]{1,0:T(8,128)(2,1)S(1)} collective-permute-done((bf16[512,1024]{1,0:T(8,128)(2,1)}, bf16[512,1024]{1,0:T(8,128)(2,1)S(1)}, u32[]{:S(2)}, u32[]{:S(2)}) %collective-permute-start.1) | collective-permute-done | bytes 1048608 | tf_op jit(solution)/shard_map/ppermute | solution.py:32
  28.5 1.2 %broadcast_select_fusion = bf16[512,1024]{1,0:T(8,128)(2,1)} fusion(bf16[512,1024]{1,0:T(8,128)(2,1)S(1)} %collective-permute-done, bf16[512,1024]{1,0:T(8,128)(2,1)S(1)} %collective-permute-done.1, pred[]{:T(512)S(6)} %eq.8), kind=kLoop, calls=%fused_computation.16 | loop fusion | flops 524288 | bytes 3145729 | tf_op jit(solution)/shard_map/jit(_where)/select_n | solution.py:33
  29.6 1.5 %collective-permute-start.2 = (bf16[512,1024]{1,0:T(8,128)(2,1)}, bf16[512,1024]{1,0:T(8,128)(2,1)}, u32[]{:S(2)}, u32[]{:S(2)}) collective-permute-start(bf16[512,1024]{1,0:T(8,128)(2,1)} %broadcast_select_fusion), channel_id=1, source_target_pairs={{0,2},{1,3},{2,0},{3,1},{4,5},{5,4},{6,7},{7,6},{8,10},{9,11},{10,... | collective-permute-start | bytes 3145736 | tf_op jit(solution)/shard_map/ppermute | solution.py:36
  31.7 4.7 %fusion.7 = f32[1024,512]{0,1:T(8,128)} fusion(bf16[512,1024]{1,0:T(8,128)(2,1)} %param.8, bf16[1024,4096]{1,0:T(8,128)(2,1)} %param.9, s32[]{:T(128)S(6)} %select_n.69), kind=kOutput, calls=%fused_computation.8 | convolution fusion | flops 1073741824 | bytes 5242884 | tf_op jit(solution)/shard_map/dot_general | solution.py:21
  36.4 2.6 %fusion.5 = f32[1024,512]{0,1:T(8,128)} fusion(bf16[512,1024]{1,0:T(8,128)(2,1)S(1)} %collective-permute-done, bf16[1024,4096]{1,0:T(8,128)(2,1)S(1)} %copy-done.7, s32[]{:T(128)S(6)} %select_n.70), kind=kOutput, calls=%fused_computation.6 | convolution fusion | flops 1073741824 | bytes 5242884 | tf_op jit(solution)/shard_map/dot_general | solution.py:21
  39.1 2.6 %fusion.3 = f32[1024,512]{0,1:T(8,128)} fusion(bf16[512,1024]{1,0:T(8,128)(2,1)S(1)} %copy-done.6, bf16[1024,4096]{1,0:T(8,128)(2,1)S(1)} %copy-done.7, s32[]{:T(128)S(6)} %select_n.71), kind=kOutput, calls=%fused_computation.4 | convolution fusion | flops 1073741824 | bytes 5242884 | tf_op jit(solution)/shard_map/dot_general | solution.py:21
  41.7 3.1 %collective-permute-done.2 = bf16[512,1024]{1,0:T(8,128)(2,1)} collective-permute-done((bf16[512,1024]{1,0:T(8,128)(2,1)}, bf16[512,1024]{1,0:T(8,128)(2,1)}, u32[]{:S(2)}, u32[]{:S(2)}) %collective-permute-start.2) | collective-permute-done | bytes 1048608 | tf_op jit(solution)/shard_map/ppermute | solution.py:36
  45.3 2.7 %fusion.26 = (bf16[8,128,128]{2,1,0:T(8,128)(2,1)}, f32[8,128,128]{2,1,0:T(8,128)}) fusion(bf16[512,8,128]{0,2,1:T(8,128)(2,1)S(1)} %bitcast.37, bf16[512,1024]{1,0:T(8,128)(2,1)} %v_ref.1), kind=kOutput, calls=%fused_computation.39 | convolution fusion | flops 134348800 | bytes 2883584 | tf_op jit(solution)/shard_map/nshd,nshe->nhde/dot_general | solution.py:189
  48.0 4.5 %fusion.refs_3_ = bf16[512,1024]{1,0:T(8,128)(2,1)S(1)} fusion(f32[1024,512]{0,1:T(8,128)} %fusion.3, f32[1024,512]{0,1:T(8,128)S(1)} %copy-done.2, f32[1024,512]{0,1:T(8,128)} %fusion.5, bf16[512,1024]{1,0:T(8,128)(2,1)} %collective-permute-done.2, bf16[1024,4096]{1,0:T(8,128)(2,1)} %param.9, s32[]{:T(128)S(6)} %select_n.75), kind=kOutput, calls=%fused_computation.1 | convolution fusion | flops 1075838976 | bytes 10485764 | tf_op jit(solution)/shard_map/dot_general | solution.py:21
  53.6 1.0 %fusion.21 = bf16[8,64,128]{2,1,0:T(8,128)(2,1)S(1)} fusion(f32[8,128,128]{2,1,0:T(8,128)S(1)} %convert_element_type.50, s32[]{:T(128)S(6)} %select_n.77, bf16[8,128,128]{2,1,0:T(8,128)(2,1)} %get-tuple-element.23), kind=kLoop, calls=%fused_computation.28 | loop fusion | flops 196608 | bytes 524292 | tf_op jit(solution)/shard_map/convert_element_type | solution.py:56
  54.7 3.5 %collective-permute-start.4 = (bf16[8,64,128]{2,1,0:T(8,128)(2,1)S(1)}, bf16[8,64,128]{2,1,0:T(8,128)(2,1)S(1)}, u32[]{:S(2)}, u32[]{:S(2)}) collective-permute-start(bf16[8,64,128]{2,1,0:T(8,128)(2,1)S(1)} %fusion.21), channel_id=1, source_target_pairs={{0,8},{4,12},{8,16},{12,20},{16,24},{20,28},{1,9},{5,13},{9,17},{1... | collective-permute-start | bytes 393224 | tf_op jit(solution)/shard_map/ppermute | solution.py:62
  58.2 4.5 %collective-permute-start.5 = (bf16[8,64,128]{2,1,0:T(8,128)(2,1)S(1)}, bf16[8,64,128]{2,1,0:T(8,128)(2,1)S(1)}, u32[]{:S(2)}, u32[]{:S(2)}) collective-permute-start(bf16[8,64,128]{2,1,0:T(8,128)(2,1)S(1)} %fusion.21), channel_id=1, source_target_pairs={{0,16},{4,20},{8,24},{12,28},{1,17},{5,21},{9,25},{13,29},{2,18},{... | collective-permute-start | bytes 393224 | tf_op jit(solution)/shard_map/ppermute | solution.py:62
  62.7 1.3 %collective-permute-start.6 = (bf16[8,64,128]{2,1,0:T(8,128)(2,1)S(1)}, bf16[8,64,128]{2,1,0:T(8,128)(2,1)S(1)}, u32[]{:S(2)}, u32[]{:S(2)}) collective-permute-start(bf16[8,64,128]{2,1,0:T(8,128)(2,1)S(1)} %fusion.21), channel_id=1, source_target_pairs={{0,24},{4,28},{1,25},{5,29},{2,26},{6,30},{3,27},{7,31}} | collective-permute-start | bytes 393224 | tf_op jit(solution)/shard_map/ppermute | solution.py:62
  64.1 1.3 %collective-permute-start.10 = (bf16[8,64,128]{2,1,0:T(8,128)(2,1)S(1)}, bf16[8,64,128]{2,1,0:T(8,128)(2,1)S(1)}, u32[]{:S(2)}, u32[]{:S(2)}) collective-permute-start(bf16[8,64,128]{2,1,0:T(8,128)(2,1)S(1)} %fusion.20), channel_id=1, source_target_pairs={{16,0},{20,4},{24,8},{28,12},{17,1},{21,5},{25,9},{29,13},{18,2},{... | collective-permute-start | bytes 393224 | tf_op jit(solution)/shard_map/ppermute | solution.py:62
  65.4 1.3 %collective-permute-start.11 = (bf16[8,64,128]{2,1,0:T(8,128)(2,1)S(1)}, bf16[8,64,128]{2,1,0:T(8,128)(2,1)S(1)}, u32[]{:S(2)}, u32[]{:S(2)}) collective-permute-start(bf16[8,64,128]{2,1,0:T(8,128)(2,1)S(1)} %fusion.20), channel_id=1, source_target_pairs={{24,0},{28,4},{25,1},{29,5},{26,2},{30,6},{27,3},{31,7}} | collective-permute-start | bytes 393224 | tf_op jit(solution)/shard_map/ppermute | solution.py:62
  66.7 1.3 %collective-permute-start.9 = (bf16[8,64,128]{2,1,0:T(8,128)(2,1)S(1)}, bf16[8,64,128]{2,1,0:T(8,128)(2,1)S(1)}, u32[]{:S(2)}, u32[]{:S(2)}) collective-permute-start(bf16[8,64,128]{2,1,0:T(8,128)(2,1)S(1)} %fusion.20), channel_id=1, source_target_pairs={{8,0},{12,4},{16,8},{20,12},{24,16},{28,20},{9,1},{13,5},{17,9},{2... | collective-permute-start | bytes 393224 | tf_op jit(solution)/shard_map/ppermute | solution.py:62
  68.3 7.8 %collective-permute-done.10 = bf16[8,64,128]{2,1,0:T(8,128)(2,1)S(1)} collective-permute-done((bf16[8,64,128]{2,1,0:T(8,128)(2,1)S(1)}, bf16[8,64,128]{2,1,0:T(8,128)(2,1)S(1)}, u32[]{:S(2)}, u32[]{:S(2)}) %collective-permute-start.10) | collective-permute-done | bytes 131104 | tf_op jit(solution)/shard_map/ppermute | solution.py:62
  76.1 2.5 %collective-permute-done.9 = bf16[8,64,128]{2,1,0:T(8,128)(2,1)S(1)} collective-permute-done((bf16[8,64,128]{2,1,0:T(8,128)(2,1)S(1)}, bf16[8,64,128]{2,1,0:T(8,128)(2,1)S(1)}, u32[]{:S(2)}, u32[]{:S(2)}) %collective-permute-start.9) | collective-permute-done | bytes 131104 | tf_op jit(solution)/shard_map/ppermute | solution.py:62
  79.7 11.1 %attention_part.1 = (bf16[512,1024]{1,0:T(8,128)(2,1)}, f32[512,1024]{1,0:T(8,128)}, f32[512,1024]{1,0:T(8,128)}) custom-call(bf16[512,1024]{1,0:T(8,128)(2,1)} %refs_0_.1, bf16[512,1024]{1,0:T(8,128)(2,1)} %k_ref.1, bf16[512,1024]{1,0:T(8,128)(2,1)} %v_ref.1, bf16[512,1024]{1,0:T(8,128)(2,1)} %copy-done.1, f32[1,8,128,128]{3,2,1,0:T(8,128)} %fusion.17.refs_4_), custom_call_target="tpu_custom_call" | custom-call | flops 3489660928 | bytes 9437184 | tf_op jit(solution)/shard_map/attention_part/pallas_call | solution.py:136
  90.9 0.9 fusion.19.qg_ref
  91.9 7.6 %state_part.1 = (bf16[512,1024]{1,0:T(8,128)(2,1)}, bf16[512,1024]{1,0:T(8,128)(2,1)}) custom-call(bf16[512,1024]{1,0:T(8,128)(2,1)} %k_ref.1, bf16[512,1024]{1,0:T(8,128)(2,1)} %v_ref.1, f32[1,8,128,128]{3,2,1,0:T(8,128)} %fusion.19.qg_ref, f32[512,1024]{1,0:T(8,128)} %get-tuple-element.15.gkp_ref, f32[512,1024]{1,0:T(8,128)} %get-tuple-element.16.gvp_ref), custom_call_target="tpu_custom_call" | custom-call | flops 536870912 | bytes 8388608 | tf_op jit(solution)/shard_map/state_part/pallas_call | solution.py:157
  (39 shorter events, 3.7 us)
Async XLA Ops:
  0.6 30.5 %copy-start.4 = (bf16[512,1024]{1,0:T(8,128)(2,1)S(1)}, bf16[512,1024]{1,0:T(8,128)(2,1)}, u32[]{:S(2)}) copy-start(bf16[512,1024]{1,0:T(8,128)(2,1)} %refs_0_.1) | copy-start | bytes 3145732
  0.6 26.4 %collective-permute-start = (bf16[512,1024]{1,0:T(8,128)(2,1)}, bf16[512,1024]{1,0:T(8,128)(2,1)S(1)}, u32[]{:S(2)}, u32[]{:S(2)}) collective-permute-start(bf16[512,1024]{1,0:T(8,128)(2,1)} %param.8), channel_id=1, source_target_pairs={{0,1},{1,0},{2,3},{3,2},{4,5},{5,4},{6,7},{7,6},{8,9},{9,8},{10,11... | collective-permute-start | bytes 3145736 | tf_op jit(solution)/shard_map/ppermute | solution.py:31
  3.6 24.8 %collective-permute-start.1 = (bf16[512,1024]{1,0:T(8,128)(2,1)}, bf16[512,1024]{1,0:T(8,128)(2,1)S(1)}, u32[]{:S(2)}, u32[]{:S(2)}) collective-permute-start(bf16[512,1024]{1,0:T(8,128)(2,1)} %param.8), channel_id=1, source_target_pairs={{0,2},{1,3},{2,0},{3,1},{4,6},{5,7},{6,4},{7,5},{8,10},{9,11},{10,... | collective-permute-start | bytes 3145736 | tf_op jit(solution)/shard_map/ppermute | solution.py:32
  28.5 2.7 %copy-start.5 = (bf16[512,1024]{1,0:T(8,128)(2,1)}, bf16[512,1024]{1,0:T(8,128)(2,1)S(1)}, u32[]{:S(2)}) copy-start(bf16[512,1024]{1,0:T(8,128)(2,1)S(1)} %collective-permute-done.1) | copy-start | bytes 3145732
  29.6 15.1 %collective-permute-start.2 = (bf16[512,1024]{1,0:T(8,128)(2,1)}, bf16[512,1024]{1,0:T(8,128)(2,1)}, u32[]{:S(2)}, u32[]{:S(2)}) collective-permute-start(bf16[512,1024]{1,0:T(8,128)(2,1)} %broadcast_select_fusion), channel_id=1, source_target_pairs={{0,2},{1,3},{2,0},{3,1},{4,5},{5,4},{6,7},{7,6},{8,10},{9,11},{10,... | collective-permute-start | bytes 3145736 | tf_op jit(solution)/shard_map/ppermute | solution.py:36
  31.7 4.7 %copy-start.7 = (bf16[1024,4096]{1,0:T(8,128)(2,1)S(1)}, bf16[1024,4096]{1,0:T(8,128)(2,1)}, u32[]{:S(2)}) copy-start(bf16[1024,4096]{1,0:T(8,128)(2,1)} %param.9) | copy-start | bytes 25165828
  36.4 2.6 %copy-start.6 = (bf16[512,1024]{1,0:T(8,128)(2,1)S(1)}, bf16[512,1024]{1,0:T(8,128)(2,1)}, u32[]{:S(2)}) copy-start(bf16[512,1024]{1,0:T(8,128)(2,1)} %copy-done.5) | copy-start | bytes 3145732
  39.1 5.7 %copy-start = (bf16[512,1024]{1,0:T(8,128)(2,1)S(1)}, bf16[512,1024]{1,0:T(8,128)(2,1)}, u32[]{:S(2)}) copy-start(bf16[512,1024]{1,0:T(8,128)(2,1)} %k_ref.1) | copy-start | bytes 3145732
  45.3 2.7 %copy-start.2 = (f32[1024,512]{0,1:T(8,128)S(1)}, f32[1024,512]{0,1:T(8,128)}, u32[]{:S(2)}) copy-start(f32[1024,512]{0,1:T(8,128)} %fusion.7) | copy-start | bytes 6291460
  48.0 5.6 %collective-permute-start.3 = (bf16[8,128,128]{2,1,0:T(8,128)(2,1)}, bf16[8,128,128]{2,1,0:T(8,128)(2,1)S(1)}, u32[]{:S(2)}, u32[]{:S(2)}) collective-permute-start(bf16[8,128,128]{2,1,0:T(8,128)(2,1)} %get-tuple-element.23), channel_id=1, source_target_pairs={{0,4},{4,0},{8,12},{12,8},{16,20},{20,16},{24,28},{28,24},{1,5},{5... | collective-permute-start | bytes 786440 | tf_op jit(solution)/shard_map/ppermute | solution.py:50
  52.5 2.1 %copy-start.1 = (bf16[512,1024]{1,0:T(8,128)(2,1)}, bf16[512,1024]{1,0:T(8,128)(2,1)S(1)}, u32[]{:S(2)}) copy-start(bf16[512,1024]{1,0:T(8,128)(2,1)S(1)} %fusion.refs_3_) | copy-start | bytes 3145732
  53.0 10.9 %collective-permute-start.8 = (bf16[8,128,128]{2,1,0:T(8,128)(2,1)S(1)}, bf16[8,128,128]{2,1,0:T(8,128)(2,1)S(1)}, u32[]{:S(2)}, u32[]{:S(2)}) collective-permute-start(bf16[8,128,128]{2,1,0:T(8,128)(2,1)S(1)} %get-tuple-element.25), channel_id=1, source_target_pairs={{0,4},{4,0},{8,12},{12,8},{16,20},{20,16},{24,28},{28,24},{1,5},{5... | collective-permute-start | bytes 786440 | tf_op jit(solution)/shard_map/ppermute | solution.py:50
  53.6 25.2 %copy-start.3 = (f32[8,128,128]{2,1,0:T(8,128)S(1)}, f32[8,128,128]{2,1,0:T(8,128)}, u32[]{:S(2)}) copy-start(f32[8,128,128]{2,1,0:T(8,128)} %get-tuple-element.24) | copy-start | bytes 1572868
  54.7 12.0 %collective-permute-start.4 = (bf16[8,64,128]{2,1,0:T(8,128)(2,1)S(1)}, bf16[8,64,128]{2,1,0:T(8,128)(2,1)S(1)}, u32[]{:S(2)}, u32[]{:S(2)}) collective-permute-start(bf16[8,64,128]{2,1,0:T(8,128)(2,1)S(1)} %fusion.21), channel_id=1, source_target_pairs={{0,8},{4,12},{8,16},{12,20},{16,24},{20,28},{1,9},{5,13},{9,17},{1... | collective-permute-start | bytes 393224 | tf_op jit(solution)/shard_map/ppermute | solution.py:62
  58.2 9.8 %collective-permute-start.5 = (bf16[8,64,128]{2,1,0:T(8,128)(2,1)S(1)}, bf16[8,64,128]{2,1,0:T(8,128)(2,1)S(1)}, u32[]{:S(2)}, u32[]{:S(2)}) collective-permute-start(bf16[8,64,128]{2,1,0:T(8,128)(2,1)S(1)} %fusion.21), channel_id=1, source_target_pairs={{0,16},{4,20},{8,24},{12,28},{1,17},{5,21},{9,25},{13,29},{2,18},{... | collective-permute-start | bytes 393224 | tf_op jit(solution)/shard_map/ppermute | solution.py:62
  62.7 5.5 %collective-permute-start.6 = (bf16[8,64,128]{2,1,0:T(8,128)(2,1)S(1)}, bf16[8,64,128]{2,1,0:T(8,128)(2,1)S(1)}, u32[]{:S(2)}, u32[]{:S(2)}) collective-permute-start(bf16[8,64,128]{2,1,0:T(8,128)(2,1)S(1)} %fusion.21), channel_id=1, source_target_pairs={{0,24},{4,28},{1,25},{5,29},{2,26},{6,30},{3,27},{7,31}} | collective-permute-start | bytes 393224 | tf_op jit(solution)/shard_map/ppermute | solution.py:62
  64.1 12.0 %collective-permute-start.10 = (bf16[8,64,128]{2,1,0:T(8,128)(2,1)S(1)}, bf16[8,64,128]{2,1,0:T(8,128)(2,1)S(1)}, u32[]{:S(2)}, u32[]{:S(2)}) collective-permute-start(bf16[8,64,128]{2,1,0:T(8,128)(2,1)S(1)} %fusion.20), channel_id=1, source_target_pairs={{16,0},{20,4},{24,8},{28,12},{17,1},{21,5},{25,9},{29,13},{18,2},{... | collective-permute-start | bytes 393224 | tf_op jit(solution)/shard_map/ppermute | solution.py:62
  65.4 10.7 %collective-permute-start.11 = (bf16[8,64,128]{2,1,0:T(8,128)(2,1)S(1)}, bf16[8,64,128]{2,1,0:T(8,128)(2,1)S(1)}, u32[]{:S(2)}, u32[]{:S(2)}) collective-permute-start(bf16[8,64,128]{2,1,0:T(8,128)(2,1)S(1)} %fusion.20), channel_id=1, source_target_pairs={{24,0},{28,4},{25,1},{29,5},{26,2},{30,6},{27,3},{31,7}} | collective-permute-start | bytes 393224 | tf_op jit(solution)/shard_map/ppermute | solution.py:62
  66.7 12.0 %collective-permute-start.9 = (bf16[8,64,128]{2,1,0:T(8,128)(2,1)S(1)}, bf16[8,64,128]{2,1,0:T(8,128)(2,1)S(1)}, u32[]{:S(2)}, u32[]{:S(2)}) collective-permute-start(bf16[8,64,128]{2,1,0:T(8,128)(2,1)S(1)} %fusion.20), channel_id=1, source_target_pairs={{8,0},{12,4},{16,8},{20,12},{24,16},{28,20},{9,1},{13,5},{17,9},{2... | collective-permute-start | bytes 393224 | tf_op jit(solution)/shard_map/ppermute | solution.py:62
  68.2 10.6 %collective-permute-start.7 = (f32[8,64,128]{2,1,0:T(8,128)S(1)}, f32[8,64,128]{2,1,0:T(8,128)S(1)}, u32[]{:S(2)}, u32[]{:S(2)}) collective-permute-start(f32[8,64,128]{2,1,0:T(8,128)S(1)} %convert_add_fusion.1), channel_id=1, source_target_pairs={{0,4},{4,0},{8,12},{12,8},{16,20},{20,16},{24,28},{28,24},{1,5},{5... | collective-permute-start | bytes 786440 | tf_op jit(solution)/shard_map/ppermute | solution.py:75
  78.7 12.2 %collective-permute-start.12 = (f32[8,64,128]{2,1,0:T(8,128)S(1)}, f32[8,64,128]{2,1,0:T(8,128)S(1)}, u32[]{:S(2)}, u32[]{:S(2)}) collective-permute-start(f32[8,64,128]{2,1,0:T(8,128)S(1)} %convert_add_fusion), channel_id=1, source_target_pairs={{0,4},{4,0},{8,12},{12,8},{16,20},{20,16},{24,28},{28,24},{1,5},{5... | collective-permute-start | bytes 786440 | tf_op jit(solution)/shard_map/ppermute | solution.py:75

commit v5 on v4

--- a/solution.py
+++ b/solution.py
@@ -89,7 +89,7 @@
     return high, low
 
 
-def scores_kernel(scale, q_ref, k_ref, v_ref, g_ref, kv_ref, gq_ref, gk_ref, gv_ref):
+def scores_kernel(scale, q_ref, k_ref, v_ref, g_ref, gq_ref, gk_ref, gv_ref):
     q, k, v, g = q_ref[...], k_ref[...], v_ref[...], g_ref[...]
     length = q.shape[0]
     row = lax.broadcasted_iota(jnp.int32, (length, length), 0)
@@ -100,76 +100,69 @@
         return jnp.where(keep, s, 0.0).astype(jnp.bfloat16)
 
     score_grad = score(g, v, row >= col)
+    gq_ref[...] = jnp.dot(score_grad, k, preferred_element_type=jnp.float32)
     score_grad_t = score(v, g, row <= col)
+    gk_ref[...] = jnp.dot(score_grad_t, q, preferred_element_type=jnp.float32)
     score_fwd_t = score(k, q, row <= col)
-    high, low = split_state(kv_ref[0, 0])
-    gq = jnp.dot(score_grad, k, preferred_element_type=jnp.float32)
-    gq = gq + lax.dot_general(g, high, NT, preferred_element_type=jnp.float32)
-    gq = gq + lax.dot_general(g, low, NT, preferred_element_type=jnp.float32)
-    gq_ref[...] = gq.astype(jnp.bfloat16)
-    gk_ref[...] = jnp.dot(score_grad_t, q, preferred_element_type=jnp.float32)
     gv_ref[...] = jnp.dot(score_fwd_t, g, preferred_element_type=jnp.float32)
 
 
-def state_kernel(k_ref, v_ref, qg_ref, gkp_ref, gvp_ref, gk_ref, gv_ref):
-    k, v = k_ref[...], v_ref[...]
-    high, low = split_state(qg_ref[0, 0])
-    gk = gkp_ref[...] + lax.dot_general(v, high, NT, preferred_element_type=jnp.float32)
-    gk = gk + lax.dot_general(v, low, NT, preferred_element_type=jnp.float32)
-    gv = gvp_ref[...] + jnp.dot(k, high, preferred_element_type=jnp.float32)
-    gv = gv + jnp.dot(k, low, preferred_element_type=jnp.float32)
-    gk_ref[...] = gk.astype(jnp.bfloat16)
-    gv_ref[...] = gv.astype(jnp.bfloat16)
-
-
-def specs(blocks, block_len, heads):
+def state_kernel(per_step, k_ref, v_ref, g_ref, kv_ref, qg_ref, gqp_ref, gkp_ref, gvp_ref,
+                 gq_ref, gk_ref, gv_ref):
+    for i in range(per_step):
+        cols = pl.ds(i * DH, DH)
+        k, v, g = k_ref[:, cols], v_ref[:, cols], g_ref[:, cols]
+        kv_high, kv_low = split_state(kv_ref[0, i])
+        qg_high, qg_low = split_state(qg_ref[0, i])
+        gq = gqp_ref[:, cols] + lax.dot_general(g, kv_high, NT, preferred_element_type=jnp.float32)
+        gq = gq + lax.dot_general(g, kv_low, NT, preferred_element_type=jnp.float32)
+        gk = gkp_ref[:, cols] + lax.dot_general(v, qg_high, NT, preferred_element_type=jnp.float32)
+        gk = gk + lax.dot_general(v, qg_low, NT, preferred_element_type=jnp.float32)
+        gv = gvp_ref[:, cols] + jnp.dot(k, qg_high, preferred_element_type=jnp.float32)
+        gv = gv + jnp.dot(k, qg_low, preferred_element_type=jnp.float32)
+        gq_ref[:, cols] = gq.astype(jnp.bfloat16)
+        gk_ref[:, cols] = gk.astype(jnp.bfloat16)
+        gv_ref[:, cols] = gv.astype(jnp.bfloat16)
+
+
+def attention_part(q, k, v, g, blocks, block_len, heads, scale):
     tok = pl.BlockSpec((block_len, DH), lambda n, h: (n, h))
-    st = pl.BlockSpec((1, 1, DH, DH), lambda n, h: (n, h, 0, 0))
-    return tok, st
-
-
-def attention_part(q, k, v, g, kv_scaled, blocks, block_len, heads, scale):
-    tok, st = specs(blocks, block_len, heads)
     rows, width = q.shape
-    steps = blocks * heads
-    flops = steps * (6 * 2 * block_len * block_len * DH + 2 * 2 * block_len * DH * DH)
+    part = jax.ShapeDtypeStruct((rows, width), jnp.float32)
     return pl.pallas_call(
         lambda *refs: scores_kernel(scale, *refs),
         grid=(blocks, heads),
-        in_specs=[tok, tok, tok, tok, st],
+        in_specs=[tok, tok, tok, tok],
         out_specs=[tok, tok, tok],
-        out_shape=[
-            jax.ShapeDtypeStruct((rows, width), jnp.bfloat16),
-            jax.ShapeDtypeStruct((rows, width), jnp.float32),
-            jax.ShapeDtypeStruct((rows, width), jnp.float32),
-        ],
+        out_shape=[part, part, part],
         cost_estimate=pl.CostEstimate(
-            flops=flops, transcendentals=0, bytes_accessed=rows * width * 18
+            flops=blocks * heads * 6 * 2 * block_len * block_len * DH,
+            transcendentals=0,
+            bytes_accessed=rows * width * 20,
         ),
         name="attention_part",
-    )(q, k, v, g, kv_scaled)
-
-
-def state_part(k, v, qg_scaled, gk_part, gv_part, blocks, block_len, heads):
-    tok, st = specs(blocks, block_len, heads)
+    )(q, k, v, g)
+
+
+def state_part(k, v, g, kv_scaled, qg_scaled, parts, blocks, block_len, heads):
+    per_step = 2 if heads % 2 == 0 else 1
+    tok = pl.BlockSpec((block_len, DH * per_step), lambda n, h: (n, h))
+    st = pl.BlockSpec((1, per_step, DH, DH), lambda n, h: (n, h, 0, 0))
     rows, width = k.shape
-    steps = blocks * heads
+    out = jax.ShapeDtypeStruct((rows, width), jnp.bfloat16)
     return pl.pallas_call(
-        state_kernel,
-        grid=(blocks, heads),
-        in_specs=[tok, tok, st, tok, tok],
-        out_specs=[tok, tok],
-        out_shape=[
-            jax.ShapeDtypeStruct((rows, width), jnp.bfloat16),
-            jax.ShapeDtypeStruct((rows, width), jnp.bfloat16),
-        ],
+        lambda *refs: state_kernel(per_step, *refs),
+        grid=(blocks, heads // per_step),
+        in_specs=[tok, tok, tok, st, st, tok, tok, tok],
+        out_specs=[tok, tok, tok],
+        out_shape=[out, out, out],
         cost_estimate=pl.CostEstimate(
-            flops=steps * 4 * 2 * block_len * DH * DH,
+            flops=blocks * heads * 6 * 2 * block_len * DH * DH,
             transcendentals=0,
-            bytes_accessed=rows * width * 16,
+            bytes_accessed=rows * width * 24,
         ),
         name="state_part",
-    )(k, v, qg_scaled, gk_part, gv_part)
+    )(k, v, g, kv_scaled, qg_scaled, *parts)
 
 
 def make_shards(ctx_size, head_size):
@@ -193,10 +186,7 @@
         kv_running = jnp.cumsum(kv_blocks, axis=0)
         kv_before = ctx_exclusive(kv_running[-1], ctx_size, False)
         kv_entry = kv_before[None] + kv_running - kv_blocks
-        gq, gk_part, gv_part = attention_part(
-            queries, keys, values, grad_heads, scale_factor * kv_entry,
-            blocks, block_len, heads, scale_factor,
-        )
+        parts = attention_part(queries, keys, values, grad_heads, blocks, block_len, heads, scale_factor)
         g_blocks = grad_heads.reshape(shape)
         qg_blocks = jnp.einsum(
             "nthd,nthe->nhde", q_blocks, g_blocks, preferred_element_type=jnp.float32
@@ -204,10 +194,10 @@
         qg_running = jnp.flip(jnp.cumsum(jnp.flip(qg_blocks, 0), axis=0), 0)
         qg_after = ctx_exclusive(qg_running[0], ctx_size, True)
         qg_entry = qg_after[None] + qg_running - qg_blocks
-        gk, gv = state_part(
-            keys, values, scale_factor * qg_entry, gk_part, gv_part, blocks, block_len, heads
-        )
-        return gq, gk, gv
+        return state_part(
+            keys, values, grad_heads, scale_factor * kv_entry, scale_factor * qg_entry,
+            parts, blocks, block_len, heads,
+        )
 
     return shards
 

time: 100 us -> 97.3 us (0.973)
  matrix products: 17.6 us -> 15.4 us
  local copies, waits for them, and re-layouts: 1.11 us -> 3.19 us
  starting transfers between devices: 19.9 us -> 18.3 us
  other arithmetic: 4.29 us -> 3.28 us
  Pallas kernels: 18.7 us -> 17.7 us
    ppermute x1, waiting for transfers between devices: 1.46 us -> 21.9 us  [project(): from_y = lax.ppermute(og, 'head', flip_pairs(4, 2))]
    ppermute x1, waiting for transfers between devices: 21.9 us -> 1.46 us  [project(): from_x = lax.ppermute(og, 'head', flip_pairs(4, 1))]
    dot_general x1, matrix products: 2.71 us -> 0.46 us  [shards(): jnp.einsum('nshd,nshe->nhde', k_tied.reshape(shape), v_tied.reshape(shape...]
    ppermute x1, starting transfers between devices: 1.52 us -> 3.03 us  [project(): from_y = lax.ppermute(og, 'head', flip_pairs(4, 2))]
    ppermute x1, starting transfers between devices: 3 us -> 1.49 us  [project(): from_x = lax.ppermute(og, 'head', flip_pairs(4, 1))]
    unnamed x16 -> x14, local copies, waits for them, and re-layouts: 0.04 us -> 1.34 us
    ppermute x1, starting transfers between devices: 1.52 us -> 0.36 us  [project(): diag = lax.ppermute(relayed, ('ctx', 'head'), route)]
  transfers between devices with their start and end apart: 13 -> 13, of which waited for: 6 -> 6; matrix products, arithmetic and copies ran while one was open for 18% -> 17% of each run, Pallas kernels for 11% -> 11%
where the time goes in v5:
time: 97.3 us; the launch traced here: 96 us
  waiting for transfers between devices  37.2 us (38%)
  starting transfers between devices  18.3 us (19%)
  Pallas kernels  17.7 us (18%)
  matrix products  15.4 us (16%)
  other arithmetic  3.28 us (3%)
  local copies, waits for them, and re-layouts  3.19 us (3%)
    ppermute x1, waiting for transfers between devices, project(): from_y = lax.ppermute(og, 'head', flip_pairs(4, 2))  21.9 us
    dot_general x4, matrix products, mm(): lax.dot_general(a, b, (((1,), (1,)), ((), ())), preferred_element_type=jn...  14.5 us
    ppermute x6, starting transfers between devices, ctx_exclusive(): others = others + lax.ppermute(sent, 'ctx', pairs).astype(jnp.float32)  13.1 us
    pallas_call x1, Pallas kernels, attention_part(): pl.pallas_call(lambda *refs: scores_kernel(scale, *refs), grid=(blocks, h...  10.9 us
    ppermute x6, waiting for transfers between devices, ctx_exclusive(): others = others + lax.ppermute(sent, 'ctx', pairs).astype(jnp.float32)  10.4 us
    pallas_call x1, Pallas kernels, state_part(): pl.pallas_call(lambda *refs: state_kernel(per_step, *refs), grid=(blocks,...  6.77 us
    ppermute x1, waiting for transfers between devices, project(): diag = lax.ppermute(relayed, ('ctx', 'head'), route)  3.46 us
    ppermute x1, starting transfers between devices, project(): from_y = lax.ppermute(og, 'head', flip_pairs(4, 2))  3.03 us
  transfers between devices with their start and end apart: 13, of which 6 were waited for; matrix products, arithmetic and copies ran while one was open for 17% of the time, Pallas kernels for 11%

profile of v5, /device:TPU:0, one launch (start us, length us, event | category | flops | bytes accessed | tf_op | source)
XLA Modules:
  0.0 96.0 jit_solution(4067756692869718703)
XLA Ops:
  0.6 3.0 %collective-permute-start.1 = (bf16[512,1024]{1,0:T(8,128)(2,1)}, bf16[512,1024]{1,0:T(8,128)(2,1)S(1)}, u32[]{:S(2)}, u32[]{:S(2)}) collective-permute-start(bf16[512,1024]{1,0:T(8,128)(2,1)} %param.8), channel_id=1, source_target_pairs={{0,2},{1,3},{2,0},{3,1},{4,6},{5,7},{6,4},{7,5},{8,10},{9,11},{10,... | collective-permute-start | bytes 3145736 | tf_op jit(solution)/shard_map/ppermute | solution.py:32
  3.7 1.5 %collective-permute-start = (bf16[512,1024]{1,0:T(8,128)(2,1)}, bf16[512,1024]{1,0:T(8,128)(2,1)S(1)}, u32[]{:S(2)}, u32[]{:S(2)}) collective-permute-start(bf16[512,1024]{1,0:T(8,128)(2,1)} %param.8), channel_id=1, source_target_pairs={{0,1},{1,0},{2,3},{3,2},{4,5},{5,4},{6,7},{7,6},{8,9},{9,8},{10,11... | collective-permute-start | bytes 3145736 | tf_op jit(solution)/shard_map/ppermute | solution.py:31
  5.2 21.9 %collective-permute-done.1 = bf16[512,1024]{1,0:T(8,128)(2,1)S(1)} collective-permute-done((bf16[512,1024]{1,0:T(8,128)(2,1)}, bf16[512,1024]{1,0:T(8,128)(2,1)S(1)}, u32[]{:S(2)}, u32[]{:S(2)}) %collective-permute-start.1) | collective-permute-done | bytes 1048608 | tf_op jit(solution)/shard_map/ppermute | solution.py:32
  27.0 1.5 %collective-permute-done = bf16[512,1024]{1,0:T(8,128)(2,1)S(1)} collective-permute-done((bf16[512,1024]{1,0:T(8,128)(2,1)}, bf16[512,1024]{1,0:T(8,128)(2,1)S(1)}, u32[]{:S(2)}, u32[]{:S(2)}) %collective-permute-start) | collective-permute-done | bytes 1048608 | tf_op jit(solution)/shard_map/ppermute | solution.py:31
  28.5 1.1 %broadcast_select_fusion = bf16[512,1024]{1,0:T(8,128)(2,1)} fusion(bf16[512,1024]{1,0:T(8,128)(2,1)S(1)} %collective-permute-done, bf16[512,1024]{1,0:T(8,128)(2,1)S(1)} %collective-permute-done.1, pred[]{:T(512)S(6)} %eq.8), kind=kLoop, calls=%fused_computation.16 | loop fusion | flops 524288 | bytes 3145729 | tf_op jit(solution)/shard_map/jit(_where)/select_n | solution.py:33
  29.9 1.3 %copy.19 = bf16[512,1024]{0,1:T(8,128)(2,1)} copy(bf16[512,1024]{1,0:T(8,128)(2,1)S(1)} %copy-done.5) | data formatting | bytes 2097152 | tf_op jit(solution)/shard_map/reshape.3
  31.3 4.6 %fusion.7 = f32[1024,512]{0,1:T(8,128)} fusion(bf16[512,1024]{1,0:T(8,128)(2,1)} %param.8, bf16[1024,4096]{1,0:T(8,128)(2,1)} %param.9, s32[]{:T(128)S(6)} %select_n.69), kind=kOutput, calls=%fused_computation.8 | convolution fusion | flops 1073741824 | bytes 5242884 | tf_op jit(solution)/shard_map/dot_general | solution.py:21
  35.9 2.7 %fusion.3 = f32[1024,512]{0,1:T(8,128)} fusion(bf16[512,1024]{1,0:T(8,128)(2,1)S(1)} %collective-permute-done.1, bf16[1024,4096]{1,0:T(8,128)(2,1)S(1)} %copy-done.6, s32[]{:T(128)S(6)} %select_n.71), kind=kOutput, calls=%fused_computation.4 | convolution fusion | flops 1073741824 | bytes 5242884 | tf_op jit(solution)/shard_map/dot_general | solution.py:21
  38.6 2.6 %fusion.5 = f32[1024,512]{0,1:T(8,128)} fusion(bf16[512,1024]{1,0:T(8,128)(2,1)S(1)} %collective-permute-done, bf16[1024,4096]{1,0:T(8,128)(2,1)S(1)} %copy-done.6, s32[]{:T(128)S(6)} %select_n.70), kind=kOutput, calls=%fused_computation.6 | convolution fusion | flops 1073741824 | bytes 5242884 | tf_op jit(solution)/shard_map/dot_general | solution.py:21
  41.2 3.5 %collective-permute-done.2 = bf16[512,1024]{1,0:T(8,128)(2,1)} collective-permute-done((bf16[512,1024]{1,0:T(8,128)(2,1)}, bf16[512,1024]{1,0:T(8,128)(2,1)}, u32[]{:S(2)}, u32[]{:S(2)}) %collective-permute-start.2) | collective-permute-done | bytes 1048608 | tf_op jit(solution)/shard_map/ppermute | solution.py:36
  45.8 1.0 %copy-done.4 = f32[1024,512]{0,1:T(8,128)S(1)} copy-done((f32[1024,512]{0,1:T(8,128)S(1)}, f32[1024,512]{0,1:T(8,128)}, u32[]{:S(2)}) %copy-start.4) | copy-done | bytes 2097176
  46.8 4.5 %fusion.refs_3_.refs_2_ = bf16[512,1024]{1,0:T(8,128)(2,1)S(1)} fusion(f32[1024,512]{0,1:T(8,128)} %fusion.3, f32[1024,512]{0,1:T(8,128)S(1)} %copy-done.4, f32[1024,512]{0,1:T(8,128)} %fusion.5, bf16[512,1024]{1,0:T(8,128)(2,1)} %collective-permute-done.2, bf16[1024,4096]{1,0:T(8,128)(2,1)} %param.9, s32[]{:T(128)S(6)} %select_n.75), kind=kOutput, calls=%fused_computation.1 | convolution fusion | flops 1075838976 | bytes 10485764 | tf_op jit(solution)/shard_map/dot_general | solution.py:21
  52.3 5.5 %collective-permute-start.6 = (bf16[8,64,128]{2,1,0:T(8,128)(2,1)S(1)}, bf16[8,64,128]{2,1,0:T(8,128)(2,1)S(1)}, u32[]{:S(2)}, u32[]{:S(2)}) collective-permute-start(bf16[8,64,128]{2,1,0:T(8,128)(2,1)S(1)} %fusion.21), channel_id=1, source_target_pairs={{0,24},{4,28},{1,25},{5,29},{2,26},{6,30},{3,27},{7,31}} | collective-permute-start | bytes 393224 | tf_op jit(solution)/shard_map/ppermute | solution.py:62
  57.8 1.3 %collective-permute-start.5 = (bf16[8,64,128]{2,1,0:T(8,128)(2,1)S(1)}, bf16[8,64,128]{2,1,0:T(8,128)(2,1)S(1)}, u32[]{:S(2)}, u32[]{:S(2)}) collective-permute-start(bf16[8,64,128]{2,1,0:T(8,128)(2,1)S(1)} %fusion.21), channel_id=1, source_target_pairs={{0,16},{4,20},{8,24},{12,28},{1,17},{5,21},{9,25},{13,29},{2,18},{... | collective-permute-start | bytes 393224 | tf_op jit(solution)/shard_map/ppermute | solution.py:62
  59.1 2.5 %collective-permute-start.4 = (bf16[8,64,128]{2,1,0:T(8,128)(2,1)S(1)}, bf16[8,64,128]{2,1,0:T(8,128)(2,1)S(1)}, u32[]{:S(2)}, u32[]{:S(2)}) collective-permute-start(bf16[8,64,128]{2,1,0:T(8,128)(2,1)S(1)} %fusion.21), channel_id=1, source_target_pairs={{0,8},{4,12},{8,16},{12,20},{16,24},{20,28},{1,9},{5,13},{9,17},{1... | collective-permute-start | bytes 393224 | tf_op jit(solution)/shard_map/ppermute | solution.py:62
  61.7 1.3 %collective-permute-start.11 = (bf16[8,64,128]{2,1,0:T(8,128)(2,1)S(1)}, bf16[8,64,128]{2,1,0:T(8,128)(2,1)S(1)}, u32[]{:S(2)}, u32[]{:S(2)}) collective-permute-start(bf16[8,64,128]{2,1,0:T(8,128)(2,1)S(1)} %fusion.20), channel_id=1, source_target_pairs={{24,0},{28,4},{25,1},{29,5},{26,2},{30,6},{27,3},{31,7}} | collective-permute-start | bytes 393224 | tf_op jit(solution)/shard_map/ppermute | solution.py:62
  63.0 1.3 %collective-permute-start.10 = (bf16[8,64,128]{2,1,0:T(8,128)(2,1)S(1)}, bf16[8,64,128]{2,1,0:T(8,128)(2,1)S(1)}, u32[]{:S(2)}, u32[]{:S(2)}) collective-permute-start(bf16[8,64,128]{2,1,0:T(8,128)(2,1)S(1)} %fusion.20), channel_id=1, source_target_pairs={{16,0},{20,4},{24,8},{28,12},{17,1},{21,5},{25,9},{29,13},{18,2},{... | collective-permute-start | bytes 393224 | tf_op jit(solution)/shard_map/ppermute | solution.py:62
  64.3 1.3 %collective-permute-start.9 = (bf16[8,64,128]{2,1,0:T(8,128)(2,1)S(1)}, bf16[8,64,128]{2,1,0:T(8,128)(2,1)S(1)}, u32[]{:S(2)}, u32[]{:S(2)}) collective-permute-start(bf16[8,64,128]{2,1,0:T(8,128)(2,1)S(1)} %fusion.20), channel_id=1, source_target_pairs={{8,0},{12,4},{16,8},{20,12},{24,16},{28,20},{9,1},{13,5},{17,9},{2... | collective-permute-start | bytes 393224 | tf_op jit(solution)/shard_map/ppermute | solution.py:62
  65.6 0.9 collective-permute-done.4
  66.7 5.2 %collective-permute-done.11 = bf16[8,64,128]{2,1,0:T(8,128)(2,1)S(1)} collective-permute-done((bf16[8,64,128]{2,1,0:T(8,128)(2,1)S(1)}, bf16[8,64,128]{2,1,0:T(8,128)(2,1)S(1)}, u32[]{:S(2)}, u32[]{:S(2)}) %collective-permute-start.11) | collective-permute-done | bytes 131104 | tf_op jit(solution)/shard_map/ppermute | solution.py:62
  71.9 4.2 %collective-permute-done.10 = bf16[8,64,128]{2,1,0:T(8,128)(2,1)S(1)} collective-permute-done((bf16[8,64,128]{2,1,0:T(8,128)(2,1)S(1)}, bf16[8,64,128]{2,1,0:T(8,128)(2,1)S(1)}, u32[]{:S(2)}, u32[]{:S(2)}) %collective-permute-start.10) | collective-permute-done | bytes 131104 | tf_op jit(solution)/shard_map/ppermute | solution.py:62
  76.3 10.9 %attention_part.1 = (f32[512,1024]{1,0:T(8,128)}, f32[512,1024]{1,0:T(8,128)}, f32[512,1024]{1,0:T(8,128)}) custom-call(bf16[512,1024]{1,0:T(8,128)(2,1)} %refs_0_.2, bf16[512,1024]{1,0:T(8,128)(2,1)} %refs_0_.3, bf16[512,1024]{1,0:T(8,128)(2,1)} %refs_1_.3, bf16[512,1024]{1,0:T(8,128)(2,1)} %copy-done), custom_call_target="tpu_custom_call" | custom-call | flops 3221225472 | bytes 10485760 | tf_op jit(solution)/shard_map/attention_part/pallas_call | solution.py:132
  87.4 0.9 fusion.19.refs_4_
  89.2 6.8 %state_part.1 = (bf16[512,1024]{1,0:T(8,128)(2,1)}, bf16[512,1024]{1,0:T(8,128)(2,1)}, bf16[512,1024]{1,0:T(8,128)(2,1)}) custom-call(bf16[512,1024]{1,0:T(8,128)(2,1)} %refs_0_.3, bf16[512,1024]{1,0:T(8,128)(2,1)} %refs_1_.3, bf16[512,1024]{1,0:T(8,128)(2,1)} %copy-done, f32[1,8,128,128]{3,2,1,0:T(8,128)} %fusion.17.refs_3_, ...), custom_call_target="tpu_custom_call" | custom-call | flops 805306368 | bytes 12582912 | tf_op jit(solution)/shard_map/state_part/pallas_call | solution.py:153
  (37 shorter events, 3.7 us)
Async XLA Ops:
  0.6 29.3 %copy-start.5 = (bf16[512,1024]{1,0:T(8,128)(2,1)S(1)}, bf16[512,1024]{1,0:T(8,128)(2,1)}, u32[]{:S(2)}) copy-start(bf16[512,1024]{1,0:T(8,128)(2,1)} %refs_0_.2) | copy-start | bytes 3145732
  0.6 26.4 %collective-permute-start.1 = (bf16[512,1024]{1,0:T(8,128)(2,1)}, bf16[512,1024]{1,0:T(8,128)(2,1)S(1)}, u32[]{:S(2)}, u32[]{:S(2)}) collective-permute-start(bf16[512,1024]{1,0:T(8,128)(2,1)} %param.8), channel_id=1, source_target_pairs={{0,2},{1,3},{2,0},{3,1},{4,6},{5,7},{6,4},{7,5},{8,10},{9,11},{10,... | collective-permute-start | bytes 3145736 | tf_op jit(solution)/shard_map/ppermute | solution.py:32
  3.7 24.8 %collective-permute-start = (bf16[512,1024]{1,0:T(8,128)(2,1)}, bf16[512,1024]{1,0:T(8,128)(2,1)S(1)}, u32[]{:S(2)}, u32[]{:S(2)}) collective-permute-start(bf16[512,1024]{1,0:T(8,128)(2,1)} %param.8), channel_id=1, source_target_pairs={{0,1},{1,0},{2,3},{3,2},{4,5},{5,4},{6,7},{7,6},{8,9},{9,8},{10,11... | collective-permute-start | bytes 3145736 | tf_op jit(solution)/shard_map/ppermute | solution.py:31
  29.6 15.1 %collective-permute-start.2 = (bf16[512,1024]{1,0:T(8,128)(2,1)}, bf16[512,1024]{1,0:T(8,128)(2,1)}, u32[]{:S(2)}, u32[]{:S(2)}) collective-permute-start(bf16[512,1024]{1,0:T(8,128)(2,1)} %broadcast_select_fusion), channel_id=1, source_target_pairs={{0,2},{1,3},{2,0},{3,1},{4,5},{5,4},{6,7},{7,6},{8,10},{9,11},{10,... | collective-permute-start | bytes 3145736 | tf_op jit(solution)/shard_map/ppermute | solution.py:36
  31.3 4.6 %copy-start.6 = (bf16[1024,4096]{1,0:T(8,128)(2,1)S(1)}, bf16[1024,4096]{1,0:T(8,128)(2,1)}, u32[]{:S(2)}) copy-start(bf16[1024,4096]{1,0:T(8,128)(2,1)} %param.9) | copy-start | bytes 25165828
  38.6 6.1 %copy-start.1 = (bf16[512,1024]{1,0:T(8,128)(2,1)S(1)}, bf16[512,1024]{1,0:T(8,128)(2,1)}, u32[]{:S(2)}) copy-start(bf16[512,1024]{1,0:T(8,128)(2,1)} %refs_0_.3) | copy-start | bytes 3145732
  41.2 4.0 %copy-start.2 = (bf16[512,1024]{1,0:T(8,128)(2,1)S(1)}, bf16[512,1024]{1,0:T(8,128)(2,1)}, u32[]{:S(2)}) copy-start(bf16[512,1024]{1,0:T(8,128)(2,1)} %refs_1_.3) | copy-start | bytes 3145732
  45.2 1.6 %copy-start.4 = (f32[1024,512]{0,1:T(8,128)S(1)}, f32[1024,512]{0,1:T(8,128)}, u32[]{:S(2)}) copy-start(f32[1024,512]{0,1:T(8,128)} %fusion.7) | copy-start | bytes 6291460
  45.7 5.6 %copy-start.3 = (bf16[512,1024]{0,1:T(8,128)(2,1)S(1)}, bf16[512,1024]{0,1:T(8,128)(2,1)}, u32[]{:S(2)}) copy-start(bf16[512,1024]{0,1:T(8,128)(2,1)} %copy.19) | copy-start | bytes 3145732
  45.7 6.2 %collective-permute-start.3 = (bf16[8,128,128]{2,1,0:T(8,128)(2,1)S(1)}, bf16[8,128,128]{2,1,0:T(8,128)(2,1)S(1)}, u32[]{:S(2)}, u32[]{:S(2)}) collective-permute-start(bf16[8,128,128]{2,1,0:T(8,128)(2,1)S(1)} %get-tuple-element.19), channel_id=1, source_target_pairs={{0,4},{4,0},{8,12},{12,8},{16,20},{20,16},{24,28},{28,24},{1,5},{5... | collective-permute-start | bytes 786440 | tf_op jit(solution)/shard_map/ppermute | solution.py:50
  51.3 1.0 %copy-start = (bf16[512,1024]{1,0:T(8,128)(2,1)}, bf16[512,1024]{1,0:T(8,128)(2,1)S(1)}, u32[]{:S(2)}) copy-start(bf16[512,1024]{1,0:T(8,128)(2,1)S(1)} %fusion.refs_3_.refs_2_) | copy-start | bytes 3145732
  51.8 9.8 %collective-permute-start.8 = (bf16[8,128,128]{2,1,0:T(8,128)(2,1)S(1)}, bf16[8,128,128]{2,1,0:T(8,128)(2,1)S(1)}, u32[]{:S(2)}, u32[]{:S(2)}) collective-permute-start(bf16[8,128,128]{2,1,0:T(8,128)(2,1)S(1)} %get-tuple-element.21), channel_id=1, source_target_pairs={{0,4},{4,0},{8,12},{12,8},{16,20},{20,16},{24,28},{28,24},{1,5},{5... | collective-permute-start | bytes 786440 | tf_op jit(solution)/shard_map/ppermute | solution.py:50
  52.3 12.0 %collective-permute-start.6 = (bf16[8,64,128]{2,1,0:T(8,128)(2,1)S(1)}, bf16[8,64,128]{2,1,0:T(8,128)(2,1)S(1)}, u32[]{:S(2)}, u32[]{:S(2)}) collective-permute-start(bf16[8,64,128]{2,1,0:T(8,128)(2,1)S(1)} %fusion.21), channel_id=1, source_target_pairs={{0,24},{4,28},{1,25},{5,29},{2,26},{6,30},{3,27},{7,31}} | collective-permute-start | bytes 393224 | tf_op jit(solution)/shard_map/ppermute | solution.py:62
  57.8 7.8 %collective-permute-start.5 = (bf16[8,64,128]{2,1,0:T(8,128)(2,1)S(1)}, bf16[8,64,128]{2,1,0:T(8,128)(2,1)S(1)}, u32[]{:S(2)}, u32[]{:S(2)}) collective-permute-start(bf16[8,64,128]{2,1,0:T(8,128)(2,1)S(1)} %fusion.21), channel_id=1, source_target_pairs={{0,16},{4,20},{8,24},{12,28},{1,17},{5,21},{9,25},{13,29},{2,18},{... | collective-permute-start | bytes 393224 | tf_op jit(solution)/shard_map/ppermute | solution.py:62
  59.1 7.5 %collective-permute-start.4 = (bf16[8,64,128]{2,1,0:T(8,128)(2,1)S(1)}, bf16[8,64,128]{2,1,0:T(8,128)(2,1)S(1)}, u32[]{:S(2)}, u32[]{:S(2)}) collective-permute-start(bf16[8,64,128]{2,1,0:T(8,128)(2,1)S(1)} %fusion.21), channel_id=1, source_target_pairs={{0,8},{4,12},{8,16},{12,20},{16,24},{20,28},{1,9},{5,13},{9,17},{1... | collective-permute-start | bytes 393224 | tf_op jit(solution)/shard_map/ppermute | solution.py:62
  61.7 10.2 %collective-permute-start.11 = (bf16[8,64,128]{2,1,0:T(8,128)(2,1)S(1)}, bf16[8,64,128]{2,1,0:T(8,128)(2,1)S(1)}, u32[]{:S(2)}, u32[]{:S(2)}) collective-permute-start(bf16[8,64,128]{2,1,0:T(8,128)(2,1)S(1)} %fusion.20), channel_id=1, source_target_pairs={{24,0},{28,4},{25,1},{29,5},{26,2},{30,6},{27,3},{31,7}} | collective-permute-start | bytes 393224 | tf_op jit(solution)/shard_map/ppermute | solution.py:62
  63.0 13.1 %collective-permute-start.10 = (bf16[8,64,128]{2,1,0:T(8,128)(2,1)S(1)}, bf16[8,64,128]{2,1,0:T(8,128)(2,1)S(1)}, u32[]{:S(2)}, u32[]{:S(2)}) collective-permute-start(bf16[8,64,128]{2,1,0:T(8,128)(2,1)S(1)} %fusion.20), channel_id=1, source_target_pairs={{16,0},{20,4},{24,8},{28,12},{17,1},{21,5},{25,9},{29,13},{18,2},{... | collective-permute-start | bytes 393224 | tf_op jit(solution)/shard_map/ppermute | solution.py:62
  64.3 11.8 %collective-permute-start.9 = (bf16[8,64,128]{2,1,0:T(8,128)(2,1)S(1)}, bf16[8,64,128]{2,1,0:T(8,128)(2,1)S(1)}, u32[]{:S(2)}, u32[]{:S(2)}) collective-permute-start(bf16[8,64,128]{2,1,0:T(8,128)(2,1)S(1)} %fusion.20), channel_id=1, source_target_pairs={{8,0},{12,4},{16,8},{20,12},{24,16},{28,20},{9,1},{13,5},{17,9},{2... | collective-permute-start | bytes 393224 | tf_op jit(solution)/shard_map/ppermute | solution.py:62
  66.6 20.6 %collective-permute-start.7 = (f32[8,64,128]{2,1,0:T(8,128)S(1)}, f32[8,64,128]{2,1,0:T(8,128)S(1)}, u32[]{:S(2)}, u32[]{:S(2)}) collective-permute-start(f32[8,64,128]{2,1,0:T(8,128)S(1)} %convert_add_fusion.1), channel_id=1, source_target_pairs={{0,4},{4,0},{8,12},{12,8},{16,20},{20,16},{24,28},{28,24},{1,5},{5... | collective-permute-start | bytes 786440 | tf_op jit(solution)/shard_map/ppermute | solution.py:75
  76.2 11.1 %collective-permute-start.12 = (f32[8,64,128]{2,1,0:T(8,128)S(1)}, f32[8,64,128]{2,1,0:T(8,128)S(1)}, u32[]{:S(2)}, u32[]{:S(2)}) collective-permute-start(f32[8,64,128]{2,1,0:T(8,128)S(1)} %convert_add_fusion), channel_id=1, source_target_pairs={{0,4},{4,0},{8,12},{12,8},{16,20},{20,16},{24,28},{28,24},{1,5},{5... | collective-permute-start | bytes 786440 | tf_op jit(solution)/shard_map/ppermute | solution.py:75

commit v6 on v5

--- a/solution.py
+++ b/solution.py
@@ -42,36 +42,42 @@
     return acc, tied
 
 
-def ctx_exclusive(state, ctx_size, reverse):
-    p = lax.axis_index("ctx")
-    core = p % 2
-    chips = ctx_size // 2
+def exchange_prepare(state, ctx_size):
+    core = lax.axis_index("ctx") % 2
     rounded = state.astype(jnp.bfloat16)
     partner = lax.ppermute(rounded, "ctx", flip_pairs(ctx_size, 1))
     chip_sum = rounded.astype(jnp.float32) + partner.astype(jnp.float32)
     half = state.shape[1] // 2
     mine = lax.dynamic_slice_in_dim(chip_sum, core * half, half, axis=1)
+    return partner, mine
+
+
+def exchange_send(mine, ctx_size, reverse):
+    chips = ctx_size // 2
+
+    def pairs(step):
+        if reverse:
+            return [(2 * (z + step) + c, 2 * z + c) for z in range(chips - step) for c in range(2)]
+        return [(2 * z + c, 2 * (z + step) + c) for z in range(chips - step) for c in range(2)]
+
     others = jnp.zeros_like(mine)
     if chips <= 4:
         sent = mine.astype(jnp.bfloat16)
         for step in range(1, chips):
-            if reverse:
-                pairs = [(2 * (z + step) + c, 2 * z + c) for z in range(chips - step) for c in range(2)]
-            else:
-                pairs = [(2 * z + c, 2 * (z + step) + c) for z in range(chips - step) for c in range(2)]
-            others = others + lax.ppermute(sent, "ctx", pairs).astype(jnp.float32)
-    else:
-        run = mine
-        step = 1
-        while step < chips:
-            if reverse:
-                pairs = [(2 * (z + step) + c, 2 * z + c) for z in range(chips - step) for c in range(2)]
-            else:
-                pairs = [(2 * z + c, 2 * (z + step) + c) for z in range(chips - step) for c in range(2)]
-            got = lax.ppermute(run.astype(jnp.bfloat16), "ctx", pairs).astype(jnp.float32)
-            run = run + got
-            others = others + got
-            step *= 2
+            others = others + lax.ppermute(sent, "ctx", pairs(step)).astype(jnp.float32)
+        return others
+    run = mine
+    step = 1
+    while step < chips:
+        got = lax.ppermute(run.astype(jnp.bfloat16), "ctx", pairs(step)).astype(jnp.float32)
+        run = run + got
+        others = others + got
+        step *= 2
+    return others
+
+
+def exchange_finish(others, partner, ctx_size, reverse):
+    core = lax.axis_index("ctx") % 2
     theirs = lax.ppermute(others, "ctx", flip_pairs(ctx_size, 1))
     lower = jnp.where(core == 0, others, theirs)
     upper = jnp.where(core == 0, theirs, others)
@@ -89,22 +95,43 @@
     return high, low
 
 
-def scores_kernel(scale, q_ref, k_ref, v_ref, g_ref, gq_ref, gk_ref, gv_ref):
-    q, k, v, g = q_ref[...], k_ref[...], v_ref[...], g_ref[...]
-    length = q.shape[0]
-    row = lax.broadcasted_iota(jnp.int32, (length, length), 0)
-    col = lax.broadcasted_iota(jnp.int32, (length, length), 1)
+def scores_kernel(scale, chunk, q_ref, k_ref, v_ref, g_ref, gq_ref, gk_ref, gv_ref):
+    length = q_ref.shape[0]
+    count = length // chunk
+    row = lax.broadcasted_iota(jnp.int32, (chunk, chunk), 0)
+    col = lax.broadcasted_iota(jnp.int32, (chunk, chunk), 1)
+
+    def piece(ref, i):
+        return ref[pl.ds(i * chunk, chunk), :]
 
     def score(a, b, keep):
         s = lax.dot_general(a, b, NT, preferred_element_type=jnp.float32) * scale
-        return jnp.where(keep, s, 0.0).astype(jnp.bfloat16)
-
-    score_grad = score(g, v, row >= col)
-    gq_ref[...] = jnp.dot(score_grad, k, preferred_element_type=jnp.float32)
-    score_grad_t = score(v, g, row <= col)
-    gk_ref[...] = jnp.dot(score_grad_t, q, preferred_element_type=jnp.float32)
-    score_fwd_t = score(k, q, row <= col)
-    gv_ref[...] = jnp.dot(score_fwd_t, g, preferred_element_type=jnp.float32)
+        if keep is not None:
+            s = jnp.where(keep, s, 0.0)
+        return s.astype(jnp.bfloat16)
+
+    for i in range(count):
+        rows = pl.ds(i * chunk, chunk)
+        g_i = piece(g_ref, i)
+        gq = None
+        for j in range(i + 1):
+            sg = score(g_i, piece(v_ref, j), row >= col if j == i else None)
+            term = jnp.dot(sg, piece(k_ref, j), preferred_element_type=jnp.float32)
+            gq = term if gq is None else gq + term
+        gq_ref[rows, :] = gq.astype(gq_ref.dtype)
+        v_i, k_i = piece(v_ref, i), piece(k_ref, i)
+        gk = None
+        gv = None
+        for j in range(i, count):
+            keep = row <= col if j == i else None
+            sgt = score(v_i, piece(g_ref, j), keep)
+            sft = score(k_i, piece(q_ref, j), keep)
+            term_k = jnp.dot(sgt, piece(q_ref, j), preferred_element_type=jnp.float32)
+            term_v = jnp.dot(sft, piece(g_ref, j), preferred_element_type=jnp.float32)
+            gk = term_k if gk is None else gk + term_k
+            gv = term_v if gv is None else gv + term_v
+        gk_ref[rows, :] = gk.astype(gk_ref.dtype)
+        gv_ref[rows, :] = gv.astype(gv_ref.dtype)
 
 
 def state_kernel(per_step, k_ref, v_ref, g_ref, kv_ref, qg_ref, gqp_ref, gkp_ref, gvp_ref,
@@ -128,9 +155,10 @@
 def attention_part(q, k, v, g, blocks, block_len, heads, scale):
     tok = pl.BlockSpec((block_len, DH), lambda n, h: (n, h))
     rows, width = q.shape
-    part = jax.ShapeDtypeStruct((rows, width), jnp.float32)
+    part = jax.ShapeDtypeStruct((rows, width), jnp.bfloat16)
+    chunk = 256 if block_len % 256 == 0 else block_len
     return pl.pallas_call(
-        lambda *refs: scores_kernel(scale, *refs),
+        lambda *refs: scores_kernel(scale, chunk, *refs),
         grid=(blocks, heads),
         in_specs=[tok, tok, tok, tok],
         out_specs=[tok, tok, tok],
@@ -138,7 +166,7 @@
         cost_estimate=pl.CostEstimate(
             flops=blocks * heads * 6 * 2 * block_len * block_len * DH,
             transcendentals=0,
-            bytes_accessed=rows * width * 20,
+            bytes_accessed=rows * width * 14,
         ),
         name="attention_part",
     )(q, k, v, g)
@@ -159,7 +187,7 @@
         cost_estimate=pl.CostEstimate(
             flops=blocks * heads * 6 * 2 * block_len * DH * DH,
             transcendentals=0,
-            bytes_accessed=rows * width * 24,
+            bytes_accessed=rows * width * 18,
         ),
         name="state_part",
     )(k, v, g, kv_scaled, qg_scaled, *parts)
@@ -184,15 +212,21 @@
             preferred_element_type=jnp.float32,
         )
         kv_running = jnp.cumsum(kv_blocks, axis=0)
-        kv_before = ctx_exclusive(kv_running[-1], ctx_size, False)
-        kv_entry = kv_before[None] + kv_running - kv_blocks
-        parts = attention_part(queries, keys, values, grad_heads, blocks, block_len, heads, scale_factor)
         g_blocks = grad_heads.reshape(shape)
         qg_blocks = jnp.einsum(
             "nthd,nthe->nhde", q_blocks, g_blocks, preferred_element_type=jnp.float32
         )
         qg_running = jnp.flip(jnp.cumsum(jnp.flip(qg_blocks, 0), axis=0), 0)
-        qg_after = ctx_exclusive(qg_running[0], ctx_size, True)
+        kv_partner, kv_mine = exchange_prepare(kv_running[-1], ctx_size)
+        qg_partner, qg_mine = exchange_prepare(qg_running[0], ctx_size)
+        kv_mine, qg_mine, g_held = lax.optimization_barrier((kv_mine, qg_mine, grad_heads))
+        kv_others = exchange_send(kv_mine, ctx_size, False)
+        qg_others = exchange_send(qg_mine, ctx_size, True)
+        parts = attention_part(queries, keys, values, g_held, blocks, block_len, heads, scale_factor)
+        kv_others, qg_others, parts = lax.optimization_barrier((kv_others, qg_others, parts))
+        kv_before = exchange_finish(kv_others, kv_partner, ctx_size, False)
+        qg_after = exchange_finish(qg_others, qg_partner, ctx_size, True)
+        kv_entry = kv_before[None] + kv_running - kv_blocks
         qg_entry = qg_after[None] + qg_running - qg_blocks
         return state_part(
             keys, values, grad_heads, scale_factor * kv_entry, scale_factor * qg_entry,

time: 97.3 us -> 92.9 us (0.955)
  waiting for transfers between devices: 37.2 us -> 32.9 us
  matrix products: 15.4 us -> 11.4 us
  starting transfers between devices: 18.3 us -> 22 us
  local copies, waits for them, and re-layouts: 3.19 us -> 4.21 us
  Pallas kernels: 17.7 us -> 16.7 us
    ppermute x1, waiting for transfers between devices: 21.9 us -> 1.46 us  [project(): from_y = lax.ppermute(og, 'head', flip_pairs(4, 2))]
    ppermute x1, waiting for transfers between devices: 1.46 us -> 21.9 us  [project(): from_x = lax.ppermute(og, 'head', flip_pairs(4, 1))]
    ppermute x10, waiting for transfers between devices: 10.4 us -> 4.26 us  [the longest x6 2.41 us: exchange_send(): others = others + lax.ppermute(sent, 'ctx', pairs(step)).astype(jnp.float32)]
    dot_general x4, matrix products: 14.5 us -> 8.41 us  [mm(): lax.dot_general(a, b, (((1,), (1,)), ((), ())), preferred_element_type=jn...]
    ppermute x10, starting transfers between devices: 13.4 us -> 16 us  [the longest x6 15.3 us: exchange_send(): others = others + lax.ppermute(sent, 'ctx', pairs(step)).astype(jnp.float32)]
    ppermute x1, waiting for transfers between devices: 3.46 us -> 5.34 us  [project(): diag = lax.ppermute(relayed, ('ctx', 'head'), route)]
    ppermute x1, starting transfers between devices: 3.03 us -> 1.52 us  [project(): from_y = lax.ppermute(og, 'head', flip_pairs(4, 2))]
    ppermute x1, starting transfers between devices: 1.49 us -> 3 us  [project(): from_x = lax.ppermute(og, 'head', flip_pairs(4, 1))]
  transfers between devices with their start and end apart: 13 -> 13, of which waited for: 6 -> 7; matrix products, arithmetic and copies ran while one was open for 17% -> 12% of each run, Pallas kernels for 11% -> 12%
where the time goes in v6:
time: 92.9 us; the launch traced here: 92.3 us
  waiting for transfers between devices  32.9 us (35%)
  starting transfers between devices  22 us (24%)
  Pallas kernels  16.7 us (18%)
  matrix products  11.4 us (12%)
  local copies, waits for them, and re-layouts  4.21 us (5%)
  other arithmetic  4.17 us (4%)
    ppermute x1, waiting for transfers between devices, project(): from_x = lax.ppermute(og, 'head', flip_pairs(4, 1))  21.9 us
    ppermute x6, starting transfers between devices, exchange_send(): others = others + lax.ppermute(sent, 'ctx', pairs(step)).astype(jnp.float32)  15.3 us
    pallas_call x1, Pallas kernels, attention_part(): pl.pallas_call(lambda *refs: scores_kernel(scale, chunk, *refs), grid=(bl...  10.7 us
    dot_general x4, matrix products, mm(): lax.dot_general(a, b, (((1,), (1,)), ((), ())), preferred_element_type=jn...  8.41 us
    pallas_call x1, Pallas kernels, state_part(): pl.pallas_call(lambda *refs: state_kernel(per_step, *refs), grid=(blocks,...  6.02 us
    ppermute x1, waiting for transfers between devices, project(): diag = lax.ppermute(relayed, ('ctx', 'head'), route)  5.34 us
    ppermute x1, starting transfers between devices, project(): from_x = lax.ppermute(og, 'head', flip_pairs(4, 1))  3 us
    ppermute x6, waiting for transfers between devices, exchange_send(): others = others + lax.ppermute(sent, 'ctx', pairs(step)).astype(jnp.float32)  2.41 us
  transfers between devices with their start and end apart: 13, of which 7 were waited for; matrix products, arithmetic and copies ran while one was open for 12% of the time, Pallas kernels for 12%

profile of v6, /device:TPU:0, one launch (start us, length us, event | category | flops | bytes accessed | tf_op | source)
XLA Modules:
  0.0 92.3 jit_solution(12422445509621698750)
XLA Ops:
  0.6 3.0 %collective-permute-start = (bf16[512,1024]{1,0:T(8,128)(2,1)}, bf16[512,1024]{1,0:T(8,128)(2,1)S(1)}, u32[]{:S(2)}, u32[]{:S(2)}) collective-permute-start(bf16[512,1024]{1,0:T(8,128)(2,1)} %param.8), channel_id=1, source_target_pairs={{0,1},{1,0},{2,3},{3,2},{4,5},{5,4},{6,7},{7,6},{8,9},{9,8},{10,11... | collective-permute-start | bytes 3145736 | tf_op jit(solution)/shard_map/ppermute | solution.py:31
  3.6 1.5 %collective-permute-start.1 = (bf16[512,1024]{1,0:T(8,128)(2,1)}, bf16[512,1024]{1,0:T(8,128)(2,1)S(1)}, u32[]{:S(2)}, u32[]{:S(2)}) collective-permute-start(bf16[512,1024]{1,0:T(8,128)(2,1)} %param.8), channel_id=1, source_target_pairs={{0,2},{1,3},{2,0},{3,1},{4,6},{5,7},{6,4},{7,5},{8,10},{9,11},{10,... | collective-permute-start | bytes 3145736 | tf_op jit(solution)/shard_map/ppermute | solution.py:32
  5.2 21.9 %collective-permute-done = bf16[512,1024]{1,0:T(8,128)(2,1)S(1)} collective-permute-done((bf16[512,1024]{1,0:T(8,128)(2,1)}, bf16[512,1024]{1,0:T(8,128)(2,1)S(1)}, u32[]{:S(2)}, u32[]{:S(2)}) %collective-permute-start) | collective-permute-done | bytes 1048608 | tf_op jit(solution)/shard_map/ppermute | solution.py:31
  27.0 1.5 %collective-permute-done.1 = bf16[512,1024]{1,0:T(8,128)(2,1)S(1)} collective-permute-done((bf16[512,1024]{1,0:T(8,128)(2,1)}, bf16[512,1024]{1,0:T(8,128)(2,1)S(1)}, u32[]{:S(2)}, u32[]{:S(2)}) %collective-permute-start.1) | collective-permute-done | bytes 1048608 | tf_op jit(solution)/shard_map/ppermute | solution.py:32
  28.5 1.1 %broadcast_select_fusion = bf16[512,1024]{1,0:T(8,128)(2,1)} fusion(bf16[512,1024]{1,0:T(8,128)(2,1)S(1)} %collective-permute-done, bf16[512,1024]{1,0:T(8,128)(2,1)S(1)} %collective-permute-done.1, pred[]{:T(512)S(6)} %eq.17), kind=kLoop, calls=%fused_computation.16 | loop fusion | flops 524288 | bytes 3145729 | tf_op jit(solution)/shard_map/jit(_where)/select_n | solution.py:33
  29.6 1.5 %collective-permute-start.2 = (bf16[512,1024]{1,0:T(8,128)(2,1)}, bf16[512,1024]{1,0:T(8,128)(2,1)}, u32[]{:S(2)}, u32[]{:S(2)}) collective-permute-start(bf16[512,1024]{1,0:T(8,128)(2,1)} %broadcast_select_fusion), channel_id=1, source_target_pairs={{0,2},{1,3},{2,0},{3,1},{4,5},{5,4},{6,7},{7,6},{8,10},{9,11},{10,... | collective-permute-start | bytes 3145736 | tf_op jit(solution)/shard_map/ppermute | solution.py:36
  31.1 1.3 %copy.19 = bf16[512,1024]{0,1:T(8,128)(2,1)} copy(bf16[512,1024]{1,0:T(8,128)(2,1)S(1)} %copy-done.5) | data formatting | bytes 2097152 | tf_op jit(solution)/shard_map/reshape.3
  32.4 3.3 %fusion.7 = f32[1024,512]{0,1:T(8,128)S(1)} fusion(bf16[512,1024]{1,0:T(8,128)(2,1)} %param.8, bf16[1024,4096]{1,0:T(8,128)(2,1)} %param.9, s32[]{:T(128)S(6)} %select_n.73), kind=kOutput, calls=%fused_computation.8 | convolution fusion | flops 1073741824 | bytes 5242884 | tf_op jit(solution)/shard_map/dot_general | solution.py:21
  36.7 1.3 %fusion.5 = f32[1024,512]{0,1:T(8,128)S(1)} fusion(bf16[512,1024]{1,0:T(8,128)(2,1)S(1)} %collective-permute-done, bf16[1024,4096]{1,0:T(8,128)(2,1)S(1)} %copy-done.6, s32[]{:T(128)S(6)} %select_n.74), kind=kOutput, calls=%fused_computation.6 | convolution fusion | flops 1073741824 | bytes 5242884 | tf_op jit(solution)/shard_map/dot_general | solution.py:21
  38.0 1.3 %fusion.3 = f32[1024,512]{0,1:T(8,128)S(1)} fusion(bf16[512,1024]{1,0:T(8,128)(2,1)S(1)} %collective-permute-done.1, bf16[1024,4096]{1,0:T(8,128)(2,1)S(1)} %copy-done.6, s32[]{:T(128)S(6)} %select_n.75), kind=kOutput, calls=%fused_computation.4 | convolution fusion | flops 1073741824 | bytes 5242884 | tf_op jit(solution)/shard_map/dot_general | solution.py:21
  39.3 5.3 %collective-permute-done.2 = bf16[512,1024]{1,0:T(8,128)(2,1)} collective-permute-done((bf16[512,1024]{1,0:T(8,128)(2,1)}, bf16[512,1024]{1,0:T(8,128)(2,1)}, u32[]{:S(2)}, u32[]{:S(2)}) %collective-permute-start.2) | collective-permute-done | bytes 1048608 | tf_op jit(solution)/shard_map/ppermute | solution.py:36
  44.7 2.5 %fusion.refs_3_.refs_2_ = bf16[512,1024]{1,0:T(8,128)(2,1)S(1)} fusion(f32[1024,512]{0,1:T(8,128)S(1)} %fusion.3, f32[1024,512]{0,1:T(8,128)S(1)} %fusion.7, f32[1024,512]{0,1:T(8,128)S(1)} %fusion.5, bf16[512,1024]{1,0:T(8,128)(2,1)} %collective-permute-done.2, bf16[1024,4096]{1,0:T(8,128)(2,1)S(1)} %copy-done.6, s32[]{:T(128)S(6)} %select_n.79), kind=kOutput, calls=%fused_computation.1 | convolution fusion | flops 1075838976 | bytes 10485764 | tf_op jit(solution)/shard_map/dot_general | solution.py:21
  47.3 1.3 %fusion.25 = (bf16[8,128,128]{2,1,0:T(8,128)(2,1)}, f32[8,128,128]{2,1,0:T(8,128)}) fusion(bf16[512,8,128]{0,2,1:T(8,128)(2,1)S(1)} %bitcast.36, bf16[512,1024]{1,0:T(8,128)(2,1)S(1)} %fusion.refs_3_.refs_2_), kind=kOutput, calls=%fused_computation.38 | convolution fusion | flops 134348800 | bytes 2883584 | tf_op jit(solution)/shard_map/nthd,nthe->nhde/dot_general | solution.py:216
  49.1 1.3 %copy.18 = bf16[512,1024]{0,1:T(8,128)(2,1)} copy(bf16[512,1024]{1,0:T(8,128)(2,1)S(1)} %copy-done.1) | data formatting | bytes 2097152 | tf_op jit(solution)/shard_map/reshape
  50.4 1.7 %fusion.24 = (bf16[8,128,128]{2,1,0:T(8,128)(2,1)S(1)}, f32[8,128,128]{2,1,0:T(8,128)S(1)}) fusion(bf16[512,8,128]{0,2,1:T(8,128)(2,1)} %bitcast.37, bf16[512,1024]{1,0:T(8,128)(2,1)S(1)} %copy-done.2), kind=kOutput, calls=%fused_computation.37 | convolution fusion | flops 134348800 | bytes 2883584 | tf_op jit(solution)/shard_map/nshd,nshe->nhde/dot_general | solution.py:210
  53.8 1.3 %collective-permute-start.10 = (bf16[8,64,128]{2,1,0:T(8,128)(2,1)S(1)}, bf16[8,64,128]{2,1,0:T(8,128)(2,1)S(1)}, u32[]{:S(2)}, u32[]{:S(2)}) collective-permute-start(bf16[8,64,128]{2,1,0:T(8,128)(2,1)S(1)} %dynamic-slice_add_fusion), channel_id=1, source_target_pairs={{24,0},{28,4},{25,1},{29,5},{26,2},{30,6},{27,3},{31,7}} | collective-permute-start | bytes 393224 | tf_op jit(solution)/shard_map/ppermute | solution.py:67
  55.1 1.3 %collective-permute-start.8 = (bf16[8,64,128]{2,1,0:T(8,128)(2,1)S(1)}, bf16[8,64,128]{2,1,0:T(8,128)(2,1)S(1)}, u32[]{:S(2)}, u32[]{:S(2)}) collective-permute-start(bf16[8,64,128]{2,1,0:T(8,128)(2,1)S(1)} %dynamic-slice_add_fusion), channel_id=1, source_target_pairs={{8,0},{12,4},{16,8},{20,12},{24,16},{28,20},{9,1},{13,5},{17,9},{2... | collective-permute-start | bytes 393224 | tf_op jit(solution)/shard_map/ppermute | solution.py:67
  56.4 1.3 %collective-permute-start.9 = (bf16[8,64,128]{2,1,0:T(8,128)(2,1)S(1)}, bf16[8,64,128]{2,1,0:T(8,128)(2,1)S(1)}, u32[]{:S(2)}, u32[]{:S(2)}) collective-permute-start(bf16[8,64,128]{2,1,0:T(8,128)(2,1)S(1)} %dynamic-slice_add_fusion), channel_id=1, source_target_pairs={{16,0},{20,4},{24,8},{28,12},{17,1},{21,5},{25,9},{29,13},{18,2},{... | collective-permute-start | bytes 393224 | tf_op jit(solution)/shard_map/ppermute | solution.py:67
  57.7 4.6 %collective-permute-start.5 = (bf16[8,64,128]{2,1,0:T(8,128)(2,1)S(1)}, bf16[8,64,128]{2,1,0:T(8,128)(2,1)S(1)}, u32[]{:S(2)}, u32[]{:S(2)}) collective-permute-start(bf16[8,64,128]{2,1,0:T(8,128)(2,1)S(1)} %dynamic-slice_add_fusion.1), channel_id=1, source_target_pairs={{0,8},{4,12},{8,16},{12,20},{16,24},{20,28},{1,9},{5,13},{9,17},{1... | collective-permute-start | bytes 393224 | tf_op jit(solution)/shard_map/ppermute | solution.py:67
  62.3 5.5 %collective-permute-start.6 = (bf16[8,64,128]{2,1,0:T(8,128)(2,1)S(1)}, bf16[8,64,128]{2,1,0:T(8,128)(2,1)S(1)}, u32[]{:S(2)}, u32[]{:S(2)}) collective-permute-start(bf16[8,64,128]{2,1,0:T(8,128)(2,1)S(1)} %dynamic-slice_add_fusion.1), channel_id=1, source_target_pairs={{0,16},{4,20},{8,24},{12,28},{1,17},{5,21},{9,25},{13,29},{2,18},{... | collective-permute-start | bytes 393224 | tf_op jit(solution)/shard_map/ppermute | solution.py:67
  67.7 10.7 %attention_part.1 = (bf16[512,1024]{1,0:T(8,128)(2,1)}, bf16[512,1024]{1,0:T(8,128)(2,1)}, bf16[512,1024]{1,0:T(8,128)(2,1)}) custom-call(bf16[512,1024]{1,0:T(8,128)(2,1)} %refs_0_.2, bf16[512,1024]{1,0:T(8,128)(2,1)} %refs_0_.3, bf16[512,1024]{1,0:T(8,128)(2,1)} %refs_1_.3, bf16[512,1024]{1,0:T(8,128)(2,1)} %copy-done), custom_call_target="tpu_custom_call" | custom-call | flops 3221225472 | bytes 7340032 | tf_op jit(solution)/shard_map/attention_part/pallas_call | solution.py:160
  78.4 1.4 %collective-permute-start.7 = (bf16[8,64,128]{2,1,0:T(8,128)(2,1)S(1)}, bf16[8,64,128]{2,1,0:T(8,128)(2,1)S(1)}, u32[]{:S(2)}, u32[]{:S(2)}) collective-permute-start(bf16[8,64,128]{2,1,0:T(8,128)(2,1)S(1)} %dynamic-slice_add_fusion.1), channel_id=1, source_target_pairs={{0,24},{4,28},{1,25},{5,29},{2,26},{6,30},{3,27},{7,31}} | collective-permute-start | bytes 393224 | tf_op jit(solution)/shard_map/ppermute | solution.py:67
  79.9 2.4 %collective-permute-done.7 = bf16[8,64,128]{2,1,0:T(8,128)(2,1)S(1)} collective-permute-done((bf16[8,64,128]{2,1,0:T(8,128)(2,1)S(1)}, bf16[8,64,128]{2,1,0:T(8,128)(2,1)S(1)}, u32[]{:S(2)}, u32[]{:S(2)}) %collective-permute-start.7) | collective-permute-done | bytes 131104 | tf_op jit(solution)/shard_map/ppermute | solution.py:67
  86.3 6.0 %state_part.1 = (bf16[512,1024]{1,0:T(8,128)(2,1)}, bf16[512,1024]{1,0:T(8,128)(2,1)}, bf16[512,1024]{1,0:T(8,128)(2,1)}) custom-call(bf16[512,1024]{1,0:T(8,128)(2,1)} %refs_0_.3, bf16[512,1024]{1,0:T(8,128)(2,1)} %refs_1_.3, bf16[512,1024]{1,0:T(8,128)(2,1)} %copy-done, f32[1,8,128,128]{3,2,1,0:T(8,128)} %fusion.17.refs_3_, ...), custom_call_target="tpu_custom_call" | custom-call | flops 805306368 | bytes 9437184 | tf_op jit(solution)/shard_map/state_part/pallas_call | solution.py:181
  (37 shorter events, 7.2 us)
Async XLA Ops:
  0.6 30.4 %copy-start.5 = (bf16[512,1024]{1,0:T(8,128)(2,1)S(1)}, bf16[512,1024]{1,0:T(8,128)(2,1)}, u32[]{:S(2)}) copy-start(bf16[512,1024]{1,0:T(8,128)(2,1)} %refs_0_.2) | copy-start | bytes 3145732
  0.6 26.4 %collective-permute-start = (bf16[512,1024]{1,0:T(8,128)(2,1)}, bf16[512,1024]{1,0:T(8,128)(2,1)S(1)}, u32[]{:S(2)}, u32[]{:S(2)}) collective-permute-start(bf16[512,1024]{1,0:T(8,128)(2,1)} %param.8), channel_id=1, source_target_pairs={{0,1},{1,0},{2,3},{3,2},{4,5},{5,4},{6,7},{7,6},{8,9},{9,8},{10,11... | collective-permute-start | bytes 3145736 | tf_op jit(solution)/shard_map/ppermute | solution.py:31
  3.6 24.8 %collective-permute-start.1 = (bf16[512,1024]{1,0:T(8,128)(2,1)}, bf16[512,1024]{1,0:T(8,128)(2,1)S(1)}, u32[]{:S(2)}, u32[]{:S(2)}) collective-permute-start(bf16[512,1024]{1,0:T(8,128)(2,1)} %param.8), channel_id=1, source_target_pairs={{0,2},{1,3},{2,0},{3,1},{4,6},{5,7},{6,4},{7,5},{8,10},{9,11},{10,... | collective-permute-start | bytes 3145736 | tf_op jit(solution)/shard_map/ppermute | solution.py:32
  29.6 15.1 %collective-permute-start.2 = (bf16[512,1024]{1,0:T(8,128)(2,1)}, bf16[512,1024]{1,0:T(8,128)(2,1)}, u32[]{:S(2)}, u32[]{:S(2)}) collective-permute-start(bf16[512,1024]{1,0:T(8,128)(2,1)} %broadcast_select_fusion), channel_id=1, source_target_pairs={{0,2},{1,3},{2,0},{3,1},{4,5},{5,4},{6,7},{7,6},{8,10},{9,11},{10,... | collective-permute-start | bytes 3145736 | tf_op jit(solution)/shard_map/ppermute | solution.py:36
  32.4 4.3 %copy-start.6 = (bf16[1024,4096]{1,0:T(8,128)(2,1)S(1)}, bf16[1024,4096]{1,0:T(8,128)(2,1)}, u32[]{:S(2)}) copy-start(bf16[1024,4096]{1,0:T(8,128)(2,1)} %param.9) | copy-start | bytes 25165828
  39.3 7.9 %copy-start.3 = (bf16[512,1024]{0,1:T(8,128)(2,1)S(1)}, bf16[512,1024]{0,1:T(8,128)(2,1)}, u32[]{:S(2)}) copy-start(bf16[512,1024]{0,1:T(8,128)(2,1)} %copy.19) | copy-start | bytes 3145732
  47.2 3.2 %copy-start = (bf16[512,1024]{1,0:T(8,128)(2,1)}, bf16[512,1024]{1,0:T(8,128)(2,1)S(1)}, u32[]{:S(2)}) copy-start(bf16[512,1024]{1,0:T(8,128)(2,1)S(1)} %fusion.refs_3_.refs_2_) | copy-start | bytes 3145732
  47.2 1.9 %copy-start.1 = (bf16[512,1024]{1,0:T(8,128)(2,1)S(1)}, bf16[512,1024]{1,0:T(8,128)(2,1)}, u32[]{:S(2)}) copy-start(bf16[512,1024]{1,0:T(8,128)(2,1)} %refs_0_.3) | copy-start | bytes 3145732
  47.2 3.2 %copy-start.2 = (bf16[512,1024]{1,0:T(8,128)(2,1)S(1)}, bf16[512,1024]{1,0:T(8,128)(2,1)}, u32[]{:S(2)}) copy-start(bf16[512,1024]{1,0:T(8,128)(2,1)} %refs_1_.3) | copy-start | bytes 3145732
  48.6 3.6 %collective-permute-start.4 = (bf16[8,128,128]{2,1,0:T(8,128)(2,1)}, bf16[8,128,128]{2,1,0:T(8,128)(2,1)S(1)}, u32[]{:S(2)}, u32[]{:S(2)}) collective-permute-start(bf16[8,128,128]{2,1,0:T(8,128)(2,1)} %get-tuple-element.37), channel_id=1, source_target_pairs={{0,4},{4,0},{8,12},{12,8},{16,20},{20,16},{24,28},{28,24},{1,5},{5... | collective-permute-start | bytes 786440 | tf_op jit(solution)/shard_map/ppermute | solution.py:48
  52.1 1.6 %collective-permute-start.3 = (bf16[8,128,128]{2,1,0:T(8,128)(2,1)S(1)}, bf16[8,128,128]{2,1,0:T(8,128)(2,1)S(1)}, u32[]{:S(2)}, u32[]{:S(2)}) collective-permute-start(bf16[8,128,128]{2,1,0:T(8,128)(2,1)S(1)} %get-tuple-element.35), channel_id=1, source_target_pairs={{0,4},{4,0},{8,12},{12,8},{16,20},{20,16},{24,28},{28,24},{1,5},{5... | collective-permute-start | bytes 786440 | tf_op jit(solution)/shard_map/ppermute | solution.py:48
  53.8 24.6 %collective-permute-start.10 = (bf16[8,64,128]{2,1,0:T(8,128)(2,1)S(1)}, bf16[8,64,128]{2,1,0:T(8,128)(2,1)S(1)}, u32[]{:S(2)}, u32[]{:S(2)}) collective-permute-start(bf16[8,64,128]{2,1,0:T(8,128)(2,1)S(1)} %dynamic-slice_add_fusion), channel_id=1, source_target_pairs={{24,0},{28,4},{25,1},{29,5},{26,2},{30,6},{27,3},{31,7}} | collective-permute-start | bytes 393224 | tf_op jit(solution)/shard_map/ppermute | solution.py:67
  55.1 24.7 %collective-permute-start.8 = (bf16[8,64,128]{2,1,0:T(8,128)(2,1)S(1)}, bf16[8,64,128]{2,1,0:T(8,128)(2,1)S(1)}, u32[]{:S(2)}, u32[]{:S(2)}) collective-permute-start(bf16[8,64,128]{2,1,0:T(8,128)(2,1)S(1)} %dynamic-slice_add_fusion), channel_id=1, source_target_pairs={{8,0},{12,4},{16,8},{20,12},{24,16},{28,20},{9,1},{13,5},{17,9},{2... | collective-permute-start | bytes 393224 | tf_op jit(solution)/shard_map/ppermute | solution.py:67
  56.4 23.4 %collective-permute-start.9 = (bf16[8,64,128]{2,1,0:T(8,128)(2,1)S(1)}, bf16[8,64,128]{2,1,0:T(8,128)(2,1)S(1)}, u32[]{:S(2)}, u32[]{:S(2)}) collective-permute-start(bf16[8,64,128]{2,1,0:T(8,128)(2,1)S(1)} %dynamic-slice_add_fusion), channel_id=1, source_target_pairs={{16,0},{20,4},{24,8},{28,12},{17,1},{21,5},{25,9},{29,13},{18,2},{... | collective-permute-start | bytes 393224 | tf_op jit(solution)/shard_map/ppermute | solution.py:67
  57.7 22.2 %collective-permute-start.5 = (bf16[8,64,128]{2,1,0:T(8,128)(2,1)S(1)}, bf16[8,64,128]{2,1,0:T(8,128)(2,1)S(1)}, u32[]{:S(2)}, u32[]{:S(2)}) collective-permute-start(bf16[8,64,128]{2,1,0:T(8,128)(2,1)S(1)} %dynamic-slice_add_fusion.1), channel_id=1, source_target_pairs={{0,8},{4,12},{8,16},{12,20},{16,24},{20,28},{1,9},{5,13},{9,17},{1... | collective-permute-start | bytes 393224 | tf_op jit(solution)/shard_map/ppermute | solution.py:67
  62.3 17.6 %collective-permute-start.6 = (bf16[8,64,128]{2,1,0:T(8,128)(2,1)S(1)}, bf16[8,64,128]{2,1,0:T(8,128)(2,1)S(1)}, u32[]{:S(2)}, u32[]{:S(2)}) collective-permute-start(bf16[8,64,128]{2,1,0:T(8,128)(2,1)S(1)} %dynamic-slice_add_fusion.1), channel_id=1, source_target_pairs={{0,16},{4,20},{8,24},{12,28},{1,17},{5,21},{9,25},{13,29},{2,18},{... | collective-permute-start | bytes 393224 | tf_op jit(solution)/shard_map/ppermute | solution.py:67
  78.4 6.0 %copy-start.4 = (f32[8,128,128]{2,1,0:T(8,128)S(1)}, f32[8,128,128]{2,1,0:T(8,128)}, u32[]{:S(2)}) copy-start(f32[8,128,128]{2,1,0:T(8,128)} %get-tuple-element.38) | copy-start | bytes 1572868
  78.4 3.9 %collective-permute-start.7 = (bf16[8,64,128]{2,1,0:T(8,128)(2,1)S(1)}, bf16[8,64,128]{2,1,0:T(8,128)(2,1)S(1)}, u32[]{:S(2)}, u32[]{:S(2)}) collective-permute-start(bf16[8,64,128]{2,1,0:T(8,128)(2,1)S(1)} %dynamic-slice_add_fusion.1), channel_id=1, source_target_pairs={{0,24},{4,28},{1,25},{5,29},{2,26},{6,30},{3,27},{7,31}} | collective-permute-start | bytes 393224 | tf_op jit(solution)/shard_map/ppermute | solution.py:67
  82.4 1.6 %collective-permute-start.12 = (f32[8,64,128]{2,1,0:T(8,128)S(1)}, f32[8,64,128]{2,1,0:T(8,128)S(1)}, u32[]{:S(2)}, u32[]{:S(2)}) collective-permute-start(f32[8,64,128]{2,1,0:T(8,128)S(1)} %convert_add_fusion), channel_id=1, source_target_pairs={{0,4},{4,0},{8,12},{12,8},{16,20},{20,16},{24,28},{28,24},{1,5},{5... | collective-permute-start | bytes 786440 | tf_op jit(solution)/shard_map/ppermute | solution.py:81
  82.5 1.9 %collective-permute-start.11 = (f32[8,64,128]{2,1,0:T(8,128)S(1)}, f32[8,64,128]{2,1,0:T(8,128)S(1)}, u32[]{:S(2)}, u32[]{:S(2)}) collective-permute-start(f32[8,64,128]{2,1,0:T(8,128)S(1)} %convert_add_fusion.1), channel_id=1, source_target_pairs={{0,4},{4,0},{8,12},{12,8},{16,20},{20,16},{24,28},{28,24},{1,5},{5... | collective-permute-start | bytes 786440 | tf_op jit(solution)/shard_map/ppermute | solution.py:81

commit v7 on v5

v7 whole, which is shorter than its diff:
```python
import jax
import jax.numpy as jnp
from jax import lax
from jax.experimental import pallas as pl
from jax.sharding import PartitionSpec as P

DH = 128


def flip_pairs(n, bit):
    return [(a, a ^ bit) for a in range(n)]


def project(og, out_weight, ctx_size, head_size):
    cols = og.shape[1]

    def weight_cols(source, lo, width):
        return lax.dynamic_slice_in_dim(out_weight, source * cols + lo, width, axis=1)

    def mm(a, b):
        return lax.dot_general(
            a, b, (((1,), (1,)), ((), ())), preferred_element_type=jnp.float32
        )

    if head_size != 4:
        full = lax.all_gather(og, "head", axis=1, tiled=True)
        return mm(full, out_weight)
    me = lax.axis_index("head")
    core = lax.axis_index("ctx") % 2
    from_x = lax.ppermute(og, "head", flip_pairs(4, 1))
    from_y = lax.ppermute(og, "head", flip_pairs(4, 2))
    relayed = jnp.where(core == 0, from_x, from_y)
    devices = [(p, j) for p in range(ctx_size) for j in range(4)]
    route = [(p * 4 + j, p * 4 + (j ^ (2 if p % 2 == 0 else 1))) for p, j in devices]
    diag = lax.ppermute(relayed, ("ctx", "head"), route)
    acc = mm(og, weight_cols(me, 0, cols))
    acc = acc + mm(from_x, weight_cols(me ^ 1, 0, cols))
    acc = acc + mm(from_y, weight_cols(me ^ 2, 0, cols))
    acc = acc + mm(diag, weight_cols(me ^ 3, 0, cols))
    return acc


def ctx_states(kv, qg, ctx_size, cover):
    core = lax.axis_index("ctx") % 2
    chips = ctx_size // 2
    own = jnp.stack([kv, qg]).astype(jnp.bfloat16)
    partner = lax.ppermute(own, "ctx", flip_pairs(ctx_size, 1)).astype(jnp.float32)
    chip_sum = own.astype(jnp.float32) + partner
    mine = jnp.where(core == 0, chip_sum[0], chip_sum[1])

    def pairs(step):
        forward = [(2 * z, 2 * (z + step)) for z in range(chips - step)]
        backward = [(2 * (z + step) + 1, 2 * z + 1) for z in range(chips - step)]
        return forward + backward

    mine, held = lax.optimization_barrier((mine, cover.args))
    others = jnp.zeros_like(mine)
    if chips <= 4:
        sent = mine.astype(jnp.bfloat16)
        for step in range(1, chips):
            others = others + lax.ppermute(sent, "ctx", pairs(step)).astype(jnp.float32)
    else:
        run = mine
        step = 1
        while step < chips:
            got = lax.ppermute(run.astype(jnp.bfloat16), "ctx", pairs(step)).astype(jnp.float32)
            run = run + got
            others = others + got
            step *= 2
    covered = cover.fn(*held)
    others, covered = lax.optimization_barrier((others, covered))
    theirs = lax.ppermute(others, "ctx", flip_pairs(ctx_size, 1))
    kv_chips = jnp.where(core == 0, others, theirs)
    qg_chips = jnp.where(core == 0, theirs, others)
    kv_before = kv_chips + jnp.where(core == 1, partner[0], 0.0)
    qg_after = qg_chips + jnp.where(core == 0, partner[1], 0.0)
    return kv_before, qg_after, covered


class Cover:
    def __init__(self, fn, args):
        self.fn = fn
        self.args = args


NT = (((1,), (1,)), ((), ()))


def split_state(state):
    high = state.astype(jnp.bfloat16)
    low = (state - high.astype(jnp.float32)).astype(jnp.bfloat16)
    return high, low


def scores_kernel(scale, chunk, per_step, q_ref, k_ref, v_ref, g_ref, gq_ref, gk_ref, gv_ref):
    length = q_ref.shape[0]
    count = length // chunk
    row = lax.broadcasted_iota(jnp.int32, (chunk, chunk), 0)
    col = lax.broadcasted_iota(jnp.int32, (chunk, chunk), 1)

    def score(a, b, keep):
        s = lax.dot_general(a, b, NT, preferred_element_type=jnp.float32) * scale
        if keep is not None:
            s = jnp.where(keep, s, 0.0)
        return s.astype(jnp.bfloat16)

    for h in range(per_step):
        cols = pl.ds(h * DH, DH)

        def piece(ref, i):
            return ref[pl.ds(i * chunk, chunk), cols]

        for i in range(count):
            rows = pl.ds(i * chunk, chunk)
            g_i = piece(g_ref, i)
            gq = None
            for j in range(i + 1):
                sg = score(g_i, piece(v_ref, j), row >= col if j == i else None)
                term = jnp.dot(sg, piece(k_ref, j), preferred_element_type=jnp.float32)
                gq = term if gq is None else gq + term
            gq_ref[rows, cols] = gq.astype(gq_ref.dtype)
            v_i, k_i = piece(v_ref, i), piece(k_ref, i)
            gk = None
            gv = None
            for j in range(i, count):
                keep = row <= col if j == i else None
                sgt = score(v_i, piece(g_ref, j), keep)
                sft = score(k_i, piece(q_ref, j), keep)
                term_k = jnp.dot(sgt, piece(q_ref, j), preferred_element_type=jnp.float32)
                term_v = jnp.dot(sft, piece(g_ref, j), preferred_element_type=jnp.float32)
                gk = term_k if gk is None else gk + term_k
                gv = term_v if gv is None else gv + term_v
            gk_ref[rows, cols] = gk.astype(gk_ref.dtype)
            gv_ref[rows, cols] = gv.astype(gv_ref.dtype)


def state_kernel(scale, per_step, k_ref, v_ref, g_ref, kv_ref, qg_ref, gqp_ref, gkp_ref, gvp_ref,
                 gq_ref, gk_ref, gv_ref):
    for i in range(per_step):
        cols = pl.ds(i * DH, DH)
        k, v, g = k_ref[:, cols], v_ref[:, cols], g_ref[:, cols]
        kv_high, kv_low = split_state(kv_ref[0, i] * scale)
        qg_high, qg_low = split_state(qg_ref[0, i] * scale)
        gq = gqp_ref[:, cols] + lax.dot_general(g, kv_high, NT, preferred_element_type=jnp.float32)
        gq = gq + lax.dot_general(g, kv_low, NT, preferred_element_type=jnp.float32)
        gk = gkp_ref[:, cols] + lax.dot_general(v, qg_high, NT, preferred_element_type=jnp.float32)
        gk = gk + lax.dot_general(v, qg_low, NT, preferred_element_type=jnp.float32)
        gv = gvp_ref[:, cols] + jnp.dot(k, qg_high, preferred_element_type=jnp.float32)
        gv = gv + jnp.dot(k, qg_low, preferred_element_type=jnp.float32)
        gq_ref[:, cols] = gq.astype(jnp.bfloat16)
        gk_ref[:, cols] = gk.astype(jnp.bfloat16)
        gv_ref[:, cols] = gv.astype(jnp.bfloat16)


def attention_part(q, k, v, g, blocks, block_len, heads, scale, per_step=1):
    tok = pl.BlockSpec((block_len, DH * per_step), lambda n, h: (n, h))
    rows, width = q.shape
    part = jax.ShapeDtypeStruct((rows, width), jnp.bfloat16)
    chunk = 256 if block_len % 256 == 0 else block_len
    return pl.pallas_call(
        lambda *refs: scores_kernel(scale, chunk, per_step, *refs),
        grid=(blocks, heads // per_step),
        in_specs=[tok, tok, tok, tok],
        out_specs=[tok, tok, tok],
        out_shape=[part, part, part],
        cost_estimate=pl.CostEstimate(
            flops=blocks * heads * 6 * 2 * block_len * block_len * DH,
            transcendentals=0,
            bytes_accessed=rows * width * 14,
        ),
        name="attention_part",
    )(q, k, v, g)


def state_part(k, v, g, kv_state, qg_state, parts, blocks, block_len, heads, scale):
    per_step = 2 if heads % 2 == 0 else 1
    tok = pl.BlockSpec((block_len, DH * per_step), lambda n, h: (n, h))
    st = pl.BlockSpec((1, per_step, DH, DH), lambda n, h: (n, h, 0, 0))
    rows, width = k.shape
    out = jax.ShapeDtypeStruct((rows, width), jnp.bfloat16)
    return pl.pallas_call(
        lambda *refs: state_kernel(scale, per_step, *refs),
        grid=(blocks, heads // per_step),
        in_specs=[tok, tok, tok, st, st, tok, tok, tok],
        out_specs=[tok, tok, tok],
        out_shape=[out, out, out],
        cost_estimate=pl.CostEstimate(
            flops=blocks * heads * 6 * 2 * block_len * DH * DH,
            transcendentals=0,
            bytes_accessed=rows * width * 18,
        ),
        name="state_part",
    )(k, v, g, kv_state, qg_state, *parts)


def make_shards(ctx_size, head_size):
    def shards(queries, keys, values, output_grad, out_weight):
        row_count = queries.shape[0]
        width = queries.shape[1]
        heads = width // DH
        block_len = min(row_count, 512)
        blocks = row_count // block_len
        scale_factor = DH ** (-0.5)
        shape = (blocks, block_len, heads, DH)
        q_blocks = queries.reshape(shape)
        k_blocks = keys.reshape(shape)
        v_blocks = values.reshape(shape)
        grad_heads = project(output_grad, out_weight, ctx_size, head_size)
        grad_heads = grad_heads.astype(jnp.bfloat16)
        kv_blocks = jnp.einsum(
            "nshd,nshe->nhde", k_blocks, v_blocks,
            preferred_element_type=jnp.float32,
        )
        kv_running = jnp.cumsum(kv_blocks, axis=0)
        g_blocks = grad_heads.reshape(shape)
        qg_blocks = jnp.einsum(
            "nthd,nthe->nhde", q_blocks, g_blocks, preferred_element_type=jnp.float32
        )
        qg_running = jnp.flip(jnp.cumsum(jnp.flip(qg_blocks, 0), axis=0), 0)
        kv_before, qg_after, parts = ctx_states(
            kv_running[-1], qg_running[0], ctx_size,
            Cover(
                lambda g: attention_part(queries, keys, values, g, blocks, block_len, heads, scale_factor),
                (grad_heads,),
            ),
        )
        kv_entry = kv_before[None] + kv_running - kv_blocks
        qg_entry = qg_after[None] + qg_running - qg_blocks
        return state_part(
            keys, values, grad_heads, kv_entry, qg_entry, parts, blocks, block_len, heads, scale_factor
        )

    return shards


def solution(mesh):
    return jax.shard_map(
        make_shards(mesh.shape["ctx"], mesh.shape["head"]),
        mesh=mesh,
        in_specs=(
            P("ctx", "head"),
            P("ctx", "head"),
            P("ctx", "head"),
            P("ctx", "head"),
            P("head", None),
        ),
        out_specs=(P("ctx", "head"), P("ctx", "head"), P("ctx", "head")),
        check_vma=False,
    )
```

time: 97.3 us -> 81.8 us (0.84)
  waiting for transfers between devices: 37.2 us -> 30.6 us
  matrix products: 15.4 us -> 11.8 us
  starting transfers between devices: 18.3 us -> 15.5 us
  Pallas kernels: 17.7 us -> 16.7 us
    ppermute x1, waiting for transfers between devices: 21.9 us -> 1.56 us  [project(): from_y = lax.ppermute(og, 'head', flip_pairs(4, 2))]
    ppermute x1, waiting for transfers between devices: 1.46 us -> 20.3 us  [project(): from_x = lax.ppermute(og, 'head', flip_pairs(4, 1))]
    ppermute x10 -> x5, waiting for transfers between devices: 10.4 us -> 3.8 us  [the longest x1 1.9 us: ctx_states(): lax.ppermute(own, 'ctx', flip_pairs(ctx_size, 1)).astype(jnp.float32)]
    dot_general x4, matrix products: 14.5 us -> 9.63 us  [mm(): lax.dot_general(a, b, (((1,), (1,)), ((), ())), preferred_element_type=jn...]
    ppermute x10 -> x5, starting transfers between devices: 13.4 us -> 9.45 us  [the longest x3 9.3 us: ctx_states(): others = others + lax.ppermute(sent, 'ctx', pairs(step)).astype(jnp.float32)]
    mul x2 -> x0, other arithmetic: 1.85 us -> none  [the longest x1 0.95 us: shards(): scale_factor * qg_entry]
    ppermute x1, starting transfers between devices: 1.49 us -> 3 us  [project(): from_x = lax.ppermute(og, 'head', flip_pairs(4, 1))]
    ppermute x1, starting transfers between devices: 3.03 us -> 1.52 us  [project(): from_y = lax.ppermute(og, 'head', flip_pairs(4, 2))]
  transfers between devices with their start and end apart: 13 -> 8, of which waited for: 6 -> 5; matrix products, arithmetic and copies ran while one was open for 17% -> 11% of each run, Pallas kernels for 11% -> 13%
where the time goes in v7:
time: 81.8 us; the launch traced here: 81.3 us
  waiting for transfers between devices  30.6 us (37%)
  Pallas kernels  16.7 us (20%)
  starting transfers between devices  15.5 us (19%)
  matrix products  11.8 us (14%)
  local copies, waits for them, and re-layouts  3.07 us (4%)
  other arithmetic  2.72 us (3%)
  between operations  0.84 us (1%)
    ppermute x1, waiting for transfers between devices, project(): from_x = lax.ppermute(og, 'head', flip_pairs(4, 1))  20.3 us
    pallas_call x1, Pallas kernels, attention_part(): pl.pallas_call(lambda *refs: scores_kernel(scale, chunk, per_step, *refs)...  10.7 us
    dot_general x4, matrix products, mm(): lax.dot_general(a, b, (((1,), (1,)), ((), ())), preferred_element_type=jn...  9.63 us
    ppermute x3, starting transfers between devices, ctx_states(): others = others + lax.ppermute(sent, 'ctx', pairs(step)).astype(jnp.float32)  9.3 us
    pallas_call x1, Pallas kernels, state_part(): pl.pallas_call(lambda *refs: state_kernel(scale, per_step, *refs), grid=(...  6.03 us
    ppermute x1, waiting for transfers between devices, project(): diag = lax.ppermute(relayed, ('ctx', 'head'), route)  4.94 us
    ppermute x1, starting transfers between devices, project(): from_x = lax.ppermute(og, 'head', flip_pairs(4, 1))  3 us
    ppermute x1, waiting for transfers between devices, ctx_states(): lax.ppermute(own, 'ctx', flip_pairs(ctx_size, 1)).astype(jnp.float32)  1.9 us
  transfers between devices with their start and end apart: 8, of which 5 were waited for; matrix products, arithmetic and copies ran while one was open for 11% of the time, Pallas kernels for 13%

profile of v7, /device:TPU:0, one launch (start us, length us, event | category | flops | bytes accessed | tf_op | source)
XLA Modules:
  0.0 81.3 jit_solution(7108642540773338778)
XLA Ops:
  0.6 3.0 %collective-permute-start = (bf16[512,1024]{1,0:T(8,128)(2,1)}, bf16[512,1024]{1,0:T(8,128)(2,1)S(1)}, u32[]{:S(2)}, u32[]{:S(2)}) collective-permute-start(bf16[512,1024]{1,0:T(8,128)(2,1)} %param.8), channel_id=1, source_target_pairs={{0,1},{1,0},{2,3},{3,2},{4,5},{5,4},{6,7},{7,6},{8,9},{9,8},{10,11... | collective-permute-start | bytes 3145736 | tf_op jit(solution)/shard_map/ppermute | solution.py:30
  3.6 1.5 %collective-permute-start.1 = (bf16[512,1024]{1,0:T(8,128)(2,1)}, bf16[512,1024]{1,0:T(8,128)(2,1)}, u32[]{:S(2)}, u32[]{:S(2)}) collective-permute-start(bf16[512,1024]{1,0:T(8,128)(2,1)} %param.8), channel_id=1, source_target_pairs={{0,2},{1,3},{2,0},{3,1},{4,6},{5,7},{6,4},{7,5},{8,10},{9,11},{10,... | collective-permute-start | bytes 3145736 | tf_op jit(solution)/shard_map/ppermute | solution.py:31
  5.2 1.5 %copy.20 = bf16[512,1024]{0,1:T(8,128)(2,1)S(1)} copy(bf16[512,1024]{1,0:T(8,128)(2,1)} %refs_0_.3) | data formatting | bytes 2097152 | tf_op jit(solution)/shard_map/reshape
  6.7 20.3 %collective-permute-done = bf16[512,1024]{1,0:T(8,128)(2,1)S(1)} collective-permute-done((bf16[512,1024]{1,0:T(8,128)(2,1)}, bf16[512,1024]{1,0:T(8,128)(2,1)S(1)}, u32[]{:S(2)}, u32[]{:S(2)}) %collective-permute-start) | collective-permute-done | bytes 1048608 | tf_op jit(solution)/shard_map/ppermute | solution.py:30
  27.0 1.6 %collective-permute-done.1 = bf16[512,1024]{1,0:T(8,128)(2,1)} collective-permute-done((bf16[512,1024]{1,0:T(8,128)(2,1)}, bf16[512,1024]{1,0:T(8,128)(2,1)}, u32[]{:S(2)}, u32[]{:S(2)}) %collective-permute-start.1) | collective-permute-done | bytes 1048608 | tf_op jit(solution)/shard_map/ppermute | solution.py:31
  28.6 1.1 %broadcast_select_fusion = bf16[512,1024]{1,0:T(8,128)(2,1)} fusion(bf16[512,1024]{1,0:T(8,128)(2,1)S(1)} %collective-permute-done, bf16[512,1024]{1,0:T(8,128)(2,1)} %collective-permute-done.1, pred[]{:T(512)S(6)} %eq.7), kind=kLoop, calls=%fused_computation.17 | loop fusion | flops 524288 | bytes 3145729 | tf_op jit(solution)/shard_map/jit(_where)/select_n | solution.py:32
  29.7 1.5 %collective-permute-start.2 = (bf16[512,1024]{1,0:T(8,128)(2,1)}, bf16[512,1024]{1,0:T(8,128)(2,1)}, u32[]{:S(2)}, u32[]{:S(2)}) collective-permute-start(bf16[512,1024]{1,0:T(8,128)(2,1)} %broadcast_select_fusion), channel_id=1, source_target_pairs={{0,2},{1,3},{2,0},{3,1},{4,5},{5,4},{6,7},{7,6},{8,10},{9,11},{10,... | collective-permute-start | bytes 3145736 | tf_op jit(solution)/shard_map/ppermute | solution.py:35
  31.2 0.5 fusion.13
  31.7 3.3 %fusion.7 = f32[1024,512]{0,1:T(8,128)S(1)} fusion(bf16[512,1024]{1,0:T(8,128)(2,1)} %param.8, bf16[1024,4096]{1,0:T(8,128)(2,1)} %param.9, s32[]{:T(128)S(6)} %select_n.68), kind=kOutput, calls=%fused_computation.8 | convolution fusion | flops 1073741824 | bytes 5242884 | tf_op jit(solution)/shard_map/dot_general | solution.py:21
  35.0 1.0 %copy-done.2 = bf16[1024,4096]{1,0:T(8,128)(2,1)S(1)} copy-done((bf16[1024,4096]{1,0:T(8,128)(2,1)S(1)}, bf16[1024,4096]{1,0:T(8,128)(2,1)}, u32[]{:S(2)}) %copy-start.2) | copy-done | bytes 8388632
  36.0 1.3 %fusion.5 = f32[1024,512]{0,1:T(8,128)S(1)} fusion(bf16[512,1024]{1,0:T(8,128)(2,1)S(1)} %collective-permute-done, bf16[1024,4096]{1,0:T(8,128)(2,1)S(1)} %copy-done.2, s32[]{:T(128)S(6)} %select_n.69), kind=kOutput, calls=%fused_computation.6 | convolution fusion | flops 1073741824 | bytes 5242884 | tf_op jit(solution)/shard_map/dot_general | solution.py:21
  37.3 2.5 %fusion.3 = f32[1024,512]{0,1:T(8,128)S(1)} fusion(bf16[512,1024]{1,0:T(8,128)(2,1)} %collective-permute-done.1, bf16[1024,4096]{1,0:T(8,128)(2,1)S(1)} %copy-done.2, s32[]{:T(128)S(6)} %select_n.70), kind=kOutput, calls=%fused_computation.4 | convolution fusion | flops 1073741824 | bytes 5242884 | tf_op jit(solution)/shard_map/dot_general | solution.py:21
  39.8 4.9 %collective-permute-done.2 = bf16[512,1024]{1,0:T(8,128)(2,1)} collective-permute-done((bf16[512,1024]{1,0:T(8,128)(2,1)}, bf16[512,1024]{1,0:T(8,128)(2,1)}, u32[]{:S(2)}, u32[]{:S(2)}) %collective-permute-start.2) | collective-permute-done | bytes 1048608 | tf_op jit(solution)/shard_map/ppermute | solution.py:35
  44.8 2.5 %fusion.refs_3_.refs_2_ = bf16[512,1024]{1,0:T(8,128)(2,1)S(1)} fusion(f32[1024,512]{0,1:T(8,128)S(1)} %fusion.3, f32[1024,512]{0,1:T(8,128)S(1)} %fusion.7, f32[1024,512]{0,1:T(8,128)S(1)} %fusion.5, bf16[512,1024]{1,0:T(8,128)(2,1)} %collective-permute-done.2, bf16[1024,4096]{1,0:T(8,128)(2,1)S(1)} %copy-done.2, s32[]{:T(128)S(6)} %select_n.74), kind=kOutput, calls=%fused_computation.1 | convolution fusion | flops 1075838976 | bytes 10485764 | tf_op jit(solution)/shard_map/dot_general | solution.py:21
  47.3 0.5 copy.21
  47.9 1.7 %convolution_bitcast_fusion = f32[8,128,128]{2,1,0:T(8,128)S(1)} fusion(bf16[512,8,128]{0,2,1:T(8,128)(2,1)S(1)} %bitcast.51, bf16[512,1024]{1,0:T(8,128)(2,1)} %refs_0_.2), kind=kOutput, calls=%fused_computation.10 | convolution fusion | flops 134217728 | bytes 2621440 | tf_op jit(solution)/shard_map/nthd,nthe->nhde/dot_general | solution.py:216
  49.8 1.9 %collective-permute-done.3 = bf16[2,8,128,128]{3,2,1,0:T(8,128)(2,1)S(1)} collective-permute-done((bf16[2,8,128,128]{3,2,1,0:T(8,128)(2,1)S(1)}, bf16[2,8,128,128]{3,2,1,0:T(8,128)(2,1)S(1)}, u32[]{:S(2)}, u32[]{:S(2)}) %collective-permute-start.3) | collective-permute-done | bytes 524320 | tf_op jit(solution)/shard_map/ppermute | solution.py:47
  52.0 3.5 %collective-permute-start.4 = (bf16[8,128,128]{2,1,0:T(8,128)(2,1)S(1)}, bf16[8,128,128]{2,1,0:T(8,128)(2,1)S(1)}, u32[]{:S(2)}, u32[]{:S(2)}) collective-permute-start(bf16[8,128,128]{2,1,0:T(8,128)(2,1)S(1)} %fusion.22), channel_id=1, source_target_pairs={{0,8},{8,16},{16,24},{12,4},{20,12},{28,20},{1,9},{9,17},{17,25},{... | collective-permute-start | bytes 786440 | tf_op jit(solution)/shard_map/ppermute | solution.py:61
  55.5 4.5 %collective-permute-start.5 = (bf16[8,128,128]{2,1,0:T(8,128)(2,1)S(1)}, bf16[8,128,128]{2,1,0:T(8,128)(2,1)S(1)}, u32[]{:S(2)}, u32[]{:S(2)}) collective-permute-start(bf16[8,128,128]{2,1,0:T(8,128)(2,1)S(1)} %fusion.22), channel_id=1, source_target_pairs={{0,16},{8,24},{20,4},{28,12},{1,17},{9,25},{21,5},{29,13},{2,18},{... | collective-permute-start | bytes 786440 | tf_op jit(solution)/shard_map/ppermute | solution.py:61
  60.0 1.3 %collective-permute-start.6 = (bf16[8,128,128]{2,1,0:T(8,128)(2,1)S(1)}, bf16[8,128,128]{2,1,0:T(8,128)(2,1)S(1)}, u32[]{:S(2)}, u32[]{:S(2)}) collective-permute-start(bf16[8,128,128]{2,1,0:T(8,128)(2,1)S(1)} %fusion.22), channel_id=1, source_target_pairs={{0,24},{28,4},{1,25},{29,5},{2,26},{30,6},{3,27},{31,7}} | collective-permute-start | bytes 786440 | tf_op jit(solution)/shard_map/ppermute | solution.py:61
  61.3 10.7 %attention_part.1 = (bf16[512,1024]{1,0:T(8,128)(2,1)}, bf16[512,1024]{1,0:T(8,128)(2,1)}, bf16[512,1024]{1,0:T(8,128)(2,1)}) custom-call(bf16[512,1024]{1,0:T(8,128)(2,1)} %refs_0_.2, bf16[512,1024]{1,0:T(8,128)(2,1)} %refs_0_.3, bf16[512,1024]{1,0:T(8,128)(2,1)} %refs_1_.3, bf16[512,1024]{1,0:T(8,128)(2,1)} %copy-done), custom_call_target="tpu_custom_call" | custom-call | flops 3221225472 | bytes 7340032 | tf_op jit(solution)/shard_map/attention_part/pallas_call | solution.py:160
  72.2 1.9 %collective-permute-done.7 = f32[8,128,128]{2,1,0:T(8,128)S(1)} collective-permute-done((f32[8,128,128]{2,1,0:T(8,128)S(1)}, f32[8,128,128]{2,1,0:T(8,128)S(1)}, u32[]{:S(2)}, u32[]{:S(2)}) %collective-permute-start.7) | collective-permute-done | bytes 524320 | tf_op jit(solution)/shard_map/ppermute | solution.py:72
  74.1 1.2 %fusion.17 = (f32[1,8,128,128]{3,2,1,0:T(8,128)}, f32[1,8,128,128]{3,2,1,0:T(8,128)}) fusion(f32[8,128,128]{2,1,0:T(8,128)S(1)} %convolution_bitcast_fusion, f32[2,8,128,128]{3,2,1,0:T(8,128)S(1)} %get-tuple-element.24, f32[8,128,128]{2,1,0:T(8,128)S(1)} %collective-permute-done.7, f32[8,128,128]{2,1,0:T(8,128)S(1)} %convert_add_fusion.1, pred[]{:T(512)S(6)} %eq.7, ...), kind=kLoop, calls=%fused_computation.21 | loop fusion | flops 1310720 | bytes 4195840 | tf_op jit(solution)/shard_map/sub | solution.py:228
  75.3 6.0 %state_part.1 = (bf16[512,1024]{1,0:T(8,128)(2,1)}, bf16[512,1024]{1,0:T(8,128)(2,1)}, bf16[512,1024]{1,0:T(8,128)(2,1)}) custom-call(bf16[512,1024]{1,0:T(8,128)(2,1)} %refs_0_.3, bf16[512,1024]{1,0:T(8,128)(2,1)} %refs_1_.3, bf16[512,1024]{1,0:T(8,128)(2,1)} %copy-done, f32[1,8,128,128]{3,2,1,0:T(8,128)} %get-tuple-element.22.refs_3_, ...), custom_call_target="tpu_custom_call" | custom-call | flops 805306368 | bytes 9437184 | tf_op jit(solution)/shard_map/state_part/pallas_call | solution.py:181
  (15 shorter events, 0.6 us)
Async XLA Ops:
  0.6 26.4 %collective-permute-start = (bf16[512,1024]{1,0:T(8,128)(2,1)}, bf16[512,1024]{1,0:T(8,128)(2,1)S(1)}, u32[]{:S(2)}, u32[]{:S(2)}) collective-permute-start(bf16[512,1024]{1,0:T(8,128)(2,1)} %param.8), channel_id=1, source_target_pairs={{0,1},{1,0},{2,3},{3,2},{4,5},{5,4},{6,7},{7,6},{8,9},{9,8},{10,11... | collective-permute-start | bytes 3145736 | tf_op jit(solution)/shard_map/ppermute | solution.py:30
  3.6 24.9 %collective-permute-start.1 = (bf16[512,1024]{1,0:T(8,128)(2,1)}, bf16[512,1024]{1,0:T(8,128)(2,1)}, u32[]{:S(2)}, u32[]{:S(2)}) collective-permute-start(bf16[512,1024]{1,0:T(8,128)(2,1)} %param.8), channel_id=1, source_target_pairs={{0,2},{1,3},{2,0},{3,1},{4,6},{5,7},{6,4},{7,5},{8,10},{9,11},{10,... | collective-permute-start | bytes 3145736 | tf_op jit(solution)/shard_map/ppermute | solution.py:31
  6.7 24.5 %copy-start.1 = (bf16[512,1024]{1,0:T(8,128)(2,1)S(1)}, bf16[512,1024]{1,0:T(8,128)(2,1)}, u32[]{:S(2)}) copy-start(bf16[512,1024]{1,0:T(8,128)(2,1)} %refs_1_.3) | copy-start | bytes 3145732
  29.7 15.1 %collective-permute-start.2 = (bf16[512,1024]{1,0:T(8,128)(2,1)}, bf16[512,1024]{1,0:T(8,128)(2,1)}, u32[]{:S(2)}, u32[]{:S(2)}) collective-permute-start(bf16[512,1024]{1,0:T(8,128)(2,1)} %broadcast_select_fusion), channel_id=1, source_target_pairs={{0,2},{1,3},{2,0},{3,1},{4,5},{5,4},{6,7},{7,6},{8,10},{9,11},{10,... | collective-permute-start | bytes 3145736 | tf_op jit(solution)/shard_map/ppermute | solution.py:35
  31.7 4.3 %copy-start.2 = (bf16[1024,4096]{1,0:T(8,128)(2,1)S(1)}, bf16[1024,4096]{1,0:T(8,128)(2,1)}, u32[]{:S(2)}) copy-start(bf16[1024,4096]{1,0:T(8,128)(2,1)} %param.9) | copy-start | bytes 25165828
  47.3 2.3 %copy-start = (bf16[512,1024]{1,0:T(8,128)(2,1)}, bf16[512,1024]{1,0:T(8,128)(2,1)S(1)}, u32[]{:S(2)}) copy-start(bf16[512,1024]{1,0:T(8,128)(2,1)S(1)} %fusion.refs_3_.refs_2_) | copy-start | bytes 3145732
  49.8 2.0 %collective-permute-start.3 = (bf16[2,8,128,128]{3,2,1,0:T(8,128)(2,1)S(1)}, bf16[2,8,128,128]{3,2,1,0:T(8,128)(2,1)S(1)}, u32[]{:S(2)}, u32[]{:S(2)}) collective-permute-start(bf16[2,8,128,128]{3,2,1,0:T(8,128)(2,1)S(1)} %pad_maximum_fusion), channel_id=1, source_target_pairs={{0,4},{4,0},{8,12},{12,8},{16,20},{20,16},{24,28},{28,24},{1,5},{5... | collective-permute-start | bytes 1572872 | tf_op jit(solution)/shard_map/ppermute | solution.py:47
  52.0 20.0 %collective-permute-start.4 = (bf16[8,128,128]{2,1,0:T(8,128)(2,1)S(1)}, bf16[8,128,128]{2,1,0:T(8,128)(2,1)S(1)}, u32[]{:S(2)}, u32[]{:S(2)}) collective-permute-start(bf16[8,128,128]{2,1,0:T(8,128)(2,1)S(1)} %fusion.22), channel_id=1, source_target_pairs={{0,8},{8,16},{16,24},{12,4},{20,12},{28,20},{1,9},{9,17},{17,25},{... | collective-permute-start | bytes 786440 | tf_op jit(solution)/shard_map/ppermute | solution.py:61
  55.5 16.5 %collective-permute-start.5 = (bf16[8,128,128]{2,1,0:T(8,128)(2,1)S(1)}, bf16[8,128,128]{2,1,0:T(8,128)(2,1)S(1)}, u32[]{:S(2)}, u32[]{:S(2)}) collective-permute-start(bf16[8,128,128]{2,1,0:T(8,128)(2,1)S(1)} %fusion.22), channel_id=1, source_target_pairs={{0,16},{8,24},{20,4},{28,12},{1,17},{9,25},{21,5},{29,13},{2,18},{... | collective-permute-start | bytes 786440 | tf_op jit(solution)/shard_map/ppermute | solution.py:61
  60.0 12.0 %collective-permute-start.6 = (bf16[8,128,128]{2,1,0:T(8,128)(2,1)S(1)}, bf16[8,128,128]{2,1,0:T(8,128)(2,1)S(1)}, u32[]{:S(2)}, u32[]{:S(2)}) collective-permute-start(bf16[8,128,128]{2,1,0:T(8,128)(2,1)S(1)} %fusion.22), channel_id=1, source_target_pairs={{0,24},{28,4},{1,25},{29,5},{2,26},{30,6},{3,27},{31,7}} | collective-permute-start | bytes 786440 | tf_op jit(solution)/shard_map/ppermute | solution.py:61
  72.1 2.0 %collective-permute-start.7 = (f32[8,128,128]{2,1,0:T(8,128)S(1)}, f32[8,128,128]{2,1,0:T(8,128)S(1)}, u32[]{:S(2)}, u32[]{:S(2)}) collective-permute-start(f32[8,128,128]{2,1,0:T(8,128)S(1)} %convert_add_fusion.1), channel_id=1, source_target_pairs={{0,4},{4,0},{8,12},{12,8},{16,20},{20,16},{24,28},{28,24},{1,5},{5... | collective-permute-start | bytes 1572872 | tf_op jit(solution)/shard_map/ppermute | solution.py:72

commit v8 on v7

--- a/solution.py
+++ b/solution.py
@@ -40,20 +40,22 @@
     return acc
 
 
-def ctx_states(kv, qg, ctx_size, cover):
+def ctx_exclusive(state, ctx_size, reverse, cover=None):
     core = lax.axis_index("ctx") % 2
     chips = ctx_size // 2
-    own = jnp.stack([kv, qg]).astype(jnp.bfloat16)
-    partner = lax.ppermute(own, "ctx", flip_pairs(ctx_size, 1)).astype(jnp.float32)
-    chip_sum = own.astype(jnp.float32) + partner
-    mine = jnp.where(core == 0, chip_sum[0], chip_sum[1])
+    rounded = state.astype(jnp.bfloat16)
+    partner = lax.ppermute(rounded, "ctx", flip_pairs(ctx_size, 1)).astype(jnp.float32)
+    chip_sum = rounded.astype(jnp.float32) + partner
+    half = state.shape[1] // 2
+    mine = lax.dynamic_slice_in_dim(chip_sum, core * half, half, axis=1)
 
     def pairs(step):
-        forward = [(2 * z, 2 * (z + step)) for z in range(chips - step)]
-        backward = [(2 * (z + step) + 1, 2 * z + 1) for z in range(chips - step)]
-        return forward + backward
-
-    mine, held = lax.optimization_barrier((mine, cover.args))
+        if reverse:
+            return [(2 * (z + step) + c, 2 * z + c) for z in range(chips - step) for c in range(2)]
+        return [(2 * z + c, 2 * (z + step) + c) for z in range(chips - step) for c in range(2)]
+
+    if cover is not None:
+        mine, held = lax.optimization_barrier((mine, cover.args))
     others = jnp.zeros_like(mine)
     if chips <= 4:
         sent = mine.astype(jnp.bfloat16)
@@ -67,14 +69,16 @@
             run = run + got
             others = others + got
             step *= 2
-    covered = cover.fn(*held)
-    others, covered = lax.optimization_barrier((others, covered))
+    covered = None
+    if cover is not None:
+        covered = cover.fn(*held)
+        others, covered = lax.optimization_barrier((others, covered))
     theirs = lax.ppermute(others, "ctx", flip_pairs(ctx_size, 1))
-    kv_chips = jnp.where(core == 0, others, theirs)
-    qg_chips = jnp.where(core == 0, theirs, others)
-    kv_before = kv_chips + jnp.where(core == 1, partner[0], 0.0)
-    qg_after = qg_chips + jnp.where(core == 0, partner[1], 0.0)
-    return kv_before, qg_after, covered
+    lower = jnp.where(core == 0, others, theirs)
+    upper = jnp.where(core == 0, theirs, others)
+    chips_side = jnp.concatenate([lower, upper], axis=1)
+    same_chip = (core == 0) if reverse else (core == 1)
+    return chips_side + jnp.where(same_chip, partner, 0.0), covered
 
 
 class Cover:
@@ -92,7 +96,7 @@
     return high, low
 
 
-def scores_kernel(scale, chunk, per_step, q_ref, k_ref, v_ref, g_ref, gq_ref, gk_ref, gv_ref):
+def scores_kernel(scale, chunk, per_step, q_ref, k_ref, v_ref, g_ref, kv_ref, gq_ref, gk_ref, gv_ref):
     length = q_ref.shape[0]
     count = length // chunk
     row = lax.broadcasted_iota(jnp.int32, (chunk, chunk), 0)
@@ -106,6 +110,7 @@
 
     for h in range(per_step):
         cols = pl.ds(h * DH, DH)
+        kv_high, kv_low = split_state(kv_ref[0, h] * scale)
 
         def piece(ref, i):
             return ref[pl.ds(i * chunk, chunk), cols]
@@ -113,11 +118,12 @@
         for i in range(count):
             rows = pl.ds(i * chunk, chunk)
             g_i = piece(g_ref, i)
-            gq = None
+            gq = lax.dot_general(g_i, kv_high, NT, preferred_element_type=jnp.float32)
+            gq = gq + lax.dot_general(g_i, kv_low, NT, preferred_element_type=jnp.float32)
             for j in range(i + 1):
                 sg = score(g_i, piece(v_ref, j), row >= col if j == i else None)
                 term = jnp.dot(sg, piece(k_ref, j), preferred_element_type=jnp.float32)
-                gq = term if gq is None else gq + term
+                gq = gq + term
             gq_ref[rows, cols] = gq.astype(gq_ref.dtype)
             v_i, k_i = piece(v_ref, i), piece(k_ref, i)
             gk = None
@@ -134,45 +140,44 @@
             gv_ref[rows, cols] = gv.astype(gv_ref.dtype)
 
 
-def state_kernel(scale, per_step, k_ref, v_ref, g_ref, kv_ref, qg_ref, gqp_ref, gkp_ref, gvp_ref,
-                 gq_ref, gk_ref, gv_ref):
+def state_kernel(scale, per_step, k_ref, v_ref, qg_ref, gkp_ref, gvp_ref, gk_ref, gv_ref):
     for i in range(per_step):
         cols = pl.ds(i * DH, DH)
-        k, v, g = k_ref[:, cols], v_ref[:, cols], g_ref[:, cols]
-        kv_high, kv_low = split_state(kv_ref[0, i] * scale)
+        k, v = k_ref[:, cols], v_ref[:, cols]
         qg_high, qg_low = split_state(qg_ref[0, i] * scale)
-        gq = gqp_ref[:, cols] + lax.dot_general(g, kv_high, NT, preferred_element_type=jnp.float32)
-        gq = gq + lax.dot_general(g, kv_low, NT, preferred_element_type=jnp.float32)
-        gk = gkp_ref[:, cols] + lax.dot_general(v, qg_high, NT, preferred_element_type=jnp.float32)
+        gk = gkp_ref[:, cols].astype(jnp.float32)
+        gk = gk + lax.dot_general(v, qg_high, NT, preferred_element_type=jnp.float32)
         gk = gk + lax.dot_general(v, qg_low, NT, preferred_element_type=jnp.float32)
-        gv = gvp_ref[:, cols] + jnp.dot(k, qg_high, preferred_element_type=jnp.float32)
+        gv = gvp_ref[:, cols].astype(jnp.float32)
+        gv = gv + jnp.dot(k, qg_high, preferred_element_type=jnp.float32)
         gv = gv + jnp.dot(k, qg_low, preferred_element_type=jnp.float32)
-        gq_ref[:, cols] = gq.astype(jnp.bfloat16)
         gk_ref[:, cols] = gk.astype(jnp.bfloat16)
         gv_ref[:, cols] = gv.astype(jnp.bfloat16)
 
 
-def attention_part(q, k, v, g, blocks, block_len, heads, scale, per_step=1):
+def attention_part(q, k, v, g, kv_state, blocks, block_len, heads, scale):
+    per_step = 2 if heads % 2 == 0 else 1
     tok = pl.BlockSpec((block_len, DH * per_step), lambda n, h: (n, h))
+    st = pl.BlockSpec((1, per_step, DH, DH), lambda n, h: (n, h, 0, 0))
     rows, width = q.shape
-    part = jax.ShapeDtypeStruct((rows, width), jnp.bfloat16)
+    out = jax.ShapeDtypeStruct((rows, width), jnp.bfloat16)
     chunk = 256 if block_len % 256 == 0 else block_len
     return pl.pallas_call(
         lambda *refs: scores_kernel(scale, chunk, per_step, *refs),
         grid=(blocks, heads // per_step),
-        in_specs=[tok, tok, tok, tok],
+        in_specs=[tok, tok, tok, tok, st],
         out_specs=[tok, tok, tok],
-        out_shape=[part, part, part],
+        out_shape=[out, out, out],
         cost_estimate=pl.CostEstimate(
             flops=blocks * heads * 6 * 2 * block_len * block_len * DH,
             transcendentals=0,
             bytes_accessed=rows * width * 14,
         ),
         name="attention_part",
-    )(q, k, v, g)
-
-
-def state_part(k, v, g, kv_state, qg_state, parts, blocks, block_len, heads, scale):
+    )(q, k, v, g, kv_state)
+
+
+def state_part(k, v, qg_state, parts, blocks, block_len, heads, scale):
     per_step = 2 if heads % 2 == 0 else 1
     tok = pl.BlockSpec((block_len, DH * per_step), lambda n, h: (n, h))
     st = pl.BlockSpec((1, per_step, DH, DH), lambda n, h: (n, h, 0, 0))
@@ -181,16 +186,16 @@
     return pl.pallas_call(
         lambda *refs: state_kernel(scale, per_step, *refs),
         grid=(blocks, heads // per_step),
-        in_specs=[tok, tok, tok, st, st, tok, tok, tok],
-        out_specs=[tok, tok, tok],
-        out_shape=[out, out, out],
+        in_specs=[tok, tok, st, tok, tok],
+        out_specs=[tok, tok],
+        out_shape=[out, out],
         cost_estimate=pl.CostEstimate(
-            flops=blocks * heads * 6 * 2 * block_len * DH * DH,
+            flops=blocks * heads * 4 * 2 * block_len * DH * DH,
             transcendentals=0,
-            bytes_accessed=rows * width * 18,
+            bytes_accessed=rows * width * 12,
         ),
         name="state_part",
-    )(k, v, g, kv_state, qg_state, *parts)
+    )(k, v, qg_state, *parts)
 
 
 def make_shards(ctx_size, head_size):
@@ -212,23 +217,33 @@
             preferred_element_type=jnp.float32,
         )
         kv_running = jnp.cumsum(kv_blocks, axis=0)
+        kv_before, _ = ctx_exclusive(kv_running[-1], ctx_size, False)
+        if blocks == 1:
+            kv_entry = kv_before[None]
+        else:
+            kv_entry = kv_before[None] + kv_running - kv_blocks
         g_blocks = grad_heads.reshape(shape)
         qg_blocks = jnp.einsum(
             "nthd,nthe->nhde", q_blocks, g_blocks, preferred_element_type=jnp.float32
         )
         qg_running = jnp.flip(jnp.cumsum(jnp.flip(qg_blocks, 0), axis=0), 0)
-        kv_before, qg_after, parts = ctx_states(
-            kv_running[-1], qg_running[0], ctx_size,
+        qg_after, (gq, gk_part, gv_part) = ctx_exclusive(
+            qg_running[0], ctx_size, True,
             Cover(
-                lambda g: attention_part(queries, keys, values, g, blocks, block_len, heads, scale_factor),
-                (grad_heads,),
+                lambda g, kv: attention_part(
+                    queries, keys, values, g, kv, blocks, block_len, heads, scale_factor
+                ),
+                (grad_heads, kv_entry),
             ),
         )
-        kv_entry = kv_before[None] + kv_running - kv_blocks
-        qg_entry = qg_after[None] + qg_running - qg_blocks
-        return state_part(
-            keys, values, grad_heads, kv_entry, qg_entry, parts, blocks, block_len, heads, scale_factor
-        )
+        if blocks == 1:
+            qg_entry = qg_after[None]
+        else:
+            qg_entry = qg_after[None] + qg_running - qg_blocks
+        gk, gv = state_part(
+            keys, values, qg_entry, (gk_part, gv_part), blocks, block_len, heads, scale_factor
+        )
+        return gq, gk, gv
 
     return shards
 

time: 81.8 us -> 73.1 us (0.89)
  waiting for transfers between devices: 30.6 us -> 12.3 us
  starting transfers between devices: 15.5 us -> 20.7 us
  matrix products: 11.8 us -> 15 us
  other arithmetic: 2.72 us -> 5.16 us
  Pallas kernels: 16.7 us -> 15.5 us
    ppermute x1, waiting for transfers between devices: 20.3 us -> 4.66 us  [project(): from_x = lax.ppermute(og, 'head', flip_pairs(4, 1))]
    ppermute x5 -> x10, starting transfers between devices: 9.45 us -> 14.7 us  [the longest x6 14.4 us: ctx_exclusive(): others = others + lax.ppermute(sent, 'ctx', pairs(step)).astype(jnp.float32)]
    ppermute x1, waiting for transfers between devices: 4.94 us -> 2.01 us  [project(): diag = lax.ppermute(relayed, ('ctx', 'head'), route)]
    dot_general x4, matrix products: 9.63 us -> 12.2 us  [mm(): lax.dot_general(a, b, (((1,), (1,)), ((), ())), preferred_element_type=jn...]
    dot_general x1, matrix products: 0.47 us -> 2.38 us  [shards(): jnp.einsum('nshd,nshe->nhde', k_blocks, v_blocks, preferred_element_type=...]
    broadcast_in_dim x0 -> x2, other arithmetic: none -> 1.72 us  [the longest x1 0.86 us: shards(): kv_entry = kv_before[None]]
    dot_general x1, matrix products: 1.72 us -> 0.45 us  [shards(): jnp.einsum('nthd,nthe->nhde', q_blocks, g_blocks, preferred_element_type=...]
    sub x1 -> x0, other arithmetic: 1.2 us -> none  [shards(): qg_entry = qg_after[None] + qg_running - qg_blocks]
  transfers between devices with their start and end apart: 8 -> 13, of which waited for: 5 -> 7; matrix products, arithmetic and copies ran while one was open for 11% -> 30% of each run, Pallas kernels for 13% -> 15%
where the time goes in v8:
time: 73.1 us; the launch traced here: 72.6 us
  starting transfers between devices  20.7 us (28%)
  Pallas kernels  15.5 us (21%)
  matrix products  15 us (21%)
  waiting for transfers between devices  12.3 us (17%)
  other arithmetic  5.16 us (7%)
  local copies, waits for them, and re-layouts  3.01 us (4%)
  between operations  0.85 us (1%)
    ppermute x6, starting transfers between devices, ctx_exclusive(): others = others + lax.ppermute(sent, 'ctx', pairs(step)).astype(jnp.float32)  14.4 us
    dot_general x4, matrix products, mm(): lax.dot_general(a, b, (((1,), (1,)), ((), ())), preferred_element_type=jn...  12.2 us
    pallas_call x1, Pallas kernels, attention_part(): pl.pallas_call(lambda *refs: scores_kernel(scale, chunk, per_step, *refs)...  10.6 us
    pallas_call x1, Pallas kernels, state_part(): pl.pallas_call(lambda *refs: state_kernel(scale, per_step, *refs), grid=(...  4.96 us
    ppermute x1, waiting for transfers between devices, project(): from_x = lax.ppermute(og, 'head', flip_pairs(4, 1))  4.66 us
    ppermute x1, starting transfers between devices, project(): from_x = lax.ppermute(og, 'head', flip_pairs(4, 1))  3 us
    dot_general x1, matrix products, shards(): jnp.einsum('nshd,nshe->nhde', k_blocks, v_blocks, preferred_element_type=...  2.38 us
    ppermute x2, waiting for transfers between devices, ctx_exclusive(): lax.ppermute(rounded, 'ctx', flip_pairs(ctx_size, 1)).astype(jnp.float32)  2.33 us
  transfers between devices with their start and end apart: 13, of which 7 were waited for; matrix products, arithmetic and copies ran while one was open for 30% of the time, Pallas kernels for 15%

profile of v8, /device:TPU:0, one launch (start us, length us, event | category | flops | bytes accessed | tf_op | source)
XLA Modules:
  0.0 72.6 jit_solution(3935917589974944930)
XLA Ops:
  0.6 3.0 %collective-permute-start = (bf16[512,1024]{1,0:T(8,128)(2,1)}, bf16[512,1024]{1,0:T(8,128)(2,1)S(1)}, u32[]{:S(2)}, u32[]{:S(2)}) collective-permute-start(bf16[512,1024]{1,0:T(8,128)(2,1)} %param.8), channel_id=1, source_target_pairs={{0,1},{1,0},{2,3},{3,2},{4,5},{5,4},{6,7},{7,6},{8,9},{9,8},{10,11... | collective-permute-start | bytes 3145736 | tf_op jit(solution)/shard_map/ppermute | solution.py:30
  3.6 1.5 %collective-permute-start.1 = (bf16[512,1024]{1,0:T(8,128)(2,1)}, bf16[512,1024]{1,0:T(8,128)(2,1)S(1)}, u32[]{:S(2)}, u32[]{:S(2)}) collective-permute-start(bf16[512,1024]{1,0:T(8,128)(2,1)} %param.8), channel_id=1, source_target_pairs={{0,2},{1,3},{2,0},{3,1},{4,6},{5,7},{6,4},{7,5},{8,10},{9,11},{10,... | collective-permute-start | bytes 3145736 | tf_op jit(solution)/shard_map/ppermute | solution.py:31
  5.2 1.5 %copy.19 = bf16[512,1024]{0,1:T(8,128)(2,1)S(1)} copy(bf16[512,1024]{1,0:T(8,128)(2,1)} %refs_0_.3) | data formatting | bytes 2097152 | tf_op jit(solution)/shard_map/reshape.3
  6.7 2.4 %convolution_convert_fusion.1 = bf16[8,128,128]{2,1,0:T(8,128)(2,1)} fusion(bf16[512,8,128]{0,2,1:T(8,128)(2,1)S(1)} %bitcast.33, bf16[512,1024]{1,0:T(8,128)(2,1)} %refs_1_.3), kind=kOutput, calls=%fused_computation.11 | convolution fusion | flops 134348800 | bytes 2359296 | tf_op jit(solution)/shard_map/nshd,nshe->nhde/dot_general | solution.py:215
  9.0 1.7 %collective-permute-done.4 = bf16[8,128,128]{2,1,0:T(8,128)(2,1)S(1)} collective-permute-done((bf16[8,128,128]{2,1,0:T(8,128)(2,1)}, bf16[8,128,128]{2,1,0:T(8,128)(2,1)S(1)}, u32[]{:S(2)}, u32[]{:S(2)}) %collective-permute-start.4) | collective-permute-done | bytes 262176 | tf_op jit(solution)/shard_map/ppermute | solution.py:47
  11.8 4.1 %collective-permute-start.5 = (bf16[8,64,128]{2,1,0:T(8,128)(2,1)S(1)}, bf16[8,64,128]{2,1,0:T(8,128)(2,1)}, u32[]{:S(2)}, u32[]{:S(2)}) collective-permute-start(bf16[8,64,128]{2,1,0:T(8,128)(2,1)S(1)} %fusion.18), channel_id=1, source_target_pairs={{0,8},{4,12},{8,16},{12,20},{16,24},{20,28},{1,9},{5,13},{9,17},{1... | collective-permute-start | bytes 393224 | tf_op jit(solution)/shard_map/ppermute | solution.py:63
  15.9 4.5 %collective-permute-start.6 = (bf16[8,64,128]{2,1,0:T(8,128)(2,1)S(1)}, bf16[8,64,128]{2,1,0:T(8,128)(2,1)}, u32[]{:S(2)}, u32[]{:S(2)}) collective-permute-start(bf16[8,64,128]{2,1,0:T(8,128)(2,1)S(1)} %fusion.18), channel_id=1, source_target_pairs={{0,16},{4,20},{8,24},{12,28},{1,17},{5,21},{9,25},{13,29},{2,18},{... | collective-permute-start | bytes 393224 | tf_op jit(solution)/shard_map/ppermute | solution.py:63
  20.4 1.9 %collective-permute-start.7 = (bf16[8,64,128]{2,1,0:T(8,128)(2,1)S(1)}, bf16[8,64,128]{2,1,0:T(8,128)(2,1)}, u32[]{:S(2)}, u32[]{:S(2)}) collective-permute-start(bf16[8,64,128]{2,1,0:T(8,128)(2,1)S(1)} %fusion.18), channel_id=1, source_target_pairs={{0,24},{4,28},{1,25},{5,29},{2,26},{6,30},{3,27},{7,31}} | collective-permute-start | bytes 393224 | tf_op jit(solution)/shard_map/ppermute | solution.py:63
  22.3 4.7 %collective-permute-done = bf16[512,1024]{1,0:T(8,128)(2,1)S(1)} collective-permute-done((bf16[512,1024]{1,0:T(8,128)(2,1)}, bf16[512,1024]{1,0:T(8,128)(2,1)S(1)}, u32[]{:S(2)}, u32[]{:S(2)}) %collective-permute-start) | collective-permute-done | bytes 1048608 | tf_op jit(solution)/shard_map/ppermute | solution.py:30
  27.0 1.5 %collective-permute-done.1 = bf16[512,1024]{1,0:T(8,128)(2,1)S(1)} collective-permute-done((bf16[512,1024]{1,0:T(8,128)(2,1)}, bf16[512,1024]{1,0:T(8,128)(2,1)S(1)}, u32[]{:S(2)}, u32[]{:S(2)}) %collective-permute-start.1) | collective-permute-done | bytes 1048608 | tf_op jit(solution)/shard_map/ppermute | solution.py:31
  28.5 1.2 %broadcast_select_fusion = bf16[512,1024]{1,0:T(8,128)(2,1)} fusion(bf16[512,1024]{1,0:T(8,128)(2,1)S(1)} %collective-permute-done, bf16[512,1024]{1,0:T(8,128)(2,1)S(1)} %collective-permute-done.1, pred[]{:T(512)S(6)} %eq.8), kind=kLoop, calls=%fused_computation.17 | loop fusion | flops 524288 | bytes 3145729 | tf_op jit(solution)/shard_map/jit(_where)/select_n | solution.py:32
  29.8 1.5 %collective-permute-start.2 = (bf16[512,1024]{1,0:T(8,128)(2,1)}, bf16[512,1024]{1,0:T(8,128)(2,1)}, u32[]{:S(2)}, u32[]{:S(2)}) collective-permute-start(bf16[512,1024]{1,0:T(8,128)(2,1)} %broadcast_select_fusion), channel_id=1, source_target_pairs={{0,2},{1,3},{2,0},{3,1},{4,5},{5,4},{6,7},{7,6},{8,10},{9,11},{10,... | collective-permute-start | bytes 3145736 | tf_op jit(solution)/shard_map/ppermute | solution.py:35
  31.3 2.9 %fusion.7 = f32[1024,512]{0,1:T(8,128)S(1)} fusion(bf16[512,1024]{1,0:T(8,128)(2,1)S(1)} %copy-done.6, bf16[1024,4096]{1,0:T(8,128)(2,1)} %param.9, s32[]{:T(128)S(6)} %select_n.69), kind=kOutput, calls=%fused_computation.8 | convolution fusion | flops 1073741824 | bytes 5242884 | tf_op jit(solution)/shard_map/dot_general | solution.py:21
  34.2 1.3 %copy.18 = bf16[512,1024]{0,1:T(8,128)(2,1)} copy(bf16[512,1024]{1,0:T(8,128)(2,1)S(1)} %copy-done) | data formatting | bytes 2097152 | tf_op jit(solution)/shard_map/reshape
  36.7 3.2 %fusion.3 = f32[1024,512]{0,1:T(8,128)S(1)} fusion(bf16[512,1024]{1,0:T(8,128)(2,1)} %copy-done.3, bf16[1024,4096]{1,0:T(8,128)(2,1)} %param.9, s32[]{:T(128)S(6)} %select_n.71), kind=kOutput, calls=%fused_computation.4 | convolution fusion | flops 1073741824 | bytes 5242884 | tf_op jit(solution)/shard_map/dot_general | solution.py:21
  40.0 2.9 %fusion.5 = f32[1024,512]{0,1:T(8,128)S(1)} fusion(bf16[512,1024]{1,0:T(8,128)(2,1)S(1)} %copy-done.2, bf16[1024,4096]{1,0:T(8,128)(2,1)} %param.9, s32[]{:T(128)S(6)} %select_n.70), kind=kOutput, calls=%fused_computation.6 | convolution fusion | flops 1073741824 | bytes 5242884 | tf_op jit(solution)/shard_map/dot_general | solution.py:21
  42.9 2.0 %collective-permute-done.2 = bf16[512,1024]{1,0:T(8,128)(2,1)} collective-permute-done((bf16[512,1024]{1,0:T(8,128)(2,1)}, bf16[512,1024]{1,0:T(8,128)(2,1)}, u32[]{:S(2)}, u32[]{:S(2)}) %collective-permute-start.2) | collective-permute-done | bytes 1048608 | tf_op jit(solution)/shard_map/ppermute | solution.py:35
  44.9 3.2 %fusion.refs_3_ = bf16[512,1024]{1,0:T(8,128)(2,1)S(1)} fusion(f32[1024,512]{0,1:T(8,128)S(1)} %fusion.3, f32[1024,512]{0,1:T(8,128)S(1)} %fusion.7, f32[1024,512]{0,1:T(8,128)S(1)} %fusion.5, bf16[512,1024]{1,0:T(8,128)(2,1)} %collective-permute-done.2, bf16[1024,4096]{1,0:T(8,128)(2,1)} %param.9, s32[]{:T(128)S(6)} %select_n.75), kind=kOutput, calls=%fused_computation.1 | convolution fusion | flops 1075838976 | bytes 10485764 | tf_op jit(solution)/shard_map/dot_general | solution.py:21
  50.3 1.3 %collective-permute-start.10 = (bf16[8,64,128]{2,1,0:T(8,128)(2,1)S(1)}, bf16[8,64,128]{2,1,0:T(8,128)(2,1)S(1)}, u32[]{:S(2)}, u32[]{:S(2)}) collective-permute-start(bf16[8,64,128]{2,1,0:T(8,128)(2,1)S(1)} %dynamic-slice_add_fusion.1), channel_id=1, source_target_pairs={{16,0},{20,4},{24,8},{28,12},{17,1},{21,5},{25,9},{29,13},{18,2},{... | collective-permute-start | bytes 393224 | tf_op jit(solution)/shard_map/ppermute | solution.py:63
  51.6 1.3 %collective-permute-start.11 = (bf16[8,64,128]{2,1,0:T(8,128)(2,1)S(1)}, bf16[8,64,128]{2,1,0:T(8,128)(2,1)S(1)}, u32[]{:S(2)}, u32[]{:S(2)}) collective-permute-start(bf16[8,64,128]{2,1,0:T(8,128)(2,1)S(1)} %dynamic-slice_add_fusion.1), channel_id=1, source_target_pairs={{24,0},{28,4},{25,1},{29,5},{26,2},{30,6},{27,3},{31,7}} | collective-permute-start | bytes 393224 | tf_op jit(solution)/shard_map/ppermute | solution.py:63
  52.9 1.3 %collective-permute-start.9 = (bf16[8,64,128]{2,1,0:T(8,128)(2,1)S(1)}, bf16[8,64,128]{2,1,0:T(8,128)(2,1)S(1)}, u32[]{:S(2)}, u32[]{:S(2)}) collective-permute-start(bf16[8,64,128]{2,1,0:T(8,128)(2,1)S(1)} %dynamic-slice_add_fusion.1), channel_id=1, source_target_pairs={{8,0},{12,4},{16,8},{20,12},{24,16},{28,20},{9,1},{13,5},{17,9},{2... | collective-permute-start | bytes 393224 | tf_op jit(solution)/shard_map/ppermute | solution.py:63
  54.2 10.6 %attention_part.1 = (bf16[512,1024]{1,0:T(8,128)(2,1)}, bf16[512,1024]{1,0:T(8,128)(2,1)}, bf16[512,1024]{1,0:T(8,128)(2,1)}) custom-call(bf16[512,1024]{1,0:T(8,128)(2,1)} %refs_0_.2, bf16[512,1024]{1,0:T(8,128)(2,1)} %refs_0_.3, bf16[512,1024]{1,0:T(8,128)(2,1)} %refs_1_.3, bf16[512,1024]{1,0:T(8,128)(2,1)} %copy-done.5, f32[1,8,128,128]{3,2,1,0:T(8,128)} %fusion.16.refs_4_), custom_call_target="tpu_custom_call" | custom-call | flops 3221225472 | bytes 7340032 | tf_op jit(solution)/shard_map/attention_part/pallas_call | solution.py:165
  65.2 1.5 %collective-permute-done.12 = f32[8,64,128]{2,1,0:T(8,128)S(1)} collective-permute-done((f32[8,64,128]{2,1,0:T(8,128)S(1)}, f32[8,64,128]{2,1,0:T(8,128)S(1)}, u32[]{:S(2)}, u32[]{:S(2)}) %collective-permute-start.12) | collective-permute-done | bytes 262176 | tf_op jit(solution)/shard_map/ppermute | solution.py:76
  67.7 5.0 %state_part.1 = (bf16[512,1024]{1,0:T(8,128)(2,1)}, bf16[512,1024]{1,0:T(8,128)(2,1)}) custom-call(bf16[512,1024]{1,0:T(8,128)(2,1)} %refs_0_.3, bf16[512,1024]{1,0:T(8,128)(2,1)} %refs_1_.3, f32[1,8,128,128]{3,2,1,0:T(8,128)} %fusion.17.refs_2_, bf16[512,1024]{1,0:T(8,128)(2,1)} %get-tuple-element.23.refs_3_, bf16[512,1024]{1,0:T(8,128)(2,1)} %get-tuple-element.24.refs_4_), custom_call_target="tpu_custom_call" | custom-call | flops 536870912 | bytes 6291456 | tf_op jit(solution)/shard_map/state_part/pallas_call | solution.py:186
  (37 shorter events, 5.8 us)
Async XLA Ops:
  0.6 26.4 %collective-permute-start = (bf16[512,1024]{1,0:T(8,128)(2,1)}, bf16[512,1024]{1,0:T(8,128)(2,1)S(1)}, u32[]{:S(2)}, u32[]{:S(2)}) collective-permute-start(bf16[512,1024]{1,0:T(8,128)(2,1)} %param.8), channel_id=1, source_target_pairs={{0,1},{1,0},{2,3},{3,2},{4,5},{5,4},{6,7},{7,6},{8,9},{9,8},{10,11... | collective-permute-start | bytes 3145736 | tf_op jit(solution)/shard_map/ppermute | solution.py:30
  3.6 24.8 %collective-permute-start.1 = (bf16[512,1024]{1,0:T(8,128)(2,1)}, bf16[512,1024]{1,0:T(8,128)(2,1)S(1)}, u32[]{:S(2)}, u32[]{:S(2)}) collective-permute-start(bf16[512,1024]{1,0:T(8,128)(2,1)} %param.8), channel_id=1, source_target_pairs={{0,2},{1,3},{2,0},{3,1},{4,6},{5,7},{6,4},{7,5},{8,10},{9,11},{10,... | collective-permute-start | bytes 3145736 | tf_op jit(solution)/shard_map/ppermute | solution.py:31
  9.0 1.7 %collective-permute-start.4 = (bf16[8,128,128]{2,1,0:T(8,128)(2,1)}, bf16[8,128,128]{2,1,0:T(8,128)(2,1)S(1)}, u32[]{:S(2)}, u32[]{:S(2)}) collective-permute-start(bf16[8,128,128]{2,1,0:T(8,128)(2,1)} %convolution_convert_fusion.1), channel_id=1, source_target_pairs={{0,4},{4,0},{8,12},{12,8},{16,20},{20,16},{24,28},{28,24},{1,5},{5... | collective-permute-start | bytes 786440 | tf_op jit(solution)/shard_map/ppermute | solution.py:47
  9.0 22.3 %copy-start.6 = (bf16[512,1024]{1,0:T(8,128)(2,1)S(1)}, bf16[512,1024]{1,0:T(8,128)(2,1)}, u32[]{:S(2)}) copy-start(bf16[512,1024]{1,0:T(8,128)(2,1)} %param.8) | copy-start | bytes 3145732
  11.8 23.8 %collective-permute-start.5 = (bf16[8,64,128]{2,1,0:T(8,128)(2,1)S(1)}, bf16[8,64,128]{2,1,0:T(8,128)(2,1)}, u32[]{:S(2)}, u32[]{:S(2)}) collective-permute-start(bf16[8,64,128]{2,1,0:T(8,128)(2,1)S(1)} %fusion.18), channel_id=1, source_target_pairs={{0,8},{4,12},{8,16},{12,20},{16,24},{20,28},{1,9},{5,13},{9,17},{1... | collective-permute-start | bytes 393224 | tf_op jit(solution)/shard_map/ppermute | solution.py:63
  15.9 19.6 %collective-permute-start.6 = (bf16[8,64,128]{2,1,0:T(8,128)(2,1)S(1)}, bf16[8,64,128]{2,1,0:T(8,128)(2,1)}, u32[]{:S(2)}, u32[]{:S(2)}) collective-permute-start(bf16[8,64,128]{2,1,0:T(8,128)(2,1)S(1)} %fusion.18), channel_id=1, source_target_pairs={{0,16},{4,20},{8,24},{12,28},{1,17},{5,21},{9,25},{13,29},{2,18},{... | collective-permute-start | bytes 393224 | tf_op jit(solution)/shard_map/ppermute | solution.py:63
  20.4 15.2 %collective-permute-start.7 = (bf16[8,64,128]{2,1,0:T(8,128)(2,1)S(1)}, bf16[8,64,128]{2,1,0:T(8,128)(2,1)}, u32[]{:S(2)}, u32[]{:S(2)}) collective-permute-start(bf16[8,64,128]{2,1,0:T(8,128)(2,1)S(1)} %fusion.18), channel_id=1, source_target_pairs={{0,24},{4,28},{1,25},{5,29},{2,26},{6,30},{3,27},{7,31}} | collective-permute-start | bytes 393224 | tf_op jit(solution)/shard_map/ppermute | solution.py:63
  27.0 2.6 %copy-start.1 = (bf16[512,1024]{1,0:T(8,128)(2,1)}, bf16[512,1024]{1,0:T(8,128)(2,1)S(1)}, u32[]{:S(2)}) copy-start(bf16[512,1024]{1,0:T(8,128)(2,1)S(1)} %collective-permute-done) | copy-start | bytes 3145732
  28.5 1.3 %copy-start.3 = (bf16[512,1024]{1,0:T(8,128)(2,1)}, bf16[512,1024]{1,0:T(8,128)(2,1)S(1)}, u32[]{:S(2)}) copy-start(bf16[512,1024]{1,0:T(8,128)(2,1)S(1)} %collective-permute-done.1) | copy-start | bytes 3145732
  29.8 4.4 %copy-start = (bf16[512,1024]{1,0:T(8,128)(2,1)S(1)}, bf16[512,1024]{1,0:T(8,128)(2,1)}, u32[]{:S(2)}) copy-start(bf16[512,1024]{1,0:T(8,128)(2,1)} %refs_0_.2) | copy-start | bytes 3145732
  29.8 15.1 %collective-permute-start.2 = (bf16[512,1024]{1,0:T(8,128)(2,1)}, bf16[512,1024]{1,0:T(8,128)(2,1)}, u32[]{:S(2)}, u32[]{:S(2)}) collective-permute-start(bf16[512,1024]{1,0:T(8,128)(2,1)} %broadcast_select_fusion), channel_id=1, source_target_pairs={{0,2},{1,3},{2,0},{3,1},{4,5},{5,4},{6,7},{7,6},{8,10},{9,11},{10,... | collective-permute-start | bytes 3145736 | tf_op jit(solution)/shard_map/ppermute | solution.py:35
  36.6 3.3 %copy-start.2 = (bf16[512,1024]{1,0:T(8,128)(2,1)S(1)}, bf16[512,1024]{1,0:T(8,128)(2,1)}, u32[]{:S(2)}) copy-start(bf16[512,1024]{1,0:T(8,128)(2,1)} %copy-done.1) | copy-start | bytes 3145732
  36.7 12.0 %collective-permute-start.8 = (f32[8,64,128]{2,1,0:T(8,128)S(1)}, f32[8,64,128]{2,1,0:T(8,128)S(1)}, u32[]{:S(2)}, u32[]{:S(2)}) collective-permute-start(f32[8,64,128]{2,1,0:T(8,128)S(1)} %convert_add_fusion.1), channel_id=1, source_target_pairs={{0,4},{4,0},{8,12},{12,8},{16,20},{20,16},{24,28},{28,24},{1,5},{5... | collective-permute-start | bytes 786440 | tf_op jit(solution)/shard_map/ppermute | solution.py:76
  42.9 5.3 %copy-start.4 = (bf16[512,1024]{0,1:T(8,128)(2,1)S(1)}, bf16[512,1024]{0,1:T(8,128)(2,1)}, u32[]{:S(2)}) copy-start(bf16[512,1024]{0,1:T(8,128)(2,1)} %copy.18) | copy-start | bytes 3145732
  48.1 1.5 %copy-start.5 = (bf16[512,1024]{1,0:T(8,128)(2,1)}, bf16[512,1024]{1,0:T(8,128)(2,1)S(1)}, u32[]{:S(2)}) copy-start(bf16[512,1024]{1,0:T(8,128)(2,1)S(1)} %fusion.refs_3_) | copy-start | bytes 3145732
  48.6 1.6 %collective-permute-start.3 = (bf16[8,128,128]{2,1,0:T(8,128)(2,1)S(1)}, bf16[8,128,128]{2,1,0:T(8,128)(2,1)S(1)}, u32[]{:S(2)}, u32[]{:S(2)}) collective-permute-start(bf16[8,128,128]{2,1,0:T(8,128)(2,1)S(1)} %fusion.11), channel_id=1, source_target_pairs={{0,4},{4,0},{8,12},{12,8},{16,20},{20,16},{24,28},{28,24},{1,5},{5... | collective-permute-start | bytes 786440 | tf_op jit(solution)/shard_map/ppermute | solution.py:47
  50.3 14.8 %collective-permute-start.10 = (bf16[8,64,128]{2,1,0:T(8,128)(2,1)S(1)}, bf16[8,64,128]{2,1,0:T(8,128)(2,1)S(1)}, u32[]{:S(2)}, u32[]{:S(2)}) collective-permute-start(bf16[8,64,128]{2,1,0:T(8,128)(2,1)S(1)} %dynamic-slice_add_fusion.1), channel_id=1, source_target_pairs={{16,0},{20,4},{24,8},{28,12},{17,1},{21,5},{25,9},{29,13},{18,2},{... | collective-permute-start | bytes 393224 | tf_op jit(solution)/shard_map/ppermute | solution.py:63
  51.6 13.5 %collective-permute-start.11 = (bf16[8,64,128]{2,1,0:T(8,128)(2,1)S(1)}, bf16[8,64,128]{2,1,0:T(8,128)(2,1)S(1)}, u32[]{:S(2)}, u32[]{:S(2)}) collective-permute-start(bf16[8,64,128]{2,1,0:T(8,128)(2,1)S(1)} %dynamic-slice_add_fusion.1), channel_id=1, source_target_pairs={{24,0},{28,4},{25,1},{29,5},{26,2},{30,6},{27,3},{31,7}} | collective-permute-start | bytes 393224 | tf_op jit(solution)/shard_map/ppermute | solution.py:63
  52.9 12.2 %collective-permute-start.9 = (bf16[8,64,128]{2,1,0:T(8,128)(2,1)S(1)}, bf16[8,64,128]{2,1,0:T(8,128)(2,1)S(1)}, u32[]{:S(2)}, u32[]{:S(2)}) collective-permute-start(bf16[8,64,128]{2,1,0:T(8,128)(2,1)S(1)} %dynamic-slice_add_fusion.1), channel_id=1, source_target_pairs={{8,0},{12,4},{16,8},{20,12},{24,16},{28,20},{9,1},{13,5},{17,9},{2... | collective-permute-start | bytes 393224 | tf_op jit(solution)/shard_map/ppermute | solution.py:63
  65.2 1.6 %collective-permute-start.12 = (f32[8,64,128]{2,1,0:T(8,128)S(1)}, f32[8,64,128]{2,1,0:T(8,128)S(1)}, u32[]{:S(2)}, u32[]{:S(2)}) collective-permute-start(f32[8,64,128]{2,1,0:T(8,128)S(1)} %convert_add_fusion), channel_id=1, source_target_pairs={{0,4},{4,0},{8,12},{12,8},{16,20},{20,16},{24,28},{28,24},{1,5},{5... | collective-permute-start | bytes 786440 | tf_op jit(solution)/shard_map/ppermute | solution.py:76

commit v9 on v8

--- a/solution.py
+++ b/solution.py
@@ -96,18 +96,17 @@
     return high, low
 
 
-def scores_kernel(scale, chunk, per_step, q_ref, k_ref, v_ref, g_ref, kv_ref, gq_ref, gk_ref, gv_ref):
-    length = q_ref.shape[0]
-    count = length // chunk
+def score(a, b, keep, scale):
+    s = lax.dot_general(a, b, NT, preferred_element_type=jnp.float32) * scale
+    if keep is not None:
+        s = jnp.where(keep, s, 0.0)
+    return s.astype(jnp.bfloat16)
+
+
+def query_kernel(scale, chunk, per_step, k_ref, v_ref, g_ref, kv_ref, gq_ref):
+    count = k_ref.shape[0] // chunk
     row = lax.broadcasted_iota(jnp.int32, (chunk, chunk), 0)
     col = lax.broadcasted_iota(jnp.int32, (chunk, chunk), 1)
-
-    def score(a, b, keep):
-        s = lax.dot_general(a, b, NT, preferred_element_type=jnp.float32) * scale
-        if keep is not None:
-            s = jnp.where(keep, s, 0.0)
-        return s.astype(jnp.bfloat16)
-
     for h in range(per_step):
         cols = pl.ds(h * DH, DH)
         kv_high, kv_low = split_state(kv_ref[0, h] * scale)
@@ -116,86 +115,61 @@
             return ref[pl.ds(i * chunk, chunk), cols]
 
         for i in range(count):
-            rows = pl.ds(i * chunk, chunk)
             g_i = piece(g_ref, i)
             gq = lax.dot_general(g_i, kv_high, NT, preferred_element_type=jnp.float32)
             gq = gq + lax.dot_general(g_i, kv_low, NT, preferred_element_type=jnp.float32)
             for j in range(i + 1):
-                sg = score(g_i, piece(v_ref, j), row >= col if j == i else None)
-                term = jnp.dot(sg, piece(k_ref, j), preferred_element_type=jnp.float32)
-                gq = gq + term
-            gq_ref[rows, cols] = gq.astype(gq_ref.dtype)
+                sg = score(g_i, piece(v_ref, j), row >= col if j == i else None, scale)
+                gq = gq + jnp.dot(sg, piece(k_ref, j), preferred_element_type=jnp.float32)
+            gq_ref[pl.ds(i * chunk, chunk), cols] = gq.astype(gq_ref.dtype)
+
+
+def key_value_kernel(scale, chunk, per_step, q_ref, k_ref, v_ref, g_ref, qg_ref, gk_ref, gv_ref):
+    count = k_ref.shape[0] // chunk
+    row = lax.broadcasted_iota(jnp.int32, (chunk, chunk), 0)
+    col = lax.broadcasted_iota(jnp.int32, (chunk, chunk), 1)
+    for h in range(per_step):
+        cols = pl.ds(h * DH, DH)
+        qg_high, qg_low = split_state(qg_ref[0, h] * scale)
+
+        def piece(ref, i):
+            return ref[pl.ds(i * chunk, chunk), cols]
+
+        for i in range(count):
             v_i, k_i = piece(v_ref, i), piece(k_ref, i)
-            gk = None
-            gv = None
+            gk = lax.dot_general(v_i, qg_high, NT, preferred_element_type=jnp.float32)
+            gk = gk + lax.dot_general(v_i, qg_low, NT, preferred_element_type=jnp.float32)
+            gv = jnp.dot(k_i, qg_high, preferred_element_type=jnp.float32)
+            gv = gv + jnp.dot(k_i, qg_low, preferred_element_type=jnp.float32)
             for j in range(i, count):
                 keep = row <= col if j == i else None
-                sgt = score(v_i, piece(g_ref, j), keep)
-                sft = score(k_i, piece(q_ref, j), keep)
-                term_k = jnp.dot(sgt, piece(q_ref, j), preferred_element_type=jnp.float32)
-                term_v = jnp.dot(sft, piece(g_ref, j), preferred_element_type=jnp.float32)
-                gk = term_k if gk is None else gk + term_k
-                gv = term_v if gv is None else gv + term_v
+                sgt = score(v_i, piece(g_ref, j), keep, scale)
+                sft = score(k_i, piece(q_ref, j), keep, scale)
+                gk = gk + jnp.dot(sgt, piece(q_ref, j), preferred_element_type=jnp.float32)
+                gv = gv + jnp.dot(sft, piece(g_ref, j), preferred_element_type=jnp.float32)
+            rows = pl.ds(i * chunk, chunk)
             gk_ref[rows, cols] = gk.astype(gk_ref.dtype)
             gv_ref[rows, cols] = gv.astype(gv_ref.dtype)
 
 
-def state_kernel(scale, per_step, k_ref, v_ref, qg_ref, gkp_ref, gvp_ref, gk_ref, gv_ref):
-    for i in range(per_step):
-        cols = pl.ds(i * DH, DH)
-        k, v = k_ref[:, cols], v_ref[:, cols]
-        qg_high, qg_low = split_state(qg_ref[0, i] * scale)
-        gk = gkp_ref[:, cols].astype(jnp.float32)
-        gk = gk + lax.dot_general(v, qg_high, NT, preferred_element_type=jnp.float32)
-        gk = gk + lax.dot_general(v, qg_low, NT, preferred_element_type=jnp.float32)
-        gv = gvp_ref[:, cols].astype(jnp.float32)
-        gv = gv + jnp.dot(k, qg_high, preferred_element_type=jnp.float32)
-        gv = gv + jnp.dot(k, qg_low, preferred_element_type=jnp.float32)
-        gk_ref[:, cols] = gk.astype(jnp.bfloat16)
-        gv_ref[:, cols] = gv.astype(jnp.bfloat16)
-
-
-def attention_part(q, k, v, g, kv_state, blocks, block_len, heads, scale):
+def head_call(kernel, scale, inputs, state, outputs, blocks, block_len, heads, flops, name):
     per_step = 2 if heads % 2 == 0 else 1
     tok = pl.BlockSpec((block_len, DH * per_step), lambda n, h: (n, h))
     st = pl.BlockSpec((1, per_step, DH, DH), lambda n, h: (n, h, 0, 0))
-    rows, width = q.shape
+    rows, width = inputs[0].shape
     out = jax.ShapeDtypeStruct((rows, width), jnp.bfloat16)
     chunk = 256 if block_len % 256 == 0 else block_len
     return pl.pallas_call(
-        lambda *refs: scores_kernel(scale, chunk, per_step, *refs),
+        lambda *refs: kernel(scale, chunk, per_step, *refs),
         grid=(blocks, heads // per_step),
-        in_specs=[tok, tok, tok, tok, st],
-        out_specs=[tok, tok, tok],
-        out_shape=[out, out, out],
+        in_specs=[tok] * len(inputs) + [st],
+        out_specs=[tok] * outputs,
+        out_shape=[out] * outputs,
         cost_estimate=pl.CostEstimate(
-            flops=blocks * heads * 6 * 2 * block_len * block_len * DH,
-            transcendentals=0,
-            bytes_accessed=rows * width * 14,
+            flops=flops, transcendentals=0, bytes_accessed=rows * width * 2 * (len(inputs) + outputs)
         ),
-        name="attention_part",
-    )(q, k, v, g, kv_state)
-
-
-def state_part(k, v, qg_state, parts, blocks, block_len, heads, scale):
-    per_step = 2 if heads % 2 == 0 else 1
-    tok = pl.BlockSpec((block_len, DH * per_step), lambda n, h: (n, h))
-    st = pl.BlockSpec((1, per_step, DH, DH), lambda n, h: (n, h, 0, 0))
-    rows, width = k.shape
-    out = jax.ShapeDtypeStruct((rows, width), jnp.bfloat16)
-    return pl.pallas_call(
-        lambda *refs: state_kernel(scale, per_step, *refs),
-        grid=(blocks, heads // per_step),
-        in_specs=[tok, tok, st, tok, tok],
-        out_specs=[tok, tok],
-        out_shape=[out, out],
-        cost_estimate=pl.CostEstimate(
-            flops=blocks * heads * 4 * 2 * block_len * DH * DH,
-            transcendentals=0,
-            bytes_accessed=rows * width * 12,
-        ),
-        name="state_part",
-    )(k, v, qg_state, *parts)
+        name=name,
+    )(*inputs, state)
 
 
 def make_shards(ctx_size, head_size):
@@ -227,12 +201,14 @@
             "nthd,nthe->nhde", q_blocks, g_blocks, preferred_element_type=jnp.float32
         )
         qg_running = jnp.flip(jnp.cumsum(jnp.flip(qg_blocks, 0), axis=0), 0)
-        qg_after, (gq, gk_part, gv_part) = ctx_exclusive(
+        pair_flops = blocks * heads * 2 * 2 * block_len * block_len * DH
+        qg_after, gq = ctx_exclusive(
             qg_running[0], ctx_size, True,
             Cover(
-                lambda g, kv: attention_part(
-                    queries, keys, values, g, kv, blocks, block_len, heads, scale_factor
-                ),
+                lambda g, kv: head_call(
+                    query_kernel, scale_factor, (keys, values, g), kv, 1,
+                    blocks, block_len, heads, pair_flops, "grad_queries",
+                )[0],
                 (grad_heads, kv_entry),
             ),
         )
@@ -240,8 +216,9 @@
             qg_entry = qg_after[None]
         else:
             qg_entry = qg_after[None] + qg_running - qg_blocks
-        gk, gv = state_part(
-            keys, values, qg_entry, (gk_part, gv_part), blocks, block_len, heads, scale_factor
+        gk, gv = head_call(
+            key_value_kernel, scale_factor, (queries, keys, values, grad_heads), qg_entry, 2,
+            blocks, block_len, heads, 2 * pair_flops, "grad_keys_values",
         )
         return gq, gk, gv
 

time: 73.1 us -> 77 us (1.053)
  waiting for transfers between devices: 12.3 us -> 16.5 us
    ppermute x6, waiting for transfers between devices: 0.34 us -> 4.5 us  [ctx_exclusive(): others = others + lax.ppermute(sent, 'ctx', pairs(step)).astype(jnp.float32)]
  transfers between devices with their start and end apart: 13 -> 13, of which waited for: 7 -> 7; matrix products, arithmetic and copies ran while one was open for 30% -> 29% of each run, Pallas kernels for 15% -> 8%
where the time goes in v9:
time: 77 us; the launch traced here: 76.4 us
  starting transfers between devices  20.7 us (27%)
  waiting for transfers between devices  16.5 us (21%)
  Pallas kernels  15.2 us (20%)
  matrix products  15 us (19%)
  other arithmetic  5.18 us (7%)
  local copies, waits for them, and re-layouts  3 us (4%)
  between operations  0.85 us (1%)
    pallas_call x2, Pallas kernels, head_call(): pl.pallas_call(lambda *refs: kernel(scale, chunk, per_step, *refs), grid=...  15.2 us
    ppermute x6, starting transfers between devices, ctx_exclusive(): others = others + lax.ppermute(sent, 'ctx', pairs(step)).astype(jnp.float32)  14.5 us
    dot_general x4, matrix products, mm(): lax.dot_general(a, b, (((1,), (1,)), ((), ())), preferred_element_type=jn...  12.2 us
    ppermute x1, waiting for transfers between devices, project(): from_x = lax.ppermute(og, 'head', flip_pairs(4, 1))  4.65 us
    ppermute x6, waiting for transfers between devices, ctx_exclusive(): others = others + lax.ppermute(sent, 'ctx', pairs(step)).astype(jnp.float32)  4.5 us
    ppermute x1, starting transfers between devices, project(): from_x = lax.ppermute(og, 'head', flip_pairs(4, 1))  3 us
    dot_general x1, matrix products, shards(): jnp.einsum('nshd,nshe->nhde', k_blocks, v_blocks, preferred_element_type=...  2.38 us
    ppermute x2, waiting for transfers between devices, ctx_exclusive(): lax.ppermute(rounded, 'ctx', flip_pairs(ctx_size, 1)).astype(jnp.float32)  2.33 us
  transfers between devices with their start and end apart: 13, of which 7 were waited for; matrix products, arithmetic and copies ran while one was open for 29% of the time, Pallas kernels for 8%

profile of v9, /device:TPU:0, one launch (start us, length us, event | category | flops | bytes accessed | tf_op | source)
XLA Modules:
  0.0 76.4 jit_solution(11913920625849468215)
XLA Ops:
  0.6 3.0 %collective-permute-start = (bf16[512,1024]{1,0:T(8,128)(2,1)}, bf16[512,1024]{1,0:T(8,128)(2,1)S(1)}, u32[]{:S(2)}, u32[]{:S(2)}) collective-permute-start(bf16[512,1024]{1,0:T(8,128)(2,1)} %param.8), channel_id=1, source_target_pairs={{0,1},{1,0},{2,3},{3,2},{4,5},{5,4},{6,7},{7,6},{8,9},{9,8},{10,11... | collective-permute-start | bytes 3145736 | tf_op jit(solution)/shard_map/ppermute | solution.py:30
  3.6 1.5 %collective-permute-start.1 = (bf16[512,1024]{1,0:T(8,128)(2,1)}, bf16[512,1024]{1,0:T(8,128)(2,1)S(1)}, u32[]{:S(2)}, u32[]{:S(2)}) collective-permute-start(bf16[512,1024]{1,0:T(8,128)(2,1)} %param.8), channel_id=1, source_target_pairs={{0,2},{1,3},{2,0},{3,1},{4,6},{5,7},{6,4},{7,5},{8,10},{9,11},{10,... | collective-permute-start | bytes 3145736 | tf_op jit(solution)/shard_map/ppermute | solution.py:31
  5.2 1.5 %copy.19 = bf16[512,1024]{0,1:T(8,128)(2,1)S(1)} copy(bf16[512,1024]{1,0:T(8,128)(2,1)} %refs_1_.3) | data formatting | bytes 2097152 | tf_op jit(solution)/shard_map/reshape.3
  6.7 2.4 %convolution_convert_fusion.1 = bf16[8,128,128]{2,1,0:T(8,128)(2,1)} fusion(bf16[512,8,128]{0,2,1:T(8,128)(2,1)S(1)} %bitcast.33, bf16[512,1024]{1,0:T(8,128)(2,1)} %refs_2_.1), kind=kOutput, calls=%fused_computation.11 | convolution fusion | flops 134348800 | bytes 2359296 | tf_op jit(solution)/shard_map/nshd,nshe->nhde/dot_general | solution.py:189
  9.0 1.7 %collective-permute-done.4 = bf16[8,128,128]{2,1,0:T(8,128)(2,1)S(1)} collective-permute-done((bf16[8,128,128]{2,1,0:T(8,128)(2,1)}, bf16[8,128,128]{2,1,0:T(8,128)(2,1)S(1)}, u32[]{:S(2)}, u32[]{:S(2)}) %collective-permute-start.4) | collective-permute-done | bytes 262176 | tf_op jit(solution)/shard_map/ppermute | solution.py:47
  11.8 4.1 %collective-permute-start.5 = (bf16[8,64,128]{2,1,0:T(8,128)(2,1)S(1)}, bf16[8,64,128]{2,1,0:T(8,128)(2,1)}, u32[]{:S(2)}, u32[]{:S(2)}) collective-permute-start(bf16[8,64,128]{2,1,0:T(8,128)(2,1)S(1)} %fusion.18), channel_id=1, source_target_pairs={{0,8},{4,12},{8,16},{12,20},{16,24},{20,28},{1,9},{5,13},{9,17},{1... | collective-permute-start | bytes 393224 | tf_op jit(solution)/shard_map/ppermute | solution.py:63
  15.9 4.5 %collective-permute-start.6 = (bf16[8,64,128]{2,1,0:T(8,128)(2,1)S(1)}, bf16[8,64,128]{2,1,0:T(8,128)(2,1)}, u32[]{:S(2)}, u32[]{:S(2)}) collective-permute-start(bf16[8,64,128]{2,1,0:T(8,128)(2,1)S(1)} %fusion.18), channel_id=1, source_target_pairs={{0,16},{4,20},{8,24},{12,28},{1,17},{5,21},{9,25},{13,29},{2,18},{... | collective-permute-start | bytes 393224 | tf_op jit(solution)/shard_map/ppermute | solution.py:63
  20.4 1.9 %collective-permute-start.7 = (bf16[8,64,128]{2,1,0:T(8,128)(2,1)S(1)}, bf16[8,64,128]{2,1,0:T(8,128)(2,1)}, u32[]{:S(2)}, u32[]{:S(2)}) collective-permute-start(bf16[8,64,128]{2,1,0:T(8,128)(2,1)S(1)} %fusion.18), channel_id=1, source_target_pairs={{0,24},{4,28},{1,25},{5,29},{2,26},{6,30},{3,27},{7,31}} | collective-permute-start | bytes 393224 | tf_op jit(solution)/shard_map/ppermute | solution.py:63
  22.4 4.6 %collective-permute-done = bf16[512,1024]{1,0:T(8,128)(2,1)S(1)} collective-permute-done((bf16[512,1024]{1,0:T(8,128)(2,1)}, bf16[512,1024]{1,0:T(8,128)(2,1)S(1)}, u32[]{:S(2)}, u32[]{:S(2)}) %collective-permute-start) | collective-permute-done | bytes 1048608 | tf_op jit(solution)/shard_map/ppermute | solution.py:30
  27.0 1.5 %collective-permute-done.1 = bf16[512,1024]{1,0:T(8,128)(2,1)S(1)} collective-permute-done((bf16[512,1024]{1,0:T(8,128)(2,1)}, bf16[512,1024]{1,0:T(8,128)(2,1)S(1)}, u32[]{:S(2)}, u32[]{:S(2)}) %collective-permute-start.1) | collective-permute-done | bytes 1048608 | tf_op jit(solution)/shard_map/ppermute | solution.py:31
  29.8 1.5 %collective-permute-start.2 = (bf16[512,1024]{1,0:T(8,128)(2,1)}, bf16[512,1024]{1,0:T(8,128)(2,1)}, u32[]{:S(2)}, u32[]{:S(2)}) collective-permute-start(bf16[512,1024]{1,0:T(8,128)(2,1)} %broadcast_select_fusion), channel_id=1, source_target_pairs={{0,2},{1,3},{2,0},{3,1},{4,5},{5,4},{6,7},{7,6},{8,10},{9,11},{10,... | collective-permute-start | bytes 3145736 | tf_op jit(solution)/shard_map/ppermute | solution.py:35
  31.3 2.9 %fusion.7 = f32[1024,512]{0,1:T(8,128)S(1)} fusion(bf16[512,1024]{1,0:T(8,128)(2,1)S(1)} %copy-done.6, bf16[1024,4096]{1,0:T(8,128)(2,1)} %param.9, s32[]{:T(128)S(6)} %select_n.69), kind=kOutput, calls=%fused_computation.8 | convolution fusion | flops 1073741824 | bytes 5242884 | tf_op jit(solution)/shard_map/dot_general | solution.py:21
  34.2 1.3 %copy.18 = bf16[512,1024]{0,1:T(8,128)(2,1)} copy(bf16[512,1024]{1,0:T(8,128)(2,1)S(1)} %copy-done.1) | data formatting | bytes 2097152 | tf_op jit(solution)/shard_map/reshape
  36.7 3.2 %fusion.3 = f32[1024,512]{0,1:T(8,128)S(1)} fusion(bf16[512,1024]{1,0:T(8,128)(2,1)} %copy-done.4, bf16[1024,4096]{1,0:T(8,128)(2,1)} %param.9, s32[]{:T(128)S(6)} %select_n.71), kind=kOutput, calls=%fused_computation.4 | convolution fusion | flops 1073741824 | bytes 5242884 | tf_op jit(solution)/shard_map/dot_general | solution.py:21
  40.0 2.9 %fusion.5 = f32[1024,512]{0,1:T(8,128)S(1)} fusion(bf16[512,1024]{1,0:T(8,128)(2,1)S(1)} %copy-done.3, bf16[1024,4096]{1,0:T(8,128)(2,1)} %param.9, s32[]{:T(128)S(6)} %select_n.70), kind=kOutput, calls=%fused_computation.6 | convolution fusion | flops 1073741824 | bytes 5242884 | tf_op jit(solution)/shard_map/dot_general | solution.py:21
  42.9 2.0 %collective-permute-done.2 = bf16[512,1024]{1,0:T(8,128)(2,1)} collective-permute-done((bf16[512,1024]{1,0:T(8,128)(2,1)}, bf16[512,1024]{1,0:T(8,128)(2,1)}, u32[]{:S(2)}, u32[]{:S(2)}) %collective-permute-start.2) | collective-permute-done | bytes 1048608 | tf_op jit(solution)/shard_map/ppermute | solution.py:35
  44.9 3.2 %fusion.refs_2_.refs_3_ = bf16[512,1024]{1,0:T(8,128)(2,1)S(1)} fusion(f32[1024,512]{0,1:T(8,128)S(1)} %fusion.3, f32[1024,512]{0,1:T(8,128)S(1)} %fusion.7, f32[1024,512]{0,1:T(8,128)S(1)} %fusion.5, bf16[512,1024]{1,0:T(8,128)(2,1)} %collective-permute-done.2, bf16[1024,4096]{1,0:T(8,128)(2,1)} %param.9, s32[]{:T(128)S(6)} %select_n.75), kind=kOutput, calls=%fused_computation.1 | convolution fusion | flops 1075838976 | bytes 10485764 | tf_op jit(solution)/shard_map/dot_general | solution.py:21
  50.3 1.3 %collective-permute-start.10 = (bf16[8,64,128]{2,1,0:T(8,128)(2,1)S(1)}, bf16[8,64,128]{2,1,0:T(8,128)(2,1)S(1)}, u32[]{:S(2)}, u32[]{:S(2)}) collective-permute-start(bf16[8,64,128]{2,1,0:T(8,128)(2,1)S(1)} %dynamic-slice_add_fusion.1), channel_id=1, source_target_pairs={{16,0},{20,4},{24,8},{28,12},{17,1},{21,5},{25,9},{29,13},{18,2},{... | collective-permute-start | bytes 393224 | tf_op jit(solution)/shard_map/ppermute | solution.py:63
  51.6 1.3 %collective-permute-start.11 = (bf16[8,64,128]{2,1,0:T(8,128)(2,1)S(1)}, bf16[8,64,128]{2,1,0:T(8,128)(2,1)S(1)}, u32[]{:S(2)}, u32[]{:S(2)}) collective-permute-start(bf16[8,64,128]{2,1,0:T(8,128)(2,1)S(1)} %dynamic-slice_add_fusion.1), channel_id=1, source_target_pairs={{24,0},{28,4},{25,1},{29,5},{26,2},{30,6},{27,3},{31,7}} | collective-permute-start | bytes 393224 | tf_op jit(solution)/shard_map/ppermute | solution.py:63
  52.9 1.3 %collective-permute-start.9 = (bf16[8,64,128]{2,1,0:T(8,128)(2,1)S(1)}, bf16[8,64,128]{2,1,0:T(8,128)(2,1)S(1)}, u32[]{:S(2)}, u32[]{:S(2)}) collective-permute-start(bf16[8,64,128]{2,1,0:T(8,128)(2,1)S(1)} %dynamic-slice_add_fusion.1), channel_id=1, source_target_pairs={{8,0},{12,4},{16,8},{20,12},{24,16},{28,20},{9,1},{13,5},{17,9},{2... | collective-permute-start | bytes 393224 | tf_op jit(solution)/shard_map/ppermute | solution.py:63
  54.2 6.4 %grad_queries.1 = bf16[512,1024]{1,0:T(8,128)(2,1)} custom-call(bf16[512,1024]{1,0:T(8,128)(2,1)} %refs_1_.3, bf16[512,1024]{1,0:T(8,128)(2,1)} %refs_2_.1, bf16[512,1024]{1,0:T(8,128)(2,1)} %copy-done, f32[1,8,128,128]{3,2,1,0:T(8,128)} %fusion.16.refs_3_), custom_call_target="tpu_custom_call" | custom-call | flops 1073741824 | bytes 4194304 | tf_op jit(solution)/shard_map/grad_queries/pallas_call | solution.py:162
  60.6 4.5 %collective-permute-done.10 = bf16[8,64,128]{2,1,0:T(8,128)(2,1)S(1)} collective-permute-done((bf16[8,64,128]{2,1,0:T(8,128)(2,1)S(1)}, bf16[8,64,128]{2,1,0:T(8,128)(2,1)S(1)}, u32[]{:S(2)}, u32[]{:S(2)}) %collective-permute-start.10) | collective-permute-done | bytes 131104 | tf_op jit(solution)/shard_map/ppermute | solution.py:63
  65.2 1.5 %collective-permute-done.12 = f32[8,64,128]{2,1,0:T(8,128)S(1)} collective-permute-done((f32[8,64,128]{2,1,0:T(8,128)S(1)}, f32[8,64,128]{2,1,0:T(8,128)S(1)}, u32[]{:S(2)}, u32[]{:S(2)}) %collective-permute-start.12) | collective-permute-done | bytes 262176 | tf_op jit(solution)/shard_map/ppermute | solution.py:76
  67.7 8.8 %grad_keys_values.1 = (bf16[512,1024]{1,0:T(8,128)(2,1)}, bf16[512,1024]{1,0:T(8,128)(2,1)}) custom-call(bf16[512,1024]{1,0:T(8,128)(2,1)} %refs_0_.3, bf16[512,1024]{1,0:T(8,128)(2,1)} %refs_1_.3, bf16[512,1024]{1,0:T(8,128)(2,1)} %refs_2_.1, bf16[512,1024]{1,0:T(8,128)(2,1)} %copy-done, f32[1,8,128,128]{3,2,1,0:T(8,128)} %fusion.17.refs_4_), custom_call_target="tpu_custom_call" | custom-call | flops 2147483648 | bytes 6291456 | tf_op jit(solution)/shard_map/grad_keys_values/pallas_call | solution.py:162
  (37 shorter events, 6.6 us)
Async XLA Ops:
  0.6 26.4 %collective-permute-start = (bf16[512,1024]{1,0:T(8,128)(2,1)}, bf16[512,1024]{1,0:T(8,128)(2,1)S(1)}, u32[]{:S(2)}, u32[]{:S(2)}) collective-permute-start(bf16[512,1024]{1,0:T(8,128)(2,1)} %param.8), channel_id=1, source_target_pairs={{0,1},{1,0},{2,3},{3,2},{4,5},{5,4},{6,7},{7,6},{8,9},{9,8},{10,11... | collective-permute-start | bytes 3145736 | tf_op jit(solution)/shard_map/ppermute | solution.py:30
  3.6 24.8 %collective-permute-start.1 = (bf16[512,1024]{1,0:T(8,128)(2,1)}, bf16[512,1024]{1,0:T(8,128)(2,1)S(1)}, u32[]{:S(2)}, u32[]{:S(2)}) collective-permute-start(bf16[512,1024]{1,0:T(8,128)(2,1)} %param.8), channel_id=1, source_target_pairs={{0,2},{1,3},{2,0},{3,1},{4,6},{5,7},{6,4},{7,5},{8,10},{9,11},{10,... | collective-permute-start | bytes 3145736 | tf_op jit(solution)/shard_map/ppermute | solution.py:31
  9.0 1.7 %collective-permute-start.4 = (bf16[8,128,128]{2,1,0:T(8,128)(2,1)}, bf16[8,128,128]{2,1,0:T(8,128)(2,1)S(1)}, u32[]{:S(2)}, u32[]{:S(2)}) collective-permute-start(bf16[8,128,128]{2,1,0:T(8,128)(2,1)} %convolution_convert_fusion.1), channel_id=1, source_target_pairs={{0,4},{4,0},{8,12},{12,8},{16,20},{20,16},{24,28},{28,24},{1,5},{5... | collective-permute-start | bytes 786440 | tf_op jit(solution)/shard_map/ppermute | solution.py:47
  9.0 22.3 %copy-start.6 = (bf16[512,1024]{1,0:T(8,128)(2,1)S(1)}, bf16[512,1024]{1,0:T(8,128)(2,1)}, u32[]{:S(2)}) copy-start(bf16[512,1024]{1,0:T(8,128)(2,1)} %param.8) | copy-start | bytes 3145732
  11.8 23.8 %collective-permute-start.5 = (bf16[8,64,128]{2,1,0:T(8,128)(2,1)S(1)}, bf16[8,64,128]{2,1,0:T(8,128)(2,1)}, u32[]{:S(2)}, u32[]{:S(2)}) collective-permute-start(bf16[8,64,128]{2,1,0:T(8,128)(2,1)S(1)} %fusion.18), channel_id=1, source_target_pairs={{0,8},{4,12},{8,16},{12,20},{16,24},{20,28},{1,9},{5,13},{9,17},{1... | collective-permute-start | bytes 393224 | tf_op jit(solution)/shard_map/ppermute | solution.py:63
  15.9 19.6 %collective-permute-start.6 = (bf16[8,64,128]{2,1,0:T(8,128)(2,1)S(1)}, bf16[8,64,128]{2,1,0:T(8,128)(2,1)}, u32[]{:S(2)}, u32[]{:S(2)}) collective-permute-start(bf16[8,64,128]{2,1,0:T(8,128)(2,1)S(1)} %fusion.18), channel_id=1, source_target_pairs={{0,16},{4,20},{8,24},{12,28},{1,17},{5,21},{9,25},{13,29},{2,18},{... | collective-permute-start | bytes 393224 | tf_op jit(solution)/shard_map/ppermute | solution.py:63
  20.4 15.1 %collective-permute-start.7 = (bf16[8,64,128]{2,1,0:T(8,128)(2,1)S(1)}, bf16[8,64,128]{2,1,0:T(8,128)(2,1)}, u32[]{:S(2)}, u32[]{:S(2)}) collective-permute-start(bf16[8,64,128]{2,1,0:T(8,128)(2,1)S(1)} %fusion.18), channel_id=1, source_target_pairs={{0,24},{4,28},{1,25},{5,29},{2,26},{6,30},{3,27},{7,31}} | collective-permute-start | bytes 393224 | tf_op jit(solution)/shard_map/ppermute | solution.py:63
  27.0 1.5 %copy-start.2 = (bf16[512,1024]{1,0:T(8,128)(2,1)}, bf16[512,1024]{1,0:T(8,128)(2,1)S(1)}, u32[]{:S(2)}) copy-start(bf16[512,1024]{1,0:T(8,128)(2,1)S(1)} %collective-permute-done) | copy-start | bytes 3145732
  28.5 1.3 %copy-start.4 = (bf16[512,1024]{1,0:T(8,128)(2,1)}, bf16[512,1024]{1,0:T(8,128)(2,1)S(1)}, u32[]{:S(2)}) copy-start(bf16[512,1024]{1,0:T(8,128)(2,1)S(1)} %collective-permute-done.1) | copy-start | bytes 3145732
  29.8 4.4 %copy-start.1 = (bf16[512,1024]{1,0:T(8,128)(2,1)S(1)}, bf16[512,1024]{1,0:T(8,128)(2,1)}, u32[]{:S(2)}) copy-start(bf16[512,1024]{1,0:T(8,128)(2,1)} %refs_0_.3) | copy-start | bytes 3145732
  29.8 15.1 %collective-permute-start.2 = (bf16[512,1024]{1,0:T(8,128)(2,1)}, bf16[512,1024]{1,0:T(8,128)(2,1)}, u32[]{:S(2)}, u32[]{:S(2)}) collective-permute-start(bf16[512,1024]{1,0:T(8,128)(2,1)} %broadcast_select_fusion), channel_id=1, source_target_pairs={{0,2},{1,3},{2,0},{3,1},{4,5},{5,4},{6,7},{7,6},{8,10},{9,11},{10,... | collective-permute-start | bytes 3145736 | tf_op jit(solution)/shard_map/ppermute | solution.py:35
  36.6 3.3 %copy-start.3 = (bf16[512,1024]{1,0:T(8,128)(2,1)S(1)}, bf16[512,1024]{1,0:T(8,128)(2,1)}, u32[]{:S(2)}) copy-start(bf16[512,1024]{1,0:T(8,128)(2,1)} %copy-done.2) | copy-start | bytes 3145732
  36.7 12.0 %collective-permute-start.8 = (f32[8,64,128]{2,1,0:T(8,128)S(1)}, f32[8,64,128]{2,1,0:T(8,128)S(1)}, u32[]{:S(2)}, u32[]{:S(2)}) collective-permute-start(f32[8,64,128]{2,1,0:T(8,128)S(1)} %convert_add_fusion.1), channel_id=1, source_target_pairs={{0,4},{4,0},{8,12},{12,8},{16,20},{20,16},{24,28},{28,24},{1,5},{5... | collective-permute-start | bytes 786440 | tf_op jit(solution)/shard_map/ppermute | solution.py:76
  42.9 5.3 %copy-start.5 = (bf16[512,1024]{0,1:T(8,128)(2,1)S(1)}, bf16[512,1024]{0,1:T(8,128)(2,1)}, u32[]{:S(2)}) copy-start(bf16[512,1024]{0,1:T(8,128)(2,1)} %copy.18) | copy-start | bytes 3145732
  48.1 1.5 %copy-start = (bf16[512,1024]{1,0:T(8,128)(2,1)}, bf16[512,1024]{1,0:T(8,128)(2,1)S(1)}, u32[]{:S(2)}) copy-start(bf16[512,1024]{1,0:T(8,128)(2,1)S(1)} %fusion.refs_2_.refs_3_) | copy-start | bytes 3145732
  48.6 1.6 %collective-permute-start.3 = (bf16[8,128,128]{2,1,0:T(8,128)(2,1)S(1)}, bf16[8,128,128]{2,1,0:T(8,128)(2,1)S(1)}, u32[]{:S(2)}, u32[]{:S(2)}) collective-permute-start(bf16[8,128,128]{2,1,0:T(8,128)(2,1)S(1)} %fusion.11), channel_id=1, source_target_pairs={{0,4},{4,0},{8,12},{12,8},{16,20},{20,16},{24,28},{28,24},{1,5},{5... | collective-permute-start | bytes 786440 | tf_op jit(solution)/shard_map/ppermute | solution.py:47
  50.3 14.8 %collective-permute-start.10 = (bf16[8,64,128]{2,1,0:T(8,128)(2,1)S(1)}, bf16[8,64,128]{2,1,0:T(8,128)(2,1)S(1)}, u32[]{:S(2)}, u32[]{:S(2)}) collective-permute-start(bf16[8,64,128]{2,1,0:T(8,128)(2,1)S(1)} %dynamic-slice_add_fusion.1), channel_id=1, source_target_pairs={{16,0},{20,4},{24,8},{28,12},{17,1},{21,5},{25,9},{29,13},{18,2},{... | collective-permute-start | bytes 393224 | tf_op jit(solution)/shard_map/ppermute | solution.py:63
  51.6 13.5 %collective-permute-start.11 = (bf16[8,64,128]{2,1,0:T(8,128)(2,1)S(1)}, bf16[8,64,128]{2,1,0:T(8,128)(2,1)S(1)}, u32[]{:S(2)}, u32[]{:S(2)}) collective-permute-start(bf16[8,64,128]{2,1,0:T(8,128)(2,1)S(1)} %dynamic-slice_add_fusion.1), channel_id=1, source_target_pairs={{24,0},{28,4},{25,1},{29,5},{26,2},{30,6},{27,3},{31,7}} | collective-permute-start | bytes 393224 | tf_op jit(solution)/shard_map/ppermute | solution.py:63
  52.9 12.2 %collective-permute-start.9 = (bf16[8,64,128]{2,1,0:T(8,128)(2,1)S(1)}, bf16[8,64,128]{2,1,0:T(8,128)(2,1)S(1)}, u32[]{:S(2)}, u32[]{:S(2)}) collective-permute-start(bf16[8,64,128]{2,1,0:T(8,128)(2,1)S(1)} %dynamic-slice_add_fusion.1), channel_id=1, source_target_pairs={{8,0},{12,4},{16,8},{20,12},{24,16},{28,20},{9,1},{13,5},{17,9},{2... | collective-permute-start | bytes 393224 | tf_op jit(solution)/shard_map/ppermute | solution.py:63
  65.2 1.6 %collective-permute-start.12 = (f32[8,64,128]{2,1,0:T(8,128)S(1)}, f32[8,64,128]{2,1,0:T(8,128)S(1)}, u32[]{:S(2)}, u32[]{:S(2)}) collective-permute-start(f32[8,64,128]{2,1,0:T(8,128)S(1)} %convert_add_fusion), channel_id=1, source_target_pairs={{0,4},{4,0},{8,12},{12,8},{16,20},{20,16},{24,28},{28,24},{1,5},{5... | collective-permute-start | bytes 786440 | tf_op jit(solution)/shard_map/ppermute | solution.py:76

commit v10 on v8

--- a/solution.py
+++ b/solution.py
@@ -11,7 +11,7 @@
     return [(a, a ^ bit) for a in range(n)]
 
 
-def project(og, out_weight, ctx_size, head_size):
+def project(og, out_weight, ctx_size, head_size, tied):
     cols = og.shape[1]
 
     def weight_cols(source, lo, width):
@@ -24,7 +24,8 @@
 
     if head_size != 4:
         full = lax.all_gather(og, "head", axis=1, tiled=True)
-        return mm(full, out_weight)
+        full, tied = lax.optimization_barrier((full, tied))
+        return mm(full, out_weight), tied
     me = lax.axis_index("head")
     core = lax.axis_index("ctx") % 2
     from_x = lax.ppermute(og, "head", flip_pairs(4, 1))
@@ -33,11 +34,12 @@
     devices = [(p, j) for p in range(ctx_size) for j in range(4)]
     route = [(p * 4 + j, p * 4 + (j ^ (2 if p % 2 == 0 else 1))) for p, j in devices]
     diag = lax.ppermute(relayed, ("ctx", "head"), route)
+    diag, tied = lax.optimization_barrier((diag, tied))
     acc = mm(og, weight_cols(me, 0, cols))
     acc = acc + mm(from_x, weight_cols(me ^ 1, 0, cols))
     acc = acc + mm(from_y, weight_cols(me ^ 2, 0, cols))
     acc = acc + mm(diag, weight_cols(me ^ 3, 0, cols))
-    return acc
+    return acc, tied
 
 
 def ctx_exclusive(state, ctx_size, reverse, cover=None):
@@ -210,8 +212,6 @@
         q_blocks = queries.reshape(shape)
         k_blocks = keys.reshape(shape)
         v_blocks = values.reshape(shape)
-        grad_heads = project(output_grad, out_weight, ctx_size, head_size)
-        grad_heads = grad_heads.astype(jnp.bfloat16)
         kv_blocks = jnp.einsum(
             "nshd,nshe->nhde", k_blocks, v_blocks,
             preferred_element_type=jnp.float32,
@@ -222,6 +222,8 @@
             kv_entry = kv_before[None]
         else:
             kv_entry = kv_before[None] + kv_running - kv_blocks
+        grad_heads, kv_entry = project(output_grad, out_weight, ctx_size, head_size, kv_entry)
+        grad_heads = grad_heads.astype(jnp.bfloat16)
         g_blocks = grad_heads.reshape(shape)
         qg_blocks = jnp.einsum(
             "nthd,nthe->nhde", q_blocks, g_blocks, preferred_element_type=jnp.float32

time: 73.1 us -> 72.7 us (level)
  waiting for transfers between devices: 12.3 us -> 14.3 us
  matrix products: 15 us -> 13.2 us
    ppermute x1, waiting for transfers between devices: 2.01 us -> 6.04 us  [project(): diag = lax.ppermute(relayed, ('ctx', 'head'), route)]
    ppermute x1, waiting for transfers between devices: 4.66 us -> 1.9 us  [project(): from_x = lax.ppermute(og, 'head', flip_pairs(4, 1))]
    dot_general x1, matrix products: 2.38 us -> 0.45 us  [shards(): jnp.einsum('nshd,nshe->nhde', k_blocks, v_blocks, preferred_element_type=...]
    convert_element_type x1, other arithmetic: 0.95 us -> 0.04 us  [ctx_exclusive(): sent = mine.astype(jnp.bfloat16)]
  transfers between devices with their start and end apart: 13 -> 13, of which waited for: 7 -> 7; matrix products, arithmetic and copies ran while one was open for 30% -> 22% of each run, Pallas kernels for 15% -> 15%
where the time goes in v10:
time: 72.7 us; the launch traced here: 72.2 us
  starting transfers between devices  21 us (29%)
  Pallas kernels  15.5 us (21%)
  waiting for transfers between devices  14.3 us (20%)
  matrix products  13.2 us (18%)
  other arithmetic  4.43 us (6%)
  local copies, waits for them, and re-layouts  2.84 us (4%)
  between operations  0.91 us (1%)
    ppermute x6, starting transfers between devices, ctx_exclusive(): others = others + lax.ppermute(sent, 'ctx', pairs(step)).astype(jnp.float32)  14.6 us
    dot_general x4, matrix products, mm(): lax.dot_general(a, b, (((1,), (1,)), ((), ())), preferred_element_type=jn...  12.3 us
    pallas_call x1, Pallas kernels, attention_part(): pl.pallas_call(lambda *refs: scores_kernel(scale, chunk, per_step, *refs)...  10.6 us
    ppermute x1, waiting for transfers between devices, project(): diag = lax.ppermute(relayed, ('ctx', 'head'), route)  6.04 us
    pallas_call x1, Pallas kernels, state_part(): pl.pallas_call(lambda *refs: state_kernel(scale, per_step, *refs), grid=(...  4.97 us
    ppermute x2, waiting for transfers between devices, ctx_exclusive(): lax.ppermute(rounded, 'ctx', flip_pairs(ctx_size, 1)).astype(jnp.float32)  3.03 us
    ppermute x1, starting transfers between devices, project(): from_x = lax.ppermute(og, 'head', flip_pairs(4, 1))  3 us
    ppermute x1, waiting for transfers between devices, project(): from_x = lax.ppermute(og, 'head', flip_pairs(4, 1))  1.9 us
  transfers between devices with their start and end apart: 13, of which 7 were waited for; matrix products, arithmetic and copies ran while one was open for 22% of the time, Pallas kernels for 15%

profile of v10, /device:TPU:0, one launch (start us, length us, event | category | flops | bytes accessed | tf_op | source)
XLA Modules:
  0.0 72.2 jit_solution(4874368115882770345)
XLA Ops:
  0.6 3.0 %collective-permute-start = (bf16[512,1024]{1,0:T(8,128)(2,1)}, bf16[512,1024]{1,0:T(8,128)(2,1)}, u32[]{:S(2)}, u32[]{:S(2)}) collective-permute-start(bf16[512,1024]{1,0:T(8,128)(2,1)} %param.8), channel_id=1, source_target_pairs={{0,1},{1,0},{2,3},{3,2},{4,5},{5,4},{6,7},{7,6},{8,9},{9,8},{10,11... | collective-permute-start | bytes 3145736 | tf_op jit(solution)/shard_map/ppermute | solution.py:31
  3.6 1.5 %collective-permute-start.1 = (bf16[512,1024]{1,0:T(8,128)(2,1)}, bf16[512,1024]{1,0:T(8,128)(2,1)}, u32[]{:S(2)}, u32[]{:S(2)}) collective-permute-start(bf16[512,1024]{1,0:T(8,128)(2,1)} %param.8), channel_id=1, source_target_pairs={{0,2},{1,3},{2,0},{3,1},{4,6},{5,7},{6,4},{7,5},{8,10},{9,11},{10,... | collective-permute-start | bytes 3145736 | tf_op jit(solution)/shard_map/ppermute | solution.py:32
  5.2 1.5 %copy.18 = bf16[512,1024]{0,1:T(8,128)(2,1)S(1)} copy(bf16[512,1024]{1,0:T(8,128)(2,1)} %refs_0_.3) | data formatting | bytes 2097152 | tf_op jit(solution)/shard_map/reshape
  7.2 1.5 %collective-permute-done.3 = bf16[8,128,128]{2,1,0:T(8,128)(2,1)S(1)} collective-permute-done((bf16[8,128,128]{2,1,0:T(8,128)(2,1)S(1)}, bf16[8,128,128]{2,1,0:T(8,128)(2,1)S(1)}, u32[]{:S(2)}, u32[]{:S(2)}) %collective-permute-start.3) | collective-permute-done | bytes 262176 | tf_op jit(solution)/shard_map/ppermute | solution.py:49
  8.8 4.3 %collective-permute-start.4 = (bf16[8,64,128]{2,1,0:T(8,128)(2,1)S(1)}, bf16[8,64,128]{2,1,0:T(8,128)(2,1)}, u32[]{:S(2)}, u32[]{:S(2)}) collective-permute-start(bf16[8,64,128]{2,1,0:T(8,128)(2,1)S(1)} %fusion.18), channel_id=1, source_target_pairs={{0,8},{4,12},{8,16},{12,20},{16,24},{20,28},{1,9},{5,13},{9,17},{1... | collective-permute-start | bytes 393224 | tf_op jit(solution)/shard_map/ppermute | solution.py:65
  13.1 4.5 %collective-permute-start.5 = (bf16[8,64,128]{2,1,0:T(8,128)(2,1)S(1)}, bf16[8,64,128]{2,1,0:T(8,128)(2,1)}, u32[]{:S(2)}, u32[]{:S(2)}) collective-permute-start(bf16[8,64,128]{2,1,0:T(8,128)(2,1)S(1)} %fusion.18), channel_id=1, source_target_pairs={{0,16},{4,20},{8,24},{12,28},{1,17},{5,21},{9,25},{13,29},{2,18},{... | collective-permute-start | bytes 393224 | tf_op jit(solution)/shard_map/ppermute | solution.py:65
  17.6 1.9 %collective-permute-start.6 = (bf16[8,64,128]{2,1,0:T(8,128)(2,1)S(1)}, bf16[8,64,128]{2,1,0:T(8,128)(2,1)}, u32[]{:S(2)}, u32[]{:S(2)}) collective-permute-start(bf16[8,64,128]{2,1,0:T(8,128)(2,1)S(1)} %fusion.18), channel_id=1, source_target_pairs={{0,24},{4,28},{1,25},{5,29},{2,26},{6,30},{3,27},{7,31}} | collective-permute-start | bytes 393224 | tf_op jit(solution)/shard_map/ppermute | solution.py:65
  19.5 3.1 %fusion.7 = f32[1024,512]{0,1:T(8,128)S(1)} fusion(bf16[512,1024]{1,0:T(8,128)(2,1)} %param.8, bf16[1024,4096]{1,0:T(8,128)(2,1)} %param.9, s32[]{:T(128)S(6)} %select_n.69), kind=kOutput, calls=%fused_computation.8 | convolution fusion | flops 1073741824 | bytes 5242884 | tf_op jit(solution)/shard_map/dot_general | solution.py:21
  22.7 1.3 %copy.19 = bf16[512,1024]{0,1:T(8,128)(2,1)} copy(bf16[512,1024]{1,0:T(8,128)(2,1)S(1)} %copy-done) | data formatting | bytes 2097152 | tf_op jit(solution)/shard_map/reshape.3
  25.2 1.9 %collective-permute-done = bf16[512,1024]{1,0:T(8,128)(2,1)} collective-permute-done((bf16[512,1024]{1,0:T(8,128)(2,1)}, bf16[512,1024]{1,0:T(8,128)(2,1)}, u32[]{:S(2)}, u32[]{:S(2)}) %collective-permute-start) | collective-permute-done | bytes 1048608 | tf_op jit(solution)/shard_map/ppermute | solution.py:31
  27.1 1.5 %collective-permute-done.1 = bf16[512,1024]{1,0:T(8,128)(2,1)} collective-permute-done((bf16[512,1024]{1,0:T(8,128)(2,1)}, bf16[512,1024]{1,0:T(8,128)(2,1)}, u32[]{:S(2)}, u32[]{:S(2)}) %collective-permute-start.1) | collective-permute-done | bytes 1048608 | tf_op jit(solution)/shard_map/ppermute | solution.py:32
  28.6 1.3 %broadcast_select_fusion = bf16[512,1024]{1,0:T(8,128)(2,1)S(1)} fusion(bf16[512,1024]{1,0:T(8,128)(2,1)} %collective-permute-done, bf16[512,1024]{1,0:T(8,128)(2,1)} %collective-permute-done.1, pred[]{:T(512)S(6)} %eq.8), kind=kLoop, calls=%fused_computation.17 | loop fusion | flops 524288 | bytes 3145729 | tf_op jit(solution)/shard_map/jit(_where)/select_n | solution.py:33
  29.9 1.6 %collective-permute-start.2 = (bf16[512,1024]{1,0:T(8,128)(2,1)S(1)}, bf16[512,1024]{1,0:T(8,128)(2,1)S(1)}, u32[]{:S(2)}, u32[]{:S(2)}) collective-permute-start(bf16[512,1024]{1,0:T(8,128)(2,1)S(1)} %broadcast_select_fusion), channel_id=1, source_target_pairs={{0,2},{1,3},{2,0},{3,1},{4,5},{5,4},{6,7},{7,6},{8,10},{9,11},{10,... | collective-permute-start | bytes 3145736 | tf_op jit(solution)/shard_map/ppermute | solution.py:36
  32.4 3.1 %fusion.3 = f32[1024,512]{0,1:T(8,128)S(1)} fusion(bf16[512,1024]{1,0:T(8,128)(2,1)} %collective-permute-done.1, bf16[1024,4096]{1,0:T(8,128)(2,1)} %param.9, s32[]{:T(128)S(6)} %select_n.71), kind=kOutput, calls=%fused_computation.4 | convolution fusion | flops 1073741824 | bytes 5242884 | tf_op jit(solution)/shard_map/dot_general | solution.py:21
  35.6 3.2 %fusion.5 = f32[1024,512]{0,1:T(8,128)S(1)} fusion(bf16[512,1024]{1,0:T(8,128)(2,1)} %collective-permute-done, bf16[1024,4096]{1,0:T(8,128)(2,1)} %param.9, s32[]{:T(128)S(6)} %select_n.70), kind=kOutput, calls=%fused_computation.6 | convolution fusion | flops 1073741824 | bytes 5242884 | tf_op jit(solution)/shard_map/dot_general | solution.py:21
  38.7 6.0 %collective-permute-done.2 = bf16[512,1024]{1,0:T(8,128)(2,1)S(1)} collective-permute-done((bf16[512,1024]{1,0:T(8,128)(2,1)S(1)}, bf16[512,1024]{1,0:T(8,128)(2,1)S(1)}, u32[]{:S(2)}, u32[]{:S(2)}) %collective-permute-start.2) | collective-permute-done | bytes 1048608 | tf_op jit(solution)/shard_map/ppermute | solution.py:36
  44.8 2.9 %fusion.refs_3_ = bf16[512,1024]{1,0:T(8,128)(2,1)S(1)} fusion(f32[1024,512]{0,1:T(8,128)S(1)} %fusion.3, f32[1024,512]{0,1:T(8,128)S(1)} %fusion.7, f32[1024,512]{0,1:T(8,128)S(1)} %fusion.5, bf16[512,1024]{1,0:T(8,128)(2,1)S(1)} %collective-permute-done.2, bf16[1024,4096]{1,0:T(8,128)(2,1)} %param.9, s32[]{:T(128)S(6)} %select_n.81), kind=kOutput, calls=%fused_computation.1 | convolution fusion | flops 1075838976 | bytes 10485764 | tf_op jit(solution)/shard_map/dot_general | solution.py:21
  48.2 1.5 %collective-permute-done.8 = bf16[8,128,128]{2,1,0:T(8,128)(2,1)S(1)} collective-permute-done((bf16[8,128,128]{2,1,0:T(8,128)(2,1)S(1)}, bf16[8,128,128]{2,1,0:T(8,128)(2,1)S(1)}, u32[]{:S(2)}, u32[]{:S(2)}) %collective-permute-start.8) | collective-permute-done | bytes 262176 | tf_op jit(solution)/shard_map/ppermute | solution.py:49
  49.9 1.3 %collective-permute-start.10 = (bf16[8,64,128]{2,1,0:T(8,128)(2,1)S(1)}, bf16[8,64,128]{2,1,0:T(8,128)(2,1)S(1)}, u32[]{:S(2)}, u32[]{:S(2)}) collective-permute-start(bf16[8,64,128]{2,1,0:T(8,128)(2,1)S(1)} %dynamic-slice_add_fusion), channel_id=1, source_target_pairs={{16,0},{20,4},{24,8},{28,12},{17,1},{21,5},{25,9},{29,13},{18,2},{... | collective-permute-start | bytes 393224 | tf_op jit(solution)/shard_map/ppermute | solution.py:65
  51.2 1.3 %collective-permute-start.11 = (bf16[8,64,128]{2,1,0:T(8,128)(2,1)S(1)}, bf16[8,64,128]{2,1,0:T(8,128)(2,1)S(1)}, u32[]{:S(2)}, u32[]{:S(2)}) collective-permute-start(bf16[8,64,128]{2,1,0:T(8,128)(2,1)S(1)} %dynamic-slice_add_fusion), channel_id=1, source_target_pairs={{24,0},{28,4},{25,1},{29,5},{26,2},{30,6},{27,3},{31,7}} | collective-permute-start | bytes 393224 | tf_op jit(solution)/shard_map/ppermute | solution.py:65
  52.5 1.3 %collective-permute-start.9 = (bf16[8,64,128]{2,1,0:T(8,128)(2,1)S(1)}, bf16[8,64,128]{2,1,0:T(8,128)(2,1)S(1)}, u32[]{:S(2)}, u32[]{:S(2)}) collective-permute-start(bf16[8,64,128]{2,1,0:T(8,128)(2,1)S(1)} %dynamic-slice_add_fusion), channel_id=1, source_target_pairs={{8,0},{12,4},{16,8},{20,12},{24,16},{28,20},{9,1},{13,5},{17,9},{2... | collective-permute-start | bytes 393224 | tf_op jit(solution)/shard_map/ppermute | solution.py:65
  53.8 10.6 %attention_part.1 = (bf16[512,1024]{1,0:T(8,128)(2,1)}, bf16[512,1024]{1,0:T(8,128)(2,1)}, bf16[512,1024]{1,0:T(8,128)(2,1)}) custom-call(bf16[512,1024]{1,0:T(8,128)(2,1)} %refs_0_.2, bf16[512,1024]{1,0:T(8,128)(2,1)} %refs_0_.3, bf16[512,1024]{1,0:T(8,128)(2,1)} %refs_1_.3, bf16[512,1024]{1,0:T(8,128)(2,1)} %copy-done.3, f32[1,8,128,128]{3,2,1,0:T(8,128)} %fusion.16.refs_4_), custom_call_target="tpu_custom_call" | custom-call | flops 3221225472 | bytes 7340032 | tf_op jit(solution)/shard_map/attention_part/pallas_call | solution.py:167
  64.8 1.5 %collective-permute-done.12 = f32[8,64,128]{2,1,0:T(8,128)S(1)} collective-permute-done((f32[8,64,128]{2,1,0:T(8,128)S(1)}, f32[8,64,128]{2,1,0:T(8,128)S(1)}, u32[]{:S(2)}, u32[]{:S(2)}) %collective-permute-start.12) | collective-permute-done | bytes 262176 | tf_op jit(solution)/shard_map/ppermute | solution.py:78
  67.2 5.0 %state_part.1 = (bf16[512,1024]{1,0:T(8,128)(2,1)}, bf16[512,1024]{1,0:T(8,128)(2,1)}) custom-call(bf16[512,1024]{1,0:T(8,128)(2,1)} %refs_0_.3, bf16[512,1024]{1,0:T(8,128)(2,1)} %refs_1_.3, f32[1,8,128,128]{3,2,1,0:T(8,128)} %fusion.17.refs_2_, bf16[512,1024]{1,0:T(8,128)(2,1)} %get-tuple-element.27.refs_3_, bf16[512,1024]{1,0:T(8,128)(2,1)} %get-tuple-element.28.refs_4_), custom_call_target="tpu_custom_call" | custom-call | flops 536870912 | bytes 6291456 | tf_op jit(solution)/shard_map/state_part/pallas_call | solution.py:188
  (31 shorter events, 4.6 us)
Async XLA Ops:
  0.6 6.0 %copy-start.2 = (bf16[512,1024]{1,0:T(8,128)(2,1)S(1)}, bf16[512,1024]{1,0:T(8,128)(2,1)}, u32[]{:S(2)}) copy-start(bf16[512,1024]{1,0:T(8,128)(2,1)} %refs_1_.3) | copy-start | bytes 3145732
  0.6 26.5 %collective-permute-start = (bf16[512,1024]{1,0:T(8,128)(2,1)}, bf16[512,1024]{1,0:T(8,128)(2,1)}, u32[]{:S(2)}, u32[]{:S(2)}) collective-permute-start(bf16[512,1024]{1,0:T(8,128)(2,1)} %param.8), channel_id=1, source_target_pairs={{0,1},{1,0},{2,3},{3,2},{4,5},{5,4},{6,7},{7,6},{8,9},{9,8},{10,11... | collective-permute-start | bytes 3145736 | tf_op jit(solution)/shard_map/ppermute | solution.py:31
  3.6 24.9 %collective-permute-start.1 = (bf16[512,1024]{1,0:T(8,128)(2,1)}, bf16[512,1024]{1,0:T(8,128)(2,1)}, u32[]{:S(2)}, u32[]{:S(2)}) collective-permute-start(bf16[512,1024]{1,0:T(8,128)(2,1)} %param.8), channel_id=1, source_target_pairs={{0,2},{1,3},{2,0},{3,1},{4,6},{5,7},{6,4},{7,5},{8,10},{9,11},{10,... | collective-permute-start | bytes 3145736 | tf_op jit(solution)/shard_map/ppermute | solution.py:32
  7.1 1.6 %collective-permute-start.3 = (bf16[8,128,128]{2,1,0:T(8,128)(2,1)S(1)}, bf16[8,128,128]{2,1,0:T(8,128)(2,1)S(1)}, u32[]{:S(2)}, u32[]{:S(2)}) collective-permute-start(bf16[8,128,128]{2,1,0:T(8,128)(2,1)S(1)} %convolution_convert_fusion.1), channel_id=1, source_target_pairs={{0,4},{4,0},{8,12},{12,8},{16,20},{20,16},{24,28},{28,24},{1,5},{5... | collective-permute-start | bytes 786440 | tf_op jit(solution)/shard_map/ppermute | solution.py:49
  8.8 13.9 %copy-start = (bf16[512,1024]{1,0:T(8,128)(2,1)S(1)}, bf16[512,1024]{1,0:T(8,128)(2,1)}, u32[]{:S(2)}) copy-start(bf16[512,1024]{1,0:T(8,128)(2,1)} %refs_0_.2) | copy-start | bytes 3145732
  8.8 15.2 %collective-permute-start.4 = (bf16[8,64,128]{2,1,0:T(8,128)(2,1)S(1)}, bf16[8,64,128]{2,1,0:T(8,128)(2,1)}, u32[]{:S(2)}, u32[]{:S(2)}) collective-permute-start(bf16[8,64,128]{2,1,0:T(8,128)(2,1)S(1)} %fusion.18), channel_id=1, source_target_pairs={{0,8},{4,12},{8,16},{12,20},{16,24},{20,28},{1,9},{5,13},{9,17},{1... | collective-permute-start | bytes 393224 | tf_op jit(solution)/shard_map/ppermute | solution.py:65
  13.1 10.9 %collective-permute-start.5 = (bf16[8,64,128]{2,1,0:T(8,128)(2,1)S(1)}, bf16[8,64,128]{2,1,0:T(8,128)(2,1)}, u32[]{:S(2)}, u32[]{:S(2)}) collective-permute-start(bf16[8,64,128]{2,1,0:T(8,128)(2,1)S(1)} %fusion.18), channel_id=1, source_target_pairs={{0,16},{4,20},{8,24},{12,28},{1,17},{5,21},{9,25},{13,29},{2,18},{... | collective-permute-start | bytes 393224 | tf_op jit(solution)/shard_map/ppermute | solution.py:65
  17.6 6.5 %collective-permute-start.6 = (bf16[8,64,128]{2,1,0:T(8,128)(2,1)S(1)}, bf16[8,64,128]{2,1,0:T(8,128)(2,1)}, u32[]{:S(2)}, u32[]{:S(2)}) collective-permute-start(bf16[8,64,128]{2,1,0:T(8,128)(2,1)S(1)} %fusion.18), channel_id=1, source_target_pairs={{0,24},{4,28},{1,25},{5,29},{2,26},{6,30},{3,27},{7,31}} | collective-permute-start | bytes 393224 | tf_op jit(solution)/shard_map/ppermute | solution.py:65
  25.1 6.4 %collective-permute-start.7 = (f32[8,64,128]{2,1,0:T(8,128)S(1)}, f32[8,64,128]{2,1,0:T(8,128)S(1)}, u32[]{:S(2)}, u32[]{:S(2)}) collective-permute-start(f32[8,64,128]{2,1,0:T(8,128)S(1)} %convert_add_fusion.1), channel_id=1, source_target_pairs={{0,4},{4,0},{8,12},{12,8},{16,20},{20,16},{24,28},{28,24},{1,5},{5... | collective-permute-start | bytes 786440 | tf_op jit(solution)/shard_map/ppermute | solution.py:78
  29.9 14.9 %collective-permute-start.2 = (bf16[512,1024]{1,0:T(8,128)(2,1)S(1)}, bf16[512,1024]{1,0:T(8,128)(2,1)S(1)}, u32[]{:S(2)}, u32[]{:S(2)}) collective-permute-start(bf16[512,1024]{1,0:T(8,128)(2,1)S(1)} %broadcast_select_fusion), channel_id=1, source_target_pairs={{0,2},{1,3},{2,0},{3,1},{4,5},{5,4},{6,7},{7,6},{8,10},{9,11},{10,... | collective-permute-start | bytes 3145736 | tf_op jit(solution)/shard_map/ppermute | solution.py:36
  38.7 9.0 %copy-start.1 = (bf16[512,1024]{0,1:T(8,128)(2,1)S(1)}, bf16[512,1024]{0,1:T(8,128)(2,1)}, u32[]{:S(2)}) copy-start(bf16[512,1024]{0,1:T(8,128)(2,1)} %copy.19) | copy-start | bytes 3145732
  47.7 6.1 %copy-start.3 = (bf16[512,1024]{1,0:T(8,128)(2,1)}, bf16[512,1024]{1,0:T(8,128)(2,1)S(1)}, u32[]{:S(2)}) copy-start(bf16[512,1024]{1,0:T(8,128)(2,1)S(1)} %fusion.refs_3_) | copy-start | bytes 3145732
  48.2 1.6 %collective-permute-start.8 = (bf16[8,128,128]{2,1,0:T(8,128)(2,1)S(1)}, bf16[8,128,128]{2,1,0:T(8,128)(2,1)S(1)}, u32[]{:S(2)}, u32[]{:S(2)}) collective-permute-start(bf16[8,128,128]{2,1,0:T(8,128)(2,1)S(1)} %fusion.11), channel_id=1, source_target_pairs={{0,4},{4,0},{8,12},{12,8},{16,20},{20,16},{24,28},{28,24},{1,5},{5... | collective-permute-start | bytes 786440 | tf_op jit(solution)/shard_map/ppermute | solution.py:49
  49.9 14.8 %collective-permute-start.10 = (bf16[8,64,128]{2,1,0:T(8,128)(2,1)S(1)}, bf16[8,64,128]{2,1,0:T(8,128)(2,1)S(1)}, u32[]{:S(2)}, u32[]{:S(2)}) collective-permute-start(bf16[8,64,128]{2,1,0:T(8,128)(2,1)S(1)} %dynamic-slice_add_fusion), channel_id=1, source_target_pairs={{16,0},{20,4},{24,8},{28,12},{17,1},{21,5},{25,9},{29,13},{18,2},{... | collective-permute-start | bytes 393224 | tf_op jit(solution)/shard_map/ppermute | solution.py:65
  51.2 13.5 %collective-permute-start.11 = (bf16[8,64,128]{2,1,0:T(8,128)(2,1)S(1)}, bf16[8,64,128]{2,1,0:T(8,128)(2,1)S(1)}, u32[]{:S(2)}, u32[]{:S(2)}) collective-permute-start(bf16[8,64,128]{2,1,0:T(8,128)(2,1)S(1)} %dynamic-slice_add_fusion), channel_id=1, source_target_pairs={{24,0},{28,4},{25,1},{29,5},{26,2},{30,6},{27,3},{31,7}} | collective-permute-start | bytes 393224 | tf_op jit(solution)/shard_map/ppermute | solution.py:65
  52.5 12.2 %collective-permute-start.9 = (bf16[8,64,128]{2,1,0:T(8,128)(2,1)S(1)}, bf16[8,64,128]{2,1,0:T(8,128)(2,1)S(1)}, u32[]{:S(2)}, u32[]{:S(2)}) collective-permute-start(bf16[8,64,128]{2,1,0:T(8,128)(2,1)S(1)} %dynamic-slice_add_fusion), channel_id=1, source_target_pairs={{8,0},{12,4},{16,8},{20,12},{24,16},{28,20},{9,1},{13,5},{17,9},{2... | collective-permute-start | bytes 393224 | tf_op jit(solution)/shard_map/ppermute | solution.py:65
  64.7 1.6 %collective-permute-start.12 = (f32[8,64,128]{2,1,0:T(8,128)S(1)}, f32[8,64,128]{2,1,0:T(8,128)S(1)}, u32[]{:S(2)}, u32[]{:S(2)}) collective-permute-start(f32[8,64,128]{2,1,0:T(8,128)S(1)} %convert_add_fusion), channel_id=1, source_target_pairs={{0,4},{4,0},{8,12},{12,8},{16,20},{20,16},{24,28},{28,24},{1,5},{5... | collective-permute-start | bytes 786440 | tf_op jit(solution)/shard_map/ppermute | solution.py:78

commit v11 on v10

--- a/solution.py
+++ b/solution.py
@@ -28,16 +28,18 @@
         return mm(full, out_weight), tied
     me = lax.axis_index("head")
     core = lax.axis_index("ctx") % 2
-    from_x = lax.ppermute(og, "head", flip_pairs(4, 1))
-    from_y = lax.ppermute(og, "head", flip_pairs(4, 2))
-    relayed = jnp.where(core == 0, from_x, from_y)
     devices = [(p, j) for p in range(ctx_size) for j in range(4)]
-    route = [(p * 4 + j, p * 4 + (j ^ (2 if p % 2 == 0 else 1))) for p, j in devices]
-    diag = lax.ppermute(relayed, ("ctx", "head"), route)
+
+    def route(core_0_bit, core_1_bit):
+        return [(p * 4 + j, p * 4 + (j ^ (core_0_bit if p % 2 == 0 else core_1_bit))) for p, j in devices]
+
+    to_relay = lax.ppermute(og, ("ctx", "head"), route(1, 2))
+    kept = lax.ppermute(og, ("ctx", "head"), route(2, 1))
+    diag = lax.ppermute(to_relay, ("ctx", "head"), route(2, 1))
     diag, tied = lax.optimization_barrier((diag, tied))
     acc = mm(og, weight_cols(me, 0, cols))
-    acc = acc + mm(from_x, weight_cols(me ^ 1, 0, cols))
-    acc = acc + mm(from_y, weight_cols(me ^ 2, 0, cols))
+    acc = acc + mm(to_relay, weight_cols(me ^ (1 + core), 0, cols))
+    acc = acc + mm(kept, weight_cols(me ^ (2 - core), 0, cols))
     acc = acc + mm(diag, weight_cols(me ^ 3, 0, cols))
     return acc, tied
 
@@ -163,7 +165,7 @@
     st = pl.BlockSpec((1, per_step, DH, DH), lambda n, h: (n, h, 0, 0))
     rows, width = q.shape
     out = jax.ShapeDtypeStruct((rows, width), jnp.bfloat16)
-    chunk = 256 if block_len % 256 == 0 else block_len
+    chunk = block_len
     return pl.pallas_call(
         lambda *refs: scores_kernel(scale, chunk, per_step, *refs),
         grid=(blocks, heads // per_step),

time: 72.7 us -> 70.2 us (0.966)
  waiting for transfers between devices: 14.3 us -> 16.6 us
  other arithmetic: 4.43 us -> 2.96 us
  starting transfers between devices: 21 us -> 19.7 us
    ppermute x6, waiting for transfers between devices: 0.34 us -> 3.75 us  [ctx_exclusive(): others = others + lax.ppermute(sent, 'ctx', pairs(step)).astype(jnp.float32)]
    ppermute x2, waiting for transfers between devices: 3.03 us -> 1.52 us  [ctx_exclusive(): lax.ppermute(rounded, 'ctx', flip_pairs(ctx_size, 1)).astype(jnp.float32)]
    dot_general x4, matrix products: 12.3 us -> 10.9 us  [mm(): lax.dot_general(a, b, (((1,), (1,)), ((), ())), preferred_element_type=jn...]
    select_n x1 -> x0, other arithmetic: 1.34 us -> none  [project(): relayed = jnp.where(core == 0, from_x, from_y)]
    ppermute x6, starting transfers between devices: 14.6 us -> 13.4 us  [ctx_exclusive(): others = others + lax.ppermute(sent, 'ctx', pairs(step)).astype(jnp.float32)]
    add x2, other arithmetic: 1.13 us -> 0.09 us  [ctx_exclusive(): others = others + lax.ppermute(sent, 'ctx', pairs(step)).astype(jnp.float32)]
    convert_element_type x1, other arithmetic: 0.04 us -> 0.95 us  [ctx_exclusive(): sent = mine.astype(jnp.bfloat16)]
    another operation x1, local copies, waits for them, and re-layouts: 1.32 us -> 0.53 us
  transfers between devices with their start and end apart: 13 -> 13, of which waited for: 7 -> 7; matrix products, arithmetic and copies ran while one was open for 22% -> 17% of each run, Pallas kernels for 15% -> 14%
where the time goes in v11:
time: 70.2 us; the launch traced here: 69.8 us
  starting transfers between devices  19.7 us (28%)
  waiting for transfers between devices  16.6 us (24%)
  Pallas kernels  15 us (21%)
  matrix products  12.5 us (18%)
  other arithmetic  2.96 us (4%)
  local copies, waits for them, and re-layouts  2.15 us (3%)
  between operations  0.89 us (1%)
    ppermute x6, starting transfers between devices, ctx_exclusive(): others = others + lax.ppermute(sent, 'ctx', pairs(step)).astype(jnp.float32)  13.4 us
    dot_general x4, matrix products, mm(): lax.dot_general(a, b, (((1,), (1,)), ((), ())), preferred_element_type=jn...  10.9 us
    pallas_call x1, Pallas kernels, attention_part(): pl.pallas_call(lambda *refs: scores_kernel(scale, chunk, per_step, *refs)...  10 us
    ppermute x1, waiting for transfers between devices, project(): diag = lax.ppermute(to_relay, ('ctx', 'head'), route(2, 1))  8.61 us
    pallas_call x1, Pallas kernels, state_part(): pl.pallas_call(lambda *refs: state_kernel(scale, per_step, *refs), grid=(...  4.96 us
    ppermute x6, waiting for transfers between devices, ctx_exclusive(): others = others + lax.ppermute(sent, 'ctx', pairs(step)).astype(jnp.float32)  3.75 us
    ppermute x1, starting transfers between devices, project(): to_relay = lax.ppermute(og, ('ctx', 'head'), route(1, 2))  2.49 us
    ppermute x1, starting transfers between devices, project(): diag = lax.ppermute(to_relay, ('ctx', 'head'), route(2, 1))  1.6 us
  transfers between devices with their start and end apart: 13, of which 7 were waited for; matrix products, arithmetic and copies ran while one was open for 17% of the time, Pallas kernels for 14%

profile of v11, /device:TPU:0, one launch (start us, length us, event | category | flops | bytes accessed | tf_op | source)
XLA Modules:
  0.0 69.8 jit_solution(10792933478529447611)
XLA Ops:
  0.6 1.6 %copy.18 = bf16[512,1024]{0,1:T(8,128)(2,1)S(1)} copy(bf16[512,1024]{1,0:T(8,128)(2,1)} %refs_0_.3) | data formatting | bytes 2097152 | tf_op jit(solution)/shard_map/reshape
  2.3 1.2 %convolution_convert_fusion.1 = bf16[8,128,128]{2,1,0:T(8,128)(2,1)} fusion(bf16[512,8,128]{0,2,1:T(8,128)(2,1)S(1)} %bitcast.33, bf16[512,1024]{1,0:T(8,128)(2,1)S(1)} %copy-done.1), kind=kOutput, calls=%fused_computation.11 | convolution fusion | flops 134348800 | bytes 2359296 | tf_op jit(solution)/shard_map/nshd,nshe->nhde/dot_general | solution.py:217
  3.9 2.5 %collective-permute-start = (bf16[512,1024]{1,0:T(8,128)(2,1)}, bf16[512,1024]{1,0:T(8,128)(2,1)}, u32[]{:S(2)}, u32[]{:S(2)}) collective-permute-start(bf16[512,1024]{1,0:T(8,128)(2,1)} %param.8), channel_id=1, source_target_pairs={{0,1},{1,0},{2,3},{3,2},{4,6},{5,7},{6,4},{7,5},{8,9},{9,8},{10,11... | collective-permute-start | bytes 3145736 | tf_op jit(solution)/shard_map/ppermute | solution.py:36
  6.4 1.0 %fusion.18 = bf16[8,64,128]{2,1,0:T(8,128)(2,1)S(1)} fusion(f32[8,128,128]{2,1,0:T(8,128)S(1)} %convert_element_type.50, s32[]{:T(128)S(6)} %select_n.66, bf16[8,128,128]{2,1,0:T(8,128)(2,1)} %convolution_convert_fusion.1), kind=kLoop, calls=%fused_computation.23 | loop fusion | flops 196608 | bytes 524292 | tf_op jit(solution)/shard_map/convert_element_type | solution.py:65
  7.4 3.7 %collective-permute-start.4 = (bf16[8,64,128]{2,1,0:T(8,128)(2,1)S(1)}, bf16[8,64,128]{2,1,0:T(8,128)(2,1)S(1)}, u32[]{:S(2)}, u32[]{:S(2)}) collective-permute-start(bf16[8,64,128]{2,1,0:T(8,128)(2,1)S(1)} %fusion.18), channel_id=1, source_target_pairs={{0,8},{4,12},{8,16},{12,20},{16,24},{20,28},{1,9},{5,13},{9,17},{1... | collective-permute-start | bytes 393224 | tf_op jit(solution)/shard_map/ppermute | solution.py:67
  11.1 4.5 %collective-permute-start.5 = (bf16[8,64,128]{2,1,0:T(8,128)(2,1)S(1)}, bf16[8,64,128]{2,1,0:T(8,128)(2,1)S(1)}, u32[]{:S(2)}, u32[]{:S(2)}) collective-permute-start(bf16[8,64,128]{2,1,0:T(8,128)(2,1)S(1)} %fusion.18), channel_id=1, source_target_pairs={{0,16},{4,20},{8,24},{12,28},{1,17},{5,21},{9,25},{13,29},{2,18},{... | collective-permute-start | bytes 393224 | tf_op jit(solution)/shard_map/ppermute | solution.py:67
  15.6 1.3 %collective-permute-start.6 = (bf16[8,64,128]{2,1,0:T(8,128)(2,1)S(1)}, bf16[8,64,128]{2,1,0:T(8,128)(2,1)S(1)}, u32[]{:S(2)}, u32[]{:S(2)}) collective-permute-start(bf16[8,64,128]{2,1,0:T(8,128)(2,1)S(1)} %fusion.18), channel_id=1, source_target_pairs={{0,24},{4,28},{1,25},{5,29},{2,26},{6,30},{3,27},{7,31}} | collective-permute-start | bytes 393224 | tf_op jit(solution)/shard_map/ppermute | solution.py:67
  16.9 1.6 %collective-permute-start.1 = (bf16[512,1024]{1,0:T(8,128)(2,1)}, bf16[512,1024]{1,0:T(8,128)(2,1)}, u32[]{:S(2)}, u32[]{:S(2)}) collective-permute-start(bf16[512,1024]{1,0:T(8,128)(2,1)} %param.8), channel_id=1, source_target_pairs={{0,2},{1,3},{2,0},{3,1},{4,5},{5,4},{6,7},{7,6},{8,10},{9,11},{10,... | collective-permute-start | bytes 3145736 | tf_op jit(solution)/shard_map/ppermute | solution.py:37
  19.5 1.7 %collective-permute-done.6 = bf16[8,64,128]{2,1,0:T(8,128)(2,1)S(1)} collective-permute-done((bf16[8,64,128]{2,1,0:T(8,128)(2,1)S(1)}, bf16[8,64,128]{2,1,0:T(8,128)(2,1)S(1)}, u32[]{:S(2)}, u32[]{:S(2)}) %collective-permute-start.6) | collective-permute-done | bytes 131104 | tf_op jit(solution)/shard_map/ppermute | solution.py:67
  21.3 3.3 %fusion.7 = f32[1024,512]{0,1:T(8,128)S(1)} fusion(bf16[512,1024]{1,0:T(8,128)(2,1)} %param.8, bf16[1024,4096]{1,0:T(8,128)(2,1)} %param.9, s32[]{:T(128)S(6)} %select_n.61), kind=kOutput, calls=%fused_computation.8 | convolution fusion | flops 1073741824 | bytes 5242884 | tf_op jit(solution)/shard_map/dot_general | solution.py:21
  24.7 1.6 %collective-permute-start.2 = (bf16[512,1024]{1,0:T(8,128)(2,1)}, bf16[512,1024]{1,0:T(8,128)(2,1)S(1)}, u32[]{:S(2)}, u32[]{:S(2)}) collective-permute-start(bf16[512,1024]{1,0:T(8,128)(2,1)} %collective-permute-done), channel_id=1, source_target_pairs={{0,2},{1,3},{2,0},{3,1},{4,5},{5,4},{6,7},{7,6},{8,10},{9,11},{10,... | collective-permute-start | bytes 3145736 | tf_op jit(solution)/shard_map/ppermute | solution.py:38
  27.2 3.7 %fusion.5 = f32[1024,512]{0,1:T(8,128)S(1)} fusion(bf16[512,1024]{1,0:T(8,128)(2,1)} %collective-permute-done, bf16[1024,4096]{1,0:T(8,128)(2,1)} %param.9, s32[]{:T(128)S(6)} %select_n.63), kind=kOutput, calls=%fused_computation.6 | convolution fusion | flops 1073741824 | bytes 5242884 | tf_op jit(solution)/shard_map/dot_general | solution.py:21
  30.9 1.2 %collective-permute-done.1 = bf16[512,1024]{1,0:T(8,128)(2,1)} collective-permute-done((bf16[512,1024]{1,0:T(8,128)(2,1)}, bf16[512,1024]{1,0:T(8,128)(2,1)}, u32[]{:S(2)}, u32[]{:S(2)}) %collective-permute-start.1) | collective-permute-done | bytes 1048608 | tf_op jit(solution)/shard_map/ppermute | solution.py:37
  32.1 2.5 %fusion.3 = f32[1024,512]{0,1:T(8,128)S(1)} fusion(bf16[512,1024]{1,0:T(8,128)(2,1)} %collective-permute-done.1, bf16[1024,4096]{1,0:T(8,128)(2,1)S(1)} %bitcast.35, s32[]{:T(128)S(6)} %select_n.64), kind=kOutput, calls=%fused_computation.4 | convolution fusion | flops 1073741824 | bytes 5242884 | tf_op jit(solution)/shard_map/dot_general | solution.py:21
  34.6 8.6 %collective-permute-done.2 = bf16[512,1024]{1,0:T(8,128)(2,1)S(1)} collective-permute-done((bf16[512,1024]{1,0:T(8,128)(2,1)}, bf16[512,1024]{1,0:T(8,128)(2,1)S(1)}, u32[]{:S(2)}, u32[]{:S(2)}) %collective-permute-start.2) | collective-permute-done | bytes 1048608 | tf_op jit(solution)/shard_map/ppermute | solution.py:38
  43.2 1.3 %fusion.refs_3_ = bf16[512,1024]{1,0:T(8,128)(2,1)S(1)} fusion(f32[1024,512]{0,1:T(8,128)S(1)} %fusion.3, f32[1024,512]{0,1:T(8,128)S(1)} %fusion.7, f32[1024,512]{0,1:T(8,128)S(1)} %fusion.5, bf16[512,1024]{1,0:T(8,128)(2,1)S(1)} %collective-permute-done.2, bf16[1024,4096]{1,0:T(8,128)(2,1)S(1)} %bitcast.35, s32[]{:T(128)S(6)} %select_n.71), kind=kOutput, calls=%fused_computation.1 | convolution fusion | flops 1075838976 | bytes 10485764 | tf_op jit(solution)/shard_map/dot_general | solution.py:21
  45.1 1.5 %collective-permute-done.8 = bf16[8,128,128]{2,1,0:T(8,128)(2,1)S(1)} collective-permute-done((bf16[8,128,128]{2,1,0:T(8,128)(2,1)S(1)}, bf16[8,128,128]{2,1,0:T(8,128)(2,1)S(1)}, u32[]{:S(2)}, u32[]{:S(2)}) %collective-permute-start.8) | collective-permute-done | bytes 262176 | tf_op jit(solution)/shard_map/ppermute | solution.py:51
  46.7 1.3 %collective-permute-start.10 = (bf16[8,64,128]{2,1,0:T(8,128)(2,1)S(1)}, bf16[8,64,128]{2,1,0:T(8,128)(2,1)S(1)}, u32[]{:S(2)}, u32[]{:S(2)}) collective-permute-start(bf16[8,64,128]{2,1,0:T(8,128)(2,1)S(1)} %dynamic-slice_add_fusion), channel_id=1, source_target_pairs={{16,0},{20,4},{24,8},{28,12},{17,1},{21,5},{25,9},{29,13},{18,2},{... | collective-permute-start | bytes 393224 | tf_op jit(solution)/shard_map/ppermute | solution.py:67
  48.0 1.3 %collective-permute-start.11 = (bf16[8,64,128]{2,1,0:T(8,128)(2,1)S(1)}, bf16[8,64,128]{2,1,0:T(8,128)(2,1)S(1)}, u32[]{:S(2)}, u32[]{:S(2)}) collective-permute-start(bf16[8,64,128]{2,1,0:T(8,128)(2,1)S(1)} %dynamic-slice_add_fusion), channel_id=1, source_target_pairs={{24,0},{28,4},{25,1},{29,5},{26,2},{30,6},{27,3},{31,7}} | collective-permute-start | bytes 393224 | tf_op jit(solution)/shard_map/ppermute | solution.py:67
  49.3 1.3 %collective-permute-start.9 = (bf16[8,64,128]{2,1,0:T(8,128)(2,1)S(1)}, bf16[8,64,128]{2,1,0:T(8,128)(2,1)S(1)}, u32[]{:S(2)}, u32[]{:S(2)}) collective-permute-start(bf16[8,64,128]{2,1,0:T(8,128)(2,1)S(1)} %dynamic-slice_add_fusion), channel_id=1, source_target_pairs={{8,0},{12,4},{16,8},{20,12},{24,16},{28,20},{9,1},{13,5},{17,9},{2... | collective-permute-start | bytes 393224 | tf_op jit(solution)/shard_map/ppermute | solution.py:67
  50.6 10.0 %attention_part.1 = (bf16[512,1024]{1,0:T(8,128)(2,1)}, bf16[512,1024]{1,0:T(8,128)(2,1)}, bf16[512,1024]{1,0:T(8,128)(2,1)}) custom-call(bf16[512,1024]{1,0:T(8,128)(2,1)} %refs_0_.2, bf16[512,1024]{1,0:T(8,128)(2,1)} %refs_0_.3, bf16[512,1024]{1,0:T(8,128)(2,1)} %refs_1_.3, bf16[512,1024]{1,0:T(8,128)(2,1)} %copy-done.2, f32[1,8,128,128]{3,2,1,0:T(8,128)} %fusion.16.refs_4_), custom_call_target="tpu_custom_call" | custom-call | flops 3221225472 | bytes 7340032 | tf_op jit(solution)/shard_map/attention_part/pallas_call | solution.py:169
  60.6 1.6 %collective-permute-done.9 = bf16[8,64,128]{2,1,0:T(8,128)(2,1)S(1)} collective-permute-done((bf16[8,64,128]{2,1,0:T(8,128)(2,1)S(1)}, bf16[8,64,128]{2,1,0:T(8,128)(2,1)S(1)}, u32[]{:S(2)}, u32[]{:S(2)}) %collective-permute-start.9) | collective-permute-done | bytes 131104 | tf_op jit(solution)/shard_map/ppermute | solution.py:67
  62.4 1.5 %collective-permute-done.12 = f32[8,64,128]{2,1,0:T(8,128)S(1)} collective-permute-done((f32[8,64,128]{2,1,0:T(8,128)S(1)}, f32[8,64,128]{2,1,0:T(8,128)S(1)}, u32[]{:S(2)}, u32[]{:S(2)}) %collective-permute-start.12) | collective-permute-done | bytes 262176 | tf_op jit(solution)/shard_map/ppermute | solution.py:80
  64.8 5.0 %state_part.1 = (bf16[512,1024]{1,0:T(8,128)(2,1)}, bf16[512,1024]{1,0:T(8,128)(2,1)}) custom-call(bf16[512,1024]{1,0:T(8,128)(2,1)} %refs_0_.3, bf16[512,1024]{1,0:T(8,128)(2,1)} %refs_1_.3, f32[1,8,128,128]{3,2,1,0:T(8,128)} %fusion.17.refs_2_, bf16[512,1024]{1,0:T(8,128)(2,1)} %get-tuple-element.27.refs_3_, bf16[512,1024]{1,0:T(8,128)(2,1)} %get-tuple-element.28.refs_4_), custom_call_target="tpu_custom_call" | custom-call | flops 536870912 | bytes 6291456 | tf_op jit(solution)/shard_map/state_part/pallas_call | solution.py:190
  (33 shorter events, 4.1 us)
Async XLA Ops:
  0.6 1.6 %copy-start.1 = (bf16[512,1024]{1,0:T(8,128)(2,1)S(1)}, bf16[512,1024]{1,0:T(8,128)(2,1)}, u32[]{:S(2)}) copy-start(bf16[512,1024]{1,0:T(8,128)(2,1)} %refs_1_.3) | copy-start | bytes 3145732
  2.2 16.3 %copy-start = (bf16[512,1024]{1,0:T(8,128)(2,1)S(1)}, bf16[512,1024]{1,0:T(8,128)(2,1)}, u32[]{:S(2)}) copy-start(bf16[512,1024]{1,0:T(8,128)(2,1)} %refs_0_.2) | copy-start | bytes 3145732
  3.4 2.9 %collective-permute-start.3 = (bf16[8,128,128]{2,1,0:T(8,128)(2,1)}, bf16[8,128,128]{2,1,0:T(8,128)(2,1)S(1)}, u32[]{:S(2)}, u32[]{:S(2)}) collective-permute-start(bf16[8,128,128]{2,1,0:T(8,128)(2,1)} %convolution_convert_fusion.1), channel_id=1, source_target_pairs={{0,4},{4,0},{8,12},{12,8},{16,20},{20,16},{24,28},{28,24},{1,5},{5... | collective-permute-start | bytes 786440 | tf_op jit(solution)/shard_map/ppermute | solution.py:51
  3.9 20.8 %collective-permute-start = (bf16[512,1024]{1,0:T(8,128)(2,1)}, bf16[512,1024]{1,0:T(8,128)(2,1)}, u32[]{:S(2)}, u32[]{:S(2)}) collective-permute-start(bf16[512,1024]{1,0:T(8,128)(2,1)} %param.8), channel_id=1, source_target_pairs={{0,1},{1,0},{2,3},{3,2},{4,6},{5,7},{6,4},{7,5},{8,9},{9,8},{10,11... | collective-permute-start | bytes 3145736 | tf_op jit(solution)/shard_map/ppermute | solution.py:36
  7.4 11.7 %collective-permute-start.4 = (bf16[8,64,128]{2,1,0:T(8,128)(2,1)S(1)}, bf16[8,64,128]{2,1,0:T(8,128)(2,1)S(1)}, u32[]{:S(2)}, u32[]{:S(2)}) collective-permute-start(bf16[8,64,128]{2,1,0:T(8,128)(2,1)S(1)} %fusion.18), channel_id=1, source_target_pairs={{0,8},{4,12},{8,16},{12,20},{16,24},{20,28},{1,9},{5,13},{9,17},{1... | collective-permute-start | bytes 393224 | tf_op jit(solution)/shard_map/ppermute | solution.py:67
  11.1 8.4 %collective-permute-start.5 = (bf16[8,64,128]{2,1,0:T(8,128)(2,1)S(1)}, bf16[8,64,128]{2,1,0:T(8,128)(2,1)S(1)}, u32[]{:S(2)}, u32[]{:S(2)}) collective-permute-start(bf16[8,64,128]{2,1,0:T(8,128)(2,1)S(1)} %fusion.18), channel_id=1, source_target_pairs={{0,16},{4,20},{8,24},{12,28},{1,17},{5,21},{9,25},{13,29},{2,18},{... | collective-permute-start | bytes 393224 | tf_op jit(solution)/shard_map/ppermute | solution.py:67
  15.6 5.6 %collective-permute-start.6 = (bf16[8,64,128]{2,1,0:T(8,128)(2,1)S(1)}, bf16[8,64,128]{2,1,0:T(8,128)(2,1)S(1)}, u32[]{:S(2)}, u32[]{:S(2)}) collective-permute-start(bf16[8,64,128]{2,1,0:T(8,128)(2,1)S(1)} %fusion.18), channel_id=1, source_target_pairs={{0,24},{4,28},{1,25},{5,29},{2,26},{6,30},{3,27},{7,31}} | collective-permute-start | bytes 393224 | tf_op jit(solution)/shard_map/ppermute | solution.py:67
  16.9 15.2 %collective-permute-start.1 = (bf16[512,1024]{1,0:T(8,128)(2,1)}, bf16[512,1024]{1,0:T(8,128)(2,1)}, u32[]{:S(2)}, u32[]{:S(2)}) collective-permute-start(bf16[512,1024]{1,0:T(8,128)(2,1)} %param.8), channel_id=1, source_target_pairs={{0,2},{1,3},{2,0},{3,1},{4,5},{5,4},{6,7},{7,6},{8,10},{9,11},{10,... | collective-permute-start | bytes 3145736 | tf_op jit(solution)/shard_map/ppermute | solution.py:37
  21.3 5.0 %collective-permute-start.7 = (f32[8,64,128]{2,1,0:T(8,128)S(1)}, f32[8,64,128]{2,1,0:T(8,128)S(1)}, u32[]{:S(2)}, u32[]{:S(2)}) collective-permute-start(f32[8,64,128]{2,1,0:T(8,128)S(1)} %convert_add_fusion.1), channel_id=1, source_target_pairs={{0,4},{4,0},{8,12},{12,8},{16,20},{20,16},{24,28},{28,24},{1,5},{5... | collective-permute-start | bytes 786440 | tf_op jit(solution)/shard_map/ppermute | solution.py:80
  21.3 10.8 %slice-start = ((s8[8388608]{0:T(1024)(128)(4,1)}), s8[4194304]{0:T(1024)(128)(4,1)S(1)}, s32[]{:S(2)}) async-start(s8[8388608]{0:T(1024)(128)(4,1)} %bitcast.34), calls=%async_computation | async-start | bytes 8388608
  24.7 18.5 %collective-permute-start.2 = (bf16[512,1024]{1,0:T(8,128)(2,1)}, bf16[512,1024]{1,0:T(8,128)(2,1)S(1)}, u32[]{:S(2)}, u32[]{:S(2)}) collective-permute-start(bf16[512,1024]{1,0:T(8,128)(2,1)} %collective-permute-done), channel_id=1, source_target_pairs={{0,2},{1,3},{2,0},{3,1},{4,5},{5,4},{6,7},{7,6},{8,10},{9,11},{10,... | collective-permute-start | bytes 3145736 | tf_op jit(solution)/shard_map/ppermute | solution.py:38
  26.3 5.8 %slice-start.1 = ((s8[8388608]{0:T(1024)(128)(4,1)}), s8[4194304]{0:T(1024)(128)(4,1)S(1)}, s32[]{:S(2)}) async-start(s8[8388608]{0:T(1024)(128)(4,1)} %bitcast.34), calls=%async_computation.1 | async-start | bytes 8388608
  44.5 6.1 %copy-start.2 = (bf16[512,1024]{1,0:T(8,128)(2,1)}, bf16[512,1024]{1,0:T(8,128)(2,1)S(1)}, u32[]{:S(2)}) copy-start(bf16[512,1024]{1,0:T(8,128)(2,1)S(1)} %fusion.refs_3_) | copy-start | bytes 3145732
  45.0 1.6 %collective-permute-start.8 = (bf16[8,128,128]{2,1,0:T(8,128)(2,1)S(1)}, bf16[8,128,128]{2,1,0:T(8,128)(2,1)S(1)}, u32[]{:S(2)}, u32[]{:S(2)}) collective-permute-start(bf16[8,128,128]{2,1,0:T(8,128)(2,1)S(1)} %fusion.11), channel_id=1, source_target_pairs={{0,4},{4,0},{8,12},{12,8},{16,20},{20,16},{24,28},{28,24},{1,5},{5... | collective-permute-start | bytes 786440 | tf_op jit(solution)/shard_map/ppermute | solution.py:51
  46.7 13.9 %collective-permute-start.10 = (bf16[8,64,128]{2,1,0:T(8,128)(2,1)S(1)}, bf16[8,64,128]{2,1,0:T(8,128)(2,1)S(1)}, u32[]{:S(2)}, u32[]{:S(2)}) collective-permute-start(bf16[8,64,128]{2,1,0:T(8,128)(2,1)S(1)} %dynamic-slice_add_fusion), channel_id=1, source_target_pairs={{16,0},{20,4},{24,8},{28,12},{17,1},{21,5},{25,9},{29,13},{18,2},{... | collective-permute-start | bytes 393224 | tf_op jit(solution)/shard_map/ppermute | solution.py:67
  48.0 12.6 %collective-permute-start.11 = (bf16[8,64,128]{2,1,0:T(8,128)(2,1)S(1)}, bf16[8,64,128]{2,1,0:T(8,128)(2,1)S(1)}, u32[]{:S(2)}, u32[]{:S(2)}) collective-permute-start(bf16[8,64,128]{2,1,0:T(8,128)(2,1)S(1)} %dynamic-slice_add_fusion), channel_id=1, source_target_pairs={{24,0},{28,4},{25,1},{29,5},{26,2},{30,6},{27,3},{31,7}} | collective-permute-start | bytes 393224 | tf_op jit(solution)/shard_map/ppermute | solution.py:67
  49.3 13.0 %collective-permute-start.9 = (bf16[8,64,128]{2,1,0:T(8,128)(2,1)S(1)}, bf16[8,64,128]{2,1,0:T(8,128)(2,1)S(1)}, u32[]{:S(2)}, u32[]{:S(2)}) collective-permute-start(bf16[8,64,128]{2,1,0:T(8,128)(2,1)S(1)} %dynamic-slice_add_fusion), channel_id=1, source_target_pairs={{8,0},{12,4},{16,8},{20,12},{24,16},{28,20},{9,1},{13,5},{17,9},{2... | collective-permute-start | bytes 393224 | tf_op jit(solution)/shard_map/ppermute | solution.py:67
  62.3 1.6 %collective-permute-start.12 = (f32[8,64,128]{2,1,0:T(8,128)S(1)}, f32[8,64,128]{2,1,0:T(8,128)S(1)}, u32[]{:S(2)}, u32[]{:S(2)}) collective-permute-start(f32[8,64,128]{2,1,0:T(8,128)S(1)} %convert_add_fusion), channel_id=1, source_target_pairs={{0,4},{4,0},{8,12},{12,8},{16,20},{20,16},{24,28},{28,24},{1,5},{5... | collective-permute-start | bytes 786440 | tf_op jit(solution)/shard_map/ppermute | solution.py:80

commit v12 on v11

--- a/solution.py
+++ b/solution.py
@@ -11,7 +11,7 @@
     return [(a, a ^ bit) for a in range(n)]
 
 
-def project(og, out_weight, ctx_size, head_size, tied):
+def project(og, out_weight, ctx_size, head_size, tied, early):
     cols = og.shape[1]
 
     def weight_cols(source, lo, width):
@@ -24,8 +24,9 @@
 
     if head_size != 4:
         full = lax.all_gather(og, "head", axis=1, tiled=True)
+        early = early[0](*early[1:])
         full, tied = lax.optimization_barrier((full, tied))
-        return mm(full, out_weight), tied
+        return mm(full, out_weight), tied, early
     me = lax.axis_index("head")
     core = lax.axis_index("ctx") % 2
     devices = [(p, j) for p in range(ctx_size) for j in range(4)]
@@ -35,13 +36,15 @@
 
     to_relay = lax.ppermute(og, ("ctx", "head"), route(1, 2))
     kept = lax.ppermute(og, ("ctx", "head"), route(2, 1))
+    to_relay, early_args = lax.optimization_barrier((to_relay, early[1:]))
+    early = early[0](*early_args)
     diag = lax.ppermute(to_relay, ("ctx", "head"), route(2, 1))
-    diag, tied = lax.optimization_barrier((diag, tied))
+    diag, tied, early = lax.optimization_barrier((diag, tied, early))
     acc = mm(og, weight_cols(me, 0, cols))
     acc = acc + mm(to_relay, weight_cols(me ^ (1 + core), 0, cols))
     acc = acc + mm(kept, weight_cols(me ^ (2 - core), 0, cols))
     acc = acc + mm(diag, weight_cols(me ^ 3, 0, cols))
-    return acc, tied
+    return acc, tied, early
 
 
 def ctx_exclusive(state, ctx_size, reverse, cover=None):
@@ -214,17 +217,20 @@
         q_blocks = queries.reshape(shape)
         k_blocks = keys.reshape(shape)
         v_blocks = values.reshape(shape)
-        kv_blocks = jnp.einsum(
-            "nshd,nshe->nhde", k_blocks, v_blocks,
-            preferred_element_type=jnp.float32,
-        )
-        kv_running = jnp.cumsum(kv_blocks, axis=0)
-        kv_before, _ = ctx_exclusive(kv_running[-1], ctx_size, False)
-        if blocks == 1:
-            kv_entry = kv_before[None]
-        else:
-            kv_entry = kv_before[None] + kv_running - kv_blocks
-        grad_heads, kv_entry = project(output_grad, out_weight, ctx_size, head_size, kv_entry)
+        def kv_state(k, v):
+            kv_blocks = jnp.einsum(
+                "nshd,nshe->nhde", k.reshape(shape), v.reshape(shape),
+                preferred_element_type=jnp.float32,
+            )
+            kv_running = jnp.cumsum(kv_blocks, axis=0)
+            kv_before, _ = ctx_exclusive(kv_running[-1], ctx_size, False)
+            if blocks == 1:
+                return kv_before[None]
+            return kv_before[None] + kv_running - kv_blocks
+
+        grad_heads, _, kv_entry = project(
+            output_grad, out_weight, ctx_size, head_size, (), (kv_state, keys, values)
+        )
         grad_heads = grad_heads.astype(jnp.bfloat16)
         g_blocks = grad_heads.reshape(shape)
         qg_blocks = jnp.einsum(

time: 70.2 us -> 79.5 us (1.13); the launches traced: 69.8 us -> 78.1 us
  waiting for transfers between devices: 16.6 us -> 26.3 us
  matrix products: 12.5 us -> 11.6 us
  other arithmetic: 2.96 us -> 2.07 us
    ppermute x1, waiting for transfers between devices: 0.01 us -> 20.7 us  [project(): to_relay = lax.ppermute(og, ('ctx', 'head'), route(1, 2))]
    ppermute x1, waiting for transfers between devices: 8.61 us -> 0.01 us  [project(): diag = lax.ppermute(to_relay, ('ctx', 'head'), route(2, 1))]
    dot_general x4, matrix products: 10.9 us -> 9.37 us  [mm(): lax.dot_general(a, b, (((1,), (1,)), ((), ())), preferred_element_type=jn...]
    ppermute x1, waiting for transfers between devices: 1.16 us -> 0.01 us  [project(): kept = lax.ppermute(og, ('ctx', 'head'), route(2, 1))]
    reshape x1, local copies, waits for them, and re-layouts: 1.58 us -> 0.53 us
    another operation x1, local copies, waits for them, and re-layouts: 0.53 us -> 1.49 us
    convert_element_type x1, other arithmetic: 0.95 us -> 0.05 us  [ctx_exclusive(): sent = mine.astype(jnp.bfloat16)]
    ppermute x6, waiting for transfers between devices: 3.75 us -> 2.86 us  [ctx_exclusive(): others = others + lax.ppermute(sent, 'ctx', pairs(step)).astype(jnp.float32)]
  transfers between devices with their start and end apart: 13 -> 13, of which waited for: 7 -> 6; matrix products, arithmetic and copies ran while one was open for 17% -> 16% of each run, Pallas kernels for 14% -> 13%
where the time goes in v12:
time: 79.5 us; the launch traced here: 78.1 us
  waiting for transfers between devices  26.3 us (33%)
  starting transfers between devices  20.2 us (25%)
  Pallas kernels  15 us (19%)
  matrix products  11.6 us (15%)
  other arithmetic  2.07 us (3%)
  local copies, waits for them, and re-layouts  2.05 us (3%)
  between operations  0.91 us (1%)
    ppermute x1, waiting for transfers between devices, project(): to_relay = lax.ppermute(og, ('ctx', 'head'), route(1, 2))  20.7 us
    ppermute x6, starting transfers between devices, ctx_exclusive(): others = others + lax.ppermute(sent, 'ctx', pairs(step)).astype(jnp.float32)  13.3 us
    pallas_call x1, Pallas kernels, attention_part(): pl.pallas_call(lambda *refs: scores_kernel(scale, chunk, per_step, *refs)...  10 us
    dot_general x4, matrix products, mm(): lax.dot_general(a, b, (((1,), (1,)), ((), ())), preferred_element_type=jn...  9.37 us
    pallas_call x1, Pallas kernels, state_part(): pl.pallas_call(lambda *refs: state_kernel(scale, per_step, *refs), grid=(...  4.96 us
    ppermute x1, starting transfers between devices, project(): to_relay = lax.ppermute(og, ('ctx', 'head'), route(1, 2))  3 us
    ppermute x6, waiting for transfers between devices, ctx_exclusive(): others = others + lax.ppermute(sent, 'ctx', pairs(step)).astype(jnp.float32)  2.86 us
    dot_general x1, matrix products, kv_state(): jnp.einsum('nshd,nshe->nhde', k.reshape(shape), v.reshape(shape), preferr...  1.76 us
  transfers between devices with their start and end apart: 13, of which 6 were waited for; matrix products, arithmetic and copies ran while one was open for 16% of the time, Pallas kernels for 13%

profile of v12, /device:TPU:0, one launch (start us, length us, event | category | flops | bytes accessed | tf_op | source)
XLA Modules:
  0.0 78.1 jit_solution(10240125977763926476)
XLA Ops:
  0.6 3.0 %collective-permute-start = (bf16[512,1024]{1,0:T(8,128)(2,1)}, bf16[512,1024]{1,0:T(8,128)(2,1)}, u32[]{:S(2)}, u32[]{:S(2)}) collective-permute-start(bf16[512,1024]{1,0:T(8,128)(2,1)} %param.8), channel_id=1, source_target_pairs={{0,1},{1,0},{2,3},{3,2},{4,6},{5,7},{6,4},{7,5},{8,9},{9,8},{10,11... | collective-permute-start | bytes 3145736 | tf_op jit(solution)/shard_map/ppermute | solution.py:37
  3.6 1.5 %collective-permute-start.1 = (bf16[512,1024]{1,0:T(8,128)(2,1)}, bf16[512,1024]{1,0:T(8,128)(2,1)}, u32[]{:S(2)}, u32[]{:S(2)}) collective-permute-start(bf16[512,1024]{1,0:T(8,128)(2,1)} %param.8), channel_id=1, source_target_pairs={{0,2},{1,3},{2,0},{3,1},{4,5},{5,4},{6,7},{7,6},{8,10},{9,11},{10,... | collective-permute-start | bytes 3145736 | tf_op jit(solution)/shard_map/ppermute | solution.py:38
  5.2 1.5 %copy.17 = bf16[512,1024]{0,1:T(8,128)(2,1)S(1)} copy(bf16[512,1024]{1,0:T(8,128)(2,1)} %refs_0_.2) | data formatting | bytes 2097152 | tf_op jit(solution)/shard_map/reshape.3
  6.7 20.7 %collective-permute-done = bf16[512,1024]{1,0:T(8,128)(2,1)} collective-permute-done((bf16[512,1024]{1,0:T(8,128)(2,1)}, bf16[512,1024]{1,0:T(8,128)(2,1)}, u32[]{:S(2)}, u32[]{:S(2)}) %collective-permute-start) | collective-permute-done | bytes 1048608 | tf_op jit(solution)/shard_map/ppermute | solution.py:37
  28.0 1.8 %convolution_convert_fusion.1 = bf16[8,128,128]{2,1,0:T(8,128)(2,1)S(1)} fusion(bf16[512,8,128]{0,2,1:T(8,128)(2,1)S(1)} %bitcast.39, bf16[512,1024]{1,0:T(8,128)(2,1)} %refs_1_.3), kind=kOutput, calls=%fused_computation.13 | convolution fusion | flops 134348800 | bytes 2359296 | tf_op jit(solution)/shard_map/nshd,nshe->nhde/dot_general | solution.py:221
  29.8 3.0 %fusion.8 = f32[1024,512]{0,1:T(8,128)S(1)} fusion(bf16[512,1024]{1,0:T(8,128)(2,1)S(1)} %copy-done.3, bf16[1024,4096]{1,0:T(8,128)(2,1)} %param.9, s32[]{:T(128)S(6)} %select_n.61), kind=kOutput, calls=%fused_computation.10 | convolution fusion | flops 1073741824 | bytes 5242884 | tf_op jit(solution)/shard_map/dot_general | solution.py:21
  32.9 1.6 %collective-permute-start.2 = (bf16[512,1024]{1,0:T(8,128)(2,1)}, bf16[512,1024]{1,0:T(8,128)(2,1)S(1)}, u32[]{:S(2)}, u32[]{:S(2)}) collective-permute-start(bf16[512,1024]{1,0:T(8,128)(2,1)} %collective-permute-done), channel_id=1, source_target_pairs={{0,2},{1,3},{2,0},{3,1},{4,5},{5,4},{6,7},{7,6},{8,10},{9,11},{10,... | collective-permute-start | bytes 3145736 | tf_op jit(solution)/shard_map/ppermute | solution.py:41
  34.6 3.6 %collective-permute-start.4 = (bf16[8,64,128]{2,1,0:T(8,128)(2,1)S(1)}, bf16[8,64,128]{2,1,0:T(8,128)(2,1)S(1)}, u32[]{:S(2)}, u32[]{:S(2)}) collective-permute-start(bf16[8,64,128]{2,1,0:T(8,128)(2,1)S(1)} %fusion.19), channel_id=1, source_target_pairs={{0,8},{4,12},{8,16},{12,20},{16,24},{20,28},{1,9},{5,13},{9,17},{1... | collective-permute-start | bytes 393224 | tf_op jit(solution)/shard_map/ppermute | solution.py:70
  38.2 4.5 %collective-permute-start.5 = (bf16[8,64,128]{2,1,0:T(8,128)(2,1)S(1)}, bf16[8,64,128]{2,1,0:T(8,128)(2,1)S(1)}, u32[]{:S(2)}, u32[]{:S(2)}) collective-permute-start(bf16[8,64,128]{2,1,0:T(8,128)(2,1)S(1)} %fusion.19), channel_id=1, source_target_pairs={{0,16},{4,20},{8,24},{12,28},{1,17},{5,21},{9,25},{13,29},{2,18},{... | collective-permute-start | bytes 393224 | tf_op jit(solution)/shard_map/ppermute | solution.py:70
  42.7 1.3 %collective-permute-start.6 = (bf16[8,64,128]{2,1,0:T(8,128)(2,1)S(1)}, bf16[8,64,128]{2,1,0:T(8,128)(2,1)S(1)}, u32[]{:S(2)}, u32[]{:S(2)}) collective-permute-start(bf16[8,64,128]{2,1,0:T(8,128)(2,1)S(1)} %fusion.19), channel_id=1, source_target_pairs={{0,24},{4,28},{1,25},{5,29},{2,26},{6,30},{3,27},{7,31}} | collective-permute-start | bytes 393224 | tf_op jit(solution)/shard_map/ppermute | solution.py:70
  44.1 2.5 %fusion.6 = f32[512,1024]{1,0:T(8,128)S(1)} fusion(bf16[512,1024]{1,0:T(8,128)(2,1)} %collective-permute-done, bf16[1024,4096]{1,0:T(8,128)(2,1)S(1)} %copy-done.2, s32[]{:T(128)S(6)} %select_n.63), kind=kOutput, calls=%fused_computation.8 | convolution fusion | flops 1073741824 | bytes 5242884 | tf_op jit(solution)/shard_map/dot_general | solution.py:21
  46.6 2.4 %collective-permute-done.6 = bf16[8,64,128]{2,1,0:T(8,128)(2,1)S(1)} collective-permute-done((bf16[8,64,128]{2,1,0:T(8,128)(2,1)S(1)}, bf16[8,64,128]{2,1,0:T(8,128)(2,1)S(1)}, u32[]{:S(2)}, u32[]{:S(2)}) %collective-permute-start.6) | collective-permute-done | bytes 131104 | tf_op jit(solution)/shard_map/ppermute | solution.py:70
  49.2 2.5 %fusion.4 = f32[1024,512]{0,1:T(8,128)S(1)} fusion(bf16[512,1024]{1,0:T(8,128)(2,1)} %collective-permute-done.1, bf16[1024,4096]{1,0:T(8,128)(2,1)S(1)} %copy-done.2, s32[]{:T(128)S(6)} %select_n.64), kind=kOutput, calls=%fused_computation.6 | convolution fusion | flops 1073741824 | bytes 5242884 | tf_op jit(solution)/shard_map/dot_general | solution.py:21
  51.8 0.9 %fusion.17.refs_4_ = f32[1,8,128,128]{3,2,1,0:T(8,128)} fusion(f32[8,64,128]{2,1,0:T(8,128)S(1)} %get-tuple-element.40, f32[8,64,128]{2,1,0:T(8,128)S(1)} %get-tuple-element.39, pred[]{:T(512)S(6)} %eq.15, bf16[8,128,128]{2,1,0:T(8,128)(2,1)S(1)} %collective-permute-done.3), kind=kLoop, calls=%fused_computation.20 | loop fusion | flops 524288 | bytes 1310721 | tf_op jit(solution)/shard_map/broadcast_in_dim | solution.py:228
  52.6 1.3 %fusion.1.refs_3_ = bf16[512,1024]{1,0:T(8,128)(2,1)S(1)} fusion(f32[1024,512]{0,1:T(8,128)S(1)} %fusion.4, f32[512,1024]{1,0:T(8,128)S(1)} %fusion.6, f32[1024,512]{0,1:T(8,128)S(1)} %fusion.8, bf16[512,1024]{1,0:T(8,128)(2,1)S(1)} %collective-permute-done.2, bf16[1024,4096]{1,0:T(8,128)(2,1)S(1)} %copy-done.2, s32[]{:T(128)S(6)} %select_n.71), kind=kOutput, calls=%fused_computation.2 | convolution fusion | flops 1075838976 | bytes 10485764 | tf_op jit(solution)/shard_map/dot_general | solution.py:21
  54.4 0.6 collective-permute-start.8
  55.0 1.2 %collective-permute-done.8 = bf16[8,128,128]{2,1,0:T(8,128)(2,1)S(1)} collective-permute-done((bf16[8,128,128]{2,1,0:T(8,128)(2,1)S(1)}, bf16[8,128,128]{2,1,0:T(8,128)(2,1)S(1)}, u32[]{:S(2)}, u32[]{:S(2)}) %collective-permute-start.8) | collective-permute-done | bytes 262176 | tf_op jit(solution)/shard_map/ppermute | solution.py:54
  56.2 1.3 %collective-permute-start.10 = (bf16[8,64,128]{2,1,0:T(8,128)(2,1)S(1)}, bf16[8,64,128]{2,1,0:T(8,128)(2,1)S(1)}, u32[]{:S(2)}, u32[]{:S(2)}) collective-permute-start(bf16[8,64,128]{2,1,0:T(8,128)(2,1)S(1)} %dynamic-slice_add_fusion), channel_id=1, source_target_pairs={{16,0},{20,4},{24,8},{28,12},{17,1},{21,5},{25,9},{29,13},{18,2},{... | collective-permute-start | bytes 393224 | tf_op jit(solution)/shard_map/ppermute | solution.py:70
  57.5 1.3 %collective-permute-start.11 = (bf16[8,64,128]{2,1,0:T(8,128)(2,1)S(1)}, bf16[8,64,128]{2,1,0:T(8,128)(2,1)S(1)}, u32[]{:S(2)}, u32[]{:S(2)}) collective-permute-start(bf16[8,64,128]{2,1,0:T(8,128)(2,1)S(1)} %dynamic-slice_add_fusion), channel_id=1, source_target_pairs={{24,0},{28,4},{25,1},{29,5},{26,2},{30,6},{27,3},{31,7}} | collective-permute-start | bytes 393224 | tf_op jit(solution)/shard_map/ppermute | solution.py:70
  58.8 1.3 %collective-permute-start.9 = (bf16[8,64,128]{2,1,0:T(8,128)(2,1)S(1)}, bf16[8,64,128]{2,1,0:T(8,128)(2,1)S(1)}, u32[]{:S(2)}, u32[]{:S(2)}) collective-permute-start(bf16[8,64,128]{2,1,0:T(8,128)(2,1)S(1)} %dynamic-slice_add_fusion), channel_id=1, source_target_pairs={{8,0},{12,4},{16,8},{20,12},{24,16},{28,20},{9,1},{13,5},{17,9},{2... | collective-permute-start | bytes 393224 | tf_op jit(solution)/shard_map/ppermute | solution.py:70
  60.1 10.0 %attention_part.1 = (bf16[512,1024]{1,0:T(8,128)(2,1)}, bf16[512,1024]{1,0:T(8,128)(2,1)}, bf16[512,1024]{1,0:T(8,128)(2,1)}) custom-call(bf16[512,1024]{1,0:T(8,128)(2,1)} %refs_0_.2, bf16[512,1024]{1,0:T(8,128)(2,1)} %refs_0_.3, bf16[512,1024]{1,0:T(8,128)(2,1)} %refs_1_.3, bf16[512,1024]{1,0:T(8,128)(2,1)} %copy-done.1, f32[1,8,128,128]{3,2,1,0:T(8,128)} %fusion.17.refs_4_), custom_call_target="tpu_custom_call" | custom-call | flops 3221225472 | bytes 7340032 | tf_op jit(solution)/shard_map/attention_part/pallas_call | solution.py:172
  70.7 1.5 %collective-permute-done.12 = f32[8,64,128]{2,1,0:T(8,128)S(1)} collective-permute-done((f32[8,64,128]{2,1,0:T(8,128)S(1)}, f32[8,64,128]{2,1,0:T(8,128)S(1)}, u32[]{:S(2)}, u32[]{:S(2)}) %collective-permute-start.12) | collective-permute-done | bytes 262176 | tf_op jit(solution)/shard_map/ppermute | solution.py:83
  72.3 0.9 %fusion.18.refs_2_ = f32[1,8,128,128]{3,2,1,0:T(8,128)} fusion(f32[8,64,128]{2,1,0:T(8,128)S(1)} %get-tuple-element.38, f32[8,64,128]{2,1,0:T(8,128)S(1)} %get-tuple-element.37, pred[]{:T(512)S(6)} %eq.14, bf16[8,128,128]{2,1,0:T(8,128)(2,1)S(1)} %collective-permute-done.8), kind=kLoop, calls=%fused_computation.22 | loop fusion | flops 524288 | bytes 1310721 | tf_op jit(solution)/shard_map/broadcast_in_dim | solution.py:250
  73.2 5.0 %state_part.1 = (bf16[512,1024]{1,0:T(8,128)(2,1)}, bf16[512,1024]{1,0:T(8,128)(2,1)}) custom-call(bf16[512,1024]{1,0:T(8,128)(2,1)} %refs_0_.3, bf16[512,1024]{1,0:T(8,128)(2,1)} %refs_1_.3, f32[1,8,128,128]{3,2,1,0:T(8,128)} %fusion.18.refs_2_, bf16[512,1024]{1,0:T(8,128)(2,1)} %get-tuple-element.33.refs_3_, bf16[512,1024]{1,0:T(8,128)(2,1)} %get-tuple-element.34.refs_4_), custom_call_target="tpu_custom_call" | custom-call | flops 536870912 | bytes 6291456 | tf_op jit(solution)/shard_map/state_part/pallas_call | solution.py:193
  (30 shorter events, 2.0 us)
Async XLA Ops:
  0.6 26.8 %copy-start = (bf16[512,1024]{1,0:T(8,128)(2,1)S(1)}, bf16[512,1024]{1,0:T(8,128)(2,1)}, u32[]{:S(2)}) copy-start(bf16[512,1024]{1,0:T(8,128)(2,1)} %refs_0_.3) | copy-start | bytes 3145732
  0.6 26.8 %collective-permute-start = (bf16[512,1024]{1,0:T(8,128)(2,1)}, bf16[512,1024]{1,0:T(8,128)(2,1)}, u32[]{:S(2)}, u32[]{:S(2)}) collective-permute-start(bf16[512,1024]{1,0:T(8,128)(2,1)} %param.8), channel_id=1, source_target_pairs={{0,1},{1,0},{2,3},{3,2},{4,6},{5,7},{6,4},{7,5},{8,9},{9,8},{10,11... | collective-permute-start | bytes 3145736 | tf_op jit(solution)/shard_map/ppermute | solution.py:37
  3.6 45.5 %collective-permute-start.1 = (bf16[512,1024]{1,0:T(8,128)(2,1)}, bf16[512,1024]{1,0:T(8,128)(2,1)}, u32[]{:S(2)}, u32[]{:S(2)}) collective-permute-start(bf16[512,1024]{1,0:T(8,128)(2,1)} %param.8), channel_id=1, source_target_pairs={{0,2},{1,3},{2,0},{3,1},{4,5},{5,4},{6,7},{7,6},{8,10},{9,11},{10,... | collective-permute-start | bytes 3145736 | tf_op jit(solution)/shard_map/ppermute | solution.py:38
  27.9 1.9 %copy-start.3 = (bf16[512,1024]{1,0:T(8,128)(2,1)S(1)}, bf16[512,1024]{1,0:T(8,128)(2,1)}, u32[]{:S(2)}) copy-start(bf16[512,1024]{1,0:T(8,128)(2,1)} %param.8) | copy-start | bytes 3145732
  29.7 14.3 %copy-start.2 = (bf16[1024,4096]{1,0:T(8,128)(2,1)S(1)}, bf16[1024,4096]{1,0:T(8,128)(2,1)}, u32[]{:S(2)}) copy-start(bf16[1024,4096]{1,0:T(8,128)(2,1)} %param.9) | copy-start | bytes 25165828
  29.7 4.8 %collective-permute-start.3 = (bf16[8,128,128]{2,1,0:T(8,128)(2,1)S(1)}, bf16[8,128,128]{2,1,0:T(8,128)(2,1)S(1)}, u32[]{:S(2)}, u32[]{:S(2)}) collective-permute-start(bf16[8,128,128]{2,1,0:T(8,128)(2,1)S(1)} %convolution_convert_fusion.1), channel_id=1, source_target_pairs={{0,4},{4,0},{8,12},{12,8},{16,20},{20,16},{24,28},{28,24},{1,5},{5... | collective-permute-start | bytes 786440 | tf_op jit(solution)/shard_map/ppermute | solution.py:54
  32.9 19.8 %collective-permute-start.2 = (bf16[512,1024]{1,0:T(8,128)(2,1)}, bf16[512,1024]{1,0:T(8,128)(2,1)S(1)}, u32[]{:S(2)}, u32[]{:S(2)}) collective-permute-start(bf16[512,1024]{1,0:T(8,128)(2,1)} %collective-permute-done), channel_id=1, source_target_pairs={{0,2},{1,3},{2,0},{3,1},{4,5},{5,4},{6,7},{7,6},{8,10},{9,11},{10,... | collective-permute-start | bytes 3145736 | tf_op jit(solution)/shard_map/ppermute | solution.py:41
  34.6 12.0 %collective-permute-start.4 = (bf16[8,64,128]{2,1,0:T(8,128)(2,1)S(1)}, bf16[8,64,128]{2,1,0:T(8,128)(2,1)S(1)}, u32[]{:S(2)}, u32[]{:S(2)}) collective-permute-start(bf16[8,64,128]{2,1,0:T(8,128)(2,1)S(1)} %fusion.19), channel_id=1, source_target_pairs={{0,8},{4,12},{8,16},{12,20},{16,24},{20,28},{1,9},{5,13},{9,17},{1... | collective-permute-start | bytes 393224 | tf_op jit(solution)/shard_map/ppermute | solution.py:70
  38.2 8.4 %collective-permute-start.5 = (bf16[8,64,128]{2,1,0:T(8,128)(2,1)S(1)}, bf16[8,64,128]{2,1,0:T(8,128)(2,1)S(1)}, u32[]{:S(2)}, u32[]{:S(2)}) collective-permute-start(bf16[8,64,128]{2,1,0:T(8,128)(2,1)S(1)} %fusion.19), channel_id=1, source_target_pairs={{0,16},{4,20},{8,24},{12,28},{1,17},{5,21},{9,25},{13,29},{2,18},{... | collective-permute-start | bytes 393224 | tf_op jit(solution)/shard_map/ppermute | solution.py:70
  42.7 6.3 %collective-permute-start.6 = (bf16[8,64,128]{2,1,0:T(8,128)(2,1)S(1)}, bf16[8,64,128]{2,1,0:T(8,128)(2,1)S(1)}, u32[]{:S(2)}, u32[]{:S(2)}) collective-permute-start(bf16[8,64,128]{2,1,0:T(8,128)(2,1)S(1)} %fusion.19), channel_id=1, source_target_pairs={{0,24},{4,28},{1,25},{5,29},{2,26},{6,30},{3,27},{7,31}} | collective-permute-start | bytes 393224 | tf_op jit(solution)/shard_map/ppermute | solution.py:70
  49.1 2.6 %collective-permute-start.7 = (f32[8,64,128]{2,1,0:T(8,128)S(1)}, f32[8,64,128]{2,1,0:T(8,128)S(1)}, u32[]{:S(2)}, u32[]{:S(2)}) collective-permute-start(f32[8,64,128]{2,1,0:T(8,128)S(1)} %convert_add_fusion.1), channel_id=1, source_target_pairs={{0,4},{4,0},{8,12},{12,8},{16,20},{20,16},{24,28},{28,24},{1,5},{5... | collective-permute-start | bytes 786440 | tf_op jit(solution)/shard_map/ppermute | solution.py:83
  53.9 6.2 %copy-start.1 = (bf16[512,1024]{1,0:T(8,128)(2,1)}, bf16[512,1024]{1,0:T(8,128)(2,1)S(1)}, u32[]{:S(2)}) copy-start(bf16[512,1024]{1,0:T(8,128)(2,1)S(1)} %fusion.1.refs_3_) | copy-start | bytes 3145732
  54.4 1.7 %collective-permute-start.8 = (bf16[8,128,128]{2,1,0:T(8,128)(2,1)S(1)}, bf16[8,128,128]{2,1,0:T(8,128)(2,1)S(1)}, u32[]{:S(2)}, u32[]{:S(2)}) collective-permute-start(bf16[8,128,128]{2,1,0:T(8,128)(2,1)S(1)} %fusion.10), channel_id=1, source_target_pairs={{0,4},{4,0},{8,12},{12,8},{16,20},{20,16},{24,28},{28,24},{1,5},{5... | collective-permute-start | bytes 786440 | tf_op jit(solution)/shard_map/ppermute | solution.py:54
  56.2 14.2 %collective-permute-start.10 = (bf16[8,64,128]{2,1,0:T(8,128)(2,1)S(1)}, bf16[8,64,128]{2,1,0:T(8,128)(2,1)S(1)}, u32[]{:S(2)}, u32[]{:S(2)}) collective-permute-start(bf16[8,64,128]{2,1,0:T(8,128)(2,1)S(1)} %dynamic-slice_add_fusion), channel_id=1, source_target_pairs={{16,0},{20,4},{24,8},{28,12},{17,1},{21,5},{25,9},{29,13},{18,2},{... | collective-permute-start | bytes 393224 | tf_op jit(solution)/shard_map/ppermute | solution.py:70
  57.5 13.1 %collective-permute-start.11 = (bf16[8,64,128]{2,1,0:T(8,128)(2,1)S(1)}, bf16[8,64,128]{2,1,0:T(8,128)(2,1)S(1)}, u32[]{:S(2)}, u32[]{:S(2)}) collective-permute-start(bf16[8,64,128]{2,1,0:T(8,128)(2,1)S(1)} %dynamic-slice_add_fusion), channel_id=1, source_target_pairs={{24,0},{28,4},{25,1},{29,5},{26,2},{30,6},{27,3},{31,7}} | collective-permute-start | bytes 393224 | tf_op jit(solution)/shard_map/ppermute | solution.py:70
  58.8 11.8 %collective-permute-start.9 = (bf16[8,64,128]{2,1,0:T(8,128)(2,1)S(1)}, bf16[8,64,128]{2,1,0:T(8,128)(2,1)S(1)}, u32[]{:S(2)}, u32[]{:S(2)}) collective-permute-start(bf16[8,64,128]{2,1,0:T(8,128)(2,1)S(1)} %dynamic-slice_add_fusion), channel_id=1, source_target_pairs={{8,0},{12,4},{16,8},{20,12},{24,16},{28,20},{9,1},{13,5},{17,9},{2... | collective-permute-start | bytes 393224 | tf_op jit(solution)/shard_map/ppermute | solution.py:70
  70.6 1.6 %collective-permute-start.12 = (f32[8,64,128]{2,1,0:T(8,128)S(1)}, f32[8,64,128]{2,1,0:T(8,128)S(1)}, u32[]{:S(2)}, u32[]{:S(2)}) collective-permute-start(f32[8,64,128]{2,1,0:T(8,128)S(1)} %convert_add_fusion), channel_id=1, source_target_pairs={{0,4},{4,0},{8,12},{12,8},{16,20},{20,16},{24,28},{28,24},{1,5},{5... | collective-permute-start | bytes 786440 | tf_op jit(solution)/shard_map/ppermute | solution.py:83

commit v13 on v11

--- a/solution.py
+++ b/solution.py
@@ -92,6 +92,7 @@
 
 
 NT = (((1,), (1,)), ((), ()))
+TN = (((0,), (0,)), ((), ()))
 
 
 def split_state(state):
@@ -100,48 +101,27 @@
     return high, low
 
 
-def scores_kernel(scale, chunk, per_step, q_ref, k_ref, v_ref, g_ref, kv_ref, gq_ref, gk_ref, gv_ref):
+def scores_kernel(scale, per_step, q_ref, k_ref, v_ref, g_ref, kv_ref, gq_ref, gk_ref, gv_ref):
     length = q_ref.shape[0]
-    count = length // chunk
-    row = lax.broadcasted_iota(jnp.int32, (chunk, chunk), 0)
-    col = lax.broadcasted_iota(jnp.int32, (chunk, chunk), 1)
-
-    def score(a, b, keep):
-        s = lax.dot_general(a, b, NT, preferred_element_type=jnp.float32) * scale
-        if keep is not None:
-            s = jnp.where(keep, s, 0.0)
-        return s.astype(jnp.bfloat16)
-
+    row = lax.broadcasted_iota(jnp.int32, (length, length), 0)
+    col = lax.broadcasted_iota(jnp.int32, (length, length), 1)
+    lower = row >= col
     for h in range(per_step):
         cols = pl.ds(h * DH, DH)
+        q, k, v, g = q_ref[:, cols], k_ref[:, cols], v_ref[:, cols], g_ref[:, cols]
         kv_high, kv_low = split_state(kv_ref[0, h] * scale)
-
-        def piece(ref, i):
-            return ref[pl.ds(i * chunk, chunk), cols]
-
-        for i in range(count):
-            rows = pl.ds(i * chunk, chunk)
-            g_i = piece(g_ref, i)
-            gq = lax.dot_general(g_i, kv_high, NT, preferred_element_type=jnp.float32)
-            gq = gq + lax.dot_general(g_i, kv_low, NT, preferred_element_type=jnp.float32)
-            for j in range(i + 1):
-                sg = score(g_i, piece(v_ref, j), row >= col if j == i else None)
-                term = jnp.dot(sg, piece(k_ref, j), preferred_element_type=jnp.float32)
-                gq = gq + term
-            gq_ref[rows, cols] = gq.astype(gq_ref.dtype)
-            v_i, k_i = piece(v_ref, i), piece(k_ref, i)
-            gk = None
-            gv = None
-            for j in range(i, count):
-                keep = row <= col if j == i else None
-                sgt = score(v_i, piece(g_ref, j), keep)
-                sft = score(k_i, piece(q_ref, j), keep)
-                term_k = jnp.dot(sgt, piece(q_ref, j), preferred_element_type=jnp.float32)
-                term_v = jnp.dot(sft, piece(g_ref, j), preferred_element_type=jnp.float32)
-                gk = term_k if gk is None else gk + term_k
-                gv = term_v if gv is None else gv + term_v
-            gk_ref[rows, cols] = gk.astype(gk_ref.dtype)
-            gv_ref[rows, cols] = gv.astype(gv_ref.dtype)
+        score_grad = lax.dot_general(g, v, NT, preferred_element_type=jnp.float32) * scale
+        score_grad = jnp.where(lower, score_grad, 0.0).astype(jnp.bfloat16)
+        score_fwd = lax.dot_general(q, k, NT, preferred_element_type=jnp.float32) * scale
+        score_fwd = jnp.where(lower, score_fwd, 0.0).astype(jnp.bfloat16)
+        gq = lax.dot_general(g, kv_high, NT, preferred_element_type=jnp.float32)
+        gq = gq + lax.dot_general(g, kv_low, NT, preferred_element_type=jnp.float32)
+        gq = gq + jnp.dot(score_grad, k, preferred_element_type=jnp.float32)
+        gq_ref[:, cols] = gq.astype(gq_ref.dtype)
+        gk_t = lax.dot_general(q, score_grad, TN, preferred_element_type=jnp.float32)
+        gv_t = lax.dot_general(g, score_fwd, TN, preferred_element_type=jnp.float32)
+        gk_ref[:, cols] = gk_t.T.astype(gk_ref.dtype)
+        gv_ref[:, cols] = gv_t.T.astype(gv_ref.dtype)
 
 
 def state_kernel(scale, per_step, k_ref, v_ref, qg_ref, gkp_ref, gvp_ref, gk_ref, gv_ref):
@@ -165,9 +145,8 @@
     st = pl.BlockSpec((1, per_step, DH, DH), lambda n, h: (n, h, 0, 0))
     rows, width = q.shape
     out = jax.ShapeDtypeStruct((rows, width), jnp.bfloat16)
-    chunk = block_len
     return pl.pallas_call(
-        lambda *refs: scores_kernel(scale, chunk, per_step, *refs),
+        lambda *refs: scores_kernel(scale, per_step, *refs),
         grid=(blocks, heads // per_step),
         in_specs=[tok, tok, tok, tok, st],
         out_specs=[tok, tok, tok],

time: 70.2 us -> 70.2 us (level)
  Pallas kernels: 15 us -> 13 us
  waiting for transfers between devices: 16.6 us -> 18.6 us
    ppermute x6, waiting for transfers between devices: 3.75 us -> 5.75 us  [ctx_exclusive(): others = others + lax.ppermute(sent, 'ctx', pairs(step)).astype(jnp.float32)]
    pallas_call x1, Pallas kernels: 10 us -> 8.03 us  [attention_part(): pl.pallas_call(lambda *refs: scores_kernel(scale, per_step, *refs), grid=...]
  transfers between devices with their start and end apart: 13 -> 13, of which waited for: 7 -> 8; matrix products, arithmetic and copies ran while one was open for 17% -> 17% of each run, Pallas kernels for 14% -> 11%
where the time goes in v13:
time: 70.2 us; the launch traced here: 69.8 us
  starting transfers between devices  19.7 us (28%)
  waiting for transfers between devices  18.6 us (26%)
  Pallas kernels  13 us (19%)
  matrix products  12.5 us (18%)
  other arithmetic  2.96 us (4%)
  local copies, waits for them, and re-layouts  2.15 us (3%)
  between operations  0.89 us (1%)
    ppermute x6, starting transfers between devices, ctx_exclusive(): others = others + lax.ppermute(sent, 'ctx', pairs(step)).astype(jnp.float32)  13.4 us
    dot_general x4, matrix products, mm(): lax.dot_general(a, b, (((1,), (1,)), ((), ())), preferred_element_type=jn...  10.9 us
    ppermute x1, waiting for transfers between devices, project(): diag = lax.ppermute(to_relay, ('ctx', 'head'), route(2, 1))  8.61 us
    pallas_call x1, Pallas kernels, attention_part(): pl.pallas_call(lambda *refs: scores_kernel(scale, per_step, *refs), grid=...  8.03 us
    ppermute x6, waiting for transfers between devices, ctx_exclusive(): others = others + lax.ppermute(sent, 'ctx', pairs(step)).astype(jnp.float32)  5.75 us
    pallas_call x1, Pallas kernels, state_part(): pl.pallas_call(lambda *refs: state_kernel(scale, per_step, *refs), grid=(...  4.96 us
    ppermute x1, starting transfers between devices, project(): to_relay = lax.ppermute(og, ('ctx', 'head'), route(1, 2))  2.49 us
    ppermute x1, starting transfers between devices, project(): diag = lax.ppermute(to_relay, ('ctx', 'head'), route(2, 1))  1.6 us
  transfers between devices with their start and end apart: 13, of which 8 were waited for; matrix products, arithmetic and copies ran while one was open for 17% of the time, Pallas kernels for 11%

profile of v13, /device:TPU:0, one launch (start us, length us, event | category | flops | bytes accessed | tf_op | source)
XLA Modules:
  0.0 69.8 jit_solution(13156061909040756058)
XLA Ops:
  0.6 1.6 %copy.18 = bf16[512,1024]{0,1:T(8,128)(2,1)S(1)} copy(bf16[512,1024]{1,0:T(8,128)(2,1)} %refs_0_.3) | data formatting | bytes 2097152 | tf_op jit(solution)/shard_map/reshape
  2.3 1.2 %convolution_convert_fusion.1 = bf16[8,128,128]{2,1,0:T(8,128)(2,1)} fusion(bf16[512,8,128]{0,2,1:T(8,128)(2,1)S(1)} %bitcast.33, bf16[512,1024]{1,0:T(8,128)(2,1)S(1)} %copy-done.1), kind=kOutput, calls=%fused_computation.11 | convolution fusion | flops 134348800 | bytes 2359296 | tf_op jit(solution)/shard_map/nshd,nshe->nhde/dot_general | solution.py:196
  3.9 2.5 %collective-permute-start = (bf16[512,1024]{1,0:T(8,128)(2,1)}, bf16[512,1024]{1,0:T(8,128)(2,1)}, u32[]{:S(2)}, u32[]{:S(2)}) collective-permute-start(bf16[512,1024]{1,0:T(8,128)(2,1)} %param.8), channel_id=1, source_target_pairs={{0,1},{1,0},{2,3},{3,2},{4,6},{5,7},{6,4},{7,5},{8,9},{9,8},{10,11... | collective-permute-start | bytes 3145736 | tf_op jit(solution)/shard_map/ppermute | solution.py:36
  7.4 3.7 %collective-permute-start.4 = (bf16[8,64,128]{2,1,0:T(8,128)(2,1)S(1)}, bf16[8,64,128]{2,1,0:T(8,128)(2,1)S(1)}, u32[]{:S(2)}, u32[]{:S(2)}) collective-permute-start(bf16[8,64,128]{2,1,0:T(8,128)(2,1)S(1)} %fusion.18), channel_id=1, source_target_pairs={{0,8},{4,12},{8,16},{12,20},{16,24},{20,28},{1,9},{5,13},{9,17},{1... | collective-permute-start | bytes 393224 | tf_op jit(solution)/shard_map/ppermute | solution.py:67
  11.1 4.5 %collective-permute-start.5 = (bf16[8,64,128]{2,1,0:T(8,128)(2,1)S(1)}, bf16[8,64,128]{2,1,0:T(8,128)(2,1)S(1)}, u32[]{:S(2)}, u32[]{:S(2)}) collective-permute-start(bf16[8,64,128]{2,1,0:T(8,128)(2,1)S(1)} %fusion.18), channel_id=1, source_target_pairs={{0,16},{4,20},{8,24},{12,28},{1,17},{5,21},{9,25},{13,29},{2,18},{... | collective-permute-start | bytes 393224 | tf_op jit(solution)/shard_map/ppermute | solution.py:67
  15.6 1.3 %collective-permute-start.6 = (bf16[8,64,128]{2,1,0:T(8,128)(2,1)S(1)}, bf16[8,64,128]{2,1,0:T(8,128)(2,1)S(1)}, u32[]{:S(2)}, u32[]{:S(2)}) collective-permute-start(bf16[8,64,128]{2,1,0:T(8,128)(2,1)S(1)} %fusion.18), channel_id=1, source_target_pairs={{0,24},{4,28},{1,25},{5,29},{2,26},{6,30},{3,27},{7,31}} | collective-permute-start | bytes 393224 | tf_op jit(solution)/shard_map/ppermute | solution.py:67
  16.9 1.6 %collective-permute-start.1 = (bf16[512,1024]{1,0:T(8,128)(2,1)}, bf16[512,1024]{1,0:T(8,128)(2,1)}, u32[]{:S(2)}, u32[]{:S(2)}) collective-permute-start(bf16[512,1024]{1,0:T(8,128)(2,1)} %param.8), channel_id=1, source_target_pairs={{0,2},{1,3},{2,0},{3,1},{4,5},{5,4},{6,7},{7,6},{8,10},{9,11},{10,... | collective-permute-start | bytes 3145736 | tf_op jit(solution)/shard_map/ppermute | solution.py:37
  19.5 1.7 %collective-permute-done.6 = bf16[8,64,128]{2,1,0:T(8,128)(2,1)S(1)} collective-permute-done((bf16[8,64,128]{2,1,0:T(8,128)(2,1)S(1)}, bf16[8,64,128]{2,1,0:T(8,128)(2,1)S(1)}, u32[]{:S(2)}, u32[]{:S(2)}) %collective-permute-start.6) | collective-permute-done | bytes 131104 | tf_op jit(solution)/shard_map/ppermute | solution.py:67
  21.3 3.3 %fusion.7 = f32[1024,512]{0,1:T(8,128)S(1)} fusion(bf16[512,1024]{1,0:T(8,128)(2,1)} %param.8, bf16[1024,4096]{1,0:T(8,128)(2,1)} %param.9, s32[]{:T(128)S(6)} %select_n.61), kind=kOutput, calls=%fused_computation.8 | convolution fusion | flops 1073741824 | bytes 5242884 | tf_op jit(solution)/shard_map/dot_general | solution.py:21
  24.7 1.6 %collective-permute-start.2 = (bf16[512,1024]{1,0:T(8,128)(2,1)}, bf16[512,1024]{1,0:T(8,128)(2,1)S(1)}, u32[]{:S(2)}, u32[]{:S(2)}) collective-permute-start(bf16[512,1024]{1,0:T(8,128)(2,1)} %collective-permute-done), channel_id=1, source_target_pairs={{0,2},{1,3},{2,0},{3,1},{4,5},{5,4},{6,7},{7,6},{8,10},{9,11},{10,... | collective-permute-start | bytes 3145736 | tf_op jit(solution)/shard_map/ppermute | solution.py:38
  27.2 3.7 %fusion.5 = f32[1024,512]{0,1:T(8,128)S(1)} fusion(bf16[512,1024]{1,0:T(8,128)(2,1)} %collective-permute-done, bf16[1024,4096]{1,0:T(8,128)(2,1)} %param.9, s32[]{:T(128)S(6)} %select_n.63), kind=kOutput, calls=%fused_computation.6 | convolution fusion | flops 1073741824 | bytes 5242884 | tf_op jit(solution)/shard_map/dot_general | solution.py:21
  30.9 1.2 %collective-permute-done.1 = bf16[512,1024]{1,0:T(8,128)(2,1)} collective-permute-done((bf16[512,1024]{1,0:T(8,128)(2,1)}, bf16[512,1024]{1,0:T(8,128)(2,1)}, u32[]{:S(2)}, u32[]{:S(2)}) %collective-permute-start.1) | collective-permute-done | bytes 1048608 | tf_op jit(solution)/shard_map/ppermute | solution.py:37
  32.1 2.5 %fusion.3 = f32[1024,512]{0,1:T(8,128)S(1)} fusion(bf16[512,1024]{1,0:T(8,128)(2,1)} %collective-permute-done.1, bf16[1024,4096]{1,0:T(8,128)(2,1)S(1)} %bitcast.35, s32[]{:T(128)S(6)} %select_n.64), kind=kOutput, calls=%fused_computation.4 | convolution fusion | flops 1073741824 | bytes 5242884 | tf_op jit(solution)/shard_map/dot_general | solution.py:21
  34.6 8.6 %collective-permute-done.2 = bf16[512,1024]{1,0:T(8,128)(2,1)S(1)} collective-permute-done((bf16[512,1024]{1,0:T(8,128)(2,1)}, bf16[512,1024]{1,0:T(8,128)(2,1)S(1)}, u32[]{:S(2)}, u32[]{:S(2)}) %collective-permute-start.2) | collective-permute-done | bytes 1048608 | tf_op jit(solution)/shard_map/ppermute | solution.py:38
  43.2 1.3 %fusion.refs_3_ = bf16[512,1024]{1,0:T(8,128)(2,1)S(1)} fusion(f32[1024,512]{0,1:T(8,128)S(1)} %fusion.3, f32[1024,512]{0,1:T(8,128)S(1)} %fusion.7, f32[1024,512]{0,1:T(8,128)S(1)} %fusion.5, bf16[512,1024]{1,0:T(8,128)(2,1)S(1)} %collective-permute-done.2, bf16[1024,4096]{1,0:T(8,128)(2,1)S(1)} %bitcast.35, s32[]{:T(128)S(6)} %select_n.71), kind=kOutput, calls=%fused_computation.1 | convolution fusion | flops 1075838976 | bytes 10485764 | tf_op jit(solution)/shard_map/dot_general | solution.py:21
  45.1 1.5 %collective-permute-done.8 = bf16[8,128,128]{2,1,0:T(8,128)(2,1)S(1)} collective-permute-done((bf16[8,128,128]{2,1,0:T(8,128)(2,1)S(1)}, bf16[8,128,128]{2,1,0:T(8,128)(2,1)S(1)}, u32[]{:S(2)}, u32[]{:S(2)}) %collective-permute-start.8) | collective-permute-done | bytes 262176 | tf_op jit(solution)/shard_map/ppermute | solution.py:51
  46.7 1.3 %collective-permute-start.10 = (bf16[8,64,128]{2,1,0:T(8,128)(2,1)S(1)}, bf16[8,64,128]{2,1,0:T(8,128)(2,1)S(1)}, u32[]{:S(2)}, u32[]{:S(2)}) collective-permute-start(bf16[8,64,128]{2,1,0:T(8,128)(2,1)S(1)} %dynamic-slice_add_fusion), channel_id=1, source_target_pairs={{16,0},{20,4},{24,8},{28,12},{17,1},{21,5},{25,9},{29,13},{18,2},{... | collective-permute-start | bytes 393224 | tf_op jit(solution)/shard_map/ppermute | solution.py:67
  48.0 1.3 %collective-permute-start.11 = (bf16[8,64,128]{2,1,0:T(8,128)(2,1)S(1)}, bf16[8,64,128]{2,1,0:T(8,128)(2,1)S(1)}, u32[]{:S(2)}, u32[]{:S(2)}) collective-permute-start(bf16[8,64,128]{2,1,0:T(8,128)(2,1)S(1)} %dynamic-slice_add_fusion), channel_id=1, source_target_pairs={{24,0},{28,4},{25,1},{29,5},{26,2},{30,6},{27,3},{31,7}} | collective-permute-start | bytes 393224 | tf_op jit(solution)/shard_map/ppermute | solution.py:67
  49.3 1.3 %collective-permute-start.9 = (bf16[8,64,128]{2,1,0:T(8,128)(2,1)S(1)}, bf16[8,64,128]{2,1,0:T(8,128)(2,1)S(1)}, u32[]{:S(2)}, u32[]{:S(2)}) collective-permute-start(bf16[8,64,128]{2,1,0:T(8,128)(2,1)S(1)} %dynamic-slice_add_fusion), channel_id=1, source_target_pairs={{8,0},{12,4},{16,8},{20,12},{24,16},{28,20},{9,1},{13,5},{17,9},{2... | collective-permute-start | bytes 393224 | tf_op jit(solution)/shard_map/ppermute | solution.py:67
  50.6 8.0 %attention_part.1 = (bf16[512,1024]{1,0:T(8,128)(2,1)}, bf16[512,1024]{1,0:T(8,128)(2,1)}, bf16[512,1024]{1,0:T(8,128)(2,1)}) custom-call(bf16[512,1024]{1,0:T(8,128)(2,1)} %refs_0_.2, bf16[512,1024]{1,0:T(8,128)(2,1)} %refs_0_.3, bf16[512,1024]{1,0:T(8,128)(2,1)} %refs_1_.3, bf16[512,1024]{1,0:T(8,128)(2,1)} %copy-done.2, f32[1,8,128,128]{3,2,1,0:T(8,128)} %fusion.16.refs_4_), custom_call_target="tpu_custom_call" | custom-call | flops 3221225472 | bytes 7340032 | tf_op jit(solution)/shard_map/attention_part/pallas_call | solution.py:148
  58.6 2.0 %collective-permute-done.10 = bf16[8,64,128]{2,1,0:T(8,128)(2,1)S(1)} collective-permute-done((bf16[8,64,128]{2,1,0:T(8,128)(2,1)S(1)}, bf16[8,64,128]{2,1,0:T(8,128)(2,1)S(1)}, u32[]{:S(2)}, u32[]{:S(2)}) %collective-permute-start.10) | collective-permute-done | bytes 131104 | tf_op jit(solution)/shard_map/ppermute | solution.py:67
  60.6 1.6 %collective-permute-done.9 = bf16[8,64,128]{2,1,0:T(8,128)(2,1)S(1)} collective-permute-done((bf16[8,64,128]{2,1,0:T(8,128)(2,1)S(1)}, bf16[8,64,128]{2,1,0:T(8,128)(2,1)S(1)}, u32[]{:S(2)}, u32[]{:S(2)}) %collective-permute-start.9) | collective-permute-done | bytes 131104 | tf_op jit(solution)/shard_map/ppermute | solution.py:67
  62.4 1.5 %collective-permute-done.12 = f32[8,64,128]{2,1,0:T(8,128)S(1)} collective-permute-done((f32[8,64,128]{2,1,0:T(8,128)S(1)}, f32[8,64,128]{2,1,0:T(8,128)S(1)}, u32[]{:S(2)}, u32[]{:S(2)}) %collective-permute-start.12) | collective-permute-done | bytes 262176 | tf_op jit(solution)/shard_map/ppermute | solution.py:80
  64.8 5.0 %state_part.1 = (bf16[512,1024]{1,0:T(8,128)(2,1)}, bf16[512,1024]{1,0:T(8,128)(2,1)}) custom-call(bf16[512,1024]{1,0:T(8,128)(2,1)} %refs_0_.3, bf16[512,1024]{1,0:T(8,128)(2,1)} %refs_1_.3, f32[1,8,128,128]{3,2,1,0:T(8,128)} %fusion.17.refs_2_, bf16[512,1024]{1,0:T(8,128)(2,1)} %get-tuple-element.27.refs_3_, bf16[512,1024]{1,0:T(8,128)(2,1)} %get-tuple-element.28.refs_4_), custom_call_target="tpu_custom_call" | custom-call | flops 536870912 | bytes 6291456 | tf_op jit(solution)/shard_map/state_part/pallas_call | solution.py:169
  (33 shorter events, 5.1 us)
Async XLA Ops:
  0.6 1.6 %copy-start.1 = (bf16[512,1024]{1,0:T(8,128)(2,1)S(1)}, bf16[512,1024]{1,0:T(8,128)(2,1)}, u32[]{:S(2)}) copy-start(bf16[512,1024]{1,0:T(8,128)(2,1)} %refs_1_.3) | copy-start | bytes 3145732
  2.2 16.3 %copy-start = (bf16[512,1024]{1,0:T(8,128)(2,1)S(1)}, bf16[512,1024]{1,0:T(8,128)(2,1)}, u32[]{:S(2)}) copy-start(bf16[512,1024]{1,0:T(8,128)(2,1)} %refs_0_.2) | copy-start | bytes 3145732
  3.4 2.9 %collective-permute-start.3 = (bf16[8,128,128]{2,1,0:T(8,128)(2,1)}, bf16[8,128,128]{2,1,0:T(8,128)(2,1)S(1)}, u32[]{:S(2)}, u32[]{:S(2)}) collective-permute-start(bf16[8,128,128]{2,1,0:T(8,128)(2,1)} %convolution_convert_fusion.1), channel_id=1, source_target_pairs={{0,4},{4,0},{8,12},{12,8},{16,20},{20,16},{24,28},{28,24},{1,5},{5... | collective-permute-start | bytes 786440 | tf_op jit(solution)/shard_map/ppermute | solution.py:51
  3.9 20.8 %collective-permute-start = (bf16[512,1024]{1,0:T(8,128)(2,1)}, bf16[512,1024]{1,0:T(8,128)(2,1)}, u32[]{:S(2)}, u32[]{:S(2)}) collective-permute-start(bf16[512,1024]{1,0:T(8,128)(2,1)} %param.8), channel_id=1, source_target_pairs={{0,1},{1,0},{2,3},{3,2},{4,6},{5,7},{6,4},{7,5},{8,9},{9,8},{10,11... | collective-permute-start | bytes 3145736 | tf_op jit(solution)/shard_map/ppermute | solution.py:36
  7.4 11.7 %collective-permute-start.4 = (bf16[8,64,128]{2,1,0:T(8,128)(2,1)S(1)}, bf16[8,64,128]{2,1,0:T(8,128)(2,1)S(1)}, u32[]{:S(2)}, u32[]{:S(2)}) collective-permute-start(bf16[8,64,128]{2,1,0:T(8,128)(2,1)S(1)} %fusion.18), channel_id=1, source_target_pairs={{0,8},{4,12},{8,16},{12,20},{16,24},{20,28},{1,9},{5,13},{9,17},{1... | collective-permute-start | bytes 393224 | tf_op jit(solution)/shard_map/ppermute | solution.py:67
  11.1 8.4 %collective-permute-start.5 = (bf16[8,64,128]{2,1,0:T(8,128)(2,1)S(1)}, bf16[8,64,128]{2,1,0:T(8,128)(2,1)S(1)}, u32[]{:S(2)}, u32[]{:S(2)}) collective-permute-start(bf16[8,64,128]{2,1,0:T(8,128)(2,1)S(1)} %fusion.18), channel_id=1, source_target_pairs={{0,16},{4,20},{8,24},{12,28},{1,17},{5,21},{9,25},{13,29},{2,18},{... | collective-permute-start | bytes 393224 | tf_op jit(solution)/shard_map/ppermute | solution.py:67
  15.6 5.6 %collective-permute-start.6 = (bf16[8,64,128]{2,1,0:T(8,128)(2,1)S(1)}, bf16[8,64,128]{2,1,0:T(8,128)(2,1)S(1)}, u32[]{:S(2)}, u32[]{:S(2)}) collective-permute-start(bf16[8,64,128]{2,1,0:T(8,128)(2,1)S(1)} %fusion.18), channel_id=1, source_target_pairs={{0,24},{4,28},{1,25},{5,29},{2,26},{6,30},{3,27},{7,31}} | collective-permute-start | bytes 393224 | tf_op jit(solution)/shard_map/ppermute | solution.py:67
  16.9 15.2 %collective-permute-start.1 = (bf16[512,1024]{1,0:T(8,128)(2,1)}, bf16[512,1024]{1,0:T(8,128)(2,1)}, u32[]{:S(2)}, u32[]{:S(2)}) collective-permute-start(bf16[512,1024]{1,0:T(8,128)(2,1)} %param.8), channel_id=1, source_target_pairs={{0,2},{1,3},{2,0},{3,1},{4,5},{5,4},{6,7},{7,6},{8,10},{9,11},{10,... | collective-permute-start | bytes 3145736 | tf_op jit(solution)/shard_map/ppermute | solution.py:37
  21.3 5.0 %collective-permute-start.7 = (f32[8,64,128]{2,1,0:T(8,128)S(1)}, f32[8,64,128]{2,1,0:T(8,128)S(1)}, u32[]{:S(2)}, u32[]{:S(2)}) collective-permute-start(f32[8,64,128]{2,1,0:T(8,128)S(1)} %convert_add_fusion.1), channel_id=1, source_target_pairs={{0,4},{4,0},{8,12},{12,8},{16,20},{20,16},{24,28},{28,24},{1,5},{5... | collective-permute-start | bytes 786440 | tf_op jit(solution)/shard_map/ppermute | solution.py:80
  21.3 10.8 %slice-start = ((s8[8388608]{0:T(1024)(128)(4,1)}), s8[4194304]{0:T(1024)(128)(4,1)S(1)}, s32[]{:S(2)}) async-start(s8[8388608]{0:T(1024)(128)(4,1)} %bitcast.34), calls=%async_computation | async-start | bytes 8388608
  24.7 18.5 %collective-permute-start.2 = (bf16[512,1024]{1,0:T(8,128)(2,1)}, bf16[512,1024]{1,0:T(8,128)(2,1)S(1)}, u32[]{:S(2)}, u32[]{:S(2)}) collective-permute-start(bf16[512,1024]{1,0:T(8,128)(2,1)} %collective-permute-done), channel_id=1, source_target_pairs={{0,2},{1,3},{2,0},{3,1},{4,5},{5,4},{6,7},{7,6},{8,10},{9,11},{10,... | collective-permute-start | bytes 3145736 | tf_op jit(solution)/shard_map/ppermute | solution.py:38
  26.3 5.8 %slice-start.1 = ((s8[8388608]{0:T(1024)(128)(4,1)}), s8[4194304]{0:T(1024)(128)(4,1)S(1)}, s32[]{:S(2)}) async-start(s8[8388608]{0:T(1024)(128)(4,1)} %bitcast.34), calls=%async_computation.1 | async-start | bytes 8388608
  44.5 6.1 %copy-start.2 = (bf16[512,1024]{1,0:T(8,128)(2,1)}, bf16[512,1024]{1,0:T(8,128)(2,1)S(1)}, u32[]{:S(2)}) copy-start(bf16[512,1024]{1,0:T(8,128)(2,1)S(1)} %fusion.refs_3_) | copy-start | bytes 3145732
  45.0 1.6 %collective-permute-start.8 = (bf16[8,128,128]{2,1,0:T(8,128)(2,1)S(1)}, bf16[8,128,128]{2,1,0:T(8,128)(2,1)S(1)}, u32[]{:S(2)}, u32[]{:S(2)}) collective-permute-start(bf16[8,128,128]{2,1,0:T(8,128)(2,1)S(1)} %fusion.11), channel_id=1, source_target_pairs={{0,4},{4,0},{8,12},{12,8},{16,20},{20,16},{24,28},{28,24},{1,5},{5... | collective-permute-start | bytes 786440 | tf_op jit(solution)/shard_map/ppermute | solution.py:51
  46.7 13.9 %collective-permute-start.10 = (bf16[8,64,128]{2,1,0:T(8,128)(2,1)S(1)}, bf16[8,64,128]{2,1,0:T(8,128)(2,1)S(1)}, u32[]{:S(2)}, u32[]{:S(2)}) collective-permute-start(bf16[8,64,128]{2,1,0:T(8,128)(2,1)S(1)} %dynamic-slice_add_fusion), channel_id=1, source_target_pairs={{16,0},{20,4},{24,8},{28,12},{17,1},{21,5},{25,9},{29,13},{18,2},{... | collective-permute-start | bytes 393224 | tf_op jit(solution)/shard_map/ppermute | solution.py:67
  48.0 12.6 %collective-permute-start.11 = (bf16[8,64,128]{2,1,0:T(8,128)(2,1)S(1)}, bf16[8,64,128]{2,1,0:T(8,128)(2,1)S(1)}, u32[]{:S(2)}, u32[]{:S(2)}) collective-permute-start(bf16[8,64,128]{2,1,0:T(8,128)(2,1)S(1)} %dynamic-slice_add_fusion), channel_id=1, source_target_pairs={{24,0},{28,4},{25,1},{29,5},{26,2},{30,6},{27,3},{31,7}} | collective-permute-start | bytes 393224 | tf_op jit(solution)/shard_map/ppermute | solution.py:67
  49.3 13.0 %collective-permute-start.9 = (bf16[8,64,128]{2,1,0:T(8,128)(2,1)S(1)}, bf16[8,64,128]{2,1,0:T(8,128)(2,1)S(1)}, u32[]{:S(2)}, u32[]{:S(2)}) collective-permute-start(bf16[8,64,128]{2,1,0:T(8,128)(2,1)S(1)} %dynamic-slice_add_fusion), channel_id=1, source_target_pairs={{8,0},{12,4},{16,8},{20,12},{24,16},{28,20},{9,1},{13,5},{17,9},{2... | collective-permute-start | bytes 393224 | tf_op jit(solution)/shard_map/ppermute | solution.py:67
  62.3 1.6 %collective-permute-start.12 = (f32[8,64,128]{2,1,0:T(8,128)S(1)}, f32[8,64,128]{2,1,0:T(8,128)S(1)}, u32[]{:S(2)}, u32[]{:S(2)}) collective-permute-start(f32[8,64,128]{2,1,0:T(8,128)S(1)} %convert_add_fusion), channel_id=1, source_target_pairs={{0,4},{4,0},{8,12},{12,8},{16,20},{20,16},{24,28},{28,24},{1,5},{5... | collective-permute-start | bytes 786440 | tf_op jit(solution)/shard_map/ppermute | solution.py:80

commit v14 on v13

--- a/solution.py
+++ b/solution.py
@@ -58,25 +58,29 @@
             return [(2 * (z + step) + c, 2 * z + c) for z in range(chips - step) for c in range(2)]
         return [(2 * z + c, 2 * (z + step) + c) for z in range(chips - step) for c in range(2)]
 
-    if cover is not None:
-        mine, held = lax.optimization_barrier((mine, cover.args))
     others = jnp.zeros_like(mine)
-    if chips <= 4:
+    if cover is None and chips <= 4:
         sent = mine.astype(jnp.bfloat16)
         for step in range(1, chips):
             others = others + lax.ppermute(sent, "ctx", pairs(step)).astype(jnp.float32)
+        covered = None
     else:
         run = mine
         step = 1
+        held = cover.args if cover is not None else None
         while step < chips:
+            last = 2 * step >= chips
+            if last and cover is not None:
+                run, others, held = lax.optimization_barrier((run, others, held))
             got = lax.ppermute(run.astype(jnp.bfloat16), "ctx", pairs(step)).astype(jnp.float32)
+            if last and cover is not None:
+                covered = cover.fn(*held)
             run = run + got
             others = others + got
             step *= 2
-    covered = None
-    if cover is not None:
-        covered = cover.fn(*held)
-        others, covered = lax.optimization_barrier((others, covered))
+        covered = None if cover is None else covered
+        if cover is not None:
+            others, covered = lax.optimization_barrier((others, covered))
     theirs = lax.ppermute(others, "ctx", flip_pairs(ctx_size, 1))
     lower = jnp.where(core == 0, others, theirs)
     upper = jnp.where(core == 0, theirs, others)

time: 70.2 us -> 72.4 us (1.031)
  waiting for transfers between devices: 18.6 us -> 22.1 us
  starting transfers between devices: 19.7 us -> 18.5 us
    ppermute x0 -> x2, waiting for transfers between devices: none -> 7.11 us  [ctx_exclusive(): lax.ppermute(run.astype(jnp.bfloat16), 'ctx', pairs(step))]
    ppermute x6 -> x3, starting transfers between devices: 13.4 us -> 9.53 us  [ctx_exclusive(): others = others + lax.ppermute(sent, 'ctx', pairs(step)).astype(jnp.float32)]
    ppermute x6 -> x3, waiting for transfers between devices: 5.75 us -> 2.13 us  [ctx_exclusive(): others = others + lax.ppermute(sent, 'ctx', pairs(step)).astype(jnp.float32)]
    ppermute x0 -> x2, starting transfers between devices: none -> 2.58 us  [ctx_exclusive(): lax.ppermute(run.astype(jnp.bfloat16), 'ctx', pairs(step))]
  transfers between devices with their start and end apart: 13 -> 12, of which waited for: 8 -> 8; matrix products, arithmetic and copies ran while one was open for 17% -> 17% of each run, Pallas kernels for 11% -> 11%
where the time goes in v14:
time: 72.4 us; the launch traced here: 72 us
  waiting for transfers between devices  22.1 us (31%)
  starting transfers between devices  18.5 us (26%)
  Pallas kernels  13 us (18%)
  matrix products  12.5 us (17%)
  other arithmetic  3 us (4%)
  local copies, waits for them, and re-layouts  2.15 us (3%)
  between operations  0.88 us (1%)
    dot_general x4, matrix products, mm(): lax.dot_general(a, b, (((1,), (1,)), ((), ())), preferred_element_type=jn...  10.9 us
    ppermute x3, starting transfers between devices, ctx_exclusive(): others = others + lax.ppermute(sent, 'ctx', pairs(step)).astype(jnp.float32)  9.53 us
    ppermute x1, waiting for transfers between devices, project(): diag = lax.ppermute(to_relay, ('ctx', 'head'), route(2, 1))  8.61 us
    pallas_call x1, Pallas kernels, attention_part(): pl.pallas_call(lambda *refs: scores_kernel(scale, per_step, *refs), grid=...  8.03 us
    ppermute x2, waiting for transfers between devices, ctx_exclusive(): lax.ppermute(run.astype(jnp.bfloat16), 'ctx', pairs(step))  7.11 us
    pallas_call x1, Pallas kernels, state_part(): pl.pallas_call(lambda *refs: state_kernel(scale, per_step, *refs), grid=(...  4.96 us
    ppermute x2, starting transfers between devices, ctx_exclusive(): lax.ppermute(run.astype(jnp.bfloat16), 'ctx', pairs(step))  2.58 us
    ppermute x1, starting transfers between devices, project(): to_relay = lax.ppermute(og, ('ctx', 'head'), route(1, 2))  2.49 us
  transfers between devices with their start and end apart: 12, of which 8 were waited for; matrix products, arithmetic and copies ran while one was open for 17% of the time, Pallas kernels for 11%

profile of v14, /device:TPU:0, one launch (start us, length us, event | category | flops | bytes accessed | tf_op | source)
XLA Modules:
  0.0 72.0 jit_solution(1819076164205828301)
XLA Ops:
  0.6 1.6 %copy.18 = bf16[512,1024]{0,1:T(8,128)(2,1)S(1)} copy(bf16[512,1024]{1,0:T(8,128)(2,1)} %refs_0_.3) | data formatting | bytes 2097152 | tf_op jit(solution)/shard_map/reshape
  2.3 1.2 %convolution_convert_fusion.1 = bf16[8,128,128]{2,1,0:T(8,128)(2,1)} fusion(bf16[512,8,128]{0,2,1:T(8,128)(2,1)S(1)} %bitcast.33, bf16[512,1024]{1,0:T(8,128)(2,1)S(1)} %copy-done.1), kind=kOutput, calls=%fused_computation.11 | convolution fusion | flops 134348800 | bytes 2359296 | tf_op jit(solution)/shard_map/nshd,nshe->nhde/dot_general | solution.py:200
  3.9 2.5 %collective-permute-start = (bf16[512,1024]{1,0:T(8,128)(2,1)}, bf16[512,1024]{1,0:T(8,128)(2,1)}, u32[]{:S(2)}, u32[]{:S(2)}) collective-permute-start(bf16[512,1024]{1,0:T(8,128)(2,1)} %param.8), channel_id=1, source_target_pairs={{0,1},{1,0},{2,3},{3,2},{4,6},{5,7},{6,4},{7,5},{8,9},{9,8},{10,11... | collective-permute-start | bytes 3145736 | tf_op jit(solution)/shard_map/ppermute | solution.py:36
  6.4 1.0 %fusion.18 = bf16[8,64,128]{2,1,0:T(8,128)(2,1)S(1)} fusion(f32[8,128,128]{2,1,0:T(8,128)S(1)} %convert_element_type.50, s32[]{:T(128)S(6)} %select_n.66, bf16[8,128,128]{2,1,0:T(8,128)(2,1)} %convolution_convert_fusion.1), kind=kLoop, calls=%fused_computation.23 | loop fusion | flops 196608 | bytes 524292 | tf_op jit(solution)/shard_map/convert_element_type | solution.py:63
  7.4 3.7 %collective-permute-start.4 = (bf16[8,64,128]{2,1,0:T(8,128)(2,1)S(1)}, bf16[8,64,128]{2,1,0:T(8,128)(2,1)S(1)}, u32[]{:S(2)}, u32[]{:S(2)}) collective-permute-start(bf16[8,64,128]{2,1,0:T(8,128)(2,1)S(1)} %fusion.18), channel_id=1, source_target_pairs={{0,8},{4,12},{8,16},{12,20},{16,24},{20,28},{1,9},{5,13},{9,17},{1... | collective-permute-start | bytes 393224 | tf_op jit(solution)/shard_map/ppermute | solution.py:65
  11.1 4.5 %collective-permute-start.5 = (bf16[8,64,128]{2,1,0:T(8,128)(2,1)S(1)}, bf16[8,64,128]{2,1,0:T(8,128)(2,1)S(1)}, u32[]{:S(2)}, u32[]{:S(2)}) collective-permute-start(bf16[8,64,128]{2,1,0:T(8,128)(2,1)S(1)} %fusion.18), channel_id=1, source_target_pairs={{0,16},{4,20},{8,24},{12,28},{1,17},{5,21},{9,25},{13,29},{2,18},{... | collective-permute-start | bytes 393224 | tf_op jit(solution)/shard_map/ppermute | solution.py:65
  15.6 1.3 %collective-permute-start.6 = (bf16[8,64,128]{2,1,0:T(8,128)(2,1)S(1)}, bf16[8,64,128]{2,1,0:T(8,128)(2,1)S(1)}, u32[]{:S(2)}, u32[]{:S(2)}) collective-permute-start(bf16[8,64,128]{2,1,0:T(8,128)(2,1)S(1)} %fusion.18), channel_id=1, source_target_pairs={{0,24},{4,28},{1,25},{5,29},{2,26},{6,30},{3,27},{7,31}} | collective-permute-start | bytes 393224 | tf_op jit(solution)/shard_map/ppermute | solution.py:65
  16.9 1.6 %collective-permute-start.1 = (bf16[512,1024]{1,0:T(8,128)(2,1)}, bf16[512,1024]{1,0:T(8,128)(2,1)}, u32[]{:S(2)}, u32[]{:S(2)}) collective-permute-start(bf16[512,1024]{1,0:T(8,128)(2,1)} %param.8), channel_id=1, source_target_pairs={{0,2},{1,3},{2,0},{3,1},{4,5},{5,4},{6,7},{7,6},{8,10},{9,11},{10,... | collective-permute-start | bytes 3145736 | tf_op jit(solution)/shard_map/ppermute | solution.py:37
  19.5 1.7 %collective-permute-done.6 = bf16[8,64,128]{2,1,0:T(8,128)(2,1)S(1)} collective-permute-done((bf16[8,64,128]{2,1,0:T(8,128)(2,1)S(1)}, bf16[8,64,128]{2,1,0:T(8,128)(2,1)S(1)}, u32[]{:S(2)}, u32[]{:S(2)}) %collective-permute-start.6) | collective-permute-done | bytes 131104 | tf_op jit(solution)/shard_map/ppermute | solution.py:65
  21.3 3.3 %fusion.7 = f32[1024,512]{0,1:T(8,128)S(1)} fusion(bf16[512,1024]{1,0:T(8,128)(2,1)} %param.8, bf16[1024,4096]{1,0:T(8,128)(2,1)} %param.9, s32[]{:T(128)S(6)} %select_n.61), kind=kOutput, calls=%fused_computation.8 | convolution fusion | flops 1073741824 | bytes 5242884 | tf_op jit(solution)/shard_map/dot_general | solution.py:21
  24.7 1.6 %collective-permute-start.2 = (bf16[512,1024]{1,0:T(8,128)(2,1)}, bf16[512,1024]{1,0:T(8,128)(2,1)S(1)}, u32[]{:S(2)}, u32[]{:S(2)}) collective-permute-start(bf16[512,1024]{1,0:T(8,128)(2,1)} %collective-permute-done), channel_id=1, source_target_pairs={{0,2},{1,3},{2,0},{3,1},{4,5},{5,4},{6,7},{7,6},{8,10},{9,11},{10,... | collective-permute-start | bytes 3145736 | tf_op jit(solution)/shard_map/ppermute | solution.py:38
  27.2 3.7 %fusion.5 = f32[1024,512]{0,1:T(8,128)S(1)} fusion(bf16[512,1024]{1,0:T(8,128)(2,1)} %collective-permute-done, bf16[1024,4096]{1,0:T(8,128)(2,1)} %param.9, s32[]{:T(128)S(6)} %select_n.63), kind=kOutput, calls=%fused_computation.6 | convolution fusion | flops 1073741824 | bytes 5242884 | tf_op jit(solution)/shard_map/dot_general | solution.py:21
  30.9 1.2 %collective-permute-done.1 = bf16[512,1024]{1,0:T(8,128)(2,1)} collective-permute-done((bf16[512,1024]{1,0:T(8,128)(2,1)}, bf16[512,1024]{1,0:T(8,128)(2,1)}, u32[]{:S(2)}, u32[]{:S(2)}) %collective-permute-start.1) | collective-permute-done | bytes 1048608 | tf_op jit(solution)/shard_map/ppermute | solution.py:37
  32.1 2.5 %fusion.3 = f32[1024,512]{0,1:T(8,128)S(1)} fusion(bf16[512,1024]{1,0:T(8,128)(2,1)} %collective-permute-done.1, bf16[1024,4096]{1,0:T(8,128)(2,1)S(1)} %bitcast.35, s32[]{:T(128)S(6)} %select_n.64), kind=kOutput, calls=%fused_computation.4 | convolution fusion | flops 1073741824 | bytes 5242884 | tf_op jit(solution)/shard_map/dot_general | solution.py:21
  34.6 8.6 %collective-permute-done.2 = bf16[512,1024]{1,0:T(8,128)(2,1)S(1)} collective-permute-done((bf16[512,1024]{1,0:T(8,128)(2,1)}, bf16[512,1024]{1,0:T(8,128)(2,1)S(1)}, u32[]{:S(2)}, u32[]{:S(2)}) %collective-permute-start.2) | collective-permute-done | bytes 1048608 | tf_op jit(solution)/shard_map/ppermute | solution.py:38
  43.2 1.3 %fusion.refs_3_ = bf16[512,1024]{1,0:T(8,128)(2,1)S(1)} fusion(f32[1024,512]{0,1:T(8,128)S(1)} %fusion.3, f32[1024,512]{0,1:T(8,128)S(1)} %fusion.7, f32[1024,512]{0,1:T(8,128)S(1)} %fusion.5, bf16[512,1024]{1,0:T(8,128)(2,1)S(1)} %collective-permute-done.2, bf16[1024,4096]{1,0:T(8,128)(2,1)S(1)} %bitcast.35, s32[]{:T(128)S(6)} %select_n.71), kind=kOutput, calls=%fused_computation.1 | convolution fusion | flops 1075838976 | bytes 10485764 | tf_op jit(solution)/shard_map/dot_general | solution.py:21
  45.1 1.5 %collective-permute-done.8 = bf16[8,128,128]{2,1,0:T(8,128)(2,1)S(1)} collective-permute-done((bf16[8,128,128]{2,1,0:T(8,128)(2,1)S(1)}, bf16[8,128,128]{2,1,0:T(8,128)(2,1)S(1)}, u32[]{:S(2)}, u32[]{:S(2)}) %collective-permute-start.8) | collective-permute-done | bytes 262176 | tf_op jit(solution)/shard_map/ppermute | solution.py:51
  46.7 1.3 %collective-permute-start.9 = (bf16[8,64,128]{2,1,0:T(8,128)(2,1)S(1)}, bf16[8,64,128]{2,1,0:T(8,128)(2,1)S(1)}, u32[]{:S(2)}, u32[]{:S(2)}) collective-permute-start(bf16[8,64,128]{2,1,0:T(8,128)(2,1)S(1)} %fusion.19), channel_id=1, source_target_pairs={{8,0},{12,4},{16,8},{20,12},{24,16},{28,20},{9,1},{13,5},{17,9},{2... | collective-permute-start | bytes 393224 | tf_op jit(solution)/shard_map/ppermute | solution.py:75
  48.0 6.1 %collective-permute-done.9 = bf16[8,64,128]{2,1,0:T(8,128)(2,1)S(1)} collective-permute-done((bf16[8,64,128]{2,1,0:T(8,128)(2,1)S(1)}, bf16[8,64,128]{2,1,0:T(8,128)(2,1)S(1)}, u32[]{:S(2)}, u32[]{:S(2)}) %collective-permute-start.9) | collective-permute-done | bytes 131104 | tf_op jit(solution)/shard_map/ppermute | solution.py:75
  54.2 1.3 %collective-permute-start.10 = (bf16[8,64,128]{2,1,0:T(8,128)(2,1)S(1)}, bf16[8,64,128]{2,1,0:T(8,128)(2,1)S(1)}, u32[]{:S(2)}, u32[]{:S(2)}) collective-permute-start(bf16[8,64,128]{2,1,0:T(8,128)(2,1)S(1)} %get-tuple-element.21), channel_id=1, source_target_pairs={{16,0},{20,4},{24,8},{28,12},{17,1},{21,5},{25,9},{29,13},{18,2},{... | collective-permute-start | bytes 393224 | tf_op jit(solution)/shard_map/ppermute | solution.py:75
  55.5 8.0 %attention_part.1 = (bf16[512,1024]{1,0:T(8,128)(2,1)}, bf16[512,1024]{1,0:T(8,128)(2,1)}, bf16[512,1024]{1,0:T(8,128)(2,1)}) custom-call(bf16[512,1024]{1,0:T(8,128)(2,1)} %refs_0_.2, bf16[512,1024]{1,0:T(8,128)(2,1)} %refs_0_.3, bf16[512,1024]{1,0:T(8,128)(2,1)} %refs_1_.3, bf16[512,1024]{1,0:T(8,128)(2,1)} %copy-done.2, f32[1,8,128,128]{3,2,1,0:T(8,128)} %fusion.16.refs_4_), custom_call_target="tpu_custom_call" | custom-call | flops 3221225472 | bytes 7340032 | tf_op jit(solution)/shard_map/attention_part/pallas_call | solution.py:152
  63.5 1.0 %collective-permute-done.10 = bf16[8,64,128]{2,1,0:T(8,128)(2,1)S(1)} collective-permute-done((bf16[8,64,128]{2,1,0:T(8,128)(2,1)S(1)}, bf16[8,64,128]{2,1,0:T(8,128)(2,1)S(1)}, u32[]{:S(2)}, u32[]{:S(2)}) %collective-permute-start.10) | collective-permute-done | bytes 131104 | tf_op jit(solution)/shard_map/ppermute | solution.py:75
  64.6 1.5 %collective-permute-done.11 = f32[8,64,128]{2,1,0:T(8,128)S(1)} collective-permute-done((f32[8,64,128]{2,1,0:T(8,128)S(1)}, f32[8,64,128]{2,1,0:T(8,128)S(1)}, u32[]{:S(2)}, u32[]{:S(2)}) %collective-permute-start.11) | collective-permute-done | bytes 262176 | tf_op jit(solution)/shard_map/ppermute | solution.py:84
  67.0 5.0 %state_part.1 = (bf16[512,1024]{1,0:T(8,128)(2,1)}, bf16[512,1024]{1,0:T(8,128)(2,1)}) custom-call(bf16[512,1024]{1,0:T(8,128)(2,1)} %refs_0_.3, bf16[512,1024]{1,0:T(8,128)(2,1)} %refs_1_.3, f32[1,8,128,128]{3,2,1,0:T(8,128)} %fusion.17.refs_2_, bf16[512,1024]{1,0:T(8,128)(2,1)} %get-tuple-element.29.refs_3_, bf16[512,1024]{1,0:T(8,128)(2,1)} %get-tuple-element.30.refs_4_), custom_call_target="tpu_custom_call" | custom-call | flops 536870912 | bytes 6291456 | tf_op jit(solution)/shard_map/state_part/pallas_call | solution.py:173
  (32 shorter events, 4.2 us)
Async XLA Ops:
  0.6 1.6 %copy-start.1 = (bf16[512,1024]{1,0:T(8,128)(2,1)S(1)}, bf16[512,1024]{1,0:T(8,128)(2,1)}, u32[]{:S(2)}) copy-start(bf16[512,1024]{1,0:T(8,128)(2,1)} %refs_1_.3) | copy-start | bytes 3145732
  2.2 16.3 %copy-start = (bf16[512,1024]{1,0:T(8,128)(2,1)S(1)}, bf16[512,1024]{1,0:T(8,128)(2,1)}, u32[]{:S(2)}) copy-start(bf16[512,1024]{1,0:T(8,128)(2,1)} %refs_0_.2) | copy-start | bytes 3145732
  3.4 2.9 %collective-permute-start.3 = (bf16[8,128,128]{2,1,0:T(8,128)(2,1)}, bf16[8,128,128]{2,1,0:T(8,128)(2,1)S(1)}, u32[]{:S(2)}, u32[]{:S(2)}) collective-permute-start(bf16[8,128,128]{2,1,0:T(8,128)(2,1)} %convolution_convert_fusion.1), channel_id=1, source_target_pairs={{0,4},{4,0},{8,12},{12,8},{16,20},{20,16},{24,28},{28,24},{1,5},{5... | collective-permute-start | bytes 786440 | tf_op jit(solution)/shard_map/ppermute | solution.py:51
  3.9 20.8 %collective-permute-start = (bf16[512,1024]{1,0:T(8,128)(2,1)}, bf16[512,1024]{1,0:T(8,128)(2,1)}, u32[]{:S(2)}, u32[]{:S(2)}) collective-permute-start(bf16[512,1024]{1,0:T(8,128)(2,1)} %param.8), channel_id=1, source_target_pairs={{0,1},{1,0},{2,3},{3,2},{4,6},{5,7},{6,4},{7,5},{8,9},{9,8},{10,11... | collective-permute-start | bytes 3145736 | tf_op jit(solution)/shard_map/ppermute | solution.py:36
  7.4 11.7 %collective-permute-start.4 = (bf16[8,64,128]{2,1,0:T(8,128)(2,1)S(1)}, bf16[8,64,128]{2,1,0:T(8,128)(2,1)S(1)}, u32[]{:S(2)}, u32[]{:S(2)}) collective-permute-start(bf16[8,64,128]{2,1,0:T(8,128)(2,1)S(1)} %fusion.18), channel_id=1, source_target_pairs={{0,8},{4,12},{8,16},{12,20},{16,24},{20,28},{1,9},{5,13},{9,17},{1... | collective-permute-start | bytes 393224 | tf_op jit(solution)/shard_map/ppermute | solution.py:65
  11.1 8.4 %collective-permute-start.5 = (bf16[8,64,128]{2,1,0:T(8,128)(2,1)S(1)}, bf16[8,64,128]{2,1,0:T(8,128)(2,1)S(1)}, u32[]{:S(2)}, u32[]{:S(2)}) collective-permute-start(bf16[8,64,128]{2,1,0:T(8,128)(2,1)S(1)} %fusion.18), channel_id=1, source_target_pairs={{0,16},{4,20},{8,24},{12,28},{1,17},{5,21},{9,25},{13,29},{2,18},{... | collective-permute-start | bytes 393224 | tf_op jit(solution)/shard_map/ppermute | solution.py:65
  15.6 5.6 %collective-permute-start.6 = (bf16[8,64,128]{2,1,0:T(8,128)(2,1)S(1)}, bf16[8,64,128]{2,1,0:T(8,128)(2,1)S(1)}, u32[]{:S(2)}, u32[]{:S(2)}) collective-permute-start(bf16[8,64,128]{2,1,0:T(8,128)(2,1)S(1)} %fusion.18), channel_id=1, source_target_pairs={{0,24},{4,28},{1,25},{5,29},{2,26},{6,30},{3,27},{7,31}} | collective-permute-start | bytes 393224 | tf_op jit(solution)/shard_map/ppermute | solution.py:65
  16.9 15.2 %collective-permute-start.1 = (bf16[512,1024]{1,0:T(8,128)(2,1)}, bf16[512,1024]{1,0:T(8,128)(2,1)}, u32[]{:S(2)}, u32[]{:S(2)}) collective-permute-start(bf16[512,1024]{1,0:T(8,128)(2,1)} %param.8), channel_id=1, source_target_pairs={{0,2},{1,3},{2,0},{3,1},{4,5},{5,4},{6,7},{7,6},{8,10},{9,11},{10,... | collective-permute-start | bytes 3145736 | tf_op jit(solution)/shard_map/ppermute | solution.py:37
  21.3 5.0 %collective-permute-start.7 = (f32[8,64,128]{2,1,0:T(8,128)S(1)}, f32[8,64,128]{2,1,0:T(8,128)S(1)}, u32[]{:S(2)}, u32[]{:S(2)}) collective-permute-start(f32[8,64,128]{2,1,0:T(8,128)S(1)} %convert_add_fusion.1), channel_id=1, source_target_pairs={{0,4},{4,0},{8,12},{12,8},{16,20},{20,16},{24,28},{28,24},{1,5},{5... | collective-permute-start | bytes 786440 | tf_op jit(solution)/shard_map/ppermute | solution.py:84
  21.3 10.8 %slice-start = ((s8[8388608]{0:T(1024)(128)(4,1)}), s8[4194304]{0:T(1024)(128)(4,1)S(1)}, s32[]{:S(2)}) async-start(s8[8388608]{0:T(1024)(128)(4,1)} %bitcast.34), calls=%async_computation | async-start | bytes 8388608
  24.7 18.5 %collective-permute-start.2 = (bf16[512,1024]{1,0:T(8,128)(2,1)}, bf16[512,1024]{1,0:T(8,128)(2,1)S(1)}, u32[]{:S(2)}, u32[]{:S(2)}) collective-permute-start(bf16[512,1024]{1,0:T(8,128)(2,1)} %collective-permute-done), channel_id=1, source_target_pairs={{0,2},{1,3},{2,0},{3,1},{4,5},{5,4},{6,7},{7,6},{8,10},{9,11},{10,... | collective-permute-start | bytes 3145736 | tf_op jit(solution)/shard_map/ppermute | solution.py:38
  26.3 5.8 %slice-start.1 = ((s8[8388608]{0:T(1024)(128)(4,1)}), s8[4194304]{0:T(1024)(128)(4,1)S(1)}, s32[]{:S(2)}) async-start(s8[8388608]{0:T(1024)(128)(4,1)} %bitcast.34), calls=%async_computation.1 | async-start | bytes 8388608
  44.5 9.7 %copy-start.2 = (bf16[512,1024]{1,0:T(8,128)(2,1)}, bf16[512,1024]{1,0:T(8,128)(2,1)S(1)}, u32[]{:S(2)}) copy-start(bf16[512,1024]{1,0:T(8,128)(2,1)S(1)} %fusion.refs_3_) | copy-start | bytes 3145732
  45.0 1.6 %collective-permute-start.8 = (bf16[8,128,128]{2,1,0:T(8,128)(2,1)S(1)}, bf16[8,128,128]{2,1,0:T(8,128)(2,1)S(1)}, u32[]{:S(2)}, u32[]{:S(2)}) collective-permute-start(bf16[8,128,128]{2,1,0:T(8,128)(2,1)S(1)} %fusion.11), channel_id=1, source_target_pairs={{0,4},{4,0},{8,12},{12,8},{16,20},{20,16},{24,28},{28,24},{1,5},{5... | collective-permute-start | bytes 786440 | tf_op jit(solution)/shard_map/ppermute | solution.py:51
  46.7 7.4 %collective-permute-start.9 = (bf16[8,64,128]{2,1,0:T(8,128)(2,1)S(1)}, bf16[8,64,128]{2,1,0:T(8,128)(2,1)S(1)}, u32[]{:S(2)}, u32[]{:S(2)}) collective-permute-start(bf16[8,64,128]{2,1,0:T(8,128)(2,1)S(1)} %fusion.19), channel_id=1, source_target_pairs={{8,0},{12,4},{16,8},{20,12},{24,16},{28,20},{9,1},{13,5},{17,9},{2... | collective-permute-start | bytes 393224 | tf_op jit(solution)/shard_map/ppermute | solution.py:75
  54.2 10.3 %collective-permute-start.10 = (bf16[8,64,128]{2,1,0:T(8,128)(2,1)S(1)}, bf16[8,64,128]{2,1,0:T(8,128)(2,1)S(1)}, u32[]{:S(2)}, u32[]{:S(2)}) collective-permute-start(bf16[8,64,128]{2,1,0:T(8,128)(2,1)S(1)} %get-tuple-element.21), channel_id=1, source_target_pairs={{16,0},{20,4},{24,8},{28,12},{17,1},{21,5},{25,9},{29,13},{18,2},{... | collective-permute-start | bytes 393224 | tf_op jit(solution)/shard_map/ppermute | solution.py:75
  64.5 1.6 %collective-permute-start.11 = (f32[8,64,128]{2,1,0:T(8,128)S(1)}, f32[8,64,128]{2,1,0:T(8,128)S(1)}, u32[]{:S(2)}, u32[]{:S(2)}) collective-permute-start(f32[8,64,128]{2,1,0:T(8,128)S(1)} %convert_add_fusion), channel_id=1, source_target_pairs={{0,4},{4,0},{8,12},{12,8},{16,20},{20,16},{24,28},{28,24},{1,5},{5... | collective-permute-start | bytes 786440 | tf_op jit(solution)/shard_map/ppermute | solution.py:84

commit v15 on v13

--- a/solution.py
+++ b/solution.py
@@ -161,7 +161,7 @@
 
 
 def state_part(k, v, qg_state, parts, blocks, block_len, heads, scale):
-    per_step = 2 if heads % 2 == 0 else 1
+    per_step = 4 if heads % 4 == 0 else (2 if heads % 2 == 0 else 1)
     tok = pl.BlockSpec((block_len, DH * per_step), lambda n, h: (n, h))
     st = pl.BlockSpec((1, per_step, DH, DH), lambda n, h: (n, h, 0, 0))
     rows, width = k.shape

time: 70.2 us -> 69.1 us (0.984)
  Pallas kernels: 13 us -> 12 us
    pallas_call x1, Pallas kernels: 4.96 us -> 3.98 us  [state_part(): pl.pallas_call(lambda *refs: state_kernel(scale, per_step, *refs), grid=(...]
  transfers between devices with their start and end apart: 13 -> 13, of which waited for: 8 -> 8; matrix products, arithmetic and copies ran while one was open for 17% -> 17% of each run, Pallas kernels for 11% -> 12%
where the time goes in v15:
time: 69.1 us; the launch traced here: 68.8 us
  starting transfers between devices  19.7 us (29%)
  waiting for transfers between devices  18.6 us (27%)
  matrix products  12.5 us (18%)
  Pallas kernels  12 us (17%)
  other arithmetic  2.96 us (4%)
  local copies, waits for them, and re-layouts  2.15 us (3%)
  between operations  0.89 us (1%)
    ppermute x6, starting transfers between devices, ctx_exclusive(): others = others + lax.ppermute(sent, 'ctx', pairs(step)).astype(jnp.float32)  13.4 us
    dot_general x4, matrix products, mm(): lax.dot_general(a, b, (((1,), (1,)), ((), ())), preferred_element_type=jn...  10.9 us
    ppermute x1, waiting for transfers between devices, project(): diag = lax.ppermute(to_relay, ('ctx', 'head'), route(2, 1))  8.61 us
    pallas_call x1, Pallas kernels, attention_part(): pl.pallas_call(lambda *refs: scores_kernel(scale, per_step, *refs), grid=...  8.03 us
    ppermute x6, waiting for transfers between devices, ctx_exclusive(): others = others + lax.ppermute(sent, 'ctx', pairs(step)).astype(jnp.float32)  5.75 us
    pallas_call x1, Pallas kernels, state_part(): pl.pallas_call(lambda *refs: state_kernel(scale, per_step, *refs), grid=(...  3.98 us
    ppermute x1, starting transfers between devices, project(): to_relay = lax.ppermute(og, ('ctx', 'head'), route(1, 2))  2.49 us
    ppermute x1, starting transfers between devices, project(): diag = lax.ppermute(to_relay, ('ctx', 'head'), route(2, 1))  1.6 us
  transfers between devices with their start and end apart: 13, of which 8 were waited for; matrix products, arithmetic and copies ran while one was open for 17% of the time, Pallas kernels for 12%

profile of v15, /device:TPU:0, one launch (start us, length us, event | category | flops | bytes accessed | tf_op | source)
XLA Modules:
  0.0 68.8 jit_solution(16126760735049668558)
XLA Ops:
  0.6 1.6 %copy.18 = bf16[512,1024]{0,1:T(8,128)(2,1)S(1)} copy(bf16[512,1024]{1,0:T(8,128)(2,1)} %refs_0_.3) | data formatting | bytes 2097152 | tf_op jit(solution)/shard_map/reshape
  2.3 1.2 %convolution_convert_fusion.1 = bf16[8,128,128]{2,1,0:T(8,128)(2,1)} fusion(bf16[512,8,128]{0,2,1:T(8,128)(2,1)S(1)} %bitcast.33, bf16[512,1024]{1,0:T(8,128)(2,1)S(1)} %copy-done.1), kind=kOutput, calls=%fused_computation.11 | convolution fusion | flops 134348800 | bytes 2359296 | tf_op jit(solution)/shard_map/nshd,nshe->nhde/dot_general | solution.py:196
  3.9 2.5 %collective-permute-start = (bf16[512,1024]{1,0:T(8,128)(2,1)}, bf16[512,1024]{1,0:T(8,128)(2,1)}, u32[]{:S(2)}, u32[]{:S(2)}) collective-permute-start(bf16[512,1024]{1,0:T(8,128)(2,1)} %param.8), channel_id=1, source_target_pairs={{0,1},{1,0},{2,3},{3,2},{4,6},{5,7},{6,4},{7,5},{8,9},{9,8},{10,11... | collective-permute-start | bytes 3145736 | tf_op jit(solution)/shard_map/ppermute | solution.py:36
  7.4 3.7 %collective-permute-start.4 = (bf16[8,64,128]{2,1,0:T(8,128)(2,1)S(1)}, bf16[8,64,128]{2,1,0:T(8,128)(2,1)S(1)}, u32[]{:S(2)}, u32[]{:S(2)}) collective-permute-start(bf16[8,64,128]{2,1,0:T(8,128)(2,1)S(1)} %fusion.18), channel_id=1, source_target_pairs={{0,8},{4,12},{8,16},{12,20},{16,24},{20,28},{1,9},{5,13},{9,17},{1... | collective-permute-start | bytes 393224 | tf_op jit(solution)/shard_map/ppermute | solution.py:67
  11.1 4.5 %collective-permute-start.5 = (bf16[8,64,128]{2,1,0:T(8,128)(2,1)S(1)}, bf16[8,64,128]{2,1,0:T(8,128)(2,1)S(1)}, u32[]{:S(2)}, u32[]{:S(2)}) collective-permute-start(bf16[8,64,128]{2,1,0:T(8,128)(2,1)S(1)} %fusion.18), channel_id=1, source_target_pairs={{0,16},{4,20},{8,24},{12,28},{1,17},{5,21},{9,25},{13,29},{2,18},{... | collective-permute-start | bytes 393224 | tf_op jit(solution)/shard_map/ppermute | solution.py:67
  15.6 1.3 %collective-permute-start.6 = (bf16[8,64,128]{2,1,0:T(8,128)(2,1)S(1)}, bf16[8,64,128]{2,1,0:T(8,128)(2,1)S(1)}, u32[]{:S(2)}, u32[]{:S(2)}) collective-permute-start(bf16[8,64,128]{2,1,0:T(8,128)(2,1)S(1)} %fusion.18), channel_id=1, source_target_pairs={{0,24},{4,28},{1,25},{5,29},{2,26},{6,30},{3,27},{7,31}} | collective-permute-start | bytes 393224 | tf_op jit(solution)/shard_map/ppermute | solution.py:67
  16.9 1.6 %collective-permute-start.1 = (bf16[512,1024]{1,0:T(8,128)(2,1)}, bf16[512,1024]{1,0:T(8,128)(2,1)}, u32[]{:S(2)}, u32[]{:S(2)}) collective-permute-start(bf16[512,1024]{1,0:T(8,128)(2,1)} %param.8), channel_id=1, source_target_pairs={{0,2},{1,3},{2,0},{3,1},{4,5},{5,4},{6,7},{7,6},{8,10},{9,11},{10,... | collective-permute-start | bytes 3145736 | tf_op jit(solution)/shard_map/ppermute | solution.py:37
  19.5 1.7 %collective-permute-done.6 = bf16[8,64,128]{2,1,0:T(8,128)(2,1)S(1)} collective-permute-done((bf16[8,64,128]{2,1,0:T(8,128)(2,1)S(1)}, bf16[8,64,128]{2,1,0:T(8,128)(2,1)S(1)}, u32[]{:S(2)}, u32[]{:S(2)}) %collective-permute-start.6) | collective-permute-done | bytes 131104 | tf_op jit(solution)/shard_map/ppermute | solution.py:67
  21.3 3.3 %fusion.7 = f32[1024,512]{0,1:T(8,128)S(1)} fusion(bf16[512,1024]{1,0:T(8,128)(2,1)} %param.8, bf16[1024,4096]{1,0:T(8,128)(2,1)} %param.9, s32[]{:T(128)S(6)} %select_n.61), kind=kOutput, calls=%fused_computation.8 | convolution fusion | flops 1073741824 | bytes 5242884 | tf_op jit(solution)/shard_map/dot_general | solution.py:21
  24.7 1.6 %collective-permute-start.2 = (bf16[512,1024]{1,0:T(8,128)(2,1)}, bf16[512,1024]{1,0:T(8,128)(2,1)S(1)}, u32[]{:S(2)}, u32[]{:S(2)}) collective-permute-start(bf16[512,1024]{1,0:T(8,128)(2,1)} %collective-permute-done), channel_id=1, source_target_pairs={{0,2},{1,3},{2,0},{3,1},{4,5},{5,4},{6,7},{7,6},{8,10},{9,11},{10,... | collective-permute-start | bytes 3145736 | tf_op jit(solution)/shard_map/ppermute | solution.py:38
  27.2 3.7 %fusion.5 = f32[1024,512]{0,1:T(8,128)S(1)} fusion(bf16[512,1024]{1,0:T(8,128)(2,1)} %collective-permute-done, bf16[1024,4096]{1,0:T(8,128)(2,1)} %param.9, s32[]{:T(128)S(6)} %select_n.63), kind=kOutput, calls=%fused_computation.6 | convolution fusion | flops 1073741824 | bytes 5242884 | tf_op jit(solution)/shard_map/dot_general | solution.py:21
  30.9 1.2 %collective-permute-done.1 = bf16[512,1024]{1,0:T(8,128)(2,1)} collective-permute-done((bf16[512,1024]{1,0:T(8,128)(2,1)}, bf16[512,1024]{1,0:T(8,128)(2,1)}, u32[]{:S(2)}, u32[]{:S(2)}) %collective-permute-start.1) | collective-permute-done | bytes 1048608 | tf_op jit(solution)/shard_map/ppermute | solution.py:37
  32.1 2.5 %fusion.3 = f32[1024,512]{0,1:T(8,128)S(1)} fusion(bf16[512,1024]{1,0:T(8,128)(2,1)} %collective-permute-done.1, bf16[1024,4096]{1,0:T(8,128)(2,1)S(1)} %bitcast.35, s32[]{:T(128)S(6)} %select_n.64), kind=kOutput, calls=%fused_computation.4 | convolution fusion | flops 1073741824 | bytes 5242884 | tf_op jit(solution)/shard_map/dot_general | solution.py:21
  34.6 8.6 %collective-permute-done.2 = bf16[512,1024]{1,0:T(8,128)(2,1)S(1)} collective-permute-done((bf16[512,1024]{1,0:T(8,128)(2,1)}, bf16[512,1024]{1,0:T(8,128)(2,1)S(1)}, u32[]{:S(2)}, u32[]{:S(2)}) %collective-permute-start.2) | collective-permute-done | bytes 1048608 | tf_op jit(solution)/shard_map/ppermute | solution.py:38
  43.2 1.3 %fusion.refs_3_ = bf16[512,1024]{1,0:T(8,128)(2,1)S(1)} fusion(f32[1024,512]{0,1:T(8,128)S(1)} %fusion.3, f32[1024,512]{0,1:T(8,128)S(1)} %fusion.7, f32[1024,512]{0,1:T(8,128)S(1)} %fusion.5, bf16[512,1024]{1,0:T(8,128)(2,1)S(1)} %collective-permute-done.2, bf16[1024,4096]{1,0:T(8,128)(2,1)S(1)} %bitcast.35, s32[]{:T(128)S(6)} %select_n.71), kind=kOutput, calls=%fused_computation.1 | convolution fusion | flops 1075838976 | bytes 10485764 | tf_op jit(solution)/shard_map/dot_general | solution.py:21
  45.1 1.5 %collective-permute-done.8 = bf16[8,128,128]{2,1,0:T(8,128)(2,1)S(1)} collective-permute-done((bf16[8,128,128]{2,1,0:T(8,128)(2,1)S(1)}, bf16[8,128,128]{2,1,0:T(8,128)(2,1)S(1)}, u32[]{:S(2)}, u32[]{:S(2)}) %collective-permute-start.8) | collective-permute-done | bytes 262176 | tf_op jit(solution)/shard_map/ppermute | solution.py:51
  46.7 1.3 %collective-permute-start.10 = (bf16[8,64,128]{2,1,0:T(8,128)(2,1)S(1)}, bf16[8,64,128]{2,1,0:T(8,128)(2,1)S(1)}, u32[]{:S(2)}, u32[]{:S(2)}) collective-permute-start(bf16[8,64,128]{2,1,0:T(8,128)(2,1)S(1)} %dynamic-slice_add_fusion), channel_id=1, source_target_pairs={{16,0},{20,4},{24,8},{28,12},{17,1},{21,5},{25,9},{29,13},{18,2},{... | collective-permute-start | bytes 393224 | tf_op jit(solution)/shard_map/ppermute | solution.py:67
  48.0 1.3 %collective-permute-start.11 = (bf16[8,64,128]{2,1,0:T(8,128)(2,1)S(1)}, bf16[8,64,128]{2,1,0:T(8,128)(2,1)S(1)}, u32[]{:S(2)}, u32[]{:S(2)}) collective-permute-start(bf16[8,64,128]{2,1,0:T(8,128)(2,1)S(1)} %dynamic-slice_add_fusion), channel_id=1, source_target_pairs={{24,0},{28,4},{25,1},{29,5},{26,2},{30,6},{27,3},{31,7}} | collective-permute-start | bytes 393224 | tf_op jit(solution)/shard_map/ppermute | solution.py:67
  49.3 1.3 %collective-permute-start.9 = (bf16[8,64,128]{2,1,0:T(8,128)(2,1)S(1)}, bf16[8,64,128]{2,1,0:T(8,128)(2,1)S(1)}, u32[]{:S(2)}, u32[]{:S(2)}) collective-permute-start(bf16[8,64,128]{2,1,0:T(8,128)(2,1)S(1)} %dynamic-slice_add_fusion), channel_id=1, source_target_pairs={{8,0},{12,4},{16,8},{20,12},{24,16},{28,20},{9,1},{13,5},{17,9},{2... | collective-permute-start | bytes 393224 | tf_op jit(solution)/shard_map/ppermute | solution.py:67
  50.6 8.0 %attention_part.1 = (bf16[512,1024]{1,0:T(8,128)(2,1)}, bf16[512,1024]{1,0:T(8,128)(2,1)}, bf16[512,1024]{1,0:T(8,128)(2,1)}) custom-call(bf16[512,1024]{1,0:T(8,128)(2,1)} %refs_0_.2, bf16[512,1024]{1,0:T(8,128)(2,1)} %refs_0_.3, bf16[512,1024]{1,0:T(8,128)(2,1)} %refs_1_.3, bf16[512,1024]{1,0:T(8,128)(2,1)} %copy-done.2, f32[1,8,128,128]{3,2,1,0:T(8,128)} %fusion.16.refs_4_), custom_call_target="tpu_custom_call" | custom-call | flops 3221225472 | bytes 7340032 | tf_op jit(solution)/shard_map/attention_part/pallas_call | solution.py:148
  58.6 2.0 %collective-permute-done.10 = bf16[8,64,128]{2,1,0:T(8,128)(2,1)S(1)} collective-permute-done((bf16[8,64,128]{2,1,0:T(8,128)(2,1)S(1)}, bf16[8,64,128]{2,1,0:T(8,128)(2,1)S(1)}, u32[]{:S(2)}, u32[]{:S(2)}) %collective-permute-start.10) | collective-permute-done | bytes 131104 | tf_op jit(solution)/shard_map/ppermute | solution.py:67
  60.6 1.6 %collective-permute-done.9 = bf16[8,64,128]{2,1,0:T(8,128)(2,1)S(1)} collective-permute-done((bf16[8,64,128]{2,1,0:T(8,128)(2,1)S(1)}, bf16[8,64,128]{2,1,0:T(8,128)(2,1)S(1)}, u32[]{:S(2)}, u32[]{:S(2)}) %collective-permute-start.9) | collective-permute-done | bytes 131104 | tf_op jit(solution)/shard_map/ppermute | solution.py:67
  62.4 1.5 %collective-permute-done.12 = f32[8,64,128]{2,1,0:T(8,128)S(1)} collective-permute-done((f32[8,64,128]{2,1,0:T(8,128)S(1)}, f32[8,64,128]{2,1,0:T(8,128)S(1)}, u32[]{:S(2)}, u32[]{:S(2)}) %collective-permute-start.12) | collective-permute-done | bytes 262176 | tf_op jit(solution)/shard_map/ppermute | solution.py:80
  64.8 4.0 %state_part.1 = (bf16[512,1024]{1,0:T(8,128)(2,1)}, bf16[512,1024]{1,0:T(8,128)(2,1)}) custom-call(bf16[512,1024]{1,0:T(8,128)(2,1)} %refs_0_.3, bf16[512,1024]{1,0:T(8,128)(2,1)} %refs_1_.3, f32[1,8,128,128]{3,2,1,0:T(8,128)} %fusion.17.refs_2_, bf16[512,1024]{1,0:T(8,128)(2,1)} %get-tuple-element.27.refs_3_, bf16[512,1024]{1,0:T(8,128)(2,1)} %get-tuple-element.28.refs_4_), custom_call_target="tpu_custom_call" | custom-call | flops 536870912 | bytes 6291456 | tf_op jit(solution)/shard_map/state_part/pallas_call | solution.py:169
  (33 shorter events, 5.1 us)
Async XLA Ops:
  0.6 1.6 %copy-start.1 = (bf16[512,1024]{1,0:T(8,128)(2,1)S(1)}, bf16[512,1024]{1,0:T(8,128)(2,1)}, u32[]{:S(2)}) copy-start(bf16[512,1024]{1,0:T(8,128)(2,1)} %refs_1_.3) | copy-start | bytes 3145732
  2.2 16.3 %copy-start = (bf16[512,1024]{1,0:T(8,128)(2,1)S(1)}, bf16[512,1024]{1,0:T(8,128)(2,1)}, u32[]{:S(2)}) copy-start(bf16[512,1024]{1,0:T(8,128)(2,1)} %refs_0_.2) | copy-start | bytes 3145732
  3.4 2.9 %collective-permute-start.3 = (bf16[8,128,128]{2,1,0:T(8,128)(2,1)}, bf16[8,128,128]{2,1,0:T(8,128)(2,1)S(1)}, u32[]{:S(2)}, u32[]{:S(2)}) collective-permute-start(bf16[8,128,128]{2,1,0:T(8,128)(2,1)} %convolution_convert_fusion.1), channel_id=1, source_target_pairs={{0,4},{4,0},{8,12},{12,8},{16,20},{20,16},{24,28},{28,24},{1,5},{5... | collective-permute-start | bytes 786440 | tf_op jit(solution)/shard_map/ppermute | solution.py:51
  3.9 20.8 %collective-permute-start = (bf16[512,1024]{1,0:T(8,128)(2,1)}, bf16[512,1024]{1,0:T(8,128)(2,1)}, u32[]{:S(2)}, u32[]{:S(2)}) collective-permute-start(bf16[512,1024]{1,0:T(8,128)(2,1)} %param.8), channel_id=1, source_target_pairs={{0,1},{1,0},{2,3},{3,2},{4,6},{5,7},{6,4},{7,5},{8,9},{9,8},{10,11... | collective-permute-start | bytes 3145736 | tf_op jit(solution)/shard_map/ppermute | solution.py:36
  7.4 11.7 %collective-permute-start.4 = (bf16[8,64,128]{2,1,0:T(8,128)(2,1)S(1)}, bf16[8,64,128]{2,1,0:T(8,128)(2,1)S(1)}, u32[]{:S(2)}, u32[]{:S(2)}) collective-permute-start(bf16[8,64,128]{2,1,0:T(8,128)(2,1)S(1)} %fusion.18), channel_id=1, source_target_pairs={{0,8},{4,12},{8,16},{12,20},{16,24},{20,28},{1,9},{5,13},{9,17},{1... | collective-permute-start | bytes 393224 | tf_op jit(solution)/shard_map/ppermute | solution.py:67
  11.1 8.4 %collective-permute-start.5 = (bf16[8,64,128]{2,1,0:T(8,128)(2,1)S(1)}, bf16[8,64,128]{2,1,0:T(8,128)(2,1)S(1)}, u32[]{:S(2)}, u32[]{:S(2)}) collective-permute-start(bf16[8,64,128]{2,1,0:T(8,128)(2,1)S(1)} %fusion.18), channel_id=1, source_target_pairs={{0,16},{4,20},{8,24},{12,28},{1,17},{5,21},{9,25},{13,29},{2,18},{... | collective-permute-start | bytes 393224 | tf_op jit(solution)/shard_map/ppermute | solution.py:67
  15.6 5.6 %collective-permute-start.6 = (bf16[8,64,128]{2,1,0:T(8,128)(2,1)S(1)}, bf16[8,64,128]{2,1,0:T(8,128)(2,1)S(1)}, u32[]{:S(2)}, u32[]{:S(2)}) collective-permute-start(bf16[8,64,128]{2,1,0:T(8,128)(2,1)S(1)} %fusion.18), channel_id=1, source_target_pairs={{0,24},{4,28},{1,25},{5,29},{2,26},{6,30},{3,27},{7,31}} | collective-permute-start | bytes 393224 | tf_op jit(solution)/shard_map/ppermute | solution.py:67
  16.9 15.2 %collective-permute-start.1 = (bf16[512,1024]{1,0:T(8,128)(2,1)}, bf16[512,1024]{1,0:T(8,128)(2,1)}, u32[]{:S(2)}, u32[]{:S(2)}) collective-permute-start(bf16[512,1024]{1,0:T(8,128)(2,1)} %param.8), channel_id=1, source_target_pairs={{0,2},{1,3},{2,0},{3,1},{4,5},{5,4},{6,7},{7,6},{8,10},{9,11},{10,... | collective-permute-start | bytes 3145736 | tf_op jit(solution)/shard_map/ppermute | solution.py:37
  21.3 5.0 %collective-permute-start.7 = (f32[8,64,128]{2,1,0:T(8,128)S(1)}, f32[8,64,128]{2,1,0:T(8,128)S(1)}, u32[]{:S(2)}, u32[]{:S(2)}) collective-permute-start(f32[8,64,128]{2,1,0:T(8,128)S(1)} %convert_add_fusion.1), channel_id=1, source_target_pairs={{0,4},{4,0},{8,12},{12,8},{16,20},{20,16},{24,28},{28,24},{1,5},{5... | collective-permute-start | bytes 786440 | tf_op jit(solution)/shard_map/ppermute | solution.py:80
  21.3 10.8 %slice-start = ((s8[8388608]{0:T(1024)(128)(4,1)}), s8[4194304]{0:T(1024)(128)(4,1)S(1)}, s32[]{:S(2)}) async-start(s8[8388608]{0:T(1024)(128)(4,1)} %bitcast.34), calls=%async_computation | async-start | bytes 8388608
  24.7 18.5 %collective-permute-start.2 = (bf16[512,1024]{1,0:T(8,128)(2,1)}, bf16[512,1024]{1,0:T(8,128)(2,1)S(1)}, u32[]{:S(2)}, u32[]{:S(2)}) collective-permute-start(bf16[512,1024]{1,0:T(8,128)(2,1)} %collective-permute-done), channel_id=1, source_target_pairs={{0,2},{1,3},{2,0},{3,1},{4,5},{5,4},{6,7},{7,6},{8,10},{9,11},{10,... | collective-permute-start | bytes 3145736 | tf_op jit(solution)/shard_map/ppermute | solution.py:38
  26.3 5.8 %slice-start.1 = ((s8[8388608]{0:T(1024)(128)(4,1)}), s8[4194304]{0:T(1024)(128)(4,1)S(1)}, s32[]{:S(2)}) async-start(s8[8388608]{0:T(1024)(128)(4,1)} %bitcast.34), calls=%async_computation.1 | async-start | bytes 8388608
  44.5 6.1 %copy-start.2 = (bf16[512,1024]{1,0:T(8,128)(2,1)}, bf16[512,1024]{1,0:T(8,128)(2,1)S(1)}, u32[]{:S(2)}) copy-start(bf16[512,1024]{1,0:T(8,128)(2,1)S(1)} %fusion.refs_3_) | copy-start | bytes 3145732
  45.0 1.6 %collective-permute-start.8 = (bf16[8,128,128]{2,1,0:T(8,128)(2,1)S(1)}, bf16[8,128,128]{2,1,0:T(8,128)(2,1)S(1)}, u32[]{:S(2)}, u32[]{:S(2)}) collective-permute-start(bf16[8,128,128]{2,1,0:T(8,128)(2,1)S(1)} %fusion.11), channel_id=1, source_target_pairs={{0,4},{4,0},{8,12},{12,8},{16,20},{20,16},{24,28},{28,24},{1,5},{5... | collective-permute-start | bytes 786440 | tf_op jit(solution)/shard_map/ppermute | solution.py:51
  46.7 13.9 %collective-permute-start.10 = (bf16[8,64,128]{2,1,0:T(8,128)(2,1)S(1)}, bf16[8,64,128]{2,1,0:T(8,128)(2,1)S(1)}, u32[]{:S(2)}, u32[]{:S(2)}) collective-permute-start(bf16[8,64,128]{2,1,0:T(8,128)(2,1)S(1)} %dynamic-slice_add_fusion), channel_id=1, source_target_pairs={{16,0},{20,4},{24,8},{28,12},{17,1},{21,5},{25,9},{29,13},{18,2},{... | collective-permute-start | bytes 393224 | tf_op jit(solution)/shard_map/ppermute | solution.py:67
  48.0 12.6 %collective-permute-start.11 = (bf16[8,64,128]{2,1,0:T(8,128)(2,1)S(1)}, bf16[8,64,128]{2,1,0:T(8,128)(2,1)S(1)}, u32[]{:S(2)}, u32[]{:S(2)}) collective-permute-start(bf16[8,64,128]{2,1,0:T(8,128)(2,1)S(1)} %dynamic-slice_add_fusion), channel_id=1, source_target_pairs={{24,0},{28,4},{25,1},{29,5},{26,2},{30,6},{27,3},{31,7}} | collective-permute-start | bytes 393224 | tf_op jit(solution)/shard_map/ppermute | solution.py:67
  49.3 13.0 %collective-permute-start.9 = (bf16[8,64,128]{2,1,0:T(8,128)(2,1)S(1)}, bf16[8,64,128]{2,1,0:T(8,128)(2,1)S(1)}, u32[]{:S(2)}, u32[]{:S(2)}) collective-permute-start(bf16[8,64,128]{2,1,0:T(8,128)(2,1)S(1)} %dynamic-slice_add_fusion), channel_id=1, source_target_pairs={{8,0},{12,4},{16,8},{20,12},{24,16},{28,20},{9,1},{13,5},{17,9},{2... | collective-permute-start | bytes 393224 | tf_op jit(solution)/shard_map/ppermute | solution.py:67
  62.3 1.6 %collective-permute-start.12 = (f32[8,64,128]{2,1,0:T(8,128)S(1)}, f32[8,64,128]{2,1,0:T(8,128)S(1)}, u32[]{:S(2)}, u32[]{:S(2)}) collective-permute-start(f32[8,64,128]{2,1,0:T(8,128)S(1)} %convert_add_fusion), channel_id=1, source_target_pairs={{0,4},{4,0},{8,12},{12,8},{16,20},{20,16},{24,28},{28,24},{1,5},{5... | collective-permute-start | bytes 786440 | tf_op jit(solution)/shard_map/ppermute | solution.py:80

commit v16 on v15

--- a/solution.py
+++ b/solution.py
@@ -44,7 +44,7 @@
     return acc, tied
 
 
-def ctx_exclusive(state, ctx_size, reverse, cover=None):
+def ctx_exclusive(state, ctx_size, reverse, cover=None, direct=True):
     core = lax.axis_index("ctx") % 2
     chips = ctx_size // 2
     rounded = state.astype(jnp.bfloat16)
@@ -61,7 +61,7 @@
     if cover is not None:
         mine, held = lax.optimization_barrier((mine, cover.args))
     others = jnp.zeros_like(mine)
-    if chips <= 4:
+    if chips <= 4 and direct:
         sent = mine.astype(jnp.bfloat16)
         for step in range(1, chips):
             others = others + lax.ppermute(sent, "ctx", pairs(step)).astype(jnp.float32)
@@ -198,7 +198,7 @@
             preferred_element_type=jnp.float32,
         )
         kv_running = jnp.cumsum(kv_blocks, axis=0)
-        kv_before, _ = ctx_exclusive(kv_running[-1], ctx_size, False)
+        kv_before, _ = ctx_exclusive(kv_running[-1], ctx_size, False, direct=False)
         if blocks == 1:
             kv_entry = kv_before[None]
         else:

time: 69.1 us -> 74.7 us (1.081)
  waiting for transfers between devices: 18.6 us -> 23.6 us
  other arithmetic: 2.96 us -> 3.92 us
    ppermute x6 -> x3, starting transfers between devices: 13.4 us -> 3.88 us  [ctx_exclusive(): others = others + lax.ppermute(sent, 'ctx', pairs(step)).astype(jnp.float32)]
    ppermute x0 -> x2, starting transfers between devices: none -> 9.15 us  [ctx_exclusive(): lax.ppermute(run.astype(jnp.bfloat16), 'ctx', pairs(step))]
    ppermute x0 -> x2, waiting for transfers between devices: none -> 3.38 us  [ctx_exclusive(): lax.ppermute(run.astype(jnp.bfloat16), 'ctx', pairs(step))]
    ppermute x1, waiting for transfers between devices: 1.16 us -> 2.98 us  [project(): kept = lax.ppermute(og, ('ctx', 'head'), route(2, 1))]
    convert_element_type x1 -> x2, other arithmetic: 0.95 us -> 1.91 us  [ctx_exclusive(): run.astype(jnp.bfloat16)]
    ppermute x6 -> x3, waiting for transfers between devices: 5.75 us -> 5.6 us  [ctx_exclusive(): others = others + lax.ppermute(sent, 'ctx', pairs(step)).astype(jnp.float32)]
  transfers between devices with their start and end apart: 13 -> 12, of which waited for: 8 -> 7; matrix products, arithmetic and copies ran while one was open for 17% -> 17% of each run, Pallas kernels for 12% -> 11%
where the time goes in v16:
time: 74.7 us; the launch traced here: 74.4 us
  waiting for transfers between devices  23.6 us (32%)
  starting transfers between devices  19.3 us (26%)
  matrix products  12.5 us (17%)
  Pallas kernels  12 us (16%)
  other arithmetic  3.92 us (5%)
  local copies, waits for them, and re-layouts  2.15 us (3%)
  between operations  0.88 us (1%)
    dot_general x4, matrix products, mm(): lax.dot_general(a, b, (((1,), (1,)), ((), ())), preferred_element_type=jn...  10.9 us
    ppermute x2, starting transfers between devices, ctx_exclusive(): lax.ppermute(run.astype(jnp.bfloat16), 'ctx', pairs(step))  9.15 us
    ppermute x1, waiting for transfers between devices, project(): diag = lax.ppermute(to_relay, ('ctx', 'head'), route(2, 1))  8.61 us
    pallas_call x1, Pallas kernels, attention_part(): pl.pallas_call(lambda *refs: scores_kernel(scale, per_step, *refs), grid=...  8.03 us
    ppermute x3, waiting for transfers between devices, ctx_exclusive(): others = others + lax.ppermute(sent, 'ctx', pairs(step)).astype(jnp.float32)  5.6 us
    pallas_call x1, Pallas kernels, state_part(): pl.pallas_call(lambda *refs: state_kernel(scale, per_step, *refs), grid=(...  3.99 us
    ppermute x3, starting transfers between devices, ctx_exclusive(): others = others + lax.ppermute(sent, 'ctx', pairs(step)).astype(jnp.float32)  3.88 us
    ppermute x2, waiting for transfers between devices, ctx_exclusive(): lax.ppermute(run.astype(jnp.bfloat16), 'ctx', pairs(step))  3.38 us
  transfers between devices with their start and end apart: 12, of which 7 were waited for; matrix products, arithmetic and copies ran while one was open for 17% of the time, Pallas kernels for 11%

profile of v16, /device:TPU:0, one launch (start us, length us, event | category | flops | bytes accessed | tf_op | source)
XLA Modules:
  0.0 74.4 jit_solution(4894670036253148794)
XLA Ops:
  0.6 1.6 %copy.18 = bf16[512,1024]{0,1:T(8,128)(2,1)S(1)} copy(bf16[512,1024]{1,0:T(8,128)(2,1)} %refs_0_.3) | data formatting | bytes 2097152 | tf_op jit(solution)/shard_map/reshape
  2.3 1.2 %convolution_convert_fusion.1 = bf16[8,128,128]{2,1,0:T(8,128)(2,1)} fusion(bf16[512,8,128]{0,2,1:T(8,128)(2,1)S(1)} %bitcast.33, bf16[512,1024]{1,0:T(8,128)(2,1)S(1)} %copy-done.1), kind=kOutput, calls=%fused_computation.11 | convolution fusion | flops 134348800 | bytes 2359296 | tf_op jit(solution)/shard_map/nshd,nshe->nhde/dot_general | solution.py:196
  3.9 2.5 %collective-permute-start = (bf16[512,1024]{1,0:T(8,128)(2,1)}, bf16[512,1024]{1,0:T(8,128)(2,1)}, u32[]{:S(2)}, u32[]{:S(2)}) collective-permute-start(bf16[512,1024]{1,0:T(8,128)(2,1)} %param.8), channel_id=1, source_target_pairs={{0,1},{1,0},{2,3},{3,2},{4,6},{5,7},{6,4},{7,5},{8,9},{9,8},{10,11... | collective-permute-start | bytes 3145736 | tf_op jit(solution)/shard_map/ppermute | solution.py:36
  6.4 1.0 %fusion.19 = bf16[8,64,128]{2,1,0:T(8,128)(2,1)S(1)} fusion(f32[8,128,128]{2,1,0:T(8,128)S(1)} %convert_element_type.50, s32[]{:T(128)S(6)} %select_n.66, bf16[8,128,128]{2,1,0:T(8,128)(2,1)} %convolution_convert_fusion.1), kind=kLoop, calls=%fused_computation.27 | loop fusion | flops 196608 | bytes 524292 | tf_op jit(solution)/shard_map/convert_element_type | solution.py:72
  7.4 3.7 %collective-permute-start.4 = (bf16[8,64,128]{2,1,0:T(8,128)(2,1)S(1)}, bf16[8,64,128]{2,1,0:T(8,128)(2,1)S(1)}, u32[]{:S(2)}, u32[]{:S(2)}) collective-permute-start(bf16[8,64,128]{2,1,0:T(8,128)(2,1)S(1)} %fusion.19), channel_id=1, source_target_pairs={{0,8},{4,12},{8,16},{12,20},{16,24},{20,28},{1,9},{5,13},{9,17},{1... | collective-permute-start | bytes 393224 | tf_op jit(solution)/shard_map/ppermute | solution.py:72
  11.1 3.0 %collective-permute-done.4 = bf16[8,64,128]{2,1,0:T(8,128)(2,1)S(1)} collective-permute-done((bf16[8,64,128]{2,1,0:T(8,128)(2,1)S(1)}, bf16[8,64,128]{2,1,0:T(8,128)(2,1)S(1)}, u32[]{:S(2)}, u32[]{:S(2)}) %collective-permute-start.4) | collective-permute-done | bytes 131104 | tf_op jit(solution)/shard_map/ppermute | solution.py:72
  14.1 1.0 %fusion.18 = bf16[8,64,128]{2,1,0:T(8,128)(2,1)S(1)} fusion(bf16[8,64,128]{2,1,0:T(8,128)(2,1)S(1)} %collective-permute-done.4, f32[8,128,128]{2,1,0:T(8,128)S(1)} %convert_element_type.50, s32[]{:T(128)S(6)} %select_n.66, bf16[8,128,128]{2,1,0:T(8,128)(2,1)} %convolution_convert_fusion.1), kind=kLoop, calls=%fused_computation.23 | loop fusion | flops 327680 | bytes 655364 | tf_op jit(solution)/shard_map/convert_element_type | solution.py:72
  15.1 5.4 %collective-permute-start.5 = (bf16[8,64,128]{2,1,0:T(8,128)(2,1)S(1)}, bf16[8,64,128]{2,1,0:T(8,128)(2,1)S(1)}, u32[]{:S(2)}, u32[]{:S(2)}) collective-permute-start(bf16[8,64,128]{2,1,0:T(8,128)(2,1)S(1)} %fusion.18), channel_id=1, source_target_pairs={{0,16},{4,20},{8,24},{12,28},{1,17},{5,21},{9,25},{13,29},{2,18},{... | collective-permute-start | bytes 393224 | tf_op jit(solution)/shard_map/ppermute | solution.py:72
  20.5 1.6 %collective-permute-start.1 = (bf16[512,1024]{1,0:T(8,128)(2,1)}, bf16[512,1024]{1,0:T(8,128)(2,1)}, u32[]{:S(2)}, u32[]{:S(2)}) collective-permute-start(bf16[512,1024]{1,0:T(8,128)(2,1)} %param.8), channel_id=1, source_target_pairs={{0,2},{1,3},{2,0},{3,1},{4,5},{5,4},{6,7},{7,6},{8,10},{9,11},{10,... | collective-permute-start | bytes 3145736 | tf_op jit(solution)/shard_map/ppermute | solution.py:37
  23.1 3.3 %fusion.7 = f32[1024,512]{0,1:T(8,128)S(1)} fusion(bf16[512,1024]{1,0:T(8,128)(2,1)} %param.8, bf16[1024,4096]{1,0:T(8,128)(2,1)} %param.9, s32[]{:T(128)S(6)} %select_n.61), kind=kOutput, calls=%fused_computation.8 | convolution fusion | flops 1073741824 | bytes 5242884 | tf_op jit(solution)/shard_map/dot_general | solution.py:21
  26.5 1.6 %collective-permute-start.2 = (bf16[512,1024]{1,0:T(8,128)(2,1)}, bf16[512,1024]{1,0:T(8,128)(2,1)S(1)}, u32[]{:S(2)}, u32[]{:S(2)}) collective-permute-start(bf16[512,1024]{1,0:T(8,128)(2,1)} %collective-permute-done), channel_id=1, source_target_pairs={{0,2},{1,3},{2,0},{3,1},{4,5},{5,4},{6,7},{7,6},{8,10},{9,11},{10,... | collective-permute-start | bytes 3145736 | tf_op jit(solution)/shard_map/ppermute | solution.py:38
  29.0 3.7 %fusion.5 = f32[1024,512]{0,1:T(8,128)S(1)} fusion(bf16[512,1024]{1,0:T(8,128)(2,1)} %collective-permute-done, bf16[1024,4096]{1,0:T(8,128)(2,1)} %param.9, s32[]{:T(128)S(6)} %select_n.63), kind=kOutput, calls=%fused_computation.6 | convolution fusion | flops 1073741824 | bytes 5242884 | tf_op jit(solution)/shard_map/dot_general | solution.py:21
  32.7 3.0 %collective-permute-done.1 = bf16[512,1024]{1,0:T(8,128)(2,1)} collective-permute-done((bf16[512,1024]{1,0:T(8,128)(2,1)}, bf16[512,1024]{1,0:T(8,128)(2,1)}, u32[]{:S(2)}, u32[]{:S(2)}) %collective-permute-start.1) | collective-permute-done | bytes 1048608 | tf_op jit(solution)/shard_map/ppermute | solution.py:37
  35.7 2.5 %fusion.3 = f32[1024,512]{0,1:T(8,128)S(1)} fusion(bf16[512,1024]{1,0:T(8,128)(2,1)} %collective-permute-done.1, bf16[1024,4096]{1,0:T(8,128)(2,1)S(1)} %bitcast.35, s32[]{:T(128)S(6)} %select_n.64), kind=kOutput, calls=%fused_computation.4 | convolution fusion | flops 1073741824 | bytes 5242884 | tf_op jit(solution)/shard_map/dot_general | solution.py:21
  38.2 8.6 %collective-permute-done.2 = bf16[512,1024]{1,0:T(8,128)(2,1)S(1)} collective-permute-done((bf16[512,1024]{1,0:T(8,128)(2,1)}, bf16[512,1024]{1,0:T(8,128)(2,1)S(1)}, u32[]{:S(2)}, u32[]{:S(2)}) %collective-permute-start.2) | collective-permute-done | bytes 1048608 | tf_op jit(solution)/shard_map/ppermute | solution.py:38
  46.8 1.3 %fusion.refs_3_ = bf16[512,1024]{1,0:T(8,128)(2,1)S(1)} fusion(f32[1024,512]{0,1:T(8,128)S(1)} %fusion.3, f32[1024,512]{0,1:T(8,128)S(1)} %fusion.7, f32[1024,512]{0,1:T(8,128)S(1)} %fusion.5, bf16[512,1024]{1,0:T(8,128)(2,1)S(1)} %collective-permute-done.2, bf16[1024,4096]{1,0:T(8,128)(2,1)S(1)} %bitcast.35, s32[]{:T(128)S(6)} %select_n.71), kind=kOutput, calls=%fused_computation.1 | convolution fusion | flops 1075838976 | bytes 10485764 | tf_op jit(solution)/shard_map/dot_general | solution.py:21
  48.7 1.5 %collective-permute-done.7 = bf16[8,128,128]{2,1,0:T(8,128)(2,1)S(1)} collective-permute-done((bf16[8,128,128]{2,1,0:T(8,128)(2,1)S(1)}, bf16[8,128,128]{2,1,0:T(8,128)(2,1)S(1)}, u32[]{:S(2)}, u32[]{:S(2)}) %collective-permute-start.7) | collective-permute-done | bytes 262176 | tf_op jit(solution)/shard_map/ppermute | solution.py:51
  50.3 1.3 %collective-permute-start.10 = (bf16[8,64,128]{2,1,0:T(8,128)(2,1)S(1)}, bf16[8,64,128]{2,1,0:T(8,128)(2,1)S(1)}, u32[]{:S(2)}, u32[]{:S(2)}) collective-permute-start(bf16[8,64,128]{2,1,0:T(8,128)(2,1)S(1)} %dynamic-slice_add_fusion), channel_id=1, source_target_pairs={{24,0},{28,4},{25,1},{29,5},{26,2},{30,6},{27,3},{31,7}} | collective-permute-start | bytes 393224 | tf_op jit(solution)/shard_map/ppermute | solution.py:67
  51.6 1.3 %collective-permute-start.8 = (bf16[8,64,128]{2,1,0:T(8,128)(2,1)S(1)}, bf16[8,64,128]{2,1,0:T(8,128)(2,1)S(1)}, u32[]{:S(2)}, u32[]{:S(2)}) collective-permute-start(bf16[8,64,128]{2,1,0:T(8,128)(2,1)S(1)} %dynamic-slice_add_fusion), channel_id=1, source_target_pairs={{8,0},{12,4},{16,8},{20,12},{24,16},{28,20},{9,1},{13,5},{17,9},{2... | collective-permute-start | bytes 393224 | tf_op jit(solution)/shard_map/ppermute | solution.py:67
  52.9 1.3 %collective-permute-start.9 = (bf16[8,64,128]{2,1,0:T(8,128)(2,1)S(1)}, bf16[8,64,128]{2,1,0:T(8,128)(2,1)S(1)}, u32[]{:S(2)}, u32[]{:S(2)}) collective-permute-start(bf16[8,64,128]{2,1,0:T(8,128)(2,1)S(1)} %dynamic-slice_add_fusion), channel_id=1, source_target_pairs={{16,0},{20,4},{24,8},{28,12},{17,1},{21,5},{25,9},{29,13},{18,2},{... | collective-permute-start | bytes 393224 | tf_op jit(solution)/shard_map/ppermute | solution.py:67
  54.2 8.0 %attention_part.1 = (bf16[512,1024]{1,0:T(8,128)(2,1)}, bf16[512,1024]{1,0:T(8,128)(2,1)}, bf16[512,1024]{1,0:T(8,128)(2,1)}) custom-call(bf16[512,1024]{1,0:T(8,128)(2,1)} %refs_0_.2, bf16[512,1024]{1,0:T(8,128)(2,1)} %refs_0_.3, bf16[512,1024]{1,0:T(8,128)(2,1)} %refs_1_.3, bf16[512,1024]{1,0:T(8,128)(2,1)} %copy-done.2, f32[1,8,128,128]{3,2,1,0:T(8,128)} %fusion.16.refs_4_), custom_call_target="tpu_custom_call" | custom-call | flops 3221225472 | bytes 7340032 | tf_op jit(solution)/shard_map/attention_part/pallas_call | solution.py:148
  62.2 5.6 %collective-permute-done.9 = bf16[8,64,128]{2,1,0:T(8,128)(2,1)S(1)} collective-permute-done((bf16[8,64,128]{2,1,0:T(8,128)(2,1)S(1)}, bf16[8,64,128]{2,1,0:T(8,128)(2,1)S(1)}, u32[]{:S(2)}, u32[]{:S(2)}) %collective-permute-start.9) | collective-permute-done | bytes 131104 | tf_op jit(solution)/shard_map/ppermute | solution.py:67
  68.0 1.5 %collective-permute-done.11 = f32[8,64,128]{2,1,0:T(8,128)S(1)} collective-permute-done((f32[8,64,128]{2,1,0:T(8,128)S(1)}, f32[8,64,128]{2,1,0:T(8,128)S(1)}, u32[]{:S(2)}, u32[]{:S(2)}) %collective-permute-start.11) | collective-permute-done | bytes 262176 | tf_op jit(solution)/shard_map/ppermute | solution.py:80
  70.4 4.0 %state_part.1 = (bf16[512,1024]{1,0:T(8,128)(2,1)}, bf16[512,1024]{1,0:T(8,128)(2,1)}) custom-call(bf16[512,1024]{1,0:T(8,128)(2,1)} %refs_0_.3, bf16[512,1024]{1,0:T(8,128)(2,1)} %refs_1_.3, f32[1,8,128,128]{3,2,1,0:T(8,128)} %fusion.17.refs_2_, bf16[512,1024]{1,0:T(8,128)(2,1)} %get-tuple-element.27.refs_3_, bf16[512,1024]{1,0:T(8,128)(2,1)} %get-tuple-element.28.refs_4_), custom_call_target="tpu_custom_call" | custom-call | flops 536870912 | bytes 6291456 | tf_op jit(solution)/shard_map/state_part/pallas_call | solution.py:169
  (32 shorter events, 4.0 us)
Async XLA Ops:
  0.6 1.6 %copy-start.1 = (bf16[512,1024]{1,0:T(8,128)(2,1)S(1)}, bf16[512,1024]{1,0:T(8,128)(2,1)}, u32[]{:S(2)}) copy-start(bf16[512,1024]{1,0:T(8,128)(2,1)} %refs_1_.3) | copy-start | bytes 3145732
  2.2 19.9 %copy-start = (bf16[512,1024]{1,0:T(8,128)(2,1)S(1)}, bf16[512,1024]{1,0:T(8,128)(2,1)}, u32[]{:S(2)}) copy-start(bf16[512,1024]{1,0:T(8,128)(2,1)} %refs_0_.2) | copy-start | bytes 3145732
  3.4 2.9 %collective-permute-start.3 = (bf16[8,128,128]{2,1,0:T(8,128)(2,1)}, bf16[8,128,128]{2,1,0:T(8,128)(2,1)S(1)}, u32[]{:S(2)}, u32[]{:S(2)}) collective-permute-start(bf16[8,128,128]{2,1,0:T(8,128)(2,1)} %convolution_convert_fusion.1), channel_id=1, source_target_pairs={{0,4},{4,0},{8,12},{12,8},{16,20},{20,16},{24,28},{28,24},{1,5},{5... | collective-permute-start | bytes 786440 | tf_op jit(solution)/shard_map/ppermute | solution.py:51
  3.9 22.6 %collective-permute-start = (bf16[512,1024]{1,0:T(8,128)(2,1)}, bf16[512,1024]{1,0:T(8,128)(2,1)}, u32[]{:S(2)}, u32[]{:S(2)}) collective-permute-start(bf16[512,1024]{1,0:T(8,128)(2,1)} %param.8), channel_id=1, source_target_pairs={{0,1},{1,0},{2,3},{3,2},{4,6},{5,7},{6,4},{7,5},{8,9},{9,8},{10,11... | collective-permute-start | bytes 3145736 | tf_op jit(solution)/shard_map/ppermute | solution.py:36
  7.4 6.8 %collective-permute-start.4 = (bf16[8,64,128]{2,1,0:T(8,128)(2,1)S(1)}, bf16[8,64,128]{2,1,0:T(8,128)(2,1)S(1)}, u32[]{:S(2)}, u32[]{:S(2)}) collective-permute-start(bf16[8,64,128]{2,1,0:T(8,128)(2,1)S(1)} %fusion.19), channel_id=1, source_target_pairs={{0,8},{4,12},{8,16},{12,20},{16,24},{20,28},{1,9},{5,13},{9,17},{1... | collective-permute-start | bytes 393224 | tf_op jit(solution)/shard_map/ppermute | solution.py:72
  15.1 7.9 %collective-permute-start.5 = (bf16[8,64,128]{2,1,0:T(8,128)(2,1)S(1)}, bf16[8,64,128]{2,1,0:T(8,128)(2,1)S(1)}, u32[]{:S(2)}, u32[]{:S(2)}) collective-permute-start(bf16[8,64,128]{2,1,0:T(8,128)(2,1)S(1)} %fusion.18), channel_id=1, source_target_pairs={{0,16},{4,20},{8,24},{12,28},{1,17},{5,21},{9,25},{13,29},{2,18},{... | collective-permute-start | bytes 393224 | tf_op jit(solution)/shard_map/ppermute | solution.py:72
  20.5 15.2 %collective-permute-start.1 = (bf16[512,1024]{1,0:T(8,128)(2,1)}, bf16[512,1024]{1,0:T(8,128)(2,1)}, u32[]{:S(2)}, u32[]{:S(2)}) collective-permute-start(bf16[512,1024]{1,0:T(8,128)(2,1)} %param.8), channel_id=1, source_target_pairs={{0,2},{1,3},{2,0},{3,1},{4,5},{5,4},{6,7},{7,6},{8,10},{9,11},{10,... | collective-permute-start | bytes 3145736 | tf_op jit(solution)/shard_map/ppermute | solution.py:37
  23.0 5.0 %collective-permute-start.6 = (f32[8,64,128]{2,1,0:T(8,128)S(1)}, f32[8,64,128]{2,1,0:T(8,128)S(1)}, u32[]{:S(2)}, u32[]{:S(2)}) collective-permute-start(f32[8,64,128]{2,1,0:T(8,128)S(1)} %convert_add_fusion), channel_id=1, source_target_pairs={{0,4},{4,0},{8,12},{12,8},{16,20},{20,16},{24,28},{28,24},{1,5},{5... | collective-permute-start | bytes 786440 | tf_op jit(solution)/shard_map/ppermute | solution.py:80
  23.1 12.6 %slice-start = ((s8[8388608]{0:T(1024)(128)(4,1)}), s8[4194304]{0:T(1024)(128)(4,1)S(1)}, s32[]{:S(2)}) async-start(s8[8388608]{0:T(1024)(128)(4,1)} %bitcast.34), calls=%async_computation | async-start | bytes 8388608
  26.5 20.4 %collective-permute-start.2 = (bf16[512,1024]{1,0:T(8,128)(2,1)}, bf16[512,1024]{1,0:T(8,128)(2,1)S(1)}, u32[]{:S(2)}, u32[]{:S(2)}) collective-permute-start(bf16[512,1024]{1,0:T(8,128)(2,1)} %collective-permute-done), channel_id=1, source_target_pairs={{0,2},{1,3},{2,0},{3,1},{4,5},{5,4},{6,7},{7,6},{8,10},{9,11},{10,... | collective-permute-start | bytes 3145736 | tf_op jit(solution)/shard_map/ppermute | solution.py:38
  28.1 7.6 %slice-start.1 = ((s8[8388608]{0:T(1024)(128)(4,1)}), s8[4194304]{0:T(1024)(128)(4,1)S(1)}, s32[]{:S(2)}) async-start(s8[8388608]{0:T(1024)(128)(4,1)} %bitcast.34), calls=%async_computation.1 | async-start | bytes 8388608
  48.1 6.1 %copy-start.2 = (bf16[512,1024]{1,0:T(8,128)(2,1)}, bf16[512,1024]{1,0:T(8,128)(2,1)S(1)}, u32[]{:S(2)}) copy-start(bf16[512,1024]{1,0:T(8,128)(2,1)S(1)} %fusion.refs_3_) | copy-start | bytes 3145732
  48.6 1.6 %collective-permute-start.7 = (bf16[8,128,128]{2,1,0:T(8,128)(2,1)S(1)}, bf16[8,128,128]{2,1,0:T(8,128)(2,1)S(1)}, u32[]{:S(2)}, u32[]{:S(2)}) collective-permute-start(bf16[8,128,128]{2,1,0:T(8,128)(2,1)S(1)} %fusion.11), channel_id=1, source_target_pairs={{0,4},{4,0},{8,12},{12,8},{16,20},{20,16},{24,28},{28,24},{1,5},{5... | collective-permute-start | bytes 786440 | tf_op jit(solution)/shard_map/ppermute | solution.py:51
  50.3 11.9 %collective-permute-start.10 = (bf16[8,64,128]{2,1,0:T(8,128)(2,1)S(1)}, bf16[8,64,128]{2,1,0:T(8,128)(2,1)S(1)}, u32[]{:S(2)}, u32[]{:S(2)}) collective-permute-start(bf16[8,64,128]{2,1,0:T(8,128)(2,1)S(1)} %dynamic-slice_add_fusion), channel_id=1, source_target_pairs={{24,0},{28,4},{25,1},{29,5},{26,2},{30,6},{27,3},{31,7}} | collective-permute-start | bytes 393224 | tf_op jit(solution)/shard_map/ppermute | solution.py:67
  51.6 10.6 %collective-permute-start.8 = (bf16[8,64,128]{2,1,0:T(8,128)(2,1)S(1)}, bf16[8,64,128]{2,1,0:T(8,128)(2,1)S(1)}, u32[]{:S(2)}, u32[]{:S(2)}) collective-permute-start(bf16[8,64,128]{2,1,0:T(8,128)(2,1)S(1)} %dynamic-slice_add_fusion), channel_id=1, source_target_pairs={{8,0},{12,4},{16,8},{20,12},{24,16},{28,20},{9,1},{13,5},{17,9},{2... | collective-permute-start | bytes 393224 | tf_op jit(solution)/shard_map/ppermute | solution.py:67
  52.9 14.9 %collective-permute-start.9 = (bf16[8,64,128]{2,1,0:T(8,128)(2,1)S(1)}, bf16[8,64,128]{2,1,0:T(8,128)(2,1)S(1)}, u32[]{:S(2)}, u32[]{:S(2)}) collective-permute-start(bf16[8,64,128]{2,1,0:T(8,128)(2,1)S(1)} %dynamic-slice_add_fusion), channel_id=1, source_target_pairs={{16,0},{20,4},{24,8},{28,12},{17,1},{21,5},{25,9},{29,13},{18,2},{... | collective-permute-start | bytes 393224 | tf_op jit(solution)/shard_map/ppermute | solution.py:67
  67.9 1.6 %collective-permute-start.11 = (f32[8,64,128]{2,1,0:T(8,128)S(1)}, f32[8,64,128]{2,1,0:T(8,128)S(1)}, u32[]{:S(2)}, u32[]{:S(2)}) collective-permute-start(f32[8,64,128]{2,1,0:T(8,128)S(1)} %convert_add_fusion.2), channel_id=1, source_target_pairs={{0,4},{4,0},{8,12},{12,8},{16,20},{20,16},{24,28},{28,24},{1,5},{5... | collective-permute-start | bytes 786440 | tf_op jit(solution)/shard_map/ppermute | solution.py:80

commit v17 on v15

--- a/solution.py
+++ b/solution.py
@@ -2,6 +2,7 @@
 import jax.numpy as jnp
 from jax import lax
 from jax.experimental import pallas as pl
+from jax.experimental.pallas import tpu as pltpu
 from jax.sharding import PartitionSpec as P
 
 DH = 128
@@ -44,14 +45,15 @@
     return acc, tied
 
 
-def ctx_exclusive(state, ctx_size, reverse, cover=None):
+def ctx_exclusive(state, ctx_size, reverse, cover=None, by_heads=False):
     core = lax.axis_index("ctx") % 2
     chips = ctx_size // 2
     rounded = state.astype(jnp.bfloat16)
     partner = lax.ppermute(rounded, "ctx", flip_pairs(ctx_size, 1)).astype(jnp.float32)
     chip_sum = rounded.astype(jnp.float32) + partner
-    half = state.shape[1] // 2
-    mine = lax.dynamic_slice_in_dim(chip_sum, core * half, half, axis=1)
+    axis = 0 if by_heads else 1
+    half = state.shape[axis] // 2
+    mine = lax.dynamic_slice_in_dim(chip_sum, core * half, half, axis=axis)
 
     def pairs(step):
         if reverse:
@@ -78,6 +80,12 @@
         covered = cover.fn(*held)
         others, covered = lax.optimization_barrier((others, covered))
     theirs = lax.ppermute(others, "ctx", flip_pairs(ctx_size, 1))
+    if by_heads:
+        same_chip = (core == 0) if reverse else (core == 1)
+        partner_kept = jnp.where(same_chip, partner, 0.0)
+        own = others + lax.dynamic_slice_in_dim(partner_kept, core * half, half, axis=0)
+        other_partner = lax.dynamic_slice_in_dim(partner_kept, (1 - core) * half, half, axis=0)
+        return (own, theirs, other_partner), covered
     lower = jnp.where(core == 0, others, theirs)
     upper = jnp.where(core == 0, theirs, others)
     chips_side = jnp.concatenate([lower, upper], axis=1)
@@ -160,25 +168,42 @@
     )(q, k, v, g, kv_state)
 
 
-def state_part(k, v, qg_state, parts, blocks, block_len, heads, scale):
-    per_step = 4 if heads % 4 == 0 else (2 if heads % 2 == 0 else 1)
-    tok = pl.BlockSpec((block_len, DH * per_step), lambda n, h: (n, h))
-    st = pl.BlockSpec((1, per_step, DH, DH), lambda n, h: (n, h, 0, 0))
+def state_part(k, v, qg_state, parts, blocks, block_len, heads, scale, first=None, into=None):
+    count = qg_state.shape[1]
+    per_step = 4 if count % 4 == 0 else (2 if count % 2 == 0 else 1)
     rows, width = k.shape
+    if first is None:
+        first = jnp.zeros((), jnp.int32)
+    offset = jnp.reshape(first // per_step, (1,)).astype(jnp.int32)
+    tok = pl.BlockSpec((block_len, DH * per_step), lambda n, h, o: (n, h + o[0]))
+    st = pl.BlockSpec((1, per_step, DH, DH), lambda n, h, o: (n, h, 0, 0))
     out = jax.ShapeDtypeStruct((rows, width), jnp.bfloat16)
+    operands = [offset, k, v, qg_state, *parts]
+    in_specs = [tok, tok, st, tok, tok]
+    aliases = {}
+    kernel = lambda o, *refs: state_kernel(scale, per_step, *refs)
+    if into is not None:
+        operands += list(into)
+        in_specs += [pl.BlockSpec(memory_space=pl.ANY)] * 2
+        aliases = {6: 0, 7: 1}
+        kernel = lambda o, *refs: state_kernel(scale, per_step, *refs[:5], *refs[7:])
     return pl.pallas_call(
-        lambda *refs: state_kernel(scale, per_step, *refs),
-        grid=(blocks, heads // per_step),
-        in_specs=[tok, tok, st, tok, tok],
-        out_specs=[tok, tok],
+        kernel,
+        grid_spec=pltpu.PrefetchScalarGridSpec(
+            num_scalar_prefetch=1,
+            grid=(blocks, count // per_step),
+            in_specs=in_specs,
+            out_specs=[tok, tok],
+        ),
         out_shape=[out, out],
+        input_output_aliases=aliases,
         cost_estimate=pl.CostEstimate(
-            flops=blocks * heads * 4 * 2 * block_len * DH * DH,
+            flops=blocks * count * 4 * 2 * block_len * DH * DH,
             transcendentals=0,
-            bytes_accessed=rows * width * 12,
+            bytes_accessed=rows * DH * count * 12,
         ),
         name="state_part",
-    )(k, v, qg_state, *parts)
+    )(*operands)
 
 
 def make_shards(ctx_size, head_size):
@@ -210,6 +235,7 @@
             "nthd,nthe->nhde", q_blocks, g_blocks, preferred_element_type=jnp.float32
         )
         qg_running = jnp.flip(jnp.cumsum(jnp.flip(qg_blocks, 0), axis=0), 0)
+        split = blocks == 1 and heads % 2 == 0
         qg_after, (gq, gk_part, gv_part) = ctx_exclusive(
             qg_running[0], ctx_size, True,
             Cover(
@@ -218,7 +244,23 @@
                 ),
                 (grad_heads, kv_entry),
             ),
-        )
+            by_heads=split,
+        )
+        if split:
+            own, theirs, other_partner = qg_after
+            half = heads // 2
+            core = lax.axis_index("ctx") % 2
+            gk, gv = state_part(
+                keys, values, own[None], (gk_part, gv_part), blocks, block_len, heads,
+                scale_factor, first=core * half,
+            )
+            theirs, gk, gv = lax.optimization_barrier((theirs, gk, gv))
+            other = theirs + other_partner
+            gk, gv = state_part(
+                keys, values, other[None], (gk_part, gv_part), blocks, block_len, heads,
+                scale_factor, first=(1 - core) * half, into=(gk, gv),
+            )
+            return gq, gk, gv
         if blocks == 1:
             qg_entry = qg_after[None]
         else:

time: 69.1 us -> 70 us (1.013)
  Pallas kernels: 12 us -> 14.5 us
  waiting for transfers between devices: 18.6 us -> 17.2 us
  matrix products: 12.5 us -> 11.2 us
  local copies, waits for them, and re-layouts: 2.15 us -> 3.27 us
    pallas_call x1 -> x2, Pallas kernels: 3.98 us -> 6.49 us  [state_part(): pl.pallas_call(kernel, grid_spec=pltpu.PrefetchScalarGridSpec(num_scalar_...]
    ppermute x2, waiting for transfers between devices: 1.52 us -> 0.01 us  [ctx_exclusive(): theirs = lax.ppermute(others, 'ctx', flip_pairs(ctx_size, 1))]
    unnamed x10 -> x12, local copies, waits for them, and re-layouts: 0.03 us -> 1.08 us
    convert_element_type x1, other arithmetic: 0.95 us -> 0.05 us  [ctx_exclusive(): sent = mine.astype(jnp.bfloat16)]
    dot_general x1, matrix products: 1.16 us -> 0.45 us  [shards(): jnp.einsum('nshd,nshe->nhde', k_blocks, v_blocks, preferred_element_type=...]
    broadcast_in_dim x1 -> x2, other arithmetic: 0.85 us -> 1.46 us  [the longest x1 0.73 us: shards(): own[None]]
  transfers between devices with their start and end apart: 13 -> 13, of which waited for: 8 -> 6; matrix products, arithmetic and copies ran while one was open for 17% -> 16% of each run, Pallas kernels for 12% -> 16%
where the time goes in v17:
time: 70 us; the launch traced here: 69.4 us
  starting transfers between devices  19.5 us (28%)
  waiting for transfers between devices  17.2 us (25%)
  Pallas kernels  14.5 us (21%)
  matrix products  11.2 us (16%)
  local copies, waits for them, and re-layouts  3.27 us (5%)
  other arithmetic  2.66 us (4%)
  between operations  0.93 us (1%)
    ppermute x6, starting transfers between devices, ctx_exclusive(): others = others + lax.ppermute(sent, 'ctx', pairs(step)).astype(jnp.float32)  13.1 us
    dot_general x4, matrix products, mm(): lax.dot_general(a, b, (((1,), (1,)), ((), ())), preferred_element_type=jn...  10.3 us
    ppermute x1, waiting for transfers between devices, project(): diag = lax.ppermute(to_relay, ('ctx', 'head'), route(2, 1))  8.61 us
    pallas_call x1, Pallas kernels, attention_part(): pl.pallas_call(lambda *refs: scores_kernel(scale, per_step, *refs), grid=...  8.03 us
    pallas_call x2, Pallas kernels, state_part(): pl.pallas_call(kernel, grid_spec=pltpu.PrefetchScalarGridSpec(num_scalar_...  6.49 us
    ppermute x6, waiting for transfers between devices, ctx_exclusive(): others = others + lax.ppermute(sent, 'ctx', pairs(step)).astype(jnp.float32)  5.57 us
    ppermute x1, starting transfers between devices, project(): to_relay = lax.ppermute(og, ('ctx', 'head'), route(1, 2))  2.57 us
    reshape x1, local copies, waits for them, and re-layouts  1.64 us
  transfers between devices with their start and end apart: 13, of which 6 were waited for; matrix products, arithmetic and copies ran while one was open for 16% of the time, Pallas kernels for 16%

profile of v17, /device:TPU:0, one launch (start us, length us, event | category | flops | bytes accessed | tf_op | source)
XLA Modules:
  0.0 69.4 jit_solution(815665186286985245)
XLA Ops:
  0.7 1.6 %copy.22 = bf16[512,1024]{0,1:T(8,128)(2,1)S(1)} copy(bf16[512,1024]{1,0:T(8,128)(2,1)} %refs_0_.5) | data formatting | bytes 2097152 | tf_op jit(solution)/shard_map/reshape
  3.3 2.6 %collective-permute-start = (bf16[512,1024]{1,0:T(8,128)(2,1)S(1)}, bf16[512,1024]{1,0:T(8,128)(2,1)S(1)}, u32[]{:S(2)}, u32[]{:S(2)}) collective-permute-start(bf16[512,1024]{1,0:T(8,128)(2,1)S(1)} %copy-done.3), channel_id=1, source_target_pairs={{0,1},{1,0},{2,3},{3,2},{4,6},{5,7},{6,4},{7,5},{8,9},{9,8},{10,11... | collective-permute-start | bytes 3145736 | tf_op jit(solution)/shard_map/ppermute | solution.py:37
  6.0 3.5 %collective-permute-start.4 = (bf16[8,64,128]{2,1,0:T(8,128)(2,1)S(1)}, bf16[8,64,128]{2,1,0:T(8,128)(2,1)S(1)}, u32[]{:S(2)}, u32[]{:S(2)}) collective-permute-start(bf16[8,64,128]{2,1,0:T(8,128)(2,1)S(1)} %fusion.17), channel_id=1, source_target_pairs={{0,8},{4,12},{8,16},{12,20},{16,24},{20,28},{1,9},{5,13},{9,17},{1... | collective-permute-start | bytes 393224 | tf_op jit(solution)/shard_map/ppermute | solution.py:69
  9.5 4.5 %collective-permute-start.5 = (bf16[8,64,128]{2,1,0:T(8,128)(2,1)S(1)}, bf16[8,64,128]{2,1,0:T(8,128)(2,1)S(1)}, u32[]{:S(2)}, u32[]{:S(2)}) collective-permute-start(bf16[8,64,128]{2,1,0:T(8,128)(2,1)S(1)} %fusion.17), channel_id=1, source_target_pairs={{0,16},{4,20},{8,24},{12,28},{1,17},{5,21},{9,25},{13,29},{2,18},{... | collective-permute-start | bytes 393224 | tf_op jit(solution)/shard_map/ppermute | solution.py:69
  14.0 1.3 %collective-permute-start.6 = (bf16[8,64,128]{2,1,0:T(8,128)(2,1)S(1)}, bf16[8,64,128]{2,1,0:T(8,128)(2,1)S(1)}, u32[]{:S(2)}, u32[]{:S(2)}) collective-permute-start(bf16[8,64,128]{2,1,0:T(8,128)(2,1)S(1)} %fusion.17), channel_id=1, source_target_pairs={{0,24},{4,28},{1,25},{5,29},{2,26},{6,30},{3,27},{7,31}} | collective-permute-start | bytes 393224 | tf_op jit(solution)/shard_map/ppermute | solution.py:69
  15.3 1.6 %collective-permute-start.1 = (bf16[512,1024]{1,0:T(8,128)(2,1)S(1)}, bf16[512,1024]{1,0:T(8,128)(2,1)}, u32[]{:S(2)}, u32[]{:S(2)}) collective-permute-start(bf16[512,1024]{1,0:T(8,128)(2,1)S(1)} %copy-done.3), channel_id=1, source_target_pairs={{0,2},{1,3},{2,0},{3,1},{4,5},{5,4},{6,7},{7,6},{8,10},{9,11},{10,... | collective-permute-start | bytes 3145736 | tf_op jit(solution)/shard_map/ppermute | solution.py:38
  16.9 1.0 %collective-permute-done.5 = bf16[8,64,128]{2,1,0:T(8,128)(2,1)S(1)} collective-permute-done((bf16[8,64,128]{2,1,0:T(8,128)(2,1)S(1)}, bf16[8,64,128]{2,1,0:T(8,128)(2,1)S(1)}, u32[]{:S(2)}, u32[]{:S(2)}) %collective-permute-start.5) | collective-permute-done | bytes 131104 | tf_op jit(solution)/shard_map/ppermute | solution.py:69
  17.8 1.8 %collective-permute-done.6 = bf16[8,64,128]{2,1,0:T(8,128)(2,1)S(1)} collective-permute-done((bf16[8,64,128]{2,1,0:T(8,128)(2,1)S(1)}, bf16[8,64,128]{2,1,0:T(8,128)(2,1)S(1)}, u32[]{:S(2)}, u32[]{:S(2)}) %collective-permute-start.6) | collective-permute-done | bytes 131104 | tf_op jit(solution)/shard_map/ppermute | solution.py:69
  19.7 3.0 %fusion.7 = f32[1024,512]{0,1:T(8,128)S(1)} fusion(bf16[512,1024]{1,0:T(8,128)(2,1)S(1)} %copy-done.3, bf16[1024,4096]{1,0:T(8,128)(2,1)} %param.9, s32[]{:T(128)S(6)} %select_n.68), kind=kOutput, calls=%fused_computation.8 | convolution fusion | flops 1073741824 | bytes 5242884 | tf_op jit(solution)/shard_map/dot_general | solution.py:22
  22.8 1.5 %collective-permute-start.2 = (bf16[512,1024]{1,0:T(8,128)(2,1)S(1)}, bf16[512,1024]{1,0:T(8,128)(2,1)S(1)}, u32[]{:S(2)}, u32[]{:S(2)}) collective-permute-start(bf16[512,1024]{1,0:T(8,128)(2,1)S(1)} %collective-permute-done), channel_id=1, source_target_pairs={{0,2},{1,3},{2,0},{3,1},{4,5},{5,4},{6,7},{7,6},{8,10},{9,11},{10,... | collective-permute-start | bytes 3145736 | tf_op jit(solution)/shard_map/ppermute | solution.py:39
  25.2 3.5 %fusion.5 = f32[1024,512]{0,1:T(8,128)S(1)} fusion(bf16[512,1024]{1,0:T(8,128)(2,1)S(1)} %collective-permute-done, bf16[1024,4096]{1,0:T(8,128)(2,1)} %param.9, s32[]{:T(128)S(6)} %select_n.70), kind=kOutput, calls=%fused_computation.6 | convolution fusion | flops 1073741824 | bytes 5242884 | tf_op jit(solution)/shard_map/dot_general | solution.py:22
  28.7 1.6 %collective-permute-done.1 = bf16[512,1024]{1,0:T(8,128)(2,1)} collective-permute-done((bf16[512,1024]{1,0:T(8,128)(2,1)S(1)}, bf16[512,1024]{1,0:T(8,128)(2,1)}, u32[]{:S(2)}, u32[]{:S(2)}) %collective-permute-start.1) | collective-permute-done | bytes 1048608 | tf_op jit(solution)/shard_map/ppermute | solution.py:38
  30.2 2.5 %fusion.3 = f32[1024,512]{0,1:T(8,128)S(1)} fusion(bf16[512,1024]{1,0:T(8,128)(2,1)} %collective-permute-done.1, bf16[1024,4096]{1,0:T(8,128)(2,1)S(1)} %bitcast.39, s32[]{:T(128)S(6)} %select_n.71), kind=kOutput, calls=%fused_computation.4 | convolution fusion | flops 1073741824 | bytes 5242884 | tf_op jit(solution)/shard_map/dot_general | solution.py:22
  32.7 8.6 %collective-permute-done.2 = bf16[512,1024]{1,0:T(8,128)(2,1)S(1)} collective-permute-done((bf16[512,1024]{1,0:T(8,128)(2,1)S(1)}, bf16[512,1024]{1,0:T(8,128)(2,1)S(1)}, u32[]{:S(2)}, u32[]{:S(2)}) %collective-permute-start.2) | collective-permute-done | bytes 1048608 | tf_op jit(solution)/shard_map/ppermute | solution.py:39
  41.4 1.3 %fusion.refs_3_ = bf16[512,1024]{1,0:T(8,128)(2,1)S(1)} fusion(f32[1024,512]{0,1:T(8,128)S(1)} %fusion.3, f32[1024,512]{0,1:T(8,128)S(1)} %fusion.7, f32[1024,512]{0,1:T(8,128)S(1)} %fusion.5, bf16[512,1024]{1,0:T(8,128)(2,1)S(1)} %collective-permute-done.2, bf16[1024,4096]{1,0:T(8,128)(2,1)S(1)} %bitcast.39, s32[]{:T(128)S(6)} %select_n.78), kind=kOutput, calls=%fused_computation.1 | convolution fusion | flops 1075838976 | bytes 10485764 | tf_op jit(solution)/shard_map/dot_general | solution.py:22
  43.2 1.0 %copy-done.2 = bf16[512,1024]{1,0:T(8,128)(2,1)S(1)} copy-done((bf16[512,1024]{1,0:T(8,128)(2,1)S(1)}, bf16[512,1024]{1,0:T(8,128)(2,1)}, u32[]{:S(2)}) %copy-start.2) | copy-done | bytes 1048600
  44.9 1.5 %collective-permute-done.8 = bf16[8,128,128]{2,1,0:T(8,128)(2,1)S(1)} collective-permute-done((bf16[8,128,128]{2,1,0:T(8,128)(2,1)S(1)}, bf16[8,128,128]{2,1,0:T(8,128)(2,1)S(1)}, u32[]{:S(2)}, u32[]{:S(2)}) %collective-permute-start.8) | collective-permute-done | bytes 262176 | tf_op jit(solution)/shard_map/ppermute | solution.py:52
  46.5 1.3 %collective-permute-start.10 = (bf16[4,128,128]{2,1,0:T(8,128)(2,1)S(1)}, bf16[4,128,128]{2,1,0:T(8,128)(2,1)S(1)}, u32[]{:S(2)}, u32[]{:S(2)}) collective-permute-start(bf16[4,128,128]{2,1,0:T(8,128)(2,1)S(1)} %dynamic-slice_add_fusion), channel_id=1, source_target_pairs={{16,0},{20,4},{24,8},{28,12},{17,1},{21,5},{25,9},{29,13},{18,2},{... | collective-permute-start | bytes 393224 | tf_op jit(solution)/shard_map/ppermute | solution.py:69
  47.8 1.3 %collective-permute-start.11 = (bf16[4,128,128]{2,1,0:T(8,128)(2,1)S(1)}, bf16[4,128,128]{2,1,0:T(8,128)(2,1)S(1)}, u32[]{:S(2)}, u32[]{:S(2)}) collective-permute-start(bf16[4,128,128]{2,1,0:T(8,128)(2,1)S(1)} %dynamic-slice_add_fusion), channel_id=1, source_target_pairs={{24,0},{28,4},{25,1},{29,5},{26,2},{30,6},{27,3},{31,7}} | collective-permute-start | bytes 393224 | tf_op jit(solution)/shard_map/ppermute | solution.py:69
  49.1 1.3 %collective-permute-start.9 = (bf16[4,128,128]{2,1,0:T(8,128)(2,1)S(1)}, bf16[4,128,128]{2,1,0:T(8,128)(2,1)S(1)}, u32[]{:S(2)}, u32[]{:S(2)}) collective-permute-start(bf16[4,128,128]{2,1,0:T(8,128)(2,1)S(1)} %dynamic-slice_add_fusion), channel_id=1, source_target_pairs={{8,0},{12,4},{16,8},{20,12},{24,16},{28,20},{9,1},{13,5},{17,9},{2... | collective-permute-start | bytes 393224 | tf_op jit(solution)/shard_map/ppermute | solution.py:69
  50.4 8.0 %attention_part.1 = (bf16[512,1024]{1,0:T(8,128)(2,1)}, bf16[512,1024]{1,0:T(8,128)(2,1)}, bf16[512,1024]{1,0:T(8,128)(2,1)}) custom-call(bf16[512,1024]{1,0:T(8,128)(2,1)} %refs_0_.3, bf16[512,1024]{1,0:T(8,128)(2,1)} %refs_0_.5, bf16[512,1024]{1,0:T(8,128)(2,1)} %refs_1_.5, bf16[512,1024]{1,0:T(8,128)(2,1)} %copy-done.1, f32[1,8,128,128]{3,2,1,0:T(8,128)} %fusion.16.refs_4_), custom_call_target="tpu_custom_call" | custom-call | flops 3221225472 | bytes 7340032 | tf_op jit(solution)/shard_map/attention_part/pallas_call | solution.py:156
  58.5 2.8 %collective-permute-done.10 = bf16[4,128,128]{2,1,0:T(8,128)(2,1)S(1)} collective-permute-done((bf16[4,128,128]{2,1,0:T(8,128)(2,1)S(1)}, bf16[4,128,128]{2,1,0:T(8,128)(2,1)S(1)}, u32[]{:S(2)}, u32[]{:S(2)}) %collective-permute-start.10) | collective-permute-done | bytes 131104 | tf_op jit(solution)/shard_map/ppermute | solution.py:69
  62.2 3.2 %state_part.2 = (bf16[512,1024]{1,0:T(8,128)(2,1)}, bf16[512,1024]{1,0:T(8,128)(2,1)}) custom-call(s32[1]{0:T(128)} %bitcast.6.o, bf16[512,1024]{1,0:T(8,128)(2,1)} %refs_0_.5, bf16[512,1024]{1,0:T(8,128)(2,1)} %refs_1_.5, f32[1,4,128,128]{3,2,1,0:T(8,128)} %add_bitcast_fusion.1.refs_2_, bf16[512,1024]{1,0:T(8,128)(2,1)} %get-tuple-element.32.refs_3_, ...), custom_call_target="tpu_custom_call" | custom-call | flops 268435456 | bytes 3145728 | tf_op jit(solution)/shard_map/state_part/pallas_call | solution.py:190
  66.1 3.2 %state_part.3 = (bf16[512,1024]{1,0:T(8,128)(2,1)}, bf16[512,1024]{1,0:T(8,128)(2,1)}) custom-call(s32[1]{0:T(128)} %bitcast.5.o, bf16[512,1024]{1,0:T(8,128)(2,1)} %refs_0_.5, bf16[512,1024]{1,0:T(8,128)(2,1)} %refs_1_.5, f32[1,4,128,128]{3,2,1,0:T(8,128)} %add_bitcast_fusion.refs_2_, ...), custom_call_target="tpu_custom_call", output_to_operand_aliasing={{0}: (6, {}), {1}: (7, {})} | custom-call | flops 268435456 | bytes 3145728 | tf_op jit(solution)/shard_map/state_part/pallas_call | solution.py:190
  (37 shorter events, 4.9 us)
Async XLA Ops:
  0.6 1.7 %copy-start = (bf16[512,1024]{1,0:T(8,128)(2,1)S(1)}, bf16[512,1024]{1,0:T(8,128)(2,1)}, u32[]{:S(2)}) copy-start(bf16[512,1024]{1,0:T(8,128)(2,1)} %refs_1_.5) | copy-start | bytes 3145732
  0.6 2.7 %copy-start.3 = (bf16[512,1024]{1,0:T(8,128)(2,1)S(1)}, bf16[512,1024]{1,0:T(8,128)(2,1)}, u32[]{:S(2)}) copy-start(bf16[512,1024]{1,0:T(8,128)(2,1)} %param.8) | copy-start | bytes 3145732
  2.8 3.1 %collective-permute-start.3 = (bf16[8,128,128]{2,1,0:T(8,128)(2,1)S(1)}, bf16[8,128,128]{2,1,0:T(8,128)(2,1)S(1)}, u32[]{:S(2)}, u32[]{:S(2)}) collective-permute-start(bf16[8,128,128]{2,1,0:T(8,128)(2,1)S(1)} %convolution_convert_fusion.1), channel_id=1, source_target_pairs={{0,4},{4,0},{8,12},{12,8},{16,20},{20,16},{24,28},{28,24},{1,5},{5... | collective-permute-start | bytes 786440 | tf_op jit(solution)/shard_map/ppermute | solution.py:52
  3.3 19.5 %collective-permute-start = (bf16[512,1024]{1,0:T(8,128)(2,1)S(1)}, bf16[512,1024]{1,0:T(8,128)(2,1)S(1)}, u32[]{:S(2)}, u32[]{:S(2)}) collective-permute-start(bf16[512,1024]{1,0:T(8,128)(2,1)S(1)} %copy-done.3), channel_id=1, source_target_pairs={{0,1},{1,0},{2,3},{3,2},{4,6},{5,7},{6,4},{7,5},{8,9},{9,8},{10,11... | collective-permute-start | bytes 3145736 | tf_op jit(solution)/shard_map/ppermute | solution.py:37
  6.0 10.9 %collective-permute-start.4 = (bf16[8,64,128]{2,1,0:T(8,128)(2,1)S(1)}, bf16[8,64,128]{2,1,0:T(8,128)(2,1)S(1)}, u32[]{:S(2)}, u32[]{:S(2)}) collective-permute-start(bf16[8,64,128]{2,1,0:T(8,128)(2,1)S(1)} %fusion.17), channel_id=1, source_target_pairs={{0,8},{4,12},{8,16},{12,20},{16,24},{20,28},{1,9},{5,13},{9,17},{1... | collective-permute-start | bytes 393224 | tf_op jit(solution)/shard_map/ppermute | solution.py:69
  9.5 8.4 %collective-permute-start.5 = (bf16[8,64,128]{2,1,0:T(8,128)(2,1)S(1)}, bf16[8,64,128]{2,1,0:T(8,128)(2,1)S(1)}, u32[]{:S(2)}, u32[]{:S(2)}) collective-permute-start(bf16[8,64,128]{2,1,0:T(8,128)(2,1)S(1)} %fusion.17), channel_id=1, source_target_pairs={{0,16},{4,20},{8,24},{12,28},{1,17},{5,21},{9,25},{13,29},{2,18},{... | collective-permute-start | bytes 393224 | tf_op jit(solution)/shard_map/ppermute | solution.py:69
  14.0 5.6 %collective-permute-start.6 = (bf16[8,64,128]{2,1,0:T(8,128)(2,1)S(1)}, bf16[8,64,128]{2,1,0:T(8,128)(2,1)S(1)}, u32[]{:S(2)}, u32[]{:S(2)}) collective-permute-start(bf16[8,64,128]{2,1,0:T(8,128)(2,1)S(1)} %fusion.17), channel_id=1, source_target_pairs={{0,24},{4,28},{1,25},{5,29},{2,26},{6,30},{3,27},{7,31}} | collective-permute-start | bytes 393224 | tf_op jit(solution)/shard_map/ppermute | solution.py:69
  15.3 15.0 %collective-permute-start.1 = (bf16[512,1024]{1,0:T(8,128)(2,1)S(1)}, bf16[512,1024]{1,0:T(8,128)(2,1)}, u32[]{:S(2)}, u32[]{:S(2)}) collective-permute-start(bf16[512,1024]{1,0:T(8,128)(2,1)S(1)} %copy-done.3), channel_id=1, source_target_pairs={{0,2},{1,3},{2,0},{3,1},{4,5},{5,4},{6,7},{7,6},{8,10},{9,11},{10,... | collective-permute-start | bytes 3145736 | tf_op jit(solution)/shard_map/ppermute | solution.py:38
  19.6 4.6 %collective-permute-start.7 = (f32[8,64,128]{2,1,0:T(8,128)S(1)}, f32[8,64,128]{2,1,0:T(8,128)S(1)}, u32[]{:S(2)}, u32[]{:S(2)}) collective-permute-start(f32[8,64,128]{2,1,0:T(8,128)S(1)} %convert_add_fusion.1), channel_id=1, source_target_pairs={{0,4},{4,0},{8,12},{12,8},{16,20},{20,16},{24,28},{28,24},{1,5},{5... | collective-permute-start | bytes 786440 | tf_op jit(solution)/shard_map/ppermute | solution.py:82
  19.7 10.5 %slice-start = ((s8[8388608]{0:T(1024)(128)(4,1)}), s8[4194304]{0:T(1024)(128)(4,1)S(1)}, s32[]{:S(2)}) async-start(s8[8388608]{0:T(1024)(128)(4,1)} %bitcast.38), calls=%async_computation | async-start | bytes 8388608
  22.8 18.6 %collective-permute-start.2 = (bf16[512,1024]{1,0:T(8,128)(2,1)S(1)}, bf16[512,1024]{1,0:T(8,128)(2,1)S(1)}, u32[]{:S(2)}, u32[]{:S(2)}) collective-permute-start(bf16[512,1024]{1,0:T(8,128)(2,1)S(1)} %collective-permute-done), channel_id=1, source_target_pairs={{0,2},{1,3},{2,0},{3,1},{4,5},{5,4},{6,7},{7,6},{8,10},{9,11},{10,... | collective-permute-start | bytes 3145736 | tf_op jit(solution)/shard_map/ppermute | solution.py:39
  24.3 5.9 %slice-start.1 = ((s8[8388608]{0:T(1024)(128)(4,1)}), s8[4194304]{0:T(1024)(128)(4,1)S(1)}, s32[]{:S(2)}) async-start(s8[8388608]{0:T(1024)(128)(4,1)} %bitcast.38), calls=%async_computation.1 | async-start | bytes 8388608
  42.7 2.1 %copy-start.1 = (bf16[512,1024]{1,0:T(8,128)(2,1)}, bf16[512,1024]{1,0:T(8,128)(2,1)S(1)}, u32[]{:S(2)}) copy-start(bf16[512,1024]{1,0:T(8,128)(2,1)S(1)} %fusion.refs_3_) | copy-start | bytes 3145732
  42.7 1.6 %copy-start.2 = (bf16[512,1024]{1,0:T(8,128)(2,1)S(1)}, bf16[512,1024]{1,0:T(8,128)(2,1)}, u32[]{:S(2)}) copy-start(bf16[512,1024]{1,0:T(8,128)(2,1)} %refs_0_.3) | copy-start | bytes 3145732
  44.8 1.6 %collective-permute-start.8 = (bf16[8,128,128]{2,1,0:T(8,128)(2,1)S(1)}, bf16[8,128,128]{2,1,0:T(8,128)(2,1)S(1)}, u32[]{:S(2)}, u32[]{:S(2)}) collective-permute-start(bf16[8,128,128]{2,1,0:T(8,128)(2,1)S(1)} %fusion.11), channel_id=1, source_target_pairs={{0,4},{4,0},{8,12},{12,8},{16,20},{20,16},{24,28},{28,24},{1,5},{5... | collective-permute-start | bytes 786440 | tf_op jit(solution)/shard_map/ppermute | solution.py:52
  46.5 14.8 %collective-permute-start.10 = (bf16[4,128,128]{2,1,0:T(8,128)(2,1)S(1)}, bf16[4,128,128]{2,1,0:T(8,128)(2,1)S(1)}, u32[]{:S(2)}, u32[]{:S(2)}) collective-permute-start(bf16[4,128,128]{2,1,0:T(8,128)(2,1)S(1)} %dynamic-slice_add_fusion), channel_id=1, source_target_pairs={{16,0},{20,4},{24,8},{28,12},{17,1},{21,5},{25,9},{29,13},{18,2},{... | collective-permute-start | bytes 393224 | tf_op jit(solution)/shard_map/ppermute | solution.py:69
  47.8 13.5 %collective-permute-start.11 = (bf16[4,128,128]{2,1,0:T(8,128)(2,1)S(1)}, bf16[4,128,128]{2,1,0:T(8,128)(2,1)S(1)}, u32[]{:S(2)}, u32[]{:S(2)}) collective-permute-start(bf16[4,128,128]{2,1,0:T(8,128)(2,1)S(1)} %dynamic-slice_add_fusion), channel_id=1, source_target_pairs={{24,0},{28,4},{25,1},{29,5},{26,2},{30,6},{27,3},{31,7}} | collective-permute-start | bytes 393224 | tf_op jit(solution)/shard_map/ppermute | solution.py:69
  49.1 12.2 %collective-permute-start.9 = (bf16[4,128,128]{2,1,0:T(8,128)(2,1)S(1)}, bf16[4,128,128]{2,1,0:T(8,128)(2,1)S(1)}, u32[]{:S(2)}, u32[]{:S(2)}) collective-permute-start(bf16[4,128,128]{2,1,0:T(8,128)(2,1)S(1)} %dynamic-slice_add_fusion), channel_id=1, source_target_pairs={{8,0},{12,4},{16,8},{20,12},{24,16},{28,20},{9,1},{13,5},{17,9},{2... | collective-permute-start | bytes 393224 | tf_op jit(solution)/shard_map/ppermute | solution.py:69
  61.3 4.1 %collective-permute-start.12 = (f32[4,128,128]{2,1,0:T(8,128)S(1)}, f32[4,128,128]{2,1,0:T(8,128)S(1)}, u32[]{:S(2)}, u32[]{:S(2)}) collective-permute-start(f32[4,128,128]{2,1,0:T(8,128)S(1)} %convert_add_fusion), channel_id=1, source_target_pairs={{0,4},{4,0},{8,12},{12,8},{16,20},{20,16},{24,28},{28,24},{1,5},{5... | collective-permute-start | bytes 786440 | tf_op jit(solution)/shard_map/ppermute | solution.py:82

commit v18 on v17

--- a/solution.py
+++ b/solution.py
@@ -170,7 +170,7 @@
 
 def state_part(k, v, qg_state, parts, blocks, block_len, heads, scale, first=None, into=None):
     count = qg_state.shape[1]
-    per_step = 4 if count % 4 == 0 else (2 if count % 2 == 0 else 1)
+    per_step = 4 if count % 4 == 0 and count > 4 else (2 if count % 2 == 0 else 1)
     rows, width = k.shape
     if first is None:
         first = jnp.zeros((), jnp.int32)

time: 70 us -> 69.4 us (level)
  no operation moved by 1% of the time
where the time goes in v18:
time: 69.4 us; the launch traced here: 68.8 us
  starting transfers between devices  19.5 us (28%)
  waiting for transfers between devices  17.2 us (25%)
  Pallas kernels  14 us (20%)
  matrix products  11.2 us (16%)
  local copies, waits for them, and re-layouts  3.27 us (5%)
  other arithmetic  2.66 us (4%)
  between operations  0.93 us (1%)
    ppermute x6, starting transfers between devices, ctx_exclusive(): others = others + lax.ppermute(sent, 'ctx', pairs(step)).astype(jnp.float32)  13.1 us
    dot_general x4, matrix products, mm(): lax.dot_general(a, b, (((1,), (1,)), ((), ())), preferred_element_type=jn...  10.3 us
    ppermute x1, waiting for transfers between devices, project(): diag = lax.ppermute(to_relay, ('ctx', 'head'), route(2, 1))  8.61 us
    pallas_call x1, Pallas kernels, attention_part(): pl.pallas_call(lambda *refs: scores_kernel(scale, per_step, *refs), grid=...  8.03 us
    pallas_call x2, Pallas kernels, state_part(): pl.pallas_call(kernel, grid_spec=pltpu.PrefetchScalarGridSpec(num_scalar_...  5.92 us
    ppermute x6, waiting for transfers between devices, ctx_exclusive(): others = others + lax.ppermute(sent, 'ctx', pairs(step)).astype(jnp.float32)  5.57 us
    ppermute x1, starting transfers between devices, project(): to_relay = lax.ppermute(og, ('ctx', 'head'), route(1, 2))  2.57 us
    reshape x1, local copies, waits for them, and re-layouts  1.64 us
  transfers between devices with their start and end apart: 13, of which 6 were waited for; matrix products, arithmetic and copies ran while one was open for 16% of the time, Pallas kernels for 16%

profile of v18, /device:TPU:0, one launch (start us, length us, event | category | flops | bytes accessed | tf_op | source)
XLA Modules:
  0.0 68.8 jit_solution(85441528898423561)
XLA Ops:
  0.7 1.6 %copy.22 = bf16[512,1024]{0,1:T(8,128)(2,1)S(1)} copy(bf16[512,1024]{1,0:T(8,128)(2,1)} %refs_0_.5) | data formatting | bytes 2097152 | tf_op jit(solution)/shard_map/reshape
  3.3 2.6 %collective-permute-start = (bf16[512,1024]{1,0:T(8,128)(2,1)S(1)}, bf16[512,1024]{1,0:T(8,128)(2,1)S(1)}, u32[]{:S(2)}, u32[]{:S(2)}) collective-permute-start(bf16[512,1024]{1,0:T(8,128)(2,1)S(1)} %copy-done.3), channel_id=1, source_target_pairs={{0,1},{1,0},{2,3},{3,2},{4,6},{5,7},{6,4},{7,5},{8,9},{9,8},{10,11... | collective-permute-start | bytes 3145736 | tf_op jit(solution)/shard_map/ppermute | solution.py:37
  6.0 3.5 %collective-permute-start.4 = (bf16[8,64,128]{2,1,0:T(8,128)(2,1)S(1)}, bf16[8,64,128]{2,1,0:T(8,128)(2,1)S(1)}, u32[]{:S(2)}, u32[]{:S(2)}) collective-permute-start(bf16[8,64,128]{2,1,0:T(8,128)(2,1)S(1)} %fusion.17), channel_id=1, source_target_pairs={{0,8},{4,12},{8,16},{12,20},{16,24},{20,28},{1,9},{5,13},{9,17},{1... | collective-permute-start | bytes 393224 | tf_op jit(solution)/shard_map/ppermute | solution.py:69
  9.5 4.5 %collective-permute-start.5 = (bf16[8,64,128]{2,1,0:T(8,128)(2,1)S(1)}, bf16[8,64,128]{2,1,0:T(8,128)(2,1)S(1)}, u32[]{:S(2)}, u32[]{:S(2)}) collective-permute-start(bf16[8,64,128]{2,1,0:T(8,128)(2,1)S(1)} %fusion.17), channel_id=1, source_target_pairs={{0,16},{4,20},{8,24},{12,28},{1,17},{5,21},{9,25},{13,29},{2,18},{... | collective-permute-start | bytes 393224 | tf_op jit(solution)/shard_map/ppermute | solution.py:69
  14.0 1.3 %collective-permute-start.6 = (bf16[8,64,128]{2,1,0:T(8,128)(2,1)S(1)}, bf16[8,64,128]{2,1,0:T(8,128)(2,1)S(1)}, u32[]{:S(2)}, u32[]{:S(2)}) collective-permute-start(bf16[8,64,128]{2,1,0:T(8,128)(2,1)S(1)} %fusion.17), channel_id=1, source_target_pairs={{0,24},{4,28},{1,25},{5,29},{2,26},{6,30},{3,27},{7,31}} | collective-permute-start | bytes 393224 | tf_op jit(solution)/shard_map/ppermute | solution.py:69
  15.3 1.6 %collective-permute-start.1 = (bf16[512,1024]{1,0:T(8,128)(2,1)S(1)}, bf16[512,1024]{1,0:T(8,128)(2,1)}, u32[]{:S(2)}, u32[]{:S(2)}) collective-permute-start(bf16[512,1024]{1,0:T(8,128)(2,1)S(1)} %copy-done.3), channel_id=1, source_target_pairs={{0,2},{1,3},{2,0},{3,1},{4,5},{5,4},{6,7},{7,6},{8,10},{9,11},{10,... | collective-permute-start | bytes 3145736 | tf_op jit(solution)/shard_map/ppermute | solution.py:38
  16.9 1.0 %collective-permute-done.5 = bf16[8,64,128]{2,1,0:T(8,128)(2,1)S(1)} collective-permute-done((bf16[8,64,128]{2,1,0:T(8,128)(2,1)S(1)}, bf16[8,64,128]{2,1,0:T(8,128)(2,1)S(1)}, u32[]{:S(2)}, u32[]{:S(2)}) %collective-permute-start.5) | collective-permute-done | bytes 131104 | tf_op jit(solution)/shard_map/ppermute | solution.py:69
  17.8 1.8 %collective-permute-done.6 = bf16[8,64,128]{2,1,0:T(8,128)(2,1)S(1)} collective-permute-done((bf16[8,64,128]{2,1,0:T(8,128)(2,1)S(1)}, bf16[8,64,128]{2,1,0:T(8,128)(2,1)S(1)}, u32[]{:S(2)}, u32[]{:S(2)}) %collective-permute-start.6) | collective-permute-done | bytes 131104 | tf_op jit(solution)/shard_map/ppermute | solution.py:69
  19.7 3.0 %fusion.7 = f32[1024,512]{0,1:T(8,128)S(1)} fusion(bf16[512,1024]{1,0:T(8,128)(2,1)S(1)} %copy-done.3, bf16[1024,4096]{1,0:T(8,128)(2,1)} %param.9, s32[]{:T(128)S(6)} %select_n.68), kind=kOutput, calls=%fused_computation.8 | convolution fusion | flops 1073741824 | bytes 5242884 | tf_op jit(solution)/shard_map/dot_general | solution.py:22
  22.8 1.5 %collective-permute-start.2 = (bf16[512,1024]{1,0:T(8,128)(2,1)S(1)}, bf16[512,1024]{1,0:T(8,128)(2,1)S(1)}, u32[]{:S(2)}, u32[]{:S(2)}) collective-permute-start(bf16[512,1024]{1,0:T(8,128)(2,1)S(1)} %collective-permute-done), channel_id=1, source_target_pairs={{0,2},{1,3},{2,0},{3,1},{4,5},{5,4},{6,7},{7,6},{8,10},{9,11},{10,... | collective-permute-start | bytes 3145736 | tf_op jit(solution)/shard_map/ppermute | solution.py:39
  25.2 3.5 %fusion.5 = f32[1024,512]{0,1:T(8,128)S(1)} fusion(bf16[512,1024]{1,0:T(8,128)(2,1)S(1)} %collective-permute-done, bf16[1024,4096]{1,0:T(8,128)(2,1)} %param.9, s32[]{:T(128)S(6)} %select_n.70), kind=kOutput, calls=%fused_computation.6 | convolution fusion | flops 1073741824 | bytes 5242884 | tf_op jit(solution)/shard_map/dot_general | solution.py:22
  28.7 1.6 %collective-permute-done.1 = bf16[512,1024]{1,0:T(8,128)(2,1)} collective-permute-done((bf16[512,1024]{1,0:T(8,128)(2,1)S(1)}, bf16[512,1024]{1,0:T(8,128)(2,1)}, u32[]{:S(2)}, u32[]{:S(2)}) %collective-permute-start.1) | collective-permute-done | bytes 1048608 | tf_op jit(solution)/shard_map/ppermute | solution.py:38
  30.2 2.5 %fusion.3 = f32[1024,512]{0,1:T(8,128)S(1)} fusion(bf16[512,1024]{1,0:T(8,128)(2,1)} %collective-permute-done.1, bf16[1024,4096]{1,0:T(8,128)(2,1)S(1)} %bitcast.39, s32[]{:T(128)S(6)} %select_n.71), kind=kOutput, calls=%fused_computation.4 | convolution fusion | flops 1073741824 | bytes 5242884 | tf_op jit(solution)/shard_map/dot_general | solution.py:22
  32.7 8.6 %collective-permute-done.2 = bf16[512,1024]{1,0:T(8,128)(2,1)S(1)} collective-permute-done((bf16[512,1024]{1,0:T(8,128)(2,1)S(1)}, bf16[512,1024]{1,0:T(8,128)(2,1)S(1)}, u32[]{:S(2)}, u32[]{:S(2)}) %collective-permute-start.2) | collective-permute-done | bytes 1048608 | tf_op jit(solution)/shard_map/ppermute | solution.py:39
  41.4 1.3 %fusion.refs_3_ = bf16[512,1024]{1,0:T(8,128)(2,1)S(1)} fusion(f32[1024,512]{0,1:T(8,128)S(1)} %fusion.3, f32[1024,512]{0,1:T(8,128)S(1)} %fusion.7, f32[1024,512]{0,1:T(8,128)S(1)} %fusion.5, bf16[512,1024]{1,0:T(8,128)(2,1)S(1)} %collective-permute-done.2, bf16[1024,4096]{1,0:T(8,128)(2,1)S(1)} %bitcast.39, s32[]{:T(128)S(6)} %select_n.78), kind=kOutput, calls=%fused_computation.1 | convolution fusion | flops 1075838976 | bytes 10485764 | tf_op jit(solution)/shard_map/dot_general | solution.py:22
  43.2 1.0 %copy-done.2 = bf16[512,1024]{1,0:T(8,128)(2,1)S(1)} copy-done((bf16[512,1024]{1,0:T(8,128)(2,1)S(1)}, bf16[512,1024]{1,0:T(8,128)(2,1)}, u32[]{:S(2)}) %copy-start.2) | copy-done | bytes 1048600
  44.9 1.5 %collective-permute-done.8 = bf16[8,128,128]{2,1,0:T(8,128)(2,1)S(1)} collective-permute-done((bf16[8,128,128]{2,1,0:T(8,128)(2,1)S(1)}, bf16[8,128,128]{2,1,0:T(8,128)(2,1)S(1)}, u32[]{:S(2)}, u32[]{:S(2)}) %collective-permute-start.8) | collective-permute-done | bytes 262176 | tf_op jit(solution)/shard_map/ppermute | solution.py:52
  46.5 1.3 %collective-permute-start.10 = (bf16[4,128,128]{2,1,0:T(8,128)(2,1)S(1)}, bf16[4,128,128]{2,1,0:T(8,128)(2,1)S(1)}, u32[]{:S(2)}, u32[]{:S(2)}) collective-permute-start(bf16[4,128,128]{2,1,0:T(8,128)(2,1)S(1)} %dynamic-slice_add_fusion), channel_id=1, source_target_pairs={{16,0},{20,4},{24,8},{28,12},{17,1},{21,5},{25,9},{29,13},{18,2},{... | collective-permute-start | bytes 393224 | tf_op jit(solution)/shard_map/ppermute | solution.py:69
  47.8 1.3 %collective-permute-start.11 = (bf16[4,128,128]{2,1,0:T(8,128)(2,1)S(1)}, bf16[4,128,128]{2,1,0:T(8,128)(2,1)S(1)}, u32[]{:S(2)}, u32[]{:S(2)}) collective-permute-start(bf16[4,128,128]{2,1,0:T(8,128)(2,1)S(1)} %dynamic-slice_add_fusion), channel_id=1, source_target_pairs={{24,0},{28,4},{25,1},{29,5},{26,2},{30,6},{27,3},{31,7}} | collective-permute-start | bytes 393224 | tf_op jit(solution)/shard_map/ppermute | solution.py:69
  49.1 1.3 %collective-permute-start.9 = (bf16[4,128,128]{2,1,0:T(8,128)(2,1)S(1)}, bf16[4,128,128]{2,1,0:T(8,128)(2,1)S(1)}, u32[]{:S(2)}, u32[]{:S(2)}) collective-permute-start(bf16[4,128,128]{2,1,0:T(8,128)(2,1)S(1)} %dynamic-slice_add_fusion), channel_id=1, source_target_pairs={{8,0},{12,4},{16,8},{20,12},{24,16},{28,20},{9,1},{13,5},{17,9},{2... | collective-permute-start | bytes 393224 | tf_op jit(solution)/shard_map/ppermute | solution.py:69
  50.4 8.0 %attention_part.1 = (bf16[512,1024]{1,0:T(8,128)(2,1)}, bf16[512,1024]{1,0:T(8,128)(2,1)}, bf16[512,1024]{1,0:T(8,128)(2,1)}) custom-call(bf16[512,1024]{1,0:T(8,128)(2,1)} %refs_0_.3, bf16[512,1024]{1,0:T(8,128)(2,1)} %refs_0_.5, bf16[512,1024]{1,0:T(8,128)(2,1)} %refs_1_.5, bf16[512,1024]{1,0:T(8,128)(2,1)} %copy-done.1, f32[1,8,128,128]{3,2,1,0:T(8,128)} %fusion.16.refs_4_), custom_call_target="tpu_custom_call" | custom-call | flops 3221225472 | bytes 7340032 | tf_op jit(solution)/shard_map/attention_part/pallas_call | solution.py:156
  58.5 2.8 %collective-permute-done.10 = bf16[4,128,128]{2,1,0:T(8,128)(2,1)S(1)} collective-permute-done((bf16[4,128,128]{2,1,0:T(8,128)(2,1)S(1)}, bf16[4,128,128]{2,1,0:T(8,128)(2,1)S(1)}, u32[]{:S(2)}, u32[]{:S(2)}) %collective-permute-start.10) | collective-permute-done | bytes 131104 | tf_op jit(solution)/shard_map/ppermute | solution.py:69
  62.2 3.0 %state_part.2 = (bf16[512,1024]{1,0:T(8,128)(2,1)}, bf16[512,1024]{1,0:T(8,128)(2,1)}) custom-call(s32[1]{0:T(128)} %bitcast.6.o, bf16[512,1024]{1,0:T(8,128)(2,1)} %refs_0_.5, bf16[512,1024]{1,0:T(8,128)(2,1)} %refs_1_.5, f32[1,4,128,128]{3,2,1,0:T(8,128)} %add_bitcast_fusion.1.refs_2_, bf16[512,1024]{1,0:T(8,128)(2,1)} %get-tuple-element.32.refs_3_, ...), custom_call_target="tpu_custom_call" | custom-call | flops 268435456 | bytes 3145728 | tf_op jit(solution)/shard_map/state_part/pallas_call | solution.py:190
  65.9 3.0 %state_part.3 = (bf16[512,1024]{1,0:T(8,128)(2,1)}, bf16[512,1024]{1,0:T(8,128)(2,1)}) custom-call(s32[1]{0:T(128)} %bitcast.5.o, bf16[512,1024]{1,0:T(8,128)(2,1)} %refs_0_.5, bf16[512,1024]{1,0:T(8,128)(2,1)} %refs_1_.5, f32[1,4,128,128]{3,2,1,0:T(8,128)} %add_bitcast_fusion.refs_2_, ...), custom_call_target="tpu_custom_call", output_to_operand_aliasing={{0}: (6, {}), {1}: (7, {})} | custom-call | flops 268435456 | bytes 3145728 | tf_op jit(solution)/shard_map/state_part/pallas_call | solution.py:190
  (37 shorter events, 4.9 us)
Async XLA Ops:
  0.6 1.7 %copy-start = (bf16[512,1024]{1,0:T(8,128)(2,1)S(1)}, bf16[512,1024]{1,0:T(8,128)(2,1)}, u32[]{:S(2)}) copy-start(bf16[512,1024]{1,0:T(8,128)(2,1)} %refs_1_.5) | copy-start | bytes 3145732
  0.6 2.7 %copy-start.3 = (bf16[512,1024]{1,0:T(8,128)(2,1)S(1)}, bf16[512,1024]{1,0:T(8,128)(2,1)}, u32[]{:S(2)}) copy-start(bf16[512,1024]{1,0:T(8,128)(2,1)} %param.8) | copy-start | bytes 3145732
  2.8 3.1 %collective-permute-start.3 = (bf16[8,128,128]{2,1,0:T(8,128)(2,1)S(1)}, bf16[8,128,128]{2,1,0:T(8,128)(2,1)S(1)}, u32[]{:S(2)}, u32[]{:S(2)}) collective-permute-start(bf16[8,128,128]{2,1,0:T(8,128)(2,1)S(1)} %convolution_convert_fusion.1), channel_id=1, source_target_pairs={{0,4},{4,0},{8,12},{12,8},{16,20},{20,16},{24,28},{28,24},{1,5},{5... | collective-permute-start | bytes 786440 | tf_op jit(solution)/shard_map/ppermute | solution.py:52
  3.3 19.5 %collective-permute-start = (bf16[512,1024]{1,0:T(8,128)(2,1)S(1)}, bf16[512,1024]{1,0:T(8,128)(2,1)S(1)}, u32[]{:S(2)}, u32[]{:S(2)}) collective-permute-start(bf16[512,1024]{1,0:T(8,128)(2,1)S(1)} %copy-done.3), channel_id=1, source_target_pairs={{0,1},{1,0},{2,3},{3,2},{4,6},{5,7},{6,4},{7,5},{8,9},{9,8},{10,11... | collective-permute-start | bytes 3145736 | tf_op jit(solution)/shard_map/ppermute | solution.py:37
  6.0 10.9 %collective-permute-start.4 = (bf16[8,64,128]{2,1,0:T(8,128)(2,1)S(1)}, bf16[8,64,128]{2,1,0:T(8,128)(2,1)S(1)}, u32[]{:S(2)}, u32[]{:S(2)}) collective-permute-start(bf16[8,64,128]{2,1,0:T(8,128)(2,1)S(1)} %fusion.17), channel_id=1, source_target_pairs={{0,8},{4,12},{8,16},{12,20},{16,24},{20,28},{1,9},{5,13},{9,17},{1... | collective-permute-start | bytes 393224 | tf_op jit(solution)/shard_map/ppermute | solution.py:69
  9.5 8.4 %collective-permute-start.5 = (bf16[8,64,128]{2,1,0:T(8,128)(2,1)S(1)}, bf16[8,64,128]{2,1,0:T(8,128)(2,1)S(1)}, u32[]{:S(2)}, u32[]{:S(2)}) collective-permute-start(bf16[8,64,128]{2,1,0:T(8,128)(2,1)S(1)} %fusion.17), channel_id=1, source_target_pairs={{0,16},{4,20},{8,24},{12,28},{1,17},{5,21},{9,25},{13,29},{2,18},{... | collective-permute-start | bytes 393224 | tf_op jit(solution)/shard_map/ppermute | solution.py:69
  14.0 5.6 %collective-permute-start.6 = (bf16[8,64,128]{2,1,0:T(8,128)(2,1)S(1)}, bf16[8,64,128]{2,1,0:T(8,128)(2,1)S(1)}, u32[]{:S(2)}, u32[]{:S(2)}) collective-permute-start(bf16[8,64,128]{2,1,0:T(8,128)(2,1)S(1)} %fusion.17), channel_id=1, source_target_pairs={{0,24},{4,28},{1,25},{5,29},{2,26},{6,30},{3,27},{7,31}} | collective-permute-start | bytes 393224 | tf_op jit(solution)/shard_map/ppermute | solution.py:69
  15.3 15.0 %collective-permute-start.1 = (bf16[512,1024]{1,0:T(8,128)(2,1)S(1)}, bf16[512,1024]{1,0:T(8,128)(2,1)}, u32[]{:S(2)}, u32[]{:S(2)}) collective-permute-start(bf16[512,1024]{1,0:T(8,128)(2,1)S(1)} %copy-done.3), channel_id=1, source_target_pairs={{0,2},{1,3},{2,0},{3,1},{4,5},{5,4},{6,7},{7,6},{8,10},{9,11},{10,... | collective-permute-start | bytes 3145736 | tf_op jit(solution)/shard_map/ppermute | solution.py:38
  19.6 4.6 %collective-permute-start.7 = (f32[8,64,128]{2,1,0:T(8,128)S(1)}, f32[8,64,128]{2,1,0:T(8,128)S(1)}, u32[]{:S(2)}, u32[]{:S(2)}) collective-permute-start(f32[8,64,128]{2,1,0:T(8,128)S(1)} %convert_add_fusion.1), channel_id=1, source_target_pairs={{0,4},{4,0},{8,12},{12,8},{16,20},{20,16},{24,28},{28,24},{1,5},{5... | collective-permute-start | bytes 786440 | tf_op jit(solution)/shard_map/ppermute | solution.py:82
  19.7 10.5 %slice-start = ((s8[8388608]{0:T(1024)(128)(4,1)}), s8[4194304]{0:T(1024)(128)(4,1)S(1)}, s32[]{:S(2)}) async-start(s8[8388608]{0:T(1024)(128)(4,1)} %bitcast.38), calls=%async_computation | async-start | bytes 8388608
  22.8 18.6 %collective-permute-start.2 = (bf16[512,1024]{1,0:T(8,128)(2,1)S(1)}, bf16[512,1024]{1,0:T(8,128)(2,1)S(1)}, u32[]{:S(2)}, u32[]{:S(2)}) collective-permute-start(bf16[512,1024]{1,0:T(8,128)(2,1)S(1)} %collective-permute-done), channel_id=1, source_target_pairs={{0,2},{1,3},{2,0},{3,1},{4,5},{5,4},{6,7},{7,6},{8,10},{9,11},{10,... | collective-permute-start | bytes 3145736 | tf_op jit(solution)/shard_map/ppermute | solution.py:39
  24.3 5.9 %slice-start.1 = ((s8[8388608]{0:T(1024)(128)(4,1)}), s8[4194304]{0:T(1024)(128)(4,1)S(1)}, s32[]{:S(2)}) async-start(s8[8388608]{0:T(1024)(128)(4,1)} %bitcast.38), calls=%async_computation.1 | async-start | bytes 8388608
  42.7 2.1 %copy-start.1 = (bf16[512,1024]{1,0:T(8,128)(2,1)}, bf16[512,1024]{1,0:T(8,128)(2,1)S(1)}, u32[]{:S(2)}) copy-start(bf16[512,1024]{1,0:T(8,128)(2,1)S(1)} %fusion.refs_3_) | copy-start | bytes 3145732
  42.7 1.6 %copy-start.2 = (bf16[512,1024]{1,0:T(8,128)(2,1)S(1)}, bf16[512,1024]{1,0:T(8,128)(2,1)}, u32[]{:S(2)}) copy-start(bf16[512,1024]{1,0:T(8,128)(2,1)} %refs_0_.3) | copy-start | bytes 3145732
  44.8 1.6 %collective-permute-start.8 = (bf16[8,128,128]{2,1,0:T(8,128)(2,1)S(1)}, bf16[8,128,128]{2,1,0:T(8,128)(2,1)S(1)}, u32[]{:S(2)}, u32[]{:S(2)}) collective-permute-start(bf16[8,128,128]{2,1,0:T(8,128)(2,1)S(1)} %fusion.11), channel_id=1, source_target_pairs={{0,4},{4,0},{8,12},{12,8},{16,20},{20,16},{24,28},{28,24},{1,5},{5... | collective-permute-start | bytes 786440 | tf_op jit(solution)/shard_map/ppermute | solution.py:52
  46.5 14.8 %collective-permute-start.10 = (bf16[4,128,128]{2,1,0:T(8,128)(2,1)S(1)}, bf16[4,128,128]{2,1,0:T(8,128)(2,1)S(1)}, u32[]{:S(2)}, u32[]{:S(2)}) collective-permute-start(bf16[4,128,128]{2,1,0:T(8,128)(2,1)S(1)} %dynamic-slice_add_fusion), channel_id=1, source_target_pairs={{16,0},{20,4},{24,8},{28,12},{17,1},{21,5},{25,9},{29,13},{18,2},{... | collective-permute-start | bytes 393224 | tf_op jit(solution)/shard_map/ppermute | solution.py:69
  47.8 13.5 %collective-permute-start.11 = (bf16[4,128,128]{2,1,0:T(8,128)(2,1)S(1)}, bf16[4,128,128]{2,1,0:T(8,128)(2,1)S(1)}, u32[]{:S(2)}, u32[]{:S(2)}) collective-permute-start(bf16[4,128,128]{2,1,0:T(8,128)(2,1)S(1)} %dynamic-slice_add_fusion), channel_id=1, source_target_pairs={{24,0},{28,4},{25,1},{29,5},{26,2},{30,6},{27,3},{31,7}} | collective-permute-start | bytes 393224 | tf_op jit(solution)/shard_map/ppermute | solution.py:69
  49.1 12.2 %collective-permute-start.9 = (bf16[4,128,128]{2,1,0:T(8,128)(2,1)S(1)}, bf16[4,128,128]{2,1,0:T(8,128)(2,1)S(1)}, u32[]{:S(2)}, u32[]{:S(2)}) collective-permute-start(bf16[4,128,128]{2,1,0:T(8,128)(2,1)S(1)} %dynamic-slice_add_fusion), channel_id=1, source_target_pairs={{8,0},{12,4},{16,8},{20,12},{24,16},{28,20},{9,1},{13,5},{17,9},{2... | collective-permute-start | bytes 393224 | tf_op jit(solution)/shard_map/ppermute | solution.py:69
  61.3 3.8 %collective-permute-start.12 = (f32[4,128,128]{2,1,0:T(8,128)S(1)}, f32[4,128,128]{2,1,0:T(8,128)S(1)}, u32[]{:S(2)}, u32[]{:S(2)}) collective-permute-start(f32[4,128,128]{2,1,0:T(8,128)S(1)} %convert_add_fusion), channel_id=1, source_target_pairs={{0,4},{4,0},{8,12},{12,8},{16,20},{20,16},{24,28},{28,24},{1,5},{5... | collective-permute-start | bytes 786440 | tf_op jit(solution)/shard_map/ppermute | solution.py:82

commit v19 on v15

--- a/solution.py
+++ b/solution.py
@@ -77,7 +77,8 @@
     if cover is not None:
         covered = cover.fn(*held)
         others, covered = lax.optimization_barrier((others, covered))
-    theirs = lax.ppermute(others, "ctx", flip_pairs(ctx_size, 1))
+    theirs = lax.ppermute(others.astype(jnp.bfloat16), "ctx", flip_pairs(ctx_size, 1))
+    theirs = theirs.astype(jnp.float32)
     lower = jnp.where(core == 0, others, theirs)
     upper = jnp.where(core == 0, theirs, others)
     chips_side = jnp.concatenate([lower, upper], axis=1)

time: 69.1 us -> 68.1 us (0.986)
  waiting for transfers between devices: 18.6 us -> 15.4 us
  other arithmetic: 2.96 us -> 3.8 us
  matrix products: 12.5 us -> 13.3 us
  local copies, waits for them, and re-layouts: 2.15 us -> 2.94 us
    ppermute x1, waiting for transfers between devices: 8.61 us -> 6.88 us  [project(): diag = lax.ppermute(to_relay, ('ctx', 'head'), route(2, 1))]
    dot_general x4, matrix products: 10.9 us -> 12.4 us  [mm(): lax.dot_general(a, b, (((1,), (1,)), ((), ())), preferred_element_type=jn...]
    ppermute x1, waiting for transfers between devices: 1.16 us -> 0.01 us  [project(): kept = lax.ppermute(og, ('ctx', 'head'), route(2, 1))]
    select_n x2, other arithmetic: 0.08 us -> 1.15 us  [ctx_exclusive(): lower = jnp.where(core == 0, others, theirs)]
    convert_element_type x1, other arithmetic: 0.95 us -> 0.05 us  [ctx_exclusive(): sent = mine.astype(jnp.bfloat16)]
    another operation x1, local copies, waits for them, and re-layouts: 0.53 us -> 1.32 us
    convert_element_type x0 -> x2, other arithmetic: none -> 0.73 us  [ctx_exclusive(): others.astype(jnp.bfloat16)]
    dot_general x1, matrix products: 1.16 us -> 0.44 us  [shards(): jnp.einsum('nshd,nshe->nhde', k_blocks, v_blocks, preferred_element_type=...]
  transfers between devices with their start and end apart: 13 -> 13, of which waited for: 8 -> 6; matrix products, arithmetic and copies ran while one was open for 17% -> 20% of each run, Pallas kernels for 12% -> 12%
where the time goes in v19:
time: 68.1 us; the launch traced here: 67.8 us
  starting transfers between devices  19.4 us (28%)
  waiting for transfers between devices  15.4 us (23%)
  matrix products  13.3 us (20%)
  Pallas kernels  12 us (18%)
  other arithmetic  3.8 us (6%)
  local copies, waits for them, and re-layouts  2.94 us (4%)
  between operations  0.89 us (1%)
    ppermute x6, starting transfers between devices, ctx_exclusive(): others = others + lax.ppermute(sent, 'ctx', pairs(step)).astype(jnp.float32)  13.2 us
    dot_general x4, matrix products, mm(): lax.dot_general(a, b, (((1,), (1,)), ((), ())), preferred_element_type=jn...  12.4 us
    pallas_call x1, Pallas kernels, attention_part(): pl.pallas_call(lambda *refs: scores_kernel(scale, per_step, *refs), grid=...  8.03 us
    ppermute x1, waiting for transfers between devices, project(): diag = lax.ppermute(to_relay, ('ctx', 'head'), route(2, 1))  6.88 us
    ppermute x6, waiting for transfers between devices, ctx_exclusive(): others = others + lax.ppermute(sent, 'ctx', pairs(step)).astype(jnp.float32)  5.62 us
    pallas_call x1, Pallas kernels, state_part(): pl.pallas_call(lambda *refs: state_kernel(scale, per_step, *refs), grid=(...  3.98 us
    ppermute x1, starting transfers between devices, project(): to_relay = lax.ppermute(og, ('ctx', 'head'), route(1, 2))  2.56 us
    reshape x1, local copies, waits for them, and re-layouts  1.58 us
  transfers between devices with their start and end apart: 13, of which 6 were waited for; matrix products, arithmetic and copies ran while one was open for 20% of the time, Pallas kernels for 12%

profile of v19, /device:TPU:0, one launch (start us, length us, event | category | flops | bytes accessed | tf_op | source)
XLA Modules:
  0.0 67.8 jit_solution(17499401753511435858)
XLA Ops:
  0.6 1.6 %copy.18 = bf16[512,1024]{0,1:T(8,128)(2,1)S(1)} copy(bf16[512,1024]{1,0:T(8,128)(2,1)} %refs_0_.3) | data formatting | bytes 2097152 | tf_op jit(solution)/shard_map/reshape
  3.2 2.6 %collective-permute-start = (bf16[512,1024]{1,0:T(8,128)(2,1)}, bf16[512,1024]{1,0:T(8,128)(2,1)}, u32[]{:S(2)}, u32[]{:S(2)}) collective-permute-start(bf16[512,1024]{1,0:T(8,128)(2,1)} %param.8), channel_id=1, source_target_pairs={{0,1},{1,0},{2,3},{3,2},{4,6},{5,7},{6,4},{7,5},{8,9},{9,8},{10,11... | collective-permute-start | bytes 3145736 | tf_op jit(solution)/shard_map/ppermute | solution.py:36
  5.9 3.5 %collective-permute-start.4 = (bf16[8,64,128]{2,1,0:T(8,128)(2,1)S(1)}, bf16[8,64,128]{2,1,0:T(8,128)(2,1)S(1)}, u32[]{:S(2)}, u32[]{:S(2)}) collective-permute-start(bf16[8,64,128]{2,1,0:T(8,128)(2,1)S(1)} %fusion.18), channel_id=1, source_target_pairs={{0,8},{4,12},{8,16},{12,20},{16,24},{20,28},{1,9},{5,13},{9,17},{1... | collective-permute-start | bytes 393224 | tf_op jit(solution)/shard_map/ppermute | solution.py:67
  9.4 4.5 %collective-permute-start.5 = (bf16[8,64,128]{2,1,0:T(8,128)(2,1)S(1)}, bf16[8,64,128]{2,1,0:T(8,128)(2,1)S(1)}, u32[]{:S(2)}, u32[]{:S(2)}) collective-permute-start(bf16[8,64,128]{2,1,0:T(8,128)(2,1)S(1)} %fusion.18), channel_id=1, source_target_pairs={{0,16},{4,20},{8,24},{12,28},{1,17},{5,21},{9,25},{13,29},{2,18},{... | collective-permute-start | bytes 393224 | tf_op jit(solution)/shard_map/ppermute | solution.py:67
  13.9 1.3 %collective-permute-start.6 = (bf16[8,64,128]{2,1,0:T(8,128)(2,1)S(1)}, bf16[8,64,128]{2,1,0:T(8,128)(2,1)S(1)}, u32[]{:S(2)}, u32[]{:S(2)}) collective-permute-start(bf16[8,64,128]{2,1,0:T(8,128)(2,1)S(1)} %fusion.18), channel_id=1, source_target_pairs={{0,24},{4,28},{1,25},{5,29},{2,26},{6,30},{3,27},{7,31}} | collective-permute-start | bytes 393224 | tf_op jit(solution)/shard_map/ppermute | solution.py:67
  15.2 1.6 %collective-permute-start.1 = (bf16[512,1024]{1,0:T(8,128)(2,1)}, bf16[512,1024]{1,0:T(8,128)(2,1)}, u32[]{:S(2)}, u32[]{:S(2)}) collective-permute-start(bf16[512,1024]{1,0:T(8,128)(2,1)} %param.8), channel_id=1, source_target_pairs={{0,2},{1,3},{2,0},{3,1},{4,5},{5,4},{6,7},{7,6},{8,10},{9,11},{10,... | collective-permute-start | bytes 3145736 | tf_op jit(solution)/shard_map/ppermute | solution.py:37
  16.8 1.0 %collective-permute-done.5 = bf16[8,64,128]{2,1,0:T(8,128)(2,1)S(1)} collective-permute-done((bf16[8,64,128]{2,1,0:T(8,128)(2,1)S(1)}, bf16[8,64,128]{2,1,0:T(8,128)(2,1)S(1)}, u32[]{:S(2)}, u32[]{:S(2)}) %collective-permute-start.5) | collective-permute-done | bytes 131104 | tf_op jit(solution)/shard_map/ppermute | solution.py:67
  17.7 1.8 %collective-permute-done.6 = bf16[8,64,128]{2,1,0:T(8,128)(2,1)S(1)} collective-permute-done((bf16[8,64,128]{2,1,0:T(8,128)(2,1)S(1)}, bf16[8,64,128]{2,1,0:T(8,128)(2,1)S(1)}, u32[]{:S(2)}, u32[]{:S(2)}) %collective-permute-start.6) | collective-permute-done | bytes 131104 | tf_op jit(solution)/shard_map/ppermute | solution.py:67
  20.3 3.2 %fusion.7 = f32[1024,512]{0,1:T(8,128)S(1)} fusion(bf16[512,1024]{1,0:T(8,128)(2,1)} %param.8, bf16[1024,4096]{1,0:T(8,128)(2,1)} %param.9, s32[]{:T(128)S(6)} %select_n.61), kind=kOutput, calls=%fused_computation.8 | convolution fusion | flops 1073741824 | bytes 5242884 | tf_op jit(solution)/shard_map/dot_general | solution.py:21
  23.5 1.3 %copy.19 = bf16[512,1024]{0,1:T(8,128)(2,1)} copy(bf16[512,1024]{1,0:T(8,128)(2,1)S(1)} %copy-done) | data formatting | bytes 2097152 | tf_op jit(solution)/shard_map/reshape.3
  24.9 1.4 %collective-permute-start.2 = (bf16[512,1024]{1,0:T(8,128)(2,1)}, bf16[512,1024]{1,0:T(8,128)(2,1)S(1)}, u32[]{:S(2)}, u32[]{:S(2)}) collective-permute-start(bf16[512,1024]{1,0:T(8,128)(2,1)} %collective-permute-done), channel_id=1, source_target_pairs={{0,2},{1,3},{2,0},{3,1},{4,5},{5,4},{6,7},{7,6},{8,10},{9,11},{10,... | collective-permute-start | bytes 3145736 | tf_op jit(solution)/shard_map/ppermute | solution.py:38
  26.3 1.1 %convert_select_fusion.3 = (f32[8,64,128]{2,1,0:T(8,128)S(1)}, f32[8,64,128]{2,1,0:T(8,128)S(1)}) fusion(bf16[8,64,128]{2,1,0:T(8,128)(2,1)} %collective-permute-done.7, pred[]{:T(512)S(6)} %eq.14, bf16[8,64,128]{2,1,0:T(8,128)(2,1)} %copy-done.5, bf16[8,64,128]{2,1,0:T(8,128)(2,1)} %copy-done.4, bf16[8,64,128]{2,1,0:T(8,128)(2,1)S(1)} %collective-permute-done.4), kind=kLoop, calls=%fused_computation.24 | loop fusion | flops 524288 | bytes 1048577 | tf_op jit(solution)/shard_map/jit(_where)/select_n | solution.py:82
  28.3 3.1 %fusion.5 = f32[1024,512]{0,1:T(8,128)S(1)} fusion(bf16[512,1024]{1,0:T(8,128)(2,1)} %collective-permute-done, bf16[1024,4096]{1,0:T(8,128)(2,1)} %param.9, s32[]{:T(128)S(6)} %select_n.63), kind=kOutput, calls=%fused_computation.6 | convolution fusion | flops 1073741824 | bytes 5242884 | tf_op jit(solution)/shard_map/dot_general | solution.py:21
  31.4 3.2 %fusion.3 = f32[1024,512]{0,1:T(8,128)S(1)} fusion(bf16[512,1024]{1,0:T(8,128)(2,1)} %collective-permute-done.1, bf16[1024,4096]{1,0:T(8,128)(2,1)} %param.9, s32[]{:T(128)S(6)} %select_n.64), kind=kOutput, calls=%fused_computation.4 | convolution fusion | flops 1073741824 | bytes 5242884 | tf_op jit(solution)/shard_map/dot_general | solution.py:21
  34.6 6.9 %collective-permute-done.2 = bf16[512,1024]{1,0:T(8,128)(2,1)S(1)} collective-permute-done((bf16[512,1024]{1,0:T(8,128)(2,1)}, bf16[512,1024]{1,0:T(8,128)(2,1)S(1)}, u32[]{:S(2)}, u32[]{:S(2)}) %collective-permute-start.2) | collective-permute-done | bytes 1048608 | tf_op jit(solution)/shard_map/ppermute | solution.py:38
  41.5 2.9 %fusion.refs_3_ = bf16[512,1024]{1,0:T(8,128)(2,1)S(1)} fusion(f32[1024,512]{0,1:T(8,128)S(1)} %fusion.3, f32[1024,512]{0,1:T(8,128)S(1)} %fusion.7, f32[1024,512]{0,1:T(8,128)S(1)} %fusion.5, bf16[512,1024]{1,0:T(8,128)(2,1)S(1)} %collective-permute-done.2, bf16[1024,4096]{1,0:T(8,128)(2,1)} %param.9, s32[]{:T(128)S(6)} %select_n.71), kind=kOutput, calls=%fused_computation.1 | convolution fusion | flops 1075838976 | bytes 10485764 | tf_op jit(solution)/shard_map/dot_general | solution.py:21
  45.0 1.5 %collective-permute-done.8 = bf16[8,128,128]{2,1,0:T(8,128)(2,1)S(1)} collective-permute-done((bf16[8,128,128]{2,1,0:T(8,128)(2,1)S(1)}, bf16[8,128,128]{2,1,0:T(8,128)(2,1)S(1)}, u32[]{:S(2)}, u32[]{:S(2)}) %collective-permute-start.8) | collective-permute-done | bytes 262176 | tf_op jit(solution)/shard_map/ppermute | solution.py:51
  46.6 1.3 %collective-permute-start.10 = (bf16[8,64,128]{2,1,0:T(8,128)(2,1)S(1)}, bf16[8,64,128]{2,1,0:T(8,128)(2,1)S(1)}, u32[]{:S(2)}, u32[]{:S(2)}) collective-permute-start(bf16[8,64,128]{2,1,0:T(8,128)(2,1)S(1)} %dynamic-slice_add_fusion), channel_id=1, source_target_pairs={{16,0},{20,4},{24,8},{28,12},{17,1},{21,5},{25,9},{29,13},{18,2},{... | collective-permute-start | bytes 393224 | tf_op jit(solution)/shard_map/ppermute | solution.py:67
  47.9 1.3 %collective-permute-start.11 = (bf16[8,64,128]{2,1,0:T(8,128)(2,1)S(1)}, bf16[8,64,128]{2,1,0:T(8,128)(2,1)S(1)}, u32[]{:S(2)}, u32[]{:S(2)}) collective-permute-start(bf16[8,64,128]{2,1,0:T(8,128)(2,1)S(1)} %dynamic-slice_add_fusion), channel_id=1, source_target_pairs={{24,0},{28,4},{25,1},{29,5},{26,2},{30,6},{27,3},{31,7}} | collective-permute-start | bytes 393224 | tf_op jit(solution)/shard_map/ppermute | solution.py:67
  49.2 1.3 %collective-permute-start.9 = (bf16[8,64,128]{2,1,0:T(8,128)(2,1)S(1)}, bf16[8,64,128]{2,1,0:T(8,128)(2,1)S(1)}, u32[]{:S(2)}, u32[]{:S(2)}) collective-permute-start(bf16[8,64,128]{2,1,0:T(8,128)(2,1)S(1)} %dynamic-slice_add_fusion), channel_id=1, source_target_pairs={{8,0},{12,4},{16,8},{20,12},{24,16},{28,20},{9,1},{13,5},{17,9},{2... | collective-permute-start | bytes 393224 | tf_op jit(solution)/shard_map/ppermute | solution.py:67
  50.5 8.0 %attention_part.1 = (bf16[512,1024]{1,0:T(8,128)(2,1)}, bf16[512,1024]{1,0:T(8,128)(2,1)}, bf16[512,1024]{1,0:T(8,128)(2,1)}) custom-call(bf16[512,1024]{1,0:T(8,128)(2,1)} %refs_0_.2, bf16[512,1024]{1,0:T(8,128)(2,1)} %refs_0_.3, bf16[512,1024]{1,0:T(8,128)(2,1)} %refs_1_.3, bf16[512,1024]{1,0:T(8,128)(2,1)} %copy-done.3, f32[1,8,128,128]{3,2,1,0:T(8,128)} %fusion.16.refs_4_), custom_call_target="tpu_custom_call" | custom-call | flops 3221225472 | bytes 7340032 | tf_op jit(solution)/shard_map/attention_part/pallas_call | solution.py:149
  58.5 2.9 %collective-permute-done.10 = bf16[8,64,128]{2,1,0:T(8,128)(2,1)S(1)} collective-permute-done((bf16[8,64,128]{2,1,0:T(8,128)(2,1)S(1)}, bf16[8,64,128]{2,1,0:T(8,128)(2,1)S(1)}, u32[]{:S(2)}, u32[]{:S(2)}) %collective-permute-start.10) | collective-permute-done | bytes 131104 | tf_op jit(solution)/shard_map/ppermute | solution.py:67
  61.5 1.3 %collective-permute-done.12 = bf16[8,64,128]{2,1,0:T(8,128)(2,1)S(1)} collective-permute-done((bf16[8,64,128]{2,1,0:T(8,128)(2,1)S(1)}, bf16[8,64,128]{2,1,0:T(8,128)(2,1)S(1)}, u32[]{:S(2)}, u32[]{:S(2)}) %collective-permute-start.12) | collective-permute-done | bytes 131104 | tf_op jit(solution)/shard_map/ppermute | solution.py:80
  63.8 4.0 %state_part.1 = (bf16[512,1024]{1,0:T(8,128)(2,1)}, bf16[512,1024]{1,0:T(8,128)(2,1)}) custom-call(bf16[512,1024]{1,0:T(8,128)(2,1)} %refs_0_.3, bf16[512,1024]{1,0:T(8,128)(2,1)} %refs_1_.3, f32[1,8,128,128]{3,2,1,0:T(8,128)} %fusion.17.refs_2_, bf16[512,1024]{1,0:T(8,128)(2,1)} %get-tuple-element.27.refs_3_, bf16[512,1024]{1,0:T(8,128)(2,1)} %get-tuple-element.28.refs_4_), custom_call_target="tpu_custom_call" | custom-call | flops 536870912 | bytes 6291456 | tf_op jit(solution)/shard_map/state_part/pallas_call | solution.py:170
  (35 shorter events, 4.3 us)
Async XLA Ops:
  0.6 1.6 %copy-start.2 = (bf16[512,1024]{1,0:T(8,128)(2,1)S(1)}, bf16[512,1024]{1,0:T(8,128)(2,1)}, u32[]{:S(2)}) copy-start(bf16[512,1024]{1,0:T(8,128)(2,1)} %refs_1_.3) | copy-start | bytes 3145732
  2.7 3.1 %collective-permute-start.3 = (bf16[8,128,128]{2,1,0:T(8,128)(2,1)S(1)}, bf16[8,128,128]{2,1,0:T(8,128)(2,1)S(1)}, u32[]{:S(2)}, u32[]{:S(2)}) collective-permute-start(bf16[8,128,128]{2,1,0:T(8,128)(2,1)S(1)} %convolution_convert_fusion.1), channel_id=1, source_target_pairs={{0,4},{4,0},{8,12},{12,8},{16,20},{20,16},{24,28},{28,24},{1,5},{5... | collective-permute-start | bytes 786440 | tf_op jit(solution)/shard_map/ppermute | solution.py:51
  3.2 21.6 %collective-permute-start = (bf16[512,1024]{1,0:T(8,128)(2,1)}, bf16[512,1024]{1,0:T(8,128)(2,1)}, u32[]{:S(2)}, u32[]{:S(2)}) collective-permute-start(bf16[512,1024]{1,0:T(8,128)(2,1)} %param.8), channel_id=1, source_target_pairs={{0,1},{1,0},{2,3},{3,2},{4,6},{5,7},{6,4},{7,5},{8,9},{9,8},{10,11... | collective-permute-start | bytes 3145736 | tf_op jit(solution)/shard_map/ppermute | solution.py:36
  5.9 10.9 %collective-permute-start.4 = (bf16[8,64,128]{2,1,0:T(8,128)(2,1)S(1)}, bf16[8,64,128]{2,1,0:T(8,128)(2,1)S(1)}, u32[]{:S(2)}, u32[]{:S(2)}) collective-permute-start(bf16[8,64,128]{2,1,0:T(8,128)(2,1)S(1)} %fusion.18), channel_id=1, source_target_pairs={{0,8},{4,12},{8,16},{12,20},{16,24},{20,28},{1,9},{5,13},{9,17},{1... | collective-permute-start | bytes 393224 | tf_op jit(solution)/shard_map/ppermute | solution.py:67
  9.4 8.4 %collective-permute-start.5 = (bf16[8,64,128]{2,1,0:T(8,128)(2,1)S(1)}, bf16[8,64,128]{2,1,0:T(8,128)(2,1)S(1)}, u32[]{:S(2)}, u32[]{:S(2)}) collective-permute-start(bf16[8,64,128]{2,1,0:T(8,128)(2,1)S(1)} %fusion.18), channel_id=1, source_target_pairs={{0,16},{4,20},{8,24},{12,28},{1,17},{5,21},{9,25},{13,29},{2,18},{... | collective-permute-start | bytes 393224 | tf_op jit(solution)/shard_map/ppermute | solution.py:67
  13.9 5.7 %collective-permute-start.6 = (bf16[8,64,128]{2,1,0:T(8,128)(2,1)S(1)}, bf16[8,64,128]{2,1,0:T(8,128)(2,1)S(1)}, u32[]{:S(2)}, u32[]{:S(2)}) collective-permute-start(bf16[8,64,128]{2,1,0:T(8,128)(2,1)S(1)} %fusion.18), channel_id=1, source_target_pairs={{0,24},{4,28},{1,25},{5,29},{2,26},{6,30},{3,27},{7,31}} | collective-permute-start | bytes 393224 | tf_op jit(solution)/shard_map/ppermute | solution.py:67
  15.2 16.2 %collective-permute-start.1 = (bf16[512,1024]{1,0:T(8,128)(2,1)}, bf16[512,1024]{1,0:T(8,128)(2,1)}, u32[]{:S(2)}, u32[]{:S(2)}) collective-permute-start(bf16[512,1024]{1,0:T(8,128)(2,1)} %param.8), channel_id=1, source_target_pairs={{0,2},{1,3},{2,0},{3,1},{4,5},{5,4},{6,7},{7,6},{8,10},{9,11},{10,... | collective-permute-start | bytes 3145736 | tf_op jit(solution)/shard_map/ppermute | solution.py:37
  17.7 2.5 %copy-start.4 = (bf16[8,64,128]{2,1,0:T(8,128)(2,1)}, bf16[8,64,128]{2,1,0:T(8,128)(2,1)S(1)}, u32[]{:S(2)}) copy-start(bf16[8,64,128]{2,1,0:T(8,128)(2,1)S(1)} %collective-permute-done.5) | copy-start | bytes 393220
  19.5 0.7 %copy-start.5 = (bf16[8,64,128]{2,1,0:T(8,128)(2,1)}, bf16[8,64,128]{2,1,0:T(8,128)(2,1)S(1)}, u32[]{:S(2)}) copy-start(bf16[8,64,128]{2,1,0:T(8,128)(2,1)S(1)} %collective-permute-done.6) | copy-start | bytes 393220
  20.2 3.3 %copy-start = (bf16[512,1024]{1,0:T(8,128)(2,1)S(1)}, bf16[512,1024]{1,0:T(8,128)(2,1)}, u32[]{:S(2)}) copy-start(bf16[512,1024]{1,0:T(8,128)(2,1)} %refs_0_.2) | copy-start | bytes 3145732
  20.2 6.1 %collective-permute-start.7 = (bf16[8,64,128]{2,1,0:T(8,128)(2,1)}, bf16[8,64,128]{2,1,0:T(8,128)(2,1)}, u32[]{:S(2)}, u32[]{:S(2)}) collective-permute-start(bf16[8,64,128]{2,1,0:T(8,128)(2,1)} %fusion.19), channel_id=1, source_target_pairs={{0,4},{4,0},{8,12},{12,8},{16,20},{20,16},{24,28},{28,24},{1,5},{5... | collective-permute-start | bytes 393224 | tf_op jit(solution)/shard_map/ppermute | solution.py:80
  24.9 16.6 %collective-permute-start.2 = (bf16[512,1024]{1,0:T(8,128)(2,1)}, bf16[512,1024]{1,0:T(8,128)(2,1)S(1)}, u32[]{:S(2)}, u32[]{:S(2)}) collective-permute-start(bf16[512,1024]{1,0:T(8,128)(2,1)} %collective-permute-done), channel_id=1, source_target_pairs={{0,2},{1,3},{2,0},{3,1},{4,5},{5,4},{6,7},{7,6},{8,10},{9,11},{10,... | collective-permute-start | bytes 3145736 | tf_op jit(solution)/shard_map/ppermute | solution.py:38
  34.6 9.8 %copy-start.1 = (bf16[512,1024]{0,1:T(8,128)(2,1)S(1)}, bf16[512,1024]{0,1:T(8,128)(2,1)}, u32[]{:S(2)}) copy-start(bf16[512,1024]{0,1:T(8,128)(2,1)} %copy.19) | copy-start | bytes 3145732
  44.4 6.1 %copy-start.3 = (bf16[512,1024]{1,0:T(8,128)(2,1)}, bf16[512,1024]{1,0:T(8,128)(2,1)S(1)}, u32[]{:S(2)}) copy-start(bf16[512,1024]{1,0:T(8,128)(2,1)S(1)} %fusion.refs_3_) | copy-start | bytes 3145732
  44.9 1.6 %collective-permute-start.8 = (bf16[8,128,128]{2,1,0:T(8,128)(2,1)S(1)}, bf16[8,128,128]{2,1,0:T(8,128)(2,1)S(1)}, u32[]{:S(2)}, u32[]{:S(2)}) collective-permute-start(bf16[8,128,128]{2,1,0:T(8,128)(2,1)S(1)} %fusion.11), channel_id=1, source_target_pairs={{0,4},{4,0},{8,12},{12,8},{16,20},{20,16},{24,28},{28,24},{1,5},{5... | collective-permute-start | bytes 786440 | tf_op jit(solution)/shard_map/ppermute | solution.py:51
  46.6 14.8 %collective-permute-start.10 = (bf16[8,64,128]{2,1,0:T(8,128)(2,1)S(1)}, bf16[8,64,128]{2,1,0:T(8,128)(2,1)S(1)}, u32[]{:S(2)}, u32[]{:S(2)}) collective-permute-start(bf16[8,64,128]{2,1,0:T(8,128)(2,1)S(1)} %dynamic-slice_add_fusion), channel_id=1, source_target_pairs={{16,0},{20,4},{24,8},{28,12},{17,1},{21,5},{25,9},{29,13},{18,2},{... | collective-permute-start | bytes 393224 | tf_op jit(solution)/shard_map/ppermute | solution.py:67
  47.9 13.5 %collective-permute-start.11 = (bf16[8,64,128]{2,1,0:T(8,128)(2,1)S(1)}, bf16[8,64,128]{2,1,0:T(8,128)(2,1)S(1)}, u32[]{:S(2)}, u32[]{:S(2)}) collective-permute-start(bf16[8,64,128]{2,1,0:T(8,128)(2,1)S(1)} %dynamic-slice_add_fusion), channel_id=1, source_target_pairs={{24,0},{28,4},{25,1},{29,5},{26,2},{30,6},{27,3},{31,7}} | collective-permute-start | bytes 393224 | tf_op jit(solution)/shard_map/ppermute | solution.py:67
  49.2 12.2 %collective-permute-start.9 = (bf16[8,64,128]{2,1,0:T(8,128)(2,1)S(1)}, bf16[8,64,128]{2,1,0:T(8,128)(2,1)S(1)}, u32[]{:S(2)}, u32[]{:S(2)}) collective-permute-start(bf16[8,64,128]{2,1,0:T(8,128)(2,1)S(1)} %dynamic-slice_add_fusion), channel_id=1, source_target_pairs={{8,0},{12,4},{16,8},{20,12},{24,16},{28,20},{9,1},{13,5},{17,9},{2... | collective-permute-start | bytes 393224 | tf_op jit(solution)/shard_map/ppermute | solution.py:67
  61.4 1.4 %collective-permute-start.12 = (bf16[8,64,128]{2,1,0:T(8,128)(2,1)S(1)}, bf16[8,64,128]{2,1,0:T(8,128)(2,1)S(1)}, u32[]{:S(2)}, u32[]{:S(2)}) collective-permute-start(bf16[8,64,128]{2,1,0:T(8,128)(2,1)S(1)} %convert_element_type.78), channel_id=1, source_target_pairs={{0,4},{4,0},{8,12},{12,8},{16,20},{20,16},{24,28},{28,24},{1,5},{5... | collective-permute-start | bytes 393224 | tf_op jit(solution)/shard_map/ppermute | solution.py:80

commit v20 on v19

--- a/solution.py
+++ b/solution.py
@@ -2,6 +2,7 @@
 import jax.numpy as jnp
 from jax import lax
 from jax.experimental import pallas as pl
+from jax.experimental.pallas import tpu as pltpu
 from jax.sharding import PartitionSpec as P
 
 DH = 128
@@ -44,7 +45,7 @@
     return acc, tied
 
 
-def ctx_exclusive(state, ctx_size, reverse, cover=None):
+def ctx_exclusive(state, ctx_size, reverse, cover=None, unassembled=False):
     core = lax.axis_index("ctx") % 2
     chips = ctx_size // 2
     rounded = state.astype(jnp.bfloat16)
@@ -78,6 +79,13 @@
         covered = cover.fn(*held)
         others, covered = lax.optimization_barrier((others, covered))
     theirs = lax.ppermute(others.astype(jnp.bfloat16), "ctx", flip_pairs(ctx_size, 1))
+    same_chip = (core == 0) if reverse else (core == 1)
+    if unassembled:
+        base = jnp.where(same_chip, partner, 0.0)
+        base = lax.dynamic_update_slice_in_dim(
+            base, lax.dynamic_slice_in_dim(base, core * half, half, axis=1) + others, core * half, axis=1
+        )
+        return (base, theirs), covered
     theirs = theirs.astype(jnp.float32)
     lower = jnp.where(core == 0, others, theirs)
     upper = jnp.where(core == 0, theirs, others)
@@ -125,11 +133,18 @@
         gv_ref[:, cols] = gv_t.T.astype(gv_ref.dtype)
 
 
-def state_kernel(scale, per_step, k_ref, v_ref, qg_ref, gkp_ref, gvp_ref, gk_ref, gv_ref):
+def state_kernel(scale, per_step, k_ref, v_ref, qg_ref, gkp_ref, gvp_ref, gk_ref, gv_ref,
+                 core_ref=None, theirs_ref=None):
     for i in range(per_step):
         cols = pl.ds(i * DH, DH)
         k, v = k_ref[:, cols], v_ref[:, cols]
-        qg_high, qg_low = split_state(qg_ref[0, i] * scale)
+        qg = qg_ref[0, i]
+        if theirs_ref is not None:
+            part = theirs_ref[0, i].astype(jnp.float32)
+            part = jnp.concatenate([part, part], axis=0)
+            row = lax.broadcasted_iota(jnp.int32, qg.shape, 0)
+            qg = qg + jnp.where((row * 2) // qg.shape[0] != core_ref[0], part, 0.0)
+        qg_high, qg_low = split_state(qg * scale)
         gk = gkp_ref[:, cols].astype(jnp.float32)
         gk = gk + lax.dot_general(v, qg_high, NT, preferred_element_type=jnp.float32)
         gk = gk + lax.dot_general(v, qg_low, NT, preferred_element_type=jnp.float32)
@@ -161,25 +176,48 @@
     )(q, k, v, g, kv_state)
 
 
-def state_part(k, v, qg_state, parts, blocks, block_len, heads, scale):
+def state_part(k, v, qg_state, parts, blocks, block_len, heads, scale, theirs=None):
     per_step = 4 if heads % 4 == 0 else (2 if heads % 2 == 0 else 1)
-    tok = pl.BlockSpec((block_len, DH * per_step), lambda n, h: (n, h))
-    st = pl.BlockSpec((1, per_step, DH, DH), lambda n, h: (n, h, 0, 0))
     rows, width = k.shape
     out = jax.ShapeDtypeStruct((rows, width), jnp.bfloat16)
+    cost = pl.CostEstimate(
+        flops=blocks * heads * 4 * 2 * block_len * DH * DH,
+        transcendentals=0,
+        bytes_accessed=rows * width * 12,
+    )
+    if theirs is None:
+        tok = pl.BlockSpec((block_len, DH * per_step), lambda n, h: (n, h))
+        st = pl.BlockSpec((1, per_step, DH, DH), lambda n, h: (n, h, 0, 0))
+        return pl.pallas_call(
+            lambda *refs: state_kernel(scale, per_step, *refs),
+            grid=(blocks, heads // per_step),
+            in_specs=[tok, tok, st, tok, tok],
+            out_specs=[tok, tok],
+            out_shape=[out, out],
+            cost_estimate=cost,
+            name="state_part",
+        )(k, v, qg_state, *parts)
+    tok = pl.BlockSpec((block_len, DH * per_step), lambda n, h, c: (n, h))
+    st = pl.BlockSpec((1, per_step, DH, DH), lambda n, h, c: (n, h, 0, 0))
+    half = pl.BlockSpec((1, per_step, DH // 2, DH), lambda n, h, c: (n, h, 0, 0))
+    core = jnp.reshape(lax.axis_index("ctx") % 2, (1,)).astype(jnp.int32)
+
+    def kernel(core_ref, k_ref, v_ref, qg_ref, gkp_ref, gvp_ref, theirs_ref, gk_ref, gv_ref):
+        state_kernel(scale, per_step, k_ref, v_ref, qg_ref, gkp_ref, gvp_ref, gk_ref, gv_ref,
+                     core_ref=core_ref, theirs_ref=theirs_ref)
+
     return pl.pallas_call(
-        lambda *refs: state_kernel(scale, per_step, *refs),
-        grid=(blocks, heads // per_step),
-        in_specs=[tok, tok, st, tok, tok],
-        out_specs=[tok, tok],
+        kernel,
+        grid_spec=pltpu.PrefetchScalarGridSpec(
+            num_scalar_prefetch=1,
+            grid=(blocks, heads // per_step),
+            in_specs=[tok, tok, st, tok, tok, half],
+            out_specs=[tok, tok],
+        ),
         out_shape=[out, out],
-        cost_estimate=pl.CostEstimate(
-            flops=blocks * heads * 4 * 2 * block_len * DH * DH,
-            transcendentals=0,
-            bytes_accessed=rows * width * 12,
-        ),
+        cost_estimate=cost,
         name="state_part",
-    )(k, v, qg_state, *parts)
+    )(core, k, v, qg_state, *parts, theirs)
 
 
 def make_shards(ctx_size, head_size):
@@ -219,11 +257,16 @@
                 ),
                 (grad_heads, kv_entry),
             ),
+            unassembled=blocks == 1,
         )
         if blocks == 1:
-            qg_entry = qg_after[None]
-        else:
-            qg_entry = qg_after[None] + qg_running - qg_blocks
+            base, theirs = qg_after
+            gk, gv = state_part(
+                keys, values, base[None], (gk_part, gv_part), blocks, block_len, heads,
+                scale_factor, theirs=theirs[None],
+            )
+            return gq, gk, gv
+        qg_entry = qg_after[None] + qg_running - qg_blocks
         gk, gv = state_part(
             keys, values, qg_entry, (gk_part, gv_part), blocks, block_len, heads, scale_factor
         )

time: 68.1 us -> 68 us (level)
  other arithmetic: 3.8 us -> 3.04 us
    broadcast_in_dim x1 -> x0, other arithmetic: 0.86 us -> none  [shards(): qg_entry = qg_after[None]]
where the time goes in v20:
time: 68 us; the launch traced here: 67.7 us
  starting transfers between devices  19.4 us (29%)
  waiting for transfers between devices  15.2 us (22%)
  matrix products  13.3 us (20%)
  Pallas kernels  12.2 us (18%)
  local copies, waits for them, and re-layouts  3.61 us (5%)
  other arithmetic  3.04 us (4%)
  between operations  0.9 us (1%)
    ppermute x6, starting transfers between devices, ctx_exclusive(): others = others + lax.ppermute(sent, 'ctx', pairs(step)).astype(jnp.float32)  13.2 us
    dot_general x4, matrix products, mm(): lax.dot_general(a, b, (((1,), (1,)), ((), ())), preferred_element_type=jn...  12.4 us
    pallas_call x1, Pallas kernels, attention_part(): pl.pallas_call(lambda *refs: scores_kernel(scale, per_step, *refs), grid=...  8.03 us
    ppermute x1, waiting for transfers between devices, project(): diag = lax.ppermute(to_relay, ('ctx', 'head'), route(2, 1))  6.86 us
    ppermute x6, waiting for transfers between devices, ctx_exclusive(): others = others + lax.ppermute(sent, 'ctx', pairs(step)).astype(jnp.float32)  5.55 us
    pallas_call x1, Pallas kernels, state_part(): pl.pallas_call(kernel, grid_spec=pltpu.PrefetchScalarGridSpec(num_scalar_...  4.12 us
    ppermute x1, starting transfers between devices, project(): to_relay = lax.ppermute(og, ('ctx', 'head'), route(1, 2))  2.56 us
    reshape x1, local copies, waits for them, and re-layouts  1.58 us
  transfers between devices with their start and end apart: 13, of which 6 were waited for; matrix products, arithmetic and copies ran while one was open for 20% of the time, Pallas kernels for 12%

profile of v20, /device:TPU:0, one launch (start us, length us, event | category | flops | bytes accessed | tf_op | source)
XLA Modules:
  0.0 67.7 jit_solution(7289086475886076815)
XLA Ops:
  0.6 1.6 %copy.18 = bf16[512,1024]{0,1:T(8,128)(2,1)S(1)} copy(bf16[512,1024]{1,0:T(8,128)(2,1)} %k_ref.1) | data formatting | bytes 2097152 | tf_op jit(solution)/shard_map/reshape
  3.2 2.6 %collective-permute-start = (bf16[512,1024]{1,0:T(8,128)(2,1)}, bf16[512,1024]{1,0:T(8,128)(2,1)}, u32[]{:S(2)}, u32[]{:S(2)}) collective-permute-start(bf16[512,1024]{1,0:T(8,128)(2,1)} %param.8), channel_id=1, source_target_pairs={{0,1},{1,0},{2,3},{3,2},{4,6},{5,7},{6,4},{7,5},{8,9},{9,8},{10,11... | collective-permute-start | bytes 3145736 | tf_op jit(solution)/shard_map/ppermute | solution.py:37
  5.9 3.5 %collective-permute-start.4 = (bf16[8,64,128]{2,1,0:T(8,128)(2,1)S(1)}, bf16[8,64,128]{2,1,0:T(8,128)(2,1)S(1)}, u32[]{:S(2)}, u32[]{:S(2)}) collective-permute-start(bf16[8,64,128]{2,1,0:T(8,128)(2,1)S(1)} %fusion.17), channel_id=1, source_target_pairs={{0,8},{4,12},{8,16},{12,20},{16,24},{20,28},{1,9},{5,13},{9,17},{1... | collective-permute-start | bytes 393224 | tf_op jit(solution)/shard_map/ppermute | solution.py:68
  9.4 4.5 %collective-permute-start.5 = (bf16[8,64,128]{2,1,0:T(8,128)(2,1)S(1)}, bf16[8,64,128]{2,1,0:T(8,128)(2,1)S(1)}, u32[]{:S(2)}, u32[]{:S(2)}) collective-permute-start(bf16[8,64,128]{2,1,0:T(8,128)(2,1)S(1)} %fusion.17), channel_id=1, source_target_pairs={{0,16},{4,20},{8,24},{12,28},{1,17},{5,21},{9,25},{13,29},{2,18},{... | collective-permute-start | bytes 393224 | tf_op jit(solution)/shard_map/ppermute | solution.py:68
  13.9 1.3 %collective-permute-start.6 = (bf16[8,64,128]{2,1,0:T(8,128)(2,1)S(1)}, bf16[8,64,128]{2,1,0:T(8,128)(2,1)S(1)}, u32[]{:S(2)}, u32[]{:S(2)}) collective-permute-start(bf16[8,64,128]{2,1,0:T(8,128)(2,1)S(1)} %fusion.17), channel_id=1, source_target_pairs={{0,24},{4,28},{1,25},{5,29},{2,26},{6,30},{3,27},{7,31}} | collective-permute-start | bytes 393224 | tf_op jit(solution)/shard_map/ppermute | solution.py:68
  15.2 1.6 %collective-permute-start.1 = (bf16[512,1024]{1,0:T(8,128)(2,1)}, bf16[512,1024]{1,0:T(8,128)(2,1)}, u32[]{:S(2)}, u32[]{:S(2)}) collective-permute-start(bf16[512,1024]{1,0:T(8,128)(2,1)} %param.8), channel_id=1, source_target_pairs={{0,2},{1,3},{2,0},{3,1},{4,5},{5,4},{6,7},{7,6},{8,10},{9,11},{10,... | collective-permute-start | bytes 3145736 | tf_op jit(solution)/shard_map/ppermute | solution.py:38
  16.8 1.0 %collective-permute-done.5 = bf16[8,64,128]{2,1,0:T(8,128)(2,1)S(1)} collective-permute-done((bf16[8,64,128]{2,1,0:T(8,128)(2,1)S(1)}, bf16[8,64,128]{2,1,0:T(8,128)(2,1)S(1)}, u32[]{:S(2)}, u32[]{:S(2)}) %collective-permute-start.5) | collective-permute-done | bytes 131104 | tf_op jit(solution)/shard_map/ppermute | solution.py:68
  17.7 1.8 %collective-permute-done.6 = bf16[8,64,128]{2,1,0:T(8,128)(2,1)S(1)} collective-permute-done((bf16[8,64,128]{2,1,0:T(8,128)(2,1)S(1)}, bf16[8,64,128]{2,1,0:T(8,128)(2,1)S(1)}, u32[]{:S(2)}, u32[]{:S(2)}) %collective-permute-start.6) | collective-permute-done | bytes 131104 | tf_op jit(solution)/shard_map/ppermute | solution.py:68
  20.3 3.2 %fusion.7 = f32[1024,512]{0,1:T(8,128)S(1)} fusion(bf16[512,1024]{1,0:T(8,128)(2,1)} %param.8, bf16[1024,4096]{1,0:T(8,128)(2,1)} %param.9, s32[]{:T(128)S(6)} %select_n.57), kind=kOutput, calls=%fused_computation.8 | convolution fusion | flops 1073741824 | bytes 5242884 | tf_op jit(solution)/shard_map/dot_general | solution.py:22
  23.5 1.3 %copy.19 = bf16[512,1024]{0,1:T(8,128)(2,1)} copy(bf16[512,1024]{1,0:T(8,128)(2,1)S(1)} %copy-done.2) | data formatting | bytes 2097152 | tf_op jit(solution)/shard_map/reshape.3
  24.9 1.4 %collective-permute-start.2 = (bf16[512,1024]{1,0:T(8,128)(2,1)}, bf16[512,1024]{1,0:T(8,128)(2,1)S(1)}, u32[]{:S(2)}, u32[]{:S(2)}) collective-permute-start(bf16[512,1024]{1,0:T(8,128)(2,1)} %collective-permute-done), channel_id=1, source_target_pairs={{0,2},{1,3},{2,0},{3,1},{4,5},{5,4},{6,7},{7,6},{8,10},{9,11},{10,... | collective-permute-start | bytes 3145736 | tf_op jit(solution)/shard_map/ppermute | solution.py:39
  26.3 1.1 %convert_select_fusion.1 = (f32[8,64,128]{2,1,0:T(8,128)S(1)}, f32[8,64,128]{2,1,0:T(8,128)S(1)}) fusion(bf16[8,64,128]{2,1,0:T(8,128)(2,1)} %collective-permute-done.7, pred[]{:T(512)S(6)} %eq.13, bf16[8,64,128]{2,1,0:T(8,128)(2,1)} %copy-done.6, bf16[8,64,128]{2,1,0:T(8,128)(2,1)} %copy-done.5, bf16[8,64,128]{2,1,0:T(8,128)(2,1)S(1)} %collective-permute-done.4), kind=kLoop, calls=%fused_computation.20 | loop fusion | flops 524288 | bytes 1048577 | tf_op jit(solution)/shard_map/jit(_where)/select_n | solution.py:90
  28.3 3.1 %fusion.5 = f32[1024,512]{0,1:T(8,128)S(1)} fusion(bf16[512,1024]{1,0:T(8,128)(2,1)} %collective-permute-done, bf16[1024,4096]{1,0:T(8,128)(2,1)} %param.9, s32[]{:T(128)S(6)} %select_n.59), kind=kOutput, calls=%fused_computation.6 | convolution fusion | flops 1073741824 | bytes 5242884 | tf_op jit(solution)/shard_map/dot_general | solution.py:22
  31.5 3.2 %fusion.3 = f32[1024,512]{0,1:T(8,128)S(1)} fusion(bf16[512,1024]{1,0:T(8,128)(2,1)} %collective-permute-done.1, bf16[1024,4096]{1,0:T(8,128)(2,1)} %param.9, s32[]{:T(128)S(6)} %select_n.60), kind=kOutput, calls=%fused_computation.4 | convolution fusion | flops 1073741824 | bytes 5242884 | tf_op jit(solution)/shard_map/dot_general | solution.py:22
  34.6 6.9 %collective-permute-done.2 = bf16[512,1024]{1,0:T(8,128)(2,1)S(1)} collective-permute-done((bf16[512,1024]{1,0:T(8,128)(2,1)}, bf16[512,1024]{1,0:T(8,128)(2,1)S(1)}, u32[]{:S(2)}, u32[]{:S(2)}) %collective-permute-start.2) | collective-permute-done | bytes 1048608 | tf_op jit(solution)/shard_map/ppermute | solution.py:39
  41.5 2.9 %fusion.refs_3_ = bf16[512,1024]{1,0:T(8,128)(2,1)S(1)} fusion(f32[1024,512]{0,1:T(8,128)S(1)} %fusion.3, f32[1024,512]{0,1:T(8,128)S(1)} %fusion.7, f32[1024,512]{0,1:T(8,128)S(1)} %fusion.5, bf16[512,1024]{1,0:T(8,128)(2,1)S(1)} %collective-permute-done.2, bf16[1024,4096]{1,0:T(8,128)(2,1)} %param.9, s32[]{:T(128)S(6)} %select_n.67), kind=kOutput, calls=%fused_computation.1 | convolution fusion | flops 1075838976 | bytes 10485764 | tf_op jit(solution)/shard_map/dot_general | solution.py:22
  45.0 1.5 %collective-permute-done.8 = bf16[8,128,128]{2,1,0:T(8,128)(2,1)S(1)} collective-permute-done((bf16[8,128,128]{2,1,0:T(8,128)(2,1)S(1)}, bf16[8,128,128]{2,1,0:T(8,128)(2,1)S(1)}, u32[]{:S(2)}, u32[]{:S(2)}) %collective-permute-start.8) | collective-permute-done | bytes 262176 | tf_op jit(solution)/shard_map/ppermute | solution.py:52
  46.6 1.3 %collective-permute-start.10 = (bf16[8,64,128]{2,1,0:T(8,128)(2,1)S(1)}, bf16[8,64,128]{2,1,0:T(8,128)(2,1)S(1)}, u32[]{:S(2)}, u32[]{:S(2)}) collective-permute-start(bf16[8,64,128]{2,1,0:T(8,128)(2,1)S(1)} %dynamic-slice_add_fusion), channel_id=1, source_target_pairs={{16,0},{20,4},{24,8},{28,12},{17,1},{21,5},{25,9},{29,13},{18,2},{... | collective-permute-start | bytes 393224 | tf_op jit(solution)/shard_map/ppermute | solution.py:68
  47.9 1.3 %collective-permute-start.11 = (bf16[8,64,128]{2,1,0:T(8,128)(2,1)S(1)}, bf16[8,64,128]{2,1,0:T(8,128)(2,1)S(1)}, u32[]{:S(2)}, u32[]{:S(2)}) collective-permute-start(bf16[8,64,128]{2,1,0:T(8,128)(2,1)S(1)} %dynamic-slice_add_fusion), channel_id=1, source_target_pairs={{24,0},{28,4},{25,1},{29,5},{26,2},{30,6},{27,3},{31,7}} | collective-permute-start | bytes 393224 | tf_op jit(solution)/shard_map/ppermute | solution.py:68
  49.2 1.3 %collective-permute-start.9 = (bf16[8,64,128]{2,1,0:T(8,128)(2,1)S(1)}, bf16[8,64,128]{2,1,0:T(8,128)(2,1)S(1)}, u32[]{:S(2)}, u32[]{:S(2)}) collective-permute-start(bf16[8,64,128]{2,1,0:T(8,128)(2,1)S(1)} %dynamic-slice_add_fusion), channel_id=1, source_target_pairs={{8,0},{12,4},{16,8},{20,12},{24,16},{28,20},{9,1},{13,5},{17,9},{2... | collective-permute-start | bytes 393224 | tf_op jit(solution)/shard_map/ppermute | solution.py:68
  50.5 8.0 %attention_part.1 = (bf16[512,1024]{1,0:T(8,128)(2,1)}, bf16[512,1024]{1,0:T(8,128)(2,1)}, bf16[512,1024]{1,0:T(8,128)(2,1)}) custom-call(bf16[512,1024]{1,0:T(8,128)(2,1)} %refs_0_.1, bf16[512,1024]{1,0:T(8,128)(2,1)} %k_ref.1, bf16[512,1024]{1,0:T(8,128)(2,1)} %v_ref.1, bf16[512,1024]{1,0:T(8,128)(2,1)} %copy-done.4, f32[1,8,128,128]{3,2,1,0:T(8,128)} %fusion.16.refs_4_), custom_call_target="tpu_custom_call" | custom-call | flops 3221225472 | bytes 7340032 | tf_op jit(solution)/shard_map/attention_part/pallas_call | solution.py:164
  58.6 2.8 %collective-permute-done.10 = bf16[8,64,128]{2,1,0:T(8,128)(2,1)S(1)} collective-permute-done((bf16[8,64,128]{2,1,0:T(8,128)(2,1)S(1)}, bf16[8,64,128]{2,1,0:T(8,128)(2,1)S(1)}, u32[]{:S(2)}, u32[]{:S(2)}) %collective-permute-start.10) | collective-permute-done | bytes 131104 | tf_op jit(solution)/shard_map/ppermute | solution.py:68
  61.6 1.3 %collective-permute-done.12 = bf16[8,64,128]{2,1,0:T(8,128)(2,1)S(1)} collective-permute-done((bf16[8,64,128]{2,1,0:T(8,128)(2,1)S(1)}, bf16[8,64,128]{2,1,0:T(8,128)(2,1)S(1)}, u32[]{:S(2)}, u32[]{:S(2)}) %collective-permute-start.12) | collective-permute-done | bytes 131104 | tf_op jit(solution)/shard_map/ppermute | solution.py:81
  63.5 4.1 %state_part.1 = (bf16[512,1024]{1,0:T(8,128)(2,1)}, bf16[512,1024]{1,0:T(8,128)(2,1)}) custom-call(s32[1]{0:T(128)} %bitcast.5.core_ref, bf16[512,1024]{1,0:T(8,128)(2,1)} %k_ref.1, bf16[512,1024]{1,0:T(8,128)(2,1)} %v_ref.1, f32[1,8,128,128]{3,2,1,0:T(8,128)} %copy-done, bf16[512,1024]{1,0:T(8,128)(2,1)} %get-tuple-element.27.gkp_ref, ...), custom_call_target="tpu_custom_call" | custom-call | flops 536870912 | bytes 6291456 | tf_op jit(solution)/shard_map/state_part/pallas_call | solution.py:209
  (39 shorter events, 4.2 us)
Async XLA Ops:
  0.6 1.6 %copy-start.1 = (bf16[512,1024]{1,0:T(8,128)(2,1)S(1)}, bf16[512,1024]{1,0:T(8,128)(2,1)}, u32[]{:S(2)}) copy-start(bf16[512,1024]{1,0:T(8,128)(2,1)} %v_ref.1) | copy-start | bytes 3145732
  2.7 3.1 %collective-permute-start.3 = (bf16[8,128,128]{2,1,0:T(8,128)(2,1)S(1)}, bf16[8,128,128]{2,1,0:T(8,128)(2,1)S(1)}, u32[]{:S(2)}, u32[]{:S(2)}) collective-permute-start(bf16[8,128,128]{2,1,0:T(8,128)(2,1)S(1)} %convolution_convert_fusion.1), channel_id=1, source_target_pairs={{0,4},{4,0},{8,12},{12,8},{16,20},{20,16},{24,28},{28,24},{1,5},{5... | collective-permute-start | bytes 786440 | tf_op jit(solution)/shard_map/ppermute | solution.py:52
  3.2 21.6 %collective-permute-start = (bf16[512,1024]{1,0:T(8,128)(2,1)}, bf16[512,1024]{1,0:T(8,128)(2,1)}, u32[]{:S(2)}, u32[]{:S(2)}) collective-permute-start(bf16[512,1024]{1,0:T(8,128)(2,1)} %param.8), channel_id=1, source_target_pairs={{0,1},{1,0},{2,3},{3,2},{4,6},{5,7},{6,4},{7,5},{8,9},{9,8},{10,11... | collective-permute-start | bytes 3145736 | tf_op jit(solution)/shard_map/ppermute | solution.py:37
  5.9 10.9 %collective-permute-start.4 = (bf16[8,64,128]{2,1,0:T(8,128)(2,1)S(1)}, bf16[8,64,128]{2,1,0:T(8,128)(2,1)S(1)}, u32[]{:S(2)}, u32[]{:S(2)}) collective-permute-start(bf16[8,64,128]{2,1,0:T(8,128)(2,1)S(1)} %fusion.17), channel_id=1, source_target_pairs={{0,8},{4,12},{8,16},{12,20},{16,24},{20,28},{1,9},{5,13},{9,17},{1... | collective-permute-start | bytes 393224 | tf_op jit(solution)/shard_map/ppermute | solution.py:68
  9.4 8.4 %collective-permute-start.5 = (bf16[8,64,128]{2,1,0:T(8,128)(2,1)S(1)}, bf16[8,64,128]{2,1,0:T(8,128)(2,1)S(1)}, u32[]{:S(2)}, u32[]{:S(2)}) collective-permute-start(bf16[8,64,128]{2,1,0:T(8,128)(2,1)S(1)} %fusion.17), channel_id=1, source_target_pairs={{0,16},{4,20},{8,24},{12,28},{1,17},{5,21},{9,25},{13,29},{2,18},{... | collective-permute-start | bytes 393224 | tf_op jit(solution)/shard_map/ppermute | solution.py:68
  13.9 5.7 %collective-permute-start.6 = (bf16[8,64,128]{2,1,0:T(8,128)(2,1)S(1)}, bf16[8,64,128]{2,1,0:T(8,128)(2,1)S(1)}, u32[]{:S(2)}, u32[]{:S(2)}) collective-permute-start(bf16[8,64,128]{2,1,0:T(8,128)(2,1)S(1)} %fusion.17), channel_id=1, source_target_pairs={{0,24},{4,28},{1,25},{5,29},{2,26},{6,30},{3,27},{7,31}} | collective-permute-start | bytes 393224 | tf_op jit(solution)/shard_map/ppermute | solution.py:68
  15.2 16.3 %collective-permute-start.1 = (bf16[512,1024]{1,0:T(8,128)(2,1)}, bf16[512,1024]{1,0:T(8,128)(2,1)}, u32[]{:S(2)}, u32[]{:S(2)}) collective-permute-start(bf16[512,1024]{1,0:T(8,128)(2,1)} %param.8), channel_id=1, source_target_pairs={{0,2},{1,3},{2,0},{3,1},{4,5},{5,4},{6,7},{7,6},{8,10},{9,11},{10,... | collective-permute-start | bytes 3145736 | tf_op jit(solution)/shard_map/ppermute | solution.py:38
  17.7 2.5 %copy-start.5 = (bf16[8,64,128]{2,1,0:T(8,128)(2,1)}, bf16[8,64,128]{2,1,0:T(8,128)(2,1)S(1)}, u32[]{:S(2)}) copy-start(bf16[8,64,128]{2,1,0:T(8,128)(2,1)S(1)} %collective-permute-done.5) | copy-start | bytes 393220
  19.5 0.7 %copy-start.6 = (bf16[8,64,128]{2,1,0:T(8,128)(2,1)}, bf16[8,64,128]{2,1,0:T(8,128)(2,1)S(1)}, u32[]{:S(2)}) copy-start(bf16[8,64,128]{2,1,0:T(8,128)(2,1)S(1)} %collective-permute-done.6) | copy-start | bytes 393220
  20.2 3.3 %copy-start.2 = (bf16[512,1024]{1,0:T(8,128)(2,1)S(1)}, bf16[512,1024]{1,0:T(8,128)(2,1)}, u32[]{:S(2)}) copy-start(bf16[512,1024]{1,0:T(8,128)(2,1)} %refs_0_.1) | copy-start | bytes 3145732
  20.2 6.1 %collective-permute-start.7 = (bf16[8,64,128]{2,1,0:T(8,128)(2,1)}, bf16[8,64,128]{2,1,0:T(8,128)(2,1)}, u32[]{:S(2)}, u32[]{:S(2)}) collective-permute-start(bf16[8,64,128]{2,1,0:T(8,128)(2,1)} %fusion.19), channel_id=1, source_target_pairs={{0,4},{4,0},{8,12},{12,8},{16,20},{20,16},{24,28},{28,24},{1,5},{5... | collective-permute-start | bytes 393224 | tf_op jit(solution)/shard_map/ppermute | solution.py:81
  24.9 16.6 %collective-permute-start.2 = (bf16[512,1024]{1,0:T(8,128)(2,1)}, bf16[512,1024]{1,0:T(8,128)(2,1)S(1)}, u32[]{:S(2)}, u32[]{:S(2)}) collective-permute-start(bf16[512,1024]{1,0:T(8,128)(2,1)} %collective-permute-done), channel_id=1, source_target_pairs={{0,2},{1,3},{2,0},{3,1},{4,5},{5,4},{6,7},{7,6},{8,10},{9,11},{10,... | collective-permute-start | bytes 3145736 | tf_op jit(solution)/shard_map/ppermute | solution.py:39
  34.6 9.8 %copy-start.3 = (bf16[512,1024]{0,1:T(8,128)(2,1)S(1)}, bf16[512,1024]{0,1:T(8,128)(2,1)}, u32[]{:S(2)}) copy-start(bf16[512,1024]{0,1:T(8,128)(2,1)} %copy.19) | copy-start | bytes 3145732
  44.4 6.1 %copy-start.4 = (bf16[512,1024]{1,0:T(8,128)(2,1)}, bf16[512,1024]{1,0:T(8,128)(2,1)S(1)}, u32[]{:S(2)}) copy-start(bf16[512,1024]{1,0:T(8,128)(2,1)S(1)} %fusion.refs_3_) | copy-start | bytes 3145732
  44.9 1.6 %collective-permute-start.8 = (bf16[8,128,128]{2,1,0:T(8,128)(2,1)S(1)}, bf16[8,128,128]{2,1,0:T(8,128)(2,1)S(1)}, u32[]{:S(2)}, u32[]{:S(2)}) collective-permute-start(bf16[8,128,128]{2,1,0:T(8,128)(2,1)S(1)} %fusion.11), channel_id=1, source_target_pairs={{0,4},{4,0},{8,12},{12,8},{16,20},{20,16},{24,28},{28,24},{1,5},{5... | collective-permute-start | bytes 786440 | tf_op jit(solution)/shard_map/ppermute | solution.py:52
  46.6 14.8 %collective-permute-start.10 = (bf16[8,64,128]{2,1,0:T(8,128)(2,1)S(1)}, bf16[8,64,128]{2,1,0:T(8,128)(2,1)S(1)}, u32[]{:S(2)}, u32[]{:S(2)}) collective-permute-start(bf16[8,64,128]{2,1,0:T(8,128)(2,1)S(1)} %dynamic-slice_add_fusion), channel_id=1, source_target_pairs={{16,0},{20,4},{24,8},{28,12},{17,1},{21,5},{25,9},{29,13},{18,2},{... | collective-permute-start | bytes 393224 | tf_op jit(solution)/shard_map/ppermute | solution.py:68
  47.9 13.5 %collective-permute-start.11 = (bf16[8,64,128]{2,1,0:T(8,128)(2,1)S(1)}, bf16[8,64,128]{2,1,0:T(8,128)(2,1)S(1)}, u32[]{:S(2)}, u32[]{:S(2)}) collective-permute-start(bf16[8,64,128]{2,1,0:T(8,128)(2,1)S(1)} %dynamic-slice_add_fusion), channel_id=1, source_target_pairs={{24,0},{28,4},{25,1},{29,5},{26,2},{30,6},{27,3},{31,7}} | collective-permute-start | bytes 393224 | tf_op jit(solution)/shard_map/ppermute | solution.py:68
  49.2 12.2 %collective-permute-start.9 = (bf16[8,64,128]{2,1,0:T(8,128)(2,1)S(1)}, bf16[8,64,128]{2,1,0:T(8,128)(2,1)S(1)}, u32[]{:S(2)}, u32[]{:S(2)}) collective-permute-start(bf16[8,64,128]{2,1,0:T(8,128)(2,1)S(1)} %dynamic-slice_add_fusion), channel_id=1, source_target_pairs={{8,0},{12,4},{16,8},{20,12},{24,16},{28,20},{9,1},{13,5},{17,9},{2... | collective-permute-start | bytes 393224 | tf_op jit(solution)/shard_map/ppermute | solution.py:68
  61.4 1.4 %collective-permute-start.12 = (bf16[8,64,128]{2,1,0:T(8,128)(2,1)S(1)}, bf16[8,64,128]{2,1,0:T(8,128)(2,1)S(1)}, u32[]{:S(2)}, u32[]{:S(2)}) collective-permute-start(bf16[8,64,128]{2,1,0:T(8,128)(2,1)S(1)} %convert_element_type.75), channel_id=1, source_target_pairs={{0,4},{4,0},{8,12},{12,8},{16,20},{20,16},{24,28},{28,24},{1,5},{5... | collective-permute-start | bytes 393224 | tf_op jit(solution)/shard_map/ppermute | solution.py:81
  61.6 1.3 %copy-start = (f32[1,8,128,128]{3,2,1,0:T(8,128)}, f32[1,8,128,128]{3,2,1,0:T(8,128)S(1)}, u32[]{:S(2)}) copy-start(f32[1,8,128,128]{3,2,1,0:T(8,128)S(1)} %bitcast_dynamic-update-slice_fusion.qg_ref) | copy-start | bytes 1572868
  62.9 0.7 copy-start.7

commit v21 on v19

--- a/solution.py
+++ b/solution.py
@@ -48,10 +48,18 @@
     core = lax.axis_index("ctx") % 2
     chips = ctx_size // 2
     rounded = state.astype(jnp.bfloat16)
-    partner = lax.ppermute(rounded, "ctx", flip_pairs(ctx_size, 1)).astype(jnp.float32)
-    chip_sum = rounded.astype(jnp.float32) + partner
     half = state.shape[1] // 2
-    mine = lax.dynamic_slice_in_dim(chip_sum, core * half, half, axis=1)
+    swap = flip_pairs(ctx_size, 1)
+    near = lax.ppermute(
+        lax.dynamic_slice_in_dim(rounded, (1 - core) * half, half, axis=1), "ctx", swap
+    ).astype(jnp.float32)
+    mine = lax.dynamic_slice_in_dim(rounded, core * half, half, axis=1).astype(jnp.float32) + near
+    far = lax.ppermute(
+        lax.dynamic_slice_in_dim(rounded, core * half, half, axis=1), "ctx", swap
+    ).astype(jnp.float32)
+    partner = jnp.where(
+        core == 0, jnp.concatenate([near, far], axis=1), jnp.concatenate([far, near], axis=1)
+    )
 
     def pairs(step):
         if reverse:

time: 68.1 us -> 71.9 us (1.056)
  waiting for transfers between devices: 15.4 us -> 19.9 us
  other arithmetic: 3.8 us -> 2.2 us
    ppermute x6, waiting for transfers between devices: 5.62 us -> 10.3 us  [ctx_exclusive(): others = others + lax.ppermute(sent, 'ctx', pairs(step)).astype(jnp.float32)]
    add x1 -> x3, other arithmetic: 0.05 us -> 1.85 us  [the longest x2 1.79 us: ctx_exclusive(): return (chips_side + jnp.where(same_chip, partner, 0.0), covered)]
    broadcast_in_dim x2 -> x0, other arithmetic: 1.71 us -> none  [the longest x1 0.86 us: shards(): kv_entry = kv_before[None]]
    select_n x2 -> x0, other arithmetic: 1.15 us -> none  [ctx_exclusive(): lower = jnp.where(core == 0, others, theirs)]
    ppermute x1, waiting for transfers between devices: 0.01 us -> 0.81 us  [project(): to_relay = lax.ppermute(og, ('ctx', 'head'), route(1, 2))]
    ppermute x1, waiting for transfers between devices: 6.88 us -> 6.09 us  [project(): diag = lax.ppermute(to_relay, ('ctx', 'head'), route(2, 1))]
    ppermute x2 -> x4, waiting for transfers between devices: 1.52 us -> 1.34 us  [the longest x2 1.34 us: ctx_exclusive(): lax.ppermute(lax.dynamic_slice_in_dim(rounded, (1 - core) * half, half, a...]
  transfers between devices with their start and end apart: 13 -> 15, of which waited for: 6 -> 7; matrix products, arithmetic and copies ran while one was open for 20% -> 20% of each run, Pallas kernels for 12% -> 11%
where the time goes in v21:
time: 71.9 us; the launch traced here: 71.6 us
  waiting for transfers between devices  19.9 us (28%)
  starting transfers between devices  19.8 us (28%)
  matrix products  13.3 us (18%)
  Pallas kernels  12 us (17%)
  local copies, waits for them, and re-layouts  3.53 us (5%)
  other arithmetic  2.2 us (3%)
  between operations  0.95 us (1%)
    ppermute x6, starting transfers between devices, ctx_exclusive(): others = others + lax.ppermute(sent, 'ctx', pairs(step)).astype(jnp.float32)  13.2 us
    dot_general x4, matrix products, mm(): lax.dot_general(a, b, (((1,), (1,)), ((), ())), preferred_element_type=jn...  12.4 us
    ppermute x6, waiting for transfers between devices, ctx_exclusive(): others = others + lax.ppermute(sent, 'ctx', pairs(step)).astype(jnp.float32)  10.3 us
    pallas_call x1, Pallas kernels, attention_part(): pl.pallas_call(lambda *refs: scores_kernel(scale, per_step, *refs), grid=...  8.01 us
    ppermute x1, waiting for transfers between devices, project(): diag = lax.ppermute(to_relay, ('ctx', 'head'), route(2, 1))  6.09 us
    pallas_call x1, Pallas kernels, state_part(): pl.pallas_call(lambda *refs: state_kernel(scale, per_step, *refs), grid=(...  3.99 us
    ppermute x1, starting transfers between devices, project(): to_relay = lax.ppermute(og, ('ctx', 'head'), route(1, 2))  3 us
    add x2, other arithmetic, ctx_exclusive(): return (chips_side + jnp.where(same_chip, partner, 0.0), covered)  1.79 us
  transfers between devices with their start and end apart: 15, of which 7 were waited for; matrix products, arithmetic and copies ran while one was open for 20% of the time, Pallas kernels for 11%

profile of v21, /device:TPU:0, one launch (start us, length us, event | category | flops | bytes accessed | tf_op | source)
XLA Modules:
  0.0 71.6 jit_solution(14367337174048411081)
XLA Ops:
  0.6 3.0 %collective-permute-start = (bf16[512,1024]{1,0:T(8,128)(2,1)}, bf16[512,1024]{1,0:T(8,128)(2,1)}, u32[]{:S(2)}, u32[]{:S(2)}) collective-permute-start(bf16[512,1024]{1,0:T(8,128)(2,1)} %param.8), channel_id=1, source_target_pairs={{0,1},{1,0},{2,3},{3,2},{4,6},{5,7},{6,4},{7,5},{8,9},{9,8},{10,11... | collective-permute-start | bytes 3145736 | tf_op jit(solution)/shard_map/ppermute | solution.py:36
  3.6 1.5 %collective-permute-start.1 = (bf16[512,1024]{1,0:T(8,128)(2,1)}, bf16[512,1024]{1,0:T(8,128)(2,1)}, u32[]{:S(2)}, u32[]{:S(2)}) collective-permute-start(bf16[512,1024]{1,0:T(8,128)(2,1)} %param.8), channel_id=1, source_target_pairs={{0,2},{1,3},{2,0},{3,1},{4,5},{5,4},{6,7},{7,6},{8,10},{9,11},{10,... | collective-permute-start | bytes 3145736 | tf_op jit(solution)/shard_map/ppermute | solution.py:37
  5.2 1.5 %copy.18 = bf16[512,1024]{0,1:T(8,128)(2,1)S(1)} copy(bf16[512,1024]{1,0:T(8,128)(2,1)} %refs_0_.3) | data formatting | bytes 2097152 | tf_op jit(solution)/shard_map/reshape
  7.8 3.2 %fusion.7 = f32[1024,512]{0,1:T(8,128)S(1)} fusion(bf16[512,1024]{1,0:T(8,128)(2,1)} %param.8, bf16[1024,4096]{1,0:T(8,128)(2,1)} %param.9, s32[]{:T(128)S(6)} %select_n.105), kind=kOutput, calls=%fused_computation.8 | convolution fusion | flops 1073741824 | bytes 5242884 | tf_op jit(solution)/shard_map/dot_general | solution.py:21
  11.1 1.3 %copy.19 = bf16[512,1024]{0,1:T(8,128)(2,1)} copy(bf16[512,1024]{1,0:T(8,128)(2,1)S(1)} %copy-done) | data formatting | bytes 2097152 | tf_op jit(solution)/shard_map/reshape.3
  12.5 3.5 %collective-permute-start.4 = (bf16[8,64,128]{2,1,0:T(8,128)(2,1)S(1)}, bf16[8,64,128]{2,1,0:T(8,128)(2,1)S(1)}, u32[]{:S(2)}, u32[]{:S(2)}) collective-permute-start(bf16[8,64,128]{2,1,0:T(8,128)(2,1)S(1)} %get-tuple-element.33), channel_id=1, source_target_pairs={{0,8},{4,12},{8,16},{12,20},{16,24},{20,28},{1,9},{5,13},{9,17},{1... | collective-permute-start | bytes 393224 | tf_op jit(solution)/shard_map/ppermute | solution.py:75
  16.0 4.5 %collective-permute-start.5 = (bf16[8,64,128]{2,1,0:T(8,128)(2,1)S(1)}, bf16[8,64,128]{2,1,0:T(8,128)(2,1)S(1)}, u32[]{:S(2)}, u32[]{:S(2)}) collective-permute-start(bf16[8,64,128]{2,1,0:T(8,128)(2,1)S(1)} %get-tuple-element.33), channel_id=1, source_target_pairs={{0,16},{4,20},{8,24},{12,28},{1,17},{5,21},{9,25},{13,29},{2,18},{... | collective-permute-start | bytes 393224 | tf_op jit(solution)/shard_map/ppermute | solution.py:75
  20.5 1.3 %collective-permute-start.6 = (bf16[8,64,128]{2,1,0:T(8,128)(2,1)S(1)}, bf16[8,64,128]{2,1,0:T(8,128)(2,1)S(1)}, u32[]{:S(2)}, u32[]{:S(2)}) collective-permute-start(bf16[8,64,128]{2,1,0:T(8,128)(2,1)S(1)} %get-tuple-element.33), channel_id=1, source_target_pairs={{0,24},{4,28},{1,25},{5,29},{2,26},{6,30},{3,27},{7,31}} | collective-permute-start | bytes 393224 | tf_op jit(solution)/shard_map/ppermute | solution.py:75
  21.9 2.4 %collective-permute-done.5 = bf16[8,64,128]{2,1,0:T(8,128)(2,1)S(1)} collective-permute-done((bf16[8,64,128]{2,1,0:T(8,128)(2,1)S(1)}, bf16[8,64,128]{2,1,0:T(8,128)(2,1)S(1)}, u32[]{:S(2)}, u32[]{:S(2)}) %collective-permute-start.5) | collective-permute-done | bytes 131104 | tf_op jit(solution)/shard_map/ppermute | solution.py:75
  24.3 2.1 %collective-permute-done.6 = bf16[8,64,128]{2,1,0:T(8,128)(2,1)S(1)} collective-permute-done((bf16[8,64,128]{2,1,0:T(8,128)(2,1)S(1)}, bf16[8,64,128]{2,1,0:T(8,128)(2,1)S(1)}, u32[]{:S(2)}, u32[]{:S(2)}) %collective-permute-start.6) | collective-permute-done | bytes 131104 | tf_op jit(solution)/shard_map/ppermute | solution.py:75
  27.4 1.6 %collective-permute-start.2 = (bf16[512,1024]{1,0:T(8,128)(2,1)}, bf16[512,1024]{1,0:T(8,128)(2,1)S(1)}, u32[]{:S(2)}, u32[]{:S(2)}) collective-permute-start(bf16[512,1024]{1,0:T(8,128)(2,1)} %collective-permute-done), channel_id=1, source_target_pairs={{0,2},{1,3},{2,0},{3,1},{4,5},{5,4},{6,7},{7,6},{8,10},{9,11},{10,... | collective-permute-start | bytes 3145736 | tf_op jit(solution)/shard_map/ppermute | solution.py:38
  29.1 0.9 %maximum_add_fusion.refs_4_ = f32[1,8,128,128]{3,2,1,0:T(8,128)} fusion(f32[1,8,64,128]{3,2,1,0:T(8,128)S(1)} %get-tuple-element.36, f32[1,8,64,128]{3,2,1,0:T(8,128)S(1)} %get-tuple-element.35, f32[1,8,64,128]{3,2,1,0:T(8,128)S(1)} %bitcast_convert_fusion.1, f32[1,8,64,128]{3,2,1,0:T(8,128)S(1)} %convert_bitcast_fusion.1, pred[]{:T(512)S(6)} %eq.8, pred[]{:T(512)S(6)} %eq.9), kind=kLoop, calls=%fused_computation.16 | loop fusion | flops 786432 | bytes 1572866 | tf_op jit(solution)/shard_map/add | solution.py:94
  30.0 3.1 %fusion.5 = f32[1024,512]{0,1:T(8,128)S(1)} fusion(bf16[512,1024]{1,0:T(8,128)(2,1)} %collective-permute-done, bf16[1024,4096]{1,0:T(8,128)(2,1)} %param.9, s32[]{:T(128)S(6)} %select_n.107), kind=kOutput, calls=%fused_computation.6 | convolution fusion | flops 1073741824 | bytes 5242884 | tf_op jit(solution)/shard_map/dot_general | solution.py:21
  33.2 3.2 %fusion.3 = f32[1024,512]{0,1:T(8,128)S(1)} fusion(bf16[512,1024]{1,0:T(8,128)(2,1)} %collective-permute-done.1, bf16[1024,4096]{1,0:T(8,128)(2,1)} %param.9, s32[]{:T(128)S(6)} %select_n.108), kind=kOutput, calls=%fused_computation.4 | convolution fusion | flops 1073741824 | bytes 5242884 | tf_op jit(solution)/shard_map/dot_general | solution.py:21
  36.3 6.1 %collective-permute-done.2 = bf16[512,1024]{1,0:T(8,128)(2,1)S(1)} collective-permute-done((bf16[512,1024]{1,0:T(8,128)(2,1)}, bf16[512,1024]{1,0:T(8,128)(2,1)S(1)}, u32[]{:S(2)}, u32[]{:S(2)}) %collective-permute-start.2) | collective-permute-done | bytes 1048608 | tf_op jit(solution)/shard_map/ppermute | solution.py:38
  42.4 2.9 %fusion.refs_3_ = bf16[512,1024]{1,0:T(8,128)(2,1)S(1)} fusion(f32[1024,512]{0,1:T(8,128)S(1)} %fusion.3, f32[1024,512]{0,1:T(8,128)S(1)} %fusion.7, f32[1024,512]{0,1:T(8,128)S(1)} %fusion.5, bf16[512,1024]{1,0:T(8,128)(2,1)S(1)} %collective-permute-done.2, bf16[1024,4096]{1,0:T(8,128)(2,1)} %param.9, s32[]{:T(128)S(6)} %select_n.118), kind=kOutput, calls=%fused_computation.1 | convolution fusion | flops 1075838976 | bytes 10485764 | tf_op jit(solution)/shard_map/dot_general | solution.py:21
  45.9 1.3 %collective-permute-done.9 = bf16[8,64,128]{2,1,0:T(8,128)(2,1)S(1)} collective-permute-done((bf16[8,64,128]{2,1,0:T(8,128)(2,1)S(1)}, bf16[8,64,128]{2,1,0:T(8,128)(2,1)S(1)}, u32[]{:S(2)}, u32[]{:S(2)}) %collective-permute-start.9) | collective-permute-done | bytes 131104 | tf_op jit(solution)/shard_map/ppermute | solution.py:53
  47.3 1.3 %collective-permute-start.10 = (bf16[8,64,128]{2,1,0:T(8,128)(2,1)S(1)}, bf16[8,64,128]{2,1,0:T(8,128)(2,1)S(1)}, u32[]{:S(2)}, u32[]{:S(2)}) collective-permute-start(bf16[8,64,128]{2,1,0:T(8,128)(2,1)S(1)} %get-tuple-element.19), channel_id=1, source_target_pairs={{8,0},{12,4},{16,8},{20,12},{24,16},{28,20},{9,1},{13,5},{17,9},{2... | collective-permute-start | bytes 393224 | tf_op jit(solution)/shard_map/ppermute | solution.py:75
  48.6 1.3 %collective-permute-start.11 = (bf16[8,64,128]{2,1,0:T(8,128)(2,1)S(1)}, bf16[8,64,128]{2,1,0:T(8,128)(2,1)S(1)}, u32[]{:S(2)}, u32[]{:S(2)}) collective-permute-start(bf16[8,64,128]{2,1,0:T(8,128)(2,1)S(1)} %get-tuple-element.19), channel_id=1, source_target_pairs={{16,0},{20,4},{24,8},{28,12},{17,1},{21,5},{25,9},{29,13},{18,2},{... | collective-permute-start | bytes 393224 | tf_op jit(solution)/shard_map/ppermute | solution.py:75
  49.9 1.3 %collective-permute-start.12 = (bf16[8,64,128]{2,1,0:T(8,128)(2,1)S(1)}, bf16[8,64,128]{2,1,0:T(8,128)(2,1)S(1)}, u32[]{:S(2)}, u32[]{:S(2)}) collective-permute-start(bf16[8,64,128]{2,1,0:T(8,128)(2,1)S(1)} %get-tuple-element.19), channel_id=1, source_target_pairs={{24,0},{28,4},{25,1},{29,5},{26,2},{30,6},{27,3},{31,7}} | collective-permute-start | bytes 393224 | tf_op jit(solution)/shard_map/ppermute | solution.py:75
  51.4 8.0 %attention_part.1 = (bf16[512,1024]{1,0:T(8,128)(2,1)}, bf16[512,1024]{1,0:T(8,128)(2,1)}, bf16[512,1024]{1,0:T(8,128)(2,1)}) custom-call(bf16[512,1024]{1,0:T(8,128)(2,1)} %refs_0_.2, bf16[512,1024]{1,0:T(8,128)(2,1)} %refs_0_.3, bf16[512,1024]{1,0:T(8,128)(2,1)} %refs_1_.3, bf16[512,1024]{1,0:T(8,128)(2,1)} %copy-done.3, ...), custom_call_target="tpu_custom_call" | custom-call | flops 3221225472 | bytes 7340032 | tf_op jit(solution)/shard_map/attention_part/pallas_call | solution.py:157
  59.4 5.8 %collective-permute-done.11 = bf16[8,64,128]{2,1,0:T(8,128)(2,1)S(1)} collective-permute-done((bf16[8,64,128]{2,1,0:T(8,128)(2,1)S(1)}, bf16[8,64,128]{2,1,0:T(8,128)(2,1)S(1)}, u32[]{:S(2)}, u32[]{:S(2)}) %collective-permute-start.11) | collective-permute-done | bytes 131104 | tf_op jit(solution)/shard_map/ppermute | solution.py:75
  65.4 1.3 %collective-permute-done.13 = bf16[8,64,128]{2,1,0:T(8,128)(2,1)S(1)} collective-permute-done((bf16[8,64,128]{2,1,0:T(8,128)(2,1)S(1)}, bf16[8,64,128]{2,1,0:T(8,128)(2,1)S(1)}, u32[]{:S(2)}, u32[]{:S(2)}) %collective-permute-start.13) | collective-permute-done | bytes 131104 | tf_op jit(solution)/shard_map/ppermute | solution.py:88
  67.6 4.0 %state_part.1 = (bf16[512,1024]{1,0:T(8,128)(2,1)}, bf16[512,1024]{1,0:T(8,128)(2,1)}) custom-call(bf16[512,1024]{1,0:T(8,128)(2,1)} %refs_0_.3, bf16[512,1024]{1,0:T(8,128)(2,1)} %refs_1_.3, f32[1,8,128,128]{3,2,1,0:T(8,128)} %maximum_add_fusion.1.refs_2_, bf16[512,1024]{1,0:T(8,128)(2,1)} %get-tuple-element.27.refs_3_, ...), custom_call_target="tpu_custom_call" | custom-call | flops 536870912 | bytes 6291456 | tf_op jit(solution)/shard_map/state_part/pallas_call | solution.py:178
  (38 shorter events, 4.2 us)
Async XLA Ops:
  0.6 6.0 %copy-start.2 = (bf16[512,1024]{1,0:T(8,128)(2,1)S(1)}, bf16[512,1024]{1,0:T(8,128)(2,1)}, u32[]{:S(2)}) copy-start(bf16[512,1024]{1,0:T(8,128)(2,1)} %refs_1_.3) | copy-start | bytes 3145732
  0.6 26.8 %collective-permute-start = (bf16[512,1024]{1,0:T(8,128)(2,1)}, bf16[512,1024]{1,0:T(8,128)(2,1)}, u32[]{:S(2)}, u32[]{:S(2)}) collective-permute-start(bf16[512,1024]{1,0:T(8,128)(2,1)} %param.8), channel_id=1, source_target_pairs={{0,1},{1,0},{2,3},{3,2},{4,6},{5,7},{6,4},{7,5},{8,9},{9,8},{10,11... | collective-permute-start | bytes 3145736 | tf_op jit(solution)/shard_map/ppermute | solution.py:36
  3.6 29.5 %collective-permute-start.1 = (bf16[512,1024]{1,0:T(8,128)(2,1)}, bf16[512,1024]{1,0:T(8,128)(2,1)}, u32[]{:S(2)}, u32[]{:S(2)}) collective-permute-start(bf16[512,1024]{1,0:T(8,128)(2,1)} %param.8), channel_id=1, source_target_pairs={{0,2},{1,3},{2,0},{3,1},{4,5},{5,4},{6,7},{7,6},{8,10},{9,11},{10,... | collective-permute-start | bytes 3145736 | tf_op jit(solution)/shard_map/ppermute | solution.py:37
  7.8 4.6 %collective-permute-start.3 = (bf16[8,64,128]{2,1,0:T(8,128)(2,1)}, bf16[8,64,128]{2,1,0:T(8,128)(2,1)S(1)}, u32[]{:S(2)}, u32[]{:S(2)}) collective-permute-start(bf16[8,64,128]{2,1,0:T(8,128)(2,1)} %constant_dynamic-slice_fusion), channel_id=1, source_target_pairs={{0,4},{4,0},{8,12},{12,8},{16,20},{20,16},{24,28},{28,24},{1,5},{5... | collective-permute-start | bytes 393224 | tf_op jit(solution)/shard_map/ppermute | solution.py:53
  7.8 3.3 %copy-start = (bf16[512,1024]{1,0:T(8,128)(2,1)S(1)}, bf16[512,1024]{1,0:T(8,128)(2,1)}, u32[]{:S(2)}) copy-start(bf16[512,1024]{1,0:T(8,128)(2,1)} %refs_0_.2) | copy-start | bytes 3145732
  12.5 9.3 %collective-permute-start.4 = (bf16[8,64,128]{2,1,0:T(8,128)(2,1)S(1)}, bf16[8,64,128]{2,1,0:T(8,128)(2,1)S(1)}, u32[]{:S(2)}, u32[]{:S(2)}) collective-permute-start(bf16[8,64,128]{2,1,0:T(8,128)(2,1)S(1)} %get-tuple-element.33), channel_id=1, source_target_pairs={{0,8},{4,12},{8,16},{12,20},{16,24},{20,28},{1,9},{5,13},{9,17},{1... | collective-permute-start | bytes 393224 | tf_op jit(solution)/shard_map/ppermute | solution.py:75
  16.0 8.4 %collective-permute-start.5 = (bf16[8,64,128]{2,1,0:T(8,128)(2,1)S(1)}, bf16[8,64,128]{2,1,0:T(8,128)(2,1)S(1)}, u32[]{:S(2)}, u32[]{:S(2)}) collective-permute-start(bf16[8,64,128]{2,1,0:T(8,128)(2,1)S(1)} %get-tuple-element.33), channel_id=1, source_target_pairs={{0,16},{4,20},{8,24},{12,28},{1,17},{5,21},{9,25},{13,29},{2,18},{... | collective-permute-start | bytes 393224 | tf_op jit(solution)/shard_map/ppermute | solution.py:75
  20.5 6.0 %collective-permute-start.6 = (bf16[8,64,128]{2,1,0:T(8,128)(2,1)S(1)}, bf16[8,64,128]{2,1,0:T(8,128)(2,1)S(1)}, u32[]{:S(2)}, u32[]{:S(2)}) collective-permute-start(bf16[8,64,128]{2,1,0:T(8,128)(2,1)S(1)} %get-tuple-element.33), channel_id=1, source_target_pairs={{0,24},{4,28},{1,25},{5,29},{2,26},{6,30},{3,27},{7,31}} | collective-permute-start | bytes 393224 | tf_op jit(solution)/shard_map/ppermute | solution.py:75
  21.8 7.2 %collective-permute-start.8 = (bf16[8,64,128]{2,1,0:T(8,128)(2,1)S(1)}, bf16[8,64,128]{2,1,0:T(8,128)(2,1)S(1)}, u32[]{:S(2)}, u32[]{:S(2)}) collective-permute-start(bf16[8,64,128]{2,1,0:T(8,128)(2,1)S(1)} %get-tuple-element.34), channel_id=1, source_target_pairs={{0,4},{4,0},{8,12},{12,8},{16,20},{20,16},{24,28},{28,24},{1,5},{5... | collective-permute-start | bytes 393224 | tf_op jit(solution)/shard_map/ppermute | solution.py:57
  26.5 2.5 %collective-permute-start.7 = (bf16[8,64,128]{2,1,0:T(8,128)(2,1)S(1)}, bf16[8,64,128]{2,1,0:T(8,128)(2,1)S(1)}, u32[]{:S(2)}, u32[]{:S(2)}) collective-permute-start(bf16[8,64,128]{2,1,0:T(8,128)(2,1)S(1)} %fusion.22), channel_id=1, source_target_pairs={{0,4},{4,0},{8,12},{12,8},{16,20},{20,16},{24,28},{28,24},{1,5},{5... | collective-permute-start | bytes 393224 | tf_op jit(solution)/shard_map/ppermute | solution.py:88
  27.4 15.0 %collective-permute-start.2 = (bf16[512,1024]{1,0:T(8,128)(2,1)}, bf16[512,1024]{1,0:T(8,128)(2,1)S(1)}, u32[]{:S(2)}, u32[]{:S(2)}) collective-permute-start(bf16[512,1024]{1,0:T(8,128)(2,1)} %collective-permute-done), channel_id=1, source_target_pairs={{0,2},{1,3},{2,0},{3,1},{4,5},{5,4},{6,7},{7,6},{8,10},{9,11},{10,... | collective-permute-start | bytes 3145736 | tf_op jit(solution)/shard_map/ppermute | solution.py:38
  36.3 9.0 %copy-start.1 = (bf16[512,1024]{0,1:T(8,128)(2,1)S(1)}, bf16[512,1024]{0,1:T(8,128)(2,1)}, u32[]{:S(2)}) copy-start(bf16[512,1024]{0,1:T(8,128)(2,1)} %copy.19) | copy-start | bytes 3145732
  45.3 6.1 %copy-start.3 = (bf16[512,1024]{1,0:T(8,128)(2,1)}, bf16[512,1024]{1,0:T(8,128)(2,1)S(1)}, u32[]{:S(2)}) copy-start(bf16[512,1024]{1,0:T(8,128)(2,1)S(1)} %fusion.refs_3_) | copy-start | bytes 3145732
  45.8 1.4 %collective-permute-start.9 = (bf16[8,64,128]{2,1,0:T(8,128)(2,1)S(1)}, bf16[8,64,128]{2,1,0:T(8,128)(2,1)S(1)}, u32[]{:S(2)}, u32[]{:S(2)}) collective-permute-start(bf16[8,64,128]{2,1,0:T(8,128)(2,1)S(1)} %dynamic-slice_bitcast_fusion), channel_id=1, source_target_pairs={{0,4},{4,0},{8,12},{12,8},{16,20},{20,16},{24,28},{28,24},{1,5},{5... | collective-permute-start | bytes 393224 | tf_op jit(solution)/shard_map/ppermute | solution.py:53
  47.3 12.1 %collective-permute-start.10 = (bf16[8,64,128]{2,1,0:T(8,128)(2,1)S(1)}, bf16[8,64,128]{2,1,0:T(8,128)(2,1)S(1)}, u32[]{:S(2)}, u32[]{:S(2)}) collective-permute-start(bf16[8,64,128]{2,1,0:T(8,128)(2,1)S(1)} %get-tuple-element.19), channel_id=1, source_target_pairs={{8,0},{12,4},{16,8},{20,12},{24,16},{28,20},{9,1},{13,5},{17,9},{2... | collective-permute-start | bytes 393224 | tf_op jit(solution)/shard_map/ppermute | solution.py:75
  48.6 16.6 %collective-permute-start.11 = (bf16[8,64,128]{2,1,0:T(8,128)(2,1)S(1)}, bf16[8,64,128]{2,1,0:T(8,128)(2,1)S(1)}, u32[]{:S(2)}, u32[]{:S(2)}) collective-permute-start(bf16[8,64,128]{2,1,0:T(8,128)(2,1)S(1)} %get-tuple-element.19), channel_id=1, source_target_pairs={{16,0},{20,4},{24,8},{28,12},{17,1},{21,5},{25,9},{29,13},{18,2},{... | collective-permute-start | bytes 393224 | tf_op jit(solution)/shard_map/ppermute | solution.py:75
  49.9 15.3 %collective-permute-start.12 = (bf16[8,64,128]{2,1,0:T(8,128)(2,1)S(1)}, bf16[8,64,128]{2,1,0:T(8,128)(2,1)S(1)}, u32[]{:S(2)}, u32[]{:S(2)}) collective-permute-start(bf16[8,64,128]{2,1,0:T(8,128)(2,1)S(1)} %get-tuple-element.19), channel_id=1, source_target_pairs={{24,0},{28,4},{25,1},{29,5},{26,2},{30,6},{27,3},{31,7}} | collective-permute-start | bytes 393224 | tf_op jit(solution)/shard_map/ppermute | solution.py:75
  51.2 14.2 %collective-permute-start.14 = (bf16[8,64,128]{2,1,0:T(8,128)(2,1)S(1)}, bf16[8,64,128]{2,1,0:T(8,128)(2,1)S(1)}, u32[]{:S(2)}, u32[]{:S(2)}) collective-permute-start(bf16[8,64,128]{2,1,0:T(8,128)(2,1)S(1)} %get-tuple-element.32), channel_id=1, source_target_pairs={{0,4},{4,0},{8,12},{12,8},{16,20},{20,16},{24,28},{28,24},{1,5},{5... | collective-permute-start | bytes 393224 | tf_op jit(solution)/shard_map/ppermute | solution.py:57
  65.3 1.4 %collective-permute-start.13 = (bf16[8,64,128]{2,1,0:T(8,128)(2,1)S(1)}, bf16[8,64,128]{2,1,0:T(8,128)(2,1)S(1)}, u32[]{:S(2)}, u32[]{:S(2)}) collective-permute-start(bf16[8,64,128]{2,1,0:T(8,128)(2,1)S(1)} %convert_element_type.77), channel_id=1, source_target_pairs={{0,4},{4,0},{8,12},{12,8},{16,20},{20,16},{24,28},{28,24},{1,5},{5... | collective-permute-start | bytes 393224 | tf_op jit(solution)/shard_map/ppermute | solution.py:88
